TPU v7x, 32 devices: a whole 2x2x4 slice. The times are simulated.
32 devices in a mesh: region: 8 (over z, y), station: 4 (over x, core).
Axes of the slice: x: 2, y: 2, z: 4, core: 2. Of those that a mesh axis runs over, the one named last changes fastest.
Arguments:
- waveforms: bfloat16 [128, 16, 3, 512], P('region', 'station'), may hold values from -6 to 6
- pair_lists: int32 [3, 256, 2], P(None, 'region'), may hold values from 0 to 15
- pair_counts: int32 [3, 8], P(None, 'region'), may hold values from 1 to 32, as said below
Outputs:
- correlations: float32 [3, 256, 256], P(None, ('region', 'station'))
Inputs may be any that keep to these rules, and one draw needn't show every extreme that they name: `pair_counts`: in every round some region has all 32 slots live.
All inputs are finite; a program needn't handle non-finite values.
Results may differ from a plain program's by a relative error of at most 0.011.
Values may be sent and summed in bfloat16 or wider, within the bound.
No kernel may reach another device: no remote copies, remote signals or barrier semaphores. Data moves between devices by JAX's collectives and lax.ppermute only.
A program may use at most 64 MiB of HBM per device.

v0:
```python
import math

import jax
import jax.numpy as jnp
from jax import lax
from jax.sharding import PartitionSpec as P

STATIONS = 16
ROUNDS = 3


TWO_PI = 2.0 * math.pi
EPS = 1e-06


def swapped(block, axis, bit):
    count = lax.axis_size(axis)
    route = []
    for low in range(count):
        high = low | 1 << bit
        if high != low and high < count:
            route += [(low, high), (high, low)]
    return lax.ppermute(block, axis, route)


def forward_table(length):
    period = 2 * length
    times = jnp.arange(length, dtype=jnp.int32)[:, None]
    freqs = jnp.arange(period, dtype=jnp.int32)[None, :]
    angle = TWO_PI / period * (times * freqs % period).astype(jnp.float32)
    return jnp.concatenate([jnp.cos(angle), -jnp.sin(angle)], axis=1).astype(jnp.bfloat16)


def inverse_table(length, channels):
    period = 2 * length
    half = length // 2
    freqs = jnp.arange(period, dtype=jnp.int32)[:, None]
    lagged = jnp.arange(half, dtype=jnp.int32)[None, :] - half // 2
    angle = TWO_PI / period * (freqs * lagged % period).astype(jnp.float32)
    factor = 1.0 / (period * math.sqrt(channels * length))
    return (jnp.concatenate([jnp.cos(angle), -jnp.sin(angle)], axis=0) * factor).astype(
        jnp.bfloat16
    )


def spectra_of(block):
    events, stations, comps, length = block.shape
    traces = block.astype(jnp.float32)
    traces = traces - jnp.mean(traces, axis=-1, keepdims=True)
    traces = traces * lax.rsqrt(jnp.mean(traces * traces, axis=-1, keepdims=True) + EPS)
    traces = traces.astype(jnp.bfloat16).reshape(events * stations * comps, length)
    spec = jnp.dot(traces, forward_table(length), preferred_element_type=jnp.float32)
    return spec.astype(jnp.bfloat16).reshape(events, stations * comps, 4 * length)


def pair_curves(left, right, lag_table):
    slots, channels, width = left.shape
    period = width // 2
    left_real = left[:, :, :period]
    left_imag = left[:, :, period:]
    right_real = right[:, :, :period]
    right_imag = right[:, :, period:]
    real_part = jnp.einsum("pck,pck->pk", left_real, right_real, preferred_element_type=jnp.float32)
    real_part = real_part + jnp.einsum(
        "pck,pck->pk", left_imag, right_imag, preferred_element_type=jnp.float32
    )
    imag_part = jnp.einsum("pck,pck->pk", left_real, right_imag, preferred_element_type=jnp.float32)
    imag_part = imag_part - jnp.einsum(
        "pck,pck->pk", left_imag, right_real, preferred_element_type=jnp.float32
    )
    cross = jnp.concatenate([real_part, imag_part], axis=-1).astype(jnp.bfloat16)
    return jnp.dot(cross, lag_table, preferred_element_type=jnp.float32)


def fetch_waves(waveforms, bit_index):
    return swapped(waveforms, "region", bit_index)


def shards(waveforms, pair_lists, pair_counts):
    local_spec = spectra_of(waveforms)
    length = waveforms.shape[-1]
    lag_table = inverse_table(length, STATIONS * waveforms.shape[2])
    groups = lax.axis_size("station")
    share = pair_lists.shape[1] // groups
    sequence = list(range(ROUNDS))
    results = [None] * ROUNDS
    for round_index in sequence:
        partner_spec = spectra_of(fetch_waves(waveforms, round_index))
        slot_table = pair_lists[round_index]
        live_count = pair_counts[round_index, 0]

        def curve_term(
            start,
            count_rows,
            slot_table=slot_table,
            live_count=live_count,
            partner_spec=partner_spec,
        ):
            left = jnp.take(local_spec, slot_table[:, 0], axis=0)
            right = jnp.take(partner_spec, slot_table[:, 1], axis=0)
            curves = pair_curves(left, right, lag_table)
            live = jnp.arange(count_rows, dtype=jnp.int32) < live_count
            return jnp.where(live[:, None], curves, jnp.zeros_like(curves))

        results[round_index] = lax.psum_scatter(
            curve_term(jnp.int32(0), share * lax.axis_size("station")).astype(jnp.bfloat16),
            "station",
            scatter_dimension=0,
            tiled=True,
        ).astype(jnp.float32)
    return jnp.stack(results)


def solution(mesh):
    return jax.shard_map(
        shards,
        mesh=mesh,
        in_specs=(P("region", "station", None, None), P(None, "region", None), P(None, "region")),
        out_specs=P(None, ("region", "station"), None),
        check_vma=False,
    )
```

profile of v0, /device:TPU:0, one launch (start us, length us, event | category | flops | bytes accessed | tf_op | source)
XLA Modules:
  0.0 130.8 jit_solution(2226328792048933461)
XLA Ops:
  6.5 3.0 %collective-permute-start = (bf16[16,4,3,512]{3,1,2,0:T(4,128)(2,1)}, bf16[16,4,3,512]{3,1,2,0:T(4,128)(2,1)}, u32[]{:S(2)}, u32[]{:S(2)}) collective-permute-start(bf16[16,4,3,512]{3,1,2,0:T(4,128)(2,1)} %param.5), channel_id=1, source_target_pairs={{0,4},{4,0},{8,12},{12,8},{16,20},{20,16},{24,28},{28,24},{1,5},{5... | collective-permute-start | bytes 589832 | tf_op jit(solution)/shard_map/ppermute | solution.py:23
  9.5 1.6 %collective-permute-start.1 = (bf16[16,4,3,512]{3,1,2,0:T(4,128)(2,1)}, bf16[16,4,3,512]{3,1,2,0:T(4,128)(2,1)}, u32[]{:S(2)}, u32[]{:S(2)}) collective-permute-start(bf16[16,4,3,512]{3,1,2,0:T(4,128)(2,1)} %param.5), channel_id=1, source_target_pairs={{0,8},{8,0},{4,12},{12,4},{16,24},{24,16},{20,28},{28,20},{1,9},{9... | collective-permute-start | bytes 589832 | tf_op jit(solution)/shard_map/ppermute | solution.py:23
  11.1 2.6 %collective-permute-start.2 = (bf16[16,4,3,512]{3,1,2,0:T(4,128)(2,1)}, bf16[16,4,3,512]{3,1,2,0:T(4,128)(2,1)S(1)}, u32[]{:S(2)}, u32[]{:S(2)}) collective-permute-start(bf16[16,4,3,512]{3,1,2,0:T(4,128)(2,1)} %param.5), channel_id=1, source_target_pairs={{0,16},{16,0},{4,20},{20,4},{8,24},{24,8},{12,28},{28,12},{1,17},{... | collective-permute-start | bytes 589832 | tf_op jit(solution)/shard_map/ppermute | solution.py:23
  13.7 8.5 %negate_convert_fusion = (bf16[512,1024]{1,0:T(8,128)(2,1)S(1)}, bf16[512,1024]{1,0:T(8,128)(2,1)S(1)}) fusion(), kind=kLoop, calls=%fused_computation.43 | loop fusion | flops 8912896 | bytes 2097152 | tf_op jit(solution)/shard_map/convert.11
  22.2 0.2 convert_reduce_fusion.3
  22.4 0.7 iota_add_fusion
  23.1 0.6 compare_and_fusion.4
  23.8 0.3 fusion.43
  24.1 0.2 fusion.44
  24.4 0.2 reshape.94
  24.6 0.6 convolution_convert_fusion.3
  25.2 0.2 reshape.95
  25.4 0.6 fusion.60
  25.9 1.2 iota_compare_fusion.2
  27.1 0.5 compare_and_fusion
  27.7 0.7 pad_clamp_fusion.4
  28.3 2.0 %gather_fusion = bf16[32,12,2048]{2,1,0:T(8,128)(2,1)} fusion(bf16[16,12,2048]{2,1,0:T(8,128)(2,1)S(1)} %reshape.95, s32[1024]{0:T(1024)S(1)} %get-tuple-element.51), kind=kCustom, calls=%fused_computation.clone | custom fusion | bytes 3145856 | tf_op jit(solution)/shard_map/jit(_take)/gather | solution.py:99
  30.3 0.7 gather_fusion.2
  31.0 1.2 iota_compare_fusion.1
  32.2 2.0 %gather_fusion.4 = bf16[32,12,2048]{2,1,0:T(8,128)(2,1)} fusion(bf16[16,12,2048]{2,1,0:T(8,128)(2,1)S(1)} %reshape.95, s32[1024]{0:T(1024)S(1)} %pad_clamp_fusion.1), kind=kCustom, calls=%fused_computation.4.clone | custom fusion | bytes 3145856 | tf_op jit(solution)/shard_map/jit(_take)/gather | solution.py:99
  34.2 1.1 iota_compare_fusion
  35.3 3.2 %broadcast_select_fusion.5 = bf16[32,12,2048]{2,1,0:T(8,128)(2,1)} fusion(bf16[32,12,2048]{2,1,0:T(8,128)(2,1)} %gather_fusion, pred[32]{0:T(512)(128)(4,1)S(1)} %copy-done.16), kind=kLoop, calls=%fused_computation.53 | loop fusion | flops 786432 | bytes 3145760 | tf_op jit(solution)/shard_map/jit(_take)/select_n | solution.py:99
  38.5 1.6 %broadcast_select_fusion.3 = bf16[32,12,2048]{2,1,0:T(8,128)(2,1)} fusion(bf16[32,12,2048]{2,1,0:T(8,128)(2,1)S(1)} %gather_fusion.2, pred[32]{0:T(512)(128)(4,1)S(1)} %get-tuple-element.46), kind=kLoop, calls=%fused_computation.51 | loop fusion | flops 786432 | bytes 3145760 | tf_op jit(solution)/shard_map/jit(_take)/select_n | solution.py:99
  40.1 0.7 copy-done.2
  40.8 0.3 broadcast_select_fusion.1
  41.1 0.4 copy-done.17
  41.5 5.1 %fusion.28 = (f32[1024,256]{1,0:T(8,128)}, f32[1024,256]{1,0:T(8,128)}) fusion(s32[256]{0:T(256)S(1)} %copy-done.17), kind=kLoop, calls=%fused_computation.82 | loop fusion | flops 3932160 | bytes 2098176 | tf_op jit(solution)/shard_map/cos | solution.py:41
  46.6 1.1 convert_reduce_fusion.2
  47.7 1.2 fusion.41
  48.9 1.1 fusion.42
  50.2 0.2 reshape.96
  50.4 3.0 %convolution_convert_fusion.2 = bf16[192,2048]{1,0:T(8,128)(2,1)} fusion(bf16[192,512]{1,0:T(8,128)(2,1)S(1)} %reshape.96, bf16[512,1024]{1,0:T(8,128)(2,1)} %copy-done.4, bf16[512,1024]{1,0:T(8,128)(2,1)} %copy-done.5), kind=kOutput, calls=%fused_computation.23 | convolution fusion | flops 407240704 | bytes 3080192 | tf_op jit(solution)/shard_map/dot_general | solution.py:52
  53.4 1.3 reshape.97
  54.7 2.0 %gather_fusion.1 = bf16[32,12,2048]{2,1,0:T(8,128)(2,1)} fusion(bf16[16,12,2048]{2,1,0:T(8,128)(2,1)S(1)} %reshape.97, s32[1024]{0:T(1024)S(1)} %get-tuple-element.50), kind=kCustom, calls=%fused_computation.1.clone | custom fusion | bytes 3145856 | tf_op jit(solution)/shard_map/jit(_take)/gather | solution.py:100
  56.6 2.0 %broadcast_select_fusion.4 = bf16[32,12,2048]{2,1,0:T(8,128)(2,1)S(1)} fusion(bf16[32,12,2048]{2,1,0:T(8,128)(2,1)} %gather_fusion.1, pred[32]{0:T(512)(128)(4,1)S(1)} %copy-done.15), kind=kLoop, calls=%fused_computation.52 | loop fusion | flops 786432 | bytes 3145760 | tf_op jit(solution)/shard_map/jit(_take)/select_n | solution.py:100
  58.6 0.2 copy-done.1
  58.9 2.2 %fusion.2 = (f32[32,1024]{1,0:T(8,128)S(1)}, f32[32,1024]{1,0:T(8,128)S(1)}, f32[32,1024]{1,0:T(8,128)S(1)}, f32[32,1024]{1,0:T(8,128)S(1)}) fusion(bf16[32,12,2048]{2,1,0:T(8,128)(2,1)S(1)} %copy-done.1, bf16[32,12,2048]{2,1,0:T(8,128)(2,1)S(1)} %broadcast_select_fusion.4), kind=kLoop, calls=%fused_computation.27 | loop fusion | flops 4587520 | bytes 3670016 | tf_op jit(solution)/shard_map/pck,pck->pk/dot_general | solution.py:64
  61.1 0.9 fusion.19
  62.1 0.2 reduce-scatter.6.cloned.1.call-start
  62.3 1.1 convert_reduce_fusion.1
  63.4 1.2 fusion.39
  64.6 1.1 fusion.40
  65.9 0.2 reshape.98
  66.1 3.1 %convolution_convert_fusion.1 = bf16[192,2048]{1,0:T(8,128)(2,1)} fusion(bf16[192,512]{1,0:T(8,128)(2,1)S(1)} %reshape.98, bf16[512,1024]{1,0:T(8,128)(2,1)} %copy-done.4, bf16[512,1024]{1,0:T(8,128)(2,1)} %copy-done.5), kind=kOutput, calls=%fused_computation.22 | convolution fusion | flops 407240704 | bytes 3080192 | tf_op jit(solution)/shard_map/dot_general | solution.py:52
  69.1 1.3 reshape.99
  70.4 0.2 convert_reduce_fusion
  70.6 0.3 fusion.37
  70.9 0.2 fusion.38
  71.1 0.1 copy.7
  71.2 0.9 reshape.100
  72.1 3.1 %convolution_convert_fusion = bf16[192,2048]{1,0:T(8,128)(2,1)} fusion(bf16[192,512]{1,0:T(8,128)(2,1)} %reshape.100, bf16[512,1024]{1,0:T(8,128)(2,1)} %copy-done.4, bf16[512,1024]{1,0:T(8,128)(2,1)} %copy-done.5), kind=kOutput, calls=%fused_computation.21 | convolution fusion | flops 407240704 | bytes 3080192 | tf_op jit(solution)/shard_map/dot_general | solution.py:52
  75.2 2.0 %gather_fusion.3 = bf16[32,12,2048]{2,1,0:T(8,128)(2,1)} fusion(bf16[16,12,2048]{2,1,0:T(8,128)(2,1)S(1)} %reshape.99, s32[1024]{0:T(1024)S(1)} %pad_clamp_fusion.2), kind=kCustom, calls=%fused_computation.3.clone | custom fusion | bytes 3145856 | tf_op jit(solution)/shard_map/jit(_take)/gather | solution.py:100
  77.2 2.0 %broadcast_select_fusion.2 = bf16[32,12,2048]{2,1,0:T(8,128)(2,1)S(1)} fusion(bf16[32,12,2048]{2,1,0:T(8,128)(2,1)} %gather_fusion.3, pred[32]{0:T(512)(128)(4,1)S(1)} %copy-done.14), kind=kLoop, calls=%fused_computation.50 | loop fusion | flops 786432 | bytes 3145760 | tf_op jit(solution)/shard_map/jit(_take)/select_n | solution.py:100
  79.2 0.2 copy-done
  79.4 2.2 %fusion.6 = (f32[32,1024]{1,0:T(8,128)S(1)}, f32[32,1024]{1,0:T(8,128)S(1)}, f32[32,1024]{1,0:T(8,128)S(1)}, f32[32,1024]{1,0:T(8,128)S(1)}) fusion(bf16[32,12,2048]{2,1,0:T(8,128)(2,1)S(1)} %copy-done, bf16[32,12,2048]{2,1,0:T(8,128)(2,1)S(1)} %broadcast_select_fusion.2), kind=kLoop, calls=%fused_computation.31 | loop fusion | flops 4587520 | bytes 3670016 | tf_op jit(solution)/shard_map/pck,pck->pk/dot_general | solution.py:64
  81.7 0.9 fusion.20
  82.6 1.3 reshape.101
  83.9 2.0 %gather_fusion.5 = bf16[32,12,2048]{2,1,0:T(8,128)(2,1)} fusion(bf16[16,12,2048]{2,1,0:T(8,128)(2,1)S(1)} %reshape.101, s32[1024]{0:T(1024)S(1)} %pad_clamp_fusion), kind=kCustom, calls=%fused_computation.5.clone | custom fusion | bytes 3145856 | tf_op jit(solution)/shard_map/jit(_take)/gather | solution.py:100
  86.0 1.8 %broadcast_select_fusion = bf16[32,12,2048]{2,1,0:T(8,128)(2,1)S(1)} fusion(bf16[32,12,2048]{2,1,0:T(8,128)(2,1)} %gather_fusion.5, pred[32]{0:T(512)(128)(4,1)S(1)} %get-tuple-element.26), kind=kLoop, calls=%fused_computation.48 | loop fusion | flops 786432 | bytes 3145760 | tf_op jit(solution)/shard_map/jit(_take)/select_n | solution.py:100
  87.8 2.2 %fusion.10 = (f32[32,1024]{1,0:T(8,128)S(1)}, f32[32,1024]{1,0:T(8,128)S(1)}, f32[32,1024]{1,0:T(8,128)S(1)}, f32[32,1024]{1,0:T(8,128)S(1)}) fusion(bf16[32,12,2048]{2,1,0:T(8,128)(2,1)S(1)} %broadcast_select_fusion.1, bf16[32,12,2048]{2,1,0:T(8,128)(2,1)S(1)} %broadcast_select_fusion), kind=kLoop, calls=%fused_computation.35 | loop fusion | flops 4587520 | bytes 3670016 | tf_op jit(solution)/shard_map/pck,pck->pk/dot_general | solution.py:64
  90.1 0.9 fusion.21
  91.0 9.9 %reduce-scatter.6.cloned.1.call-done = bf16[8,256]{1,0:T(8,128)(2,1)} async-done(((bf16[32,256]{1,0:T(8,128)(2,1)}), bf16[8,256]{1,0:T(8,128)(2,1)}) %reduce-scatter.6.cloned.1.call-update) | async-done | bytes 4112 | tf_op jit(solution)/shard_map/reduce_scatter | solution.py:105
  101.0 22.0 %reduce-scatter.8.cloned.1.call-done = bf16[8,256]{1,0:T(8,128)(2,1)} async-done(((bf16[32,256]{1,0:T(8,128)(2,1)}), bf16[8,256]{1,0:T(8,128)(2,1)}) %reduce-scatter.8.cloned.1.call-update) | async-done | bytes 4112 | tf_op jit(solution)/shard_map/reduce_scatter | solution.py:105
  122.9 1.3 %maximum_convert_fusion = f32[3,8,256]{2,1,0:T(8,128)} fusion(bf16[1,8,256]{2,1,0:T(8,128)(2,1)} %bitcast.120, bf16[1,8,256]{2,1,0:T(8,128)(2,1)} %bitcast.119, bf16[1,8,256]{2,1,0:T(8,128)(2,1)} %bitcast.118), kind=kLoop, calls=%fused_computation.130 | loop fusion | flops 18432 | bytes 36864 | tf_op jit(solution)/shard_map/stack | solution.py:111
  (69 shorter events, 0.8 us)
Async XLA Ops:
  6.5 15.7 %copy-start.3 = (bf16[16,4,3,512]{3,1,2,0:T(4,128)(2,1)S(1)}, bf16[16,4,3,512]{3,1,2,0:T(4,128)(2,1)}, u32[]{:S(2)}) copy-start(bf16[16,4,3,512]{3,1,2,0:T(4,128)(2,1)} %param.5) | copy-start | bytes 589828
  6.5 16.6 %copy-start.13 = (s32[3,32,2]{1,2,0:T(2,128)S(1)}, s32[3,32,2]{1,2,0:T(2,128)}, u32[]{:S(2)}) copy-start(s32[3,32,2]{1,2,0:T(2,128)} %param.6) | copy-start | bytes 2308
  6.5 84.5 %reduce-scatter.4.cloned.1.call-start = ((), (), s32[]{:S(2)}) async-start(), calls=%async_computation.3 | async-start | bytes 20480 | tf_op jit(solution)/shard_map/reduce_scatter | solution.py:105
  6.5 40.0 %collective-permute-start = (bf16[16,4,3,512]{3,1,2,0:T(4,128)(2,1)}, bf16[16,4,3,512]{3,1,2,0:T(4,128)(2,1)}, u32[]{:S(2)}, u32[]{:S(2)}) collective-permute-start(bf16[16,4,3,512]{3,1,2,0:T(4,128)(2,1)} %param.5), channel_id=1, source_target_pairs={{0,4},{4,0},{8,12},{12,8},{16,20},{20,16},{24,28},{28,24},{1,5},{5... | collective-permute-start | bytes 589832 | tf_op jit(solution)/shard_map/ppermute | solution.py:23
  9.5 52.8 %collective-permute-start.1 = (bf16[16,4,3,512]{3,1,2,0:T(4,128)(2,1)}, bf16[16,4,3,512]{3,1,2,0:T(4,128)(2,1)}, u32[]{:S(2)}, u32[]{:S(2)}) collective-permute-start(bf16[16,4,3,512]{3,1,2,0:T(4,128)(2,1)} %param.5), channel_id=1, source_target_pairs={{0,8},{8,0},{4,12},{12,4},{16,24},{24,16},{20,28},{28,20},{1,9},{9... | collective-permute-start | bytes 589832 | tf_op jit(solution)/shard_map/ppermute | solution.py:23
  11.1 59.3 %collective-permute-start.2 = (bf16[16,4,3,512]{3,1,2,0:T(4,128)(2,1)}, bf16[16,4,3,512]{3,1,2,0:T(4,128)(2,1)S(1)}, u32[]{:S(2)}, u32[]{:S(2)}) collective-permute-start(bf16[16,4,3,512]{3,1,2,0:T(4,128)(2,1)} %param.5), channel_id=1, source_target_pairs={{0,16},{16,0},{4,20},{20,4},{8,24},{24,8},{12,28},{28,12},{1,17},{... | collective-permute-start | bytes 589832 | tf_op jit(solution)/shard_map/ppermute | solution.py:23
  22.2 2.3 %copy-start.4 = (bf16[512,1024]{1,0:T(8,128)(2,1)}, bf16[512,1024]{1,0:T(8,128)(2,1)S(1)}, u32[]{:S(2)}) copy-start(bf16[512,1024]{1,0:T(8,128)(2,1)S(1)} %get-tuple-element.44) | copy-start | bytes 3145732
  22.2 2.9 %copy-start.5 = (bf16[512,1024]{1,0:T(8,128)(2,1)}, bf16[512,1024]{1,0:T(8,128)(2,1)S(1)}, u32[]{:S(2)}) copy-start(bf16[512,1024]{1,0:T(8,128)(2,1)S(1)} %get-tuple-element.45) | copy-start | bytes 3145732
  24.6 0.8 copy-start.12
  32.2 3.1 %copy-start.16 = (pred[32]{0:T(512)(128)(4,1)S(1)}, pred[32]{0:T(512)(128)(4,1)}, u32[]{:S(2)}) copy-start(pred[32]{0:T(512)(128)(4,1)} %get-tuple-element.33) | copy-start | bytes 100
  38.4 2.3 %copy-start.2 = (bf16[32,12,2048]{2,1,0:T(8,128)(2,1)S(1)}, bf16[32,12,2048]{2,1,0:T(8,128)(2,1)}, u32[]{:S(2)}) copy-start(bf16[32,12,2048]{2,1,0:T(8,128)(2,1)} %gather_fusion.4) | copy-start | bytes 4718596
  40.8 0.7 copy-start.17
  54.7 2.0 %copy-start.15 = (pred[32]{0:T(512)(128)(4,1)S(1)}, pred[32]{0:T(512)(128)(4,1)}, u32[]{:S(2)}) copy-start(pred[32]{0:T(512)(128)(4,1)} %get-tuple-element.18) | copy-start | bytes 100
  56.6 2.2 %copy-start.1 = (bf16[32,12,2048]{2,1,0:T(8,128)(2,1)S(1)}, bf16[32,12,2048]{2,1,0:T(8,128)(2,1)}, u32[]{:S(2)}) copy-start(bf16[32,12,2048]{2,1,0:T(8,128)(2,1)} %broadcast_select_fusion.5) | copy-start | bytes 4718596
  58.9 2.2 %copy-start.6 = (f32[1024,256]{1,0:T(8,128)S(1)}, f32[1024,256]{1,0:T(8,128)}, u32[]{:S(2)}) copy-start(f32[1024,256]{1,0:T(8,128)} %get-tuple-element.37) | copy-start | bytes 3145732
  58.9 2.3 %copy-start.9 = (f32[1024,256]{1,0:T(8,128)S(1)}, f32[1024,256]{1,0:T(8,128)}, u32[]{:S(2)}) copy-start(f32[1024,256]{1,0:T(8,128)} %get-tuple-element.38) | copy-start | bytes 3145732
  58.9 2.3 %copy-start.20 = (pred[32]{0:T(512)(128)(4,1)S(1)}, pred[32]{0:T(512)(128)(4,1)}, u32[]{:S(2)}) copy-start(pred[32]{0:T(512)(128)(4,1)} %iota_compare_fusion.2) | copy-start | bytes 100
  62.1 38.9 %reduce-scatter.6.cloned.1.call-start = ((), (), s32[]{:S(2)}) async-start(), calls=%async_computation.4 | async-start | bytes 20480 | tf_op jit(solution)/shard_map/reduce_scatter | solution.py:105
  75.2 2.0 %copy-start.14 = (pred[32]{0:T(512)(128)(4,1)S(1)}, pred[32]{0:T(512)(128)(4,1)}, u32[]{:S(2)}) copy-start(pred[32]{0:T(512)(128)(4,1)} %get-tuple-element.48) | copy-start | bytes 100
  77.2 2.2 %copy-start = (bf16[32,12,2048]{2,1,0:T(8,128)(2,1)S(1)}, bf16[32,12,2048]{2,1,0:T(8,128)(2,1)}, u32[]{:S(2)}) copy-start(bf16[32,12,2048]{2,1,0:T(8,128)(2,1)} %broadcast_select_fusion.3) | copy-start | bytes 4718596
  79.4 2.3 %copy-start.7 = (f32[1024,256]{1,0:T(8,128)S(1)}, f32[1024,256]{1,0:T(8,128)}, u32[]{:S(2)}) copy-start(f32[1024,256]{1,0:T(8,128)} %get-tuple-element.37) | copy-start | bytes 3145732
  79.4 2.3 %copy-start.10 = (f32[1024,256]{1,0:T(8,128)S(1)}, f32[1024,256]{1,0:T(8,128)}, u32[]{:S(2)}) copy-start(f32[1024,256]{1,0:T(8,128)} %get-tuple-element.38) | copy-start | bytes 3145732
  79.4 2.3 %copy-start.19 = (pred[32]{0:T(512)(128)(4,1)S(1)}, pred[32]{0:T(512)(128)(4,1)}, u32[]{:S(2)}) copy-start(pred[32]{0:T(512)(128)(4,1)} %iota_compare_fusion.1) | copy-start | bytes 100
  83.9 39.0 %reduce-scatter.8.cloned.1.call-start = ((), (), s32[]{:S(2)}) async-start(), calls=%async_computation.5 | async-start | bytes 20480 | tf_op jit(solution)/shard_map/reduce_scatter | solution.py:105
  87.8 2.2 %copy-start.8 = (f32[1024,256]{1,0:T(8,128)S(1)}, f32[1024,256]{1,0:T(8,128)}, u32[]{:S(2)}) copy-start(f32[1024,256]{1,0:T(8,128)} %get-tuple-element.37) | copy-start | bytes 3145732
  87.8 2.2 %copy-start.11 = (f32[1024,256]{1,0:T(8,128)S(1)}, f32[1024,256]{1,0:T(8,128)}, u32[]{:S(2)}) copy-start(f32[1024,256]{1,0:T(8,128)} %get-tuple-element.38) | copy-start | bytes 3145732
  87.8 2.2 %copy-start.18 = (pred[32]{0:T(512)(128)(4,1)S(1)}, pred[32]{0:T(512)(128)(4,1)}, u32[]{:S(2)}) copy-start(pred[32]{0:T(512)(128)(4,1)} %iota_compare_fusion) | copy-start | bytes 100
Sparse Core Ops, SparseCore 0:
  62.2 16.8 reduce-scatter.3
  84.0 16.9 reduce-scatter.5
  103.4 19.4 reduce-scatter.7
where the time goes:
time: 131 us
  other arithmetic  46.6 us (36%)
  waiting for transfers between devices  32 us (24%)
  local copies, waits for them, and re-layouts  18.7 us (14%)
  between operations  13.6 us (10%)
  matrix products  12.5 us (10%)
  starting transfers between devices  7.43 us (6%)
    reduce_scatter x3, waiting for transfers between devices, shards(): lax.psum_scatter(curve_term(jnp.int32(0), share * lax.axis_size('station'...  31.9 us
    dot_general x4, matrix products, spectra_of(): jnp.dot(traces, forward_table(length), preferred_element_type=jnp.float32)  9.79 us
    another operation x7, other arithmetic  8.6 us
    ppermute x3, starting transfers between devices, swapped(): return lax.ppermute(block, axis, route)  7.16 us
    dot_general x3, other arithmetic, pair_curves(): jnp.einsum('pck,pck->pk', left_imag, right_imag, preferred_element_type=j...  6.54 us
    gather x3, local copies, waits for them, and re-layouts, curve_term(): right = jnp.take(partner_spec, slot_table[:, 1], axis=0)  5.98 us
    select_n x3, other arithmetic, curve_term(): right = jnp.take(partner_spec, slot_table[:, 1], axis=0)  5.83 us
    cos x1, other arithmetic, inverse_table(): jnp.cos(angle)  5.1 us
  transfers between devices with their start and end apart: 6, of which 2 were waited for; matrix products, arithmetic and copies ran while one was open for 57% of the time, Pallas kernels for 0%

commit v1 on v0

v1 whole, which is shorter than its diff:
```python
import math

import ml_dtypes
import numpy as np

import jax
import jax.numpy as jnp
from jax import lax
from jax.experimental import pallas as pl
from jax.experimental.pallas import tpu as pltpu
from jax.sharding import PartitionSpec as P

EPS = 1e-06
LAGS = 256


def swapped(block, axis, bit):
    count = lax.axis_size(axis)
    route = []
    for low in range(count):
        high = low | 1 << bit
        if high != low and high < count:
            route += [(low, high), (high, low)]
    return lax.ppermute(block, axis, route)


def half_tables(length, channels, lags):
    period = 2 * length
    half = period // 2
    step = np.float32(2.0 * math.pi / period)
    times = np.arange(length, dtype=np.int64)[:, None]
    freqs = np.arange(half, dtype=np.int64)[None, :]
    angle = step * ((times * freqs) % period).astype(np.float32)
    fwd = np.concatenate([np.cos(angle), -np.sin(angle)], axis=1).astype(np.float32)
    fwd[:, half] = np.where(times[:, 0] % 2 == 0, 1.0, -1.0)
    fwd = fwd.astype(ml_dtypes.bfloat16)

    factor = np.float32(1.0 / (period * math.sqrt(channels * length)))
    rows = np.arange(half, dtype=np.int64)[:, None]
    lagged = np.arange(lags, dtype=np.int64)[None, :] - lags // 2
    angle = step * ((rows * lagged) % period).astype(np.float32)
    cos_t = (np.cos(angle).astype(np.float32) * factor).astype(ml_dtypes.bfloat16).astype(np.float32)
    sin_t = ((-np.sin(angle)).astype(np.float32) * factor).astype(ml_dtypes.bfloat16).astype(np.float32)
    inv = np.zeros((period, lags), np.float32)
    inv[0] = cos_t[0]
    inv[1:half] = 2.0 * cos_t[1:]
    nyq_angle = step * ((half * lagged[0]) % period).astype(np.float32)
    inv[half] = (np.cos(nyq_angle).astype(np.float32) * factor).astype(ml_dtypes.bfloat16).astype(np.float32)
    inv[half + 1:] = 2.0 * sin_t[1:]
    return fwd, inv.astype(ml_dtypes.bfloat16)


def make_round_kernel(events, chans, pad, length, slots, groups, share):
    half = length

    def kernel(pl_ref, cnt_ref, sid_ref, wl_ref, wp_ref, f_ref, g_ref, out_ref,
               nscr, xpad, specl, specp, cross):
        xpad[...] = jnp.zeros(xpad.shape, jnp.float32)

        def spectra(w_ref, spec_ref):
            x = w_ref[...].astype(jnp.float32)
            x = x - jnp.mean(x, axis=-1, keepdims=True)
            x = x * lax.rsqrt(jnp.mean(x * x, axis=-1, keepdims=True) + EPS)
            nscr[...] = x
            for e in range(events):
                xpad[e * pad:e * pad + chans, :] = nscr[e * chans:(e + 1) * chans, :]
            xb = xpad[...].astype(jnp.bfloat16)
            spec = jnp.dot(xb, f_ref[...], preferred_element_type=jnp.float32)
            spec_ref[...] = spec.astype(jnp.bfloat16).astype(jnp.float32)

        spectra(wl_ref, specl)
        spectra(wp_ref, specp)

        sid = sid_ref[0]
        lane = lax.broadcasted_iota(jnp.int32, (1, 128), 1)
        for r in range(slots):
            d, ip = divmod(r, share)
            slot = ((sid + d) % groups) * share + ip
            a = jnp.minimum(jnp.maximum(pl_ref[2 * slot], 0), events - 1)
            b = jnp.minimum(jnp.maximum(pl_ref[2 * slot + 1], 0), events - 1)
            left = specl[pl.ds(pl.multiple_of(a * pad, pad), pad), :]
            right = specp[pl.ds(pl.multiple_of(b * pad, pad), pad), :]
            lr, li = left[:, :half], left[:, half:]
            rr, ri = right[:, :half], right[:, half:]
            pp = lr * rr
            qq = li * ri
            re = jnp.sum(pp + qq, axis=0, keepdims=True)
            im = jnp.sum(lr * ri - li * rr, axis=0, keepdims=True)
            p0 = jnp.sum(pp[:, :128], axis=0, keepdims=True)
            q0 = jnp.sum(qq[:, :128], axis=0, keepdims=True)
            cross[r:r + 1, 0:128] = jnp.where(lane == 0, p0, re[:, :128])
            cross[r:r + 1, 128:half] = re[:, 128:]
            cross[r:r + 1, half:half + 128] = jnp.where(lane == 0, q0, im[:, :128])
            cross[r:r + 1, half + 128:] = im[:, 128:]

        cb = cross[...].astype(jnp.bfloat16)
        corr = jnp.dot(cb, g_ref[...], preferred_element_type=jnp.float32)
        rows = lax.broadcasted_iota(jnp.int32, corr.shape, 0)
        slot_of = ((sid + rows // share) % groups) * share + rows % share
        out_ref[...] = jnp.where(slot_of < cnt_ref[0], corr, 0.0)

    return kernel


def round_call(pairs, count, sid, local, partner, fwd, inv, events, chans, slots, groups):
    length = fwd.shape[0]
    pad = 16
    share = slots // groups
    kernel = make_round_kernel(events, chans, pad, length, slots, groups, share)
    smem = pl.BlockSpec(memory_space=pltpu.SMEM)
    vmem = pl.BlockSpec(memory_space=pltpu.VMEM)
    return pl.pallas_call(
        kernel,
        out_shape=jax.ShapeDtypeStruct((slots, inv.shape[1]), jnp.float32),
        in_specs=[smem, smem, smem, vmem, vmem, vmem, vmem],
        out_specs=vmem,
        scratch_shapes=[
            pltpu.VMEM((events * chans, length), jnp.float32),
            pltpu.VMEM((events * pad, length), jnp.float32),
            pltpu.VMEM((events * pad, 2 * length), jnp.float32),
            pltpu.VMEM((events * pad, 2 * length), jnp.float32),
            pltpu.VMEM((slots, 2 * length), jnp.float32),
        ],
    )(pairs, count, sid, local, partner, fwd, inv)


def shards(waveforms, pair_lists, pair_counts):
    events, stations, comps, length = waveforms.shape
    groups = lax.axis_size("station")
    rounds, slots, _ = pair_lists.shape
    chans = stations * comps
    fwd_np, inv_np = half_tables(length, stations * groups * comps, LAGS)
    fwd = jnp.asarray(fwd_np)
    inv = jnp.asarray(inv_np)
    flat = waveforms.reshape(events * chans, length)
    sid = lax.axis_index("station").astype(jnp.int32).reshape(1)
    share = slots // groups
    outs = []
    for q in range(rounds):
        partner = swapped(flat, "region", q)
        outs.append(
            round_call(pair_lists[q].reshape(-1), pair_counts[q], sid, flat, partner, fwd, inv,
                       events, chans, slots, groups)
        )
    stacked = jnp.stack(outs).reshape(rounds, groups, share, LAGS)
    total = stacked[:, 0]
    for d in range(1, groups):
        perm = [(s, (s + d) % groups) for s in range(groups)]
        got = lax.ppermute(stacked[:, d].astype(jnp.bfloat16), "station", perm)
        total = total + got.astype(jnp.float32)
    return total


def solution(mesh):
    return jax.shard_map(
        shards,
        mesh=mesh,
        in_specs=(P("region", "station", None, None), P(None, "region", None), P(None, "region")),
        out_specs=P(None, ("region", "station"), None),
        check_vma=False,
    )
```

time: 131 us -> 37.7 us (0.29)
  other arithmetic: 46.6 us -> 1.39 us
  waiting for transfers between devices: 32 us -> 5.47 us
  Pallas kernels: 0 us -> 13.8 us
  between operations: 13.6 us -> 0.09 us
  local copies, waits for them, and re-layouts: 18.7 us -> 6.06 us
  matrix products: 12.5 us -> 0 us
  starting transfers between devices: 7.43 us -> 10.6 us
    reduce_scatter x3 -> x0, waiting for transfers between devices: 31.9 us -> none  [shards(): lax.psum_scatter(curve_term(jnp.int32(0), share * lax.axis_size('station'...]
    pallas_call x0 -> x3, Pallas kernels: none -> 13.8 us  [round_call(): pl.pallas_call(kernel, out_shape=jax.ShapeDtypeStruct((slots, inv.shape[1...]
    dot_general x7 -> x0, matrix products: 12.5 us -> none  [the longest x4 9.79 us: spectra_of(): jnp.dot(traces, forward_table(length), preferred_element_type=jnp.float32)]
    select_n x6 -> x0, other arithmetic: 10.9 us -> none  [the longest x3 5.83 us: curve_term(): right = jnp.take(partner_spec, slot_table[:, 1], axis=0)]
    gather x6 -> x0, local copies, waits for them, and re-layouts: 10.6 us -> none  [the longest x3 5.98 us: curve_term(): right = jnp.take(partner_spec, slot_table[:, 1], axis=0)]
    another operation x8 -> x2, other arithmetic: 9.93 us -> 0.77 us
    dot_general x3 -> x0, other arithmetic: 6.54 us -> none  [pair_curves(): jnp.einsum('pck,pck->pk', left_imag, right_imag, preferred_element_type=j...]
    reduce_sum x8 -> x0, other arithmetic: 5.49 us -> none  [the longest x4 2.97 us: spectra_of(): jnp.mean(traces * traces, axis=-1, keepdims=True) + EPS]
  transfers between devices with their start and end apart: 6 -> 6, of which waited for: 2 -> 2; matrix products, arithmetic and copies ran while one was open for 57% -> 7% of each run, Pallas kernels for 0% -> 25%
where the time goes in v1:
time: 37.7 us; the launch traced here: 37.3 us
  Pallas kernels  13.8 us (37%)
  starting transfers between devices  10.6 us (28%)
  local copies, waits for them, and re-layouts  6.06 us (16%)
  waiting for transfers between devices  5.47 us (15%)
  other arithmetic  1.39 us (4%)
    pallas_call x3, Pallas kernels, round_call(): pl.pallas_call(kernel, out_shape=jax.ShapeDtypeStruct((slots, inv.shape[1...  13.8 us
    ppermute x3, starting transfers between devices, swapped(): return lax.ppermute(block, axis, route)  7.23 us
    ppermute x3, waiting for transfers between devices, swapped(): return lax.ppermute(block, axis, route)  3.34 us
    ppermute x3, starting transfers between devices, shards(): got = lax.ppermute(stacked[:, d].astype(jnp.bfloat16), 'station', perm)  3.33 us
    unnamed x19, local copies, waits for them, and re-layouts  3.11 us
    ppermute x3, waiting for transfers between devices, shards(): got = lax.ppermute(stacked[:, d].astype(jnp.bfloat16), 'station', perm)  2.13 us
    another operation x3, local copies, waits for them, and re-layouts, shards(): pair_lists[q].reshape(-1)  1.89 us
    another operation x1, other arithmetic  0.77 us
  transfers between devices with their start and end apart: 6, of which 2 were waited for; matrix products, arithmetic and copies ran while one was open for 7% of the time, Pallas kernels for 25%

profile of v1, /device:TPU:0, one launch (start us, length us, event | category | flops | bytes accessed | tf_op | source)
XLA Modules:
  0.0 37.3 jit_solution(4219042904582063107)
XLA Ops:
  0.0 1.0 %copy.14 = bf16[16,4,3,512]{3,2,1,0:T(4,128)(2,1)S(1)} copy(bf16[16,4,3,512]{3,1,2,0:T(4,128)(2,1)} %param.5) | data formatting | bytes 393216 | tf_op args[0]
  1.1 0.0 copy-start.8
  1.1 0.2 reshape.17.wl_ref
  1.2 0.0 copy-start
  1.2 4.1 %collective-permute-start.2 = (bf16[192,512]{1,0:T(8,128)(2,1)S(1)}, bf16[192,512]{1,0:T(8,128)(2,1)S(1)}, u32[]{:S(2)}, u32[]{:S(2)}) collective-permute-start(bf16[192,512]{1,0:T(8,128)(2,1)S(1)} %reshape.17.wl_ref), channel_id=1, source_target_pairs={{0,16},{16,0},{4,20},{20,4},{8,24},{24,8},{12,28},{28,12},{1,17},{... | collective-permute-start | bytes 589832 | tf_op jit(solution)/shard_map/ppermute | solution.py:24
  5.4 1.6 %collective-permute-start.1 = (bf16[192,512]{1,0:T(8,128)(2,1)S(1)}, bf16[192,512]{1,0:T(8,128)(2,1)S(1)}, u32[]{:S(2)}, u32[]{:S(2)}) collective-permute-start(bf16[192,512]{1,0:T(8,128)(2,1)S(1)} %reshape.17.wl_ref), channel_id=1, source_target_pairs={{0,8},{8,0},{4,12},{12,4},{16,24},{24,16},{20,28},{28,20},{1,9},{9... | collective-permute-start | bytes 589832 | tf_op jit(solution)/shard_map/ppermute | solution.py:24
  7.0 1.5 %collective-permute-start = (bf16[192,512]{1,0:T(8,128)(2,1)S(1)}, bf16[192,512]{1,0:T(8,128)(2,1)S(1)}, u32[]{:S(2)}, u32[]{:S(2)}) collective-permute-start(bf16[192,512]{1,0:T(8,128)(2,1)S(1)} %reshape.17.wl_ref), channel_id=1, source_target_pairs={{0,4},{4,0},{8,12},{12,8},{16,20},{20,16},{24,28},{28,24},{1,5},{5... | collective-permute-start | bytes 589832 | tf_op jit(solution)/shard_map/ppermute | solution.py:24
  8.5 0.0 copy-done.8
  8.5 0.1 copy.13
  8.6 0.6 %reshape_squeeze.9.pl_ref = s32[64]{0:T(128)} reshape(s32[1,32,2]{2,1,0:T(8,128)S(1)} %copy.13) | data formatting | bytes 512 | tf_op jit(solution)/shard_map/reshape;squeeze | solution.py:142
  9.2 0.1 copy.16
  9.2 0.6 %reshape_squeeze.11.pl_ref = s32[64]{0:T(128)} reshape(s32[1,32,2]{2,1,0:T(8,128)S(1)} %copy.16) | data formatting | bytes 512 | tf_op jit(solution)/shard_map/reshape;squeeze | solution.py:142
  9.9 0.1 copy.15
  10.0 0.0 copy-start.7
  10.0 0.7 %reshape_squeeze.10.pl_ref = s32[64]{0:T(128)} reshape(s32[1,32,2]{2,1,0:T(8,128)S(1)} %copy.15) | data formatting | bytes 512 | tf_op jit(solution)/shard_map/reshape;squeeze | solution.py:142
  10.6 0.0 copy-done.7
  10.6 0.6 %fusion.5 = (s32[1,1]{0,1:T(1,128)}, s32[1,1]{0,1:T(1,128)}, s32[1,1]{0,1:T(1,128)}) fusion(s32[3,1]{0,1:T(1,128)S(1)} %copy-done.7), kind=kLoop, calls=%fused_computation.10 | loop fusion | bytes 24 | tf_op jit(solution)/shard_map/slice | solution.py:142
  11.3 3.3 %collective-permute-done.2.wp_ref = bf16[192,512]{1,0:T(8,128)(2,1)S(1)} collective-permute-done((bf16[192,512]{1,0:T(8,128)(2,1)S(1)}, bf16[192,512]{1,0:T(8,128)(2,1)S(1)}, u32[]{:S(2)}, u32[]{:S(2)}) %collective-permute-start.2) | collective-permute-done | bytes 196640 | tf_op jit(solution)/shard_map/ppermute | solution.py:24
  14.6 0.0 copy-start.6
  14.6 0.0 copy-done
  14.6 0.7 %copy-done.6 = bf16[192,512]{1,0:T(8,128)(2,1)} copy-done((bf16[192,512]{1,0:T(8,128)(2,1)}, bf16[192,512]{1,0:T(8,128)(2,1)S(1)}, u32[]{:S(2)}) %copy-start.6) | copy-done | bytes 196632
  15.3 4.6 %shard_map.57 = f32[32,256]{1,0:T(8,128)} custom-call(s32[64]{0:T(128)} %reshape_squeeze.11.pl_ref, s32[1]{0:T(128)} %bitcast.7.cnt_ref, s32[1]{0:T(128)} %bitcast.1.sid_ref, bf16[192,512]{1,0:T(8,128)(2,1)} %copy-done, bf16[192,512]{1,0:T(8,128)(2,1)} %copy-done.6, bf16[512,1024]{1,0:T(8,128)(2,1)} %constant.8.clone.f_ref, ...), custom_call_target="tpu_custom_call" | custom-call | tf_op jit(solution)/shard_map/pallas_call | solution.py:112
  19.9 0.0 collective-permute-done.1.wp_ref
  19.9 0.0 copy-start.5
  19.9 0.7 %copy-done.5 = bf16[192,512]{1,0:T(8,128)(2,1)} copy-done((bf16[192,512]{1,0:T(8,128)(2,1)}, bf16[192,512]{1,0:T(8,128)(2,1)S(1)}, u32[]{:S(2)}) %copy-start.5) | copy-done | bytes 196632
  20.6 4.5 %shard_map.56 = f32[32,256]{1,0:T(8,128)} custom-call(s32[64]{0:T(128)} %reshape_squeeze.10.pl_ref, s32[1]{0:T(128)} %bitcast.4.cnt_ref, s32[1]{0:T(128)} %bitcast.1.sid_ref, bf16[192,512]{1,0:T(8,128)(2,1)} %copy-done, bf16[192,512]{1,0:T(8,128)(2,1)} %copy-done.5, bf16[512,1024]{1,0:T(8,128)(2,1)} %constant.8.clone.f_ref, ...), custom_call_target="tpu_custom_call" | custom-call | tf_op jit(solution)/shard_map/pallas_call | solution.py:112
  25.1 0.0 collective-permute-done.wp_ref
  25.1 0.0 copy-start.4
  25.1 0.7 %copy-done.4 = bf16[192,512]{1,0:T(8,128)(2,1)} copy-done((bf16[192,512]{1,0:T(8,128)(2,1)}, bf16[192,512]{1,0:T(8,128)(2,1)S(1)}, u32[]{:S(2)}) %copy-start.4) | copy-done | bytes 196632
  25.8 0.0 copy-start.1
  25.8 0.0 copy-start.2
  25.8 4.6 %shard_map.55 = f32[32,256]{1,0:T(8,128)} custom-call(s32[64]{0:T(128)} %reshape_squeeze.9.pl_ref, s32[1]{0:T(128)} %bitcast.cnt_ref, s32[1]{0:T(128)} %bitcast.1.sid_ref, bf16[192,512]{1,0:T(8,128)(2,1)} %copy-done, bf16[192,512]{1,0:T(8,128)(2,1)} %copy-done.4, bf16[512,1024]{1,0:T(8,128)(2,1)} %constant.8.clone.f_ref, bf16[1024,256]{1,0:T(8,128)(2,1)} %constant.9.clone.g_ref), custom_call_target="tpu_custom_call" | custom-call | tf_op jit(solution)/shard_map/pallas_call | solution.py:112
  30.4 0.0 copy-done.1
  30.4 0.0 copy-done.2
  30.4 0.8 %fusion.3 = bf16[3,4,8,256]{3,2,0,1:T(8,128)(2,1)S(1)} fusion(f32[1,4,8,256]{3,2,0,1:T(8,128)S(1)} %bitcast.27, f32[1,4,8,256]{3,2,0,1:T(8,128)S(1)} %bitcast.29, f32[1,4,8,256]{3,2,0,1:T(8,128)} %bitcast.31), kind=kLoop, calls=%fused_computation.8 | loop fusion | flops 49152 | bytes 147456 | tf_op jit(solution)/shard_map/convert.2
  31.2 0.0 copy-start.3
  31.2 0.1 collective-permute-start.3
  31.3 1.7 %collective-permute-start.5 = (bf16[3,8,256]{2,1,0:T(8,128)(2,1)S(1)}, bf16[3,8,256]{2,1,0:T(8,128)(2,1)S(1)}, u32[]{:S(2)}, u32[]{:S(2)}) collective-permute-start(bf16[3,8,256]{2,1,0:T(8,128)(2,1)S(1)} %get-tuple-element.6), channel_id=1, source_target_pairs={{0,3},{1,0},{2,1},{3,2},{4,7},{5,4},{6,5},{7,6},{8,11},{9,8},{10,9... | collective-permute-start | bytes 36872 | tf_op jit(solution)/shard_map/ppermute | solution.py:149
  33.0 1.5 %collective-permute-start.4 = (bf16[3,8,256]{2,1,0:T(8,128)(2,1)S(1)}, bf16[3,8,256]{2,1,0:T(8,128)(2,1)S(1)}, u32[]{:S(2)}, u32[]{:S(2)}) collective-permute-start(bf16[3,8,256]{2,1,0:T(8,128)(2,1)S(1)} %get-tuple-element.7), channel_id=1, source_target_pairs={{0,2},{1,3},{2,0},{3,1},{4,6},{5,7},{6,4},{7,5},{8,10},{9,11},{10,... | collective-permute-start | bytes 36872 | tf_op jit(solution)/shard_map/ppermute | solution.py:149
  34.6 0.0 copy-done.3
  34.6 0.0 collective-permute-done.3
  34.6 0.0 collective-permute-done.5
  34.6 2.1 %collective-permute-done.4 = bf16[3,8,256]{2,1,0:T(8,128)(2,1)S(1)} collective-permute-done((bf16[3,8,256]{2,1,0:T(8,128)(2,1)S(1)}, bf16[3,8,256]{2,1,0:T(8,128)(2,1)S(1)}, u32[]{:S(2)}, u32[]{:S(2)}) %collective-permute-start.4) | collective-permute-done | bytes 12320 | tf_op jit(solution)/shard_map/ppermute | solution.py:149
  36.7 0.6 %fusion.2 = f32[3,8,256]{2,1,0:T(8,128)} fusion(f32[3,4,8,256]{3,2,0,1:T(8,128)S(1)} %pad_maximum_fusion, bf16[3,8,256]{2,1,0:T(8,128)(2,1)S(1)} %collective-permute-done.5, bf16[3,8,256]{2,1,0:T(8,128)(2,1)S(1)} %collective-permute-done.4, bf16[3,8,256]{2,1,0:T(8,128)(2,1)S(1)} %collective-permute-done.3), kind=kLoop, calls=%fused_computation.4 | loop fusion | flops 36864 | bytes 86016 | tf_op jit(solution)/shard_map/add | solution.py:150
  (3 shorter events, 0.0 us)
Async XLA Ops:
  1.1 7.4 %copy-start.8 = (s32[3,32,2]{1,2,0:T(2,128)S(1)}, s32[3,32,2]{1,2,0:T(2,128)}, u32[]{:S(2)}) copy-start(s32[3,32,2]{1,2,0:T(2,128)} %param.6) | copy-start | bytes 2308
  1.2 13.4 %copy-start = (bf16[192,512]{1,0:T(8,128)(2,1)}, bf16[192,512]{1,0:T(8,128)(2,1)S(1)}, u32[]{:S(2)}) copy-start(bf16[192,512]{1,0:T(8,128)(2,1)S(1)} %reshape.17.wl_ref) | copy-start | bytes 589828
  1.2 13.3 %collective-permute-start.2 = (bf16[192,512]{1,0:T(8,128)(2,1)S(1)}, bf16[192,512]{1,0:T(8,128)(2,1)S(1)}, u32[]{:S(2)}, u32[]{:S(2)}) collective-permute-start(bf16[192,512]{1,0:T(8,128)(2,1)S(1)} %reshape.17.wl_ref), channel_id=1, source_target_pairs={{0,16},{16,0},{4,20},{20,4},{8,24},{24,8},{12,28},{28,12},{1,17},{... | collective-permute-start | bytes 589832 | tf_op jit(solution)/shard_map/ppermute | solution.py:24
  5.4 14.5 %collective-permute-start.1 = (bf16[192,512]{1,0:T(8,128)(2,1)S(1)}, bf16[192,512]{1,0:T(8,128)(2,1)S(1)}, u32[]{:S(2)}, u32[]{:S(2)}) collective-permute-start(bf16[192,512]{1,0:T(8,128)(2,1)S(1)} %reshape.17.wl_ref), channel_id=1, source_target_pairs={{0,8},{8,0},{4,12},{12,4},{16,24},{24,16},{20,28},{28,20},{1,9},{9... | collective-permute-start | bytes 589832 | tf_op jit(solution)/shard_map/ppermute | solution.py:24
  7.0 18.2 %collective-permute-start = (bf16[192,512]{1,0:T(8,128)(2,1)S(1)}, bf16[192,512]{1,0:T(8,128)(2,1)S(1)}, u32[]{:S(2)}, u32[]{:S(2)}) collective-permute-start(bf16[192,512]{1,0:T(8,128)(2,1)S(1)} %reshape.17.wl_ref), channel_id=1, source_target_pairs={{0,4},{4,0},{8,12},{12,8},{16,20},{20,16},{24,28},{28,24},{1,5},{5... | collective-permute-start | bytes 589832 | tf_op jit(solution)/shard_map/ppermute | solution.py:24
  10.0 0.7 %copy-start.7 = (s32[3,1]{0,1:T(1,128)S(1)}, s32[3,1]{0,1:T(1,128)}, u32[]{:S(2)}) copy-start(s32[3,1]{0,1:T(1,128)} %param.7) | copy-start | bytes 40
  14.6 0.7 %copy-start.6 = (bf16[192,512]{1,0:T(8,128)(2,1)}, bf16[192,512]{1,0:T(8,128)(2,1)S(1)}, u32[]{:S(2)}) copy-start(bf16[192,512]{1,0:T(8,128)(2,1)S(1)} %collective-permute-done.2.wp_ref) | copy-start | bytes 589828
  19.9 0.7 %copy-start.5 = (bf16[192,512]{1,0:T(8,128)(2,1)}, bf16[192,512]{1,0:T(8,128)(2,1)S(1)}, u32[]{:S(2)}) copy-start(bf16[192,512]{1,0:T(8,128)(2,1)S(1)} %collective-permute-done.1.wp_ref) | copy-start | bytes 589828
  25.1 0.7 %copy-start.4 = (bf16[192,512]{1,0:T(8,128)(2,1)}, bf16[192,512]{1,0:T(8,128)(2,1)S(1)}, u32[]{:S(2)}) copy-start(bf16[192,512]{1,0:T(8,128)(2,1)S(1)} %collective-permute-done.wp_ref) | copy-start | bytes 589828
  25.8 4.6 %copy-start.1 = (f32[32,256]{1,0:T(8,128)S(1)}, f32[32,256]{1,0:T(8,128)}, u32[]{:S(2)}) copy-start(f32[32,256]{1,0:T(8,128)} %shard_map.57) | copy-start | bytes 98308
  25.8 4.6 %copy-start.2 = (f32[32,256]{1,0:T(8,128)S(1)}, f32[32,256]{1,0:T(8,128)}, u32[]{:S(2)}) copy-start(f32[32,256]{1,0:T(8,128)} %shard_map.56) | copy-start | bytes 98308
  31.2 3.4 %copy-start.3 = (f32[32,256]{1,0:T(8,128)S(1)}, f32[32,256]{1,0:T(8,128)}, u32[]{:S(2)}) copy-start(f32[32,256]{1,0:T(8,128)} %shard_map.55) | copy-start | bytes 98308
  31.2 3.4 %collective-permute-start.3 = (bf16[3,8,256]{2,1,0:T(8,128)(2,1)S(1)}, bf16[3,8,256]{2,1,0:T(8,128)(2,1)S(1)}, u32[]{:S(2)}, u32[]{:S(2)}) collective-permute-start(bf16[3,8,256]{2,1,0:T(8,128)(2,1)S(1)} %get-tuple-element.5), channel_id=1, source_target_pairs={{0,1},{1,2},{2,3},{3,0},{4,5},{5,6},{6,7},{7,4},{8,9},{9,10},{10,1... | collective-permute-start | bytes 36872 | tf_op jit(solution)/shard_map/ppermute | solution.py:149
  31.3 3.3 %collective-permute-start.5 = (bf16[3,8,256]{2,1,0:T(8,128)(2,1)S(1)}, bf16[3,8,256]{2,1,0:T(8,128)(2,1)S(1)}, u32[]{:S(2)}, u32[]{:S(2)}) collective-permute-start(bf16[3,8,256]{2,1,0:T(8,128)(2,1)S(1)} %get-tuple-element.6), channel_id=1, source_target_pairs={{0,3},{1,0},{2,1},{3,2},{4,7},{5,4},{6,5},{7,6},{8,11},{9,8},{10,9... | collective-permute-start | bytes 36872 | tf_op jit(solution)/shard_map/ppermute | solution.py:149
  33.0 3.7 %collective-permute-start.4 = (bf16[3,8,256]{2,1,0:T(8,128)(2,1)S(1)}, bf16[3,8,256]{2,1,0:T(8,128)(2,1)S(1)}, u32[]{:S(2)}, u32[]{:S(2)}) collective-permute-start(bf16[3,8,256]{2,1,0:T(8,128)(2,1)S(1)} %get-tuple-element.7), channel_id=1, source_target_pairs={{0,2},{1,3},{2,0},{3,1},{4,6},{5,7},{6,4},{7,5},{8,10},{9,11},{10,... | collective-permute-start | bytes 36872 | tf_op jit(solution)/shard_map/ppermute | solution.py:149

commit v2 on v1

v2 whole, which is shorter than its diff:
```python
import math

import ml_dtypes
import numpy as np

import jax
import jax.numpy as jnp
from jax import lax
from jax.experimental import pallas as pl
from jax.experimental.pallas import tpu as pltpu
from jax.sharding import PartitionSpec as P

EPS = 1e-06
LAGS = 256


def swapped(block, axis, bit):
    count = lax.axis_size(axis)
    route = []
    for low in range(count):
        high = low | 1 << bit
        if high != low and high < count:
            route += [(low, high), (high, low)]
    return lax.ppermute(block, axis, route)


def half_tables(length, channels, lags):
    period = 2 * length
    half = period // 2
    step = np.float32(2.0 * math.pi / period)
    times = np.arange(length, dtype=np.int64)[:, None]
    freqs = np.arange(half, dtype=np.int64)[None, :]
    angle = step * ((times * freqs) % period).astype(np.float32)
    fwd = np.concatenate([np.cos(angle), -np.sin(angle)], axis=1).astype(np.float32)
    fwd[:, half] = np.where(times[:, 0] % 2 == 0, 1.0, -1.0)
    fwd = fwd.astype(ml_dtypes.bfloat16)

    factor = np.float32(1.0 / (period * math.sqrt(channels * length)))
    rows = np.arange(half, dtype=np.int64)[:, None]
    lagged = np.arange(lags, dtype=np.int64)[None, :] - lags // 2
    angle = step * ((rows * lagged) % period).astype(np.float32)
    cos_t = (np.cos(angle).astype(np.float32) * factor).astype(ml_dtypes.bfloat16).astype(np.float32)
    sin_t = ((-np.sin(angle)).astype(np.float32) * factor).astype(ml_dtypes.bfloat16).astype(np.float32)
    inv = np.zeros((period, lags), np.float32)
    inv[0] = cos_t[0]
    inv[1:half] = 2.0 * cos_t[1:]
    nyq_angle = step * ((half * lagged[0]) % period).astype(np.float32)
    inv[half] = (np.cos(nyq_angle).astype(np.float32) * factor).astype(ml_dtypes.bfloat16).astype(np.float32)
    inv[half + 1:] = 2.0 * sin_t[1:]
    return fwd, inv.astype(ml_dtypes.bfloat16)


def make_kernel(events, chans, pad, length, slots, groups, share, rounds, first, from_waves):
    half = length
    n_part = len(rounds)

    def kernel(*refs):
        pl_ref, cnt_ref, sid_ref, own_ref = refs[:4]
        part_refs = refs[4:4 + n_part]
        f_ref, g_ref = refs[4 + n_part:6 + n_part]
        outs = refs[6 + n_part:]
        out_ref = outs[0]
        spec_out = outs[1] if from_waves else None
        nscr, xpad, specl, specp, cross = outs[1 + int(from_waves):]

        def spectra(w_ref, spec_ref):
            x = w_ref[...].astype(jnp.float32)
            x = x - jnp.mean(x, axis=-1, keepdims=True)
            x = x * lax.rsqrt(jnp.mean(x * x, axis=-1, keepdims=True) + EPS)
            nscr[...] = x
            for e in range(events):
                xpad[e * pad:e * pad + chans, :] = nscr[e * chans:(e + 1) * chans, :]
            xb = xpad[...].astype(jnp.bfloat16)
            spec = jnp.dot(xb, f_ref[...], preferred_element_type=jnp.float32)
            spec_ref[...] = spec.astype(jnp.bfloat16).astype(jnp.float32)

        xpad[...] = jnp.zeros(xpad.shape, jnp.float32)
        if from_waves:
            spectra(own_ref, specl)
            spec_out[...] = specl[...].astype(jnp.bfloat16)
        else:
            specl[...] = own_ref[...].astype(jnp.float32)

        sid = sid_ref[0]
        lane = lax.broadcasted_iota(jnp.int32, (1, 128), 1)
        for n, q in enumerate(rounds):
            spectra(part_refs[n], specp)
            base = q * slots * 2
            for r in range(slots):
                d, ip = divmod(r, share)
                slot = ((sid + d) % groups) * share + ip
                a = jnp.minimum(jnp.maximum(pl_ref[base + 2 * slot], 0), events - 1)
                b = jnp.minimum(jnp.maximum(pl_ref[base + 2 * slot + 1], 0), events - 1)
                left = specl[pl.ds(pl.multiple_of(a * pad, pad), pad), :]
                right = specp[pl.ds(pl.multiple_of(b * pad, pad), pad), :]
                lr, li = left[:, :half], left[:, half:]
                rr, ri = right[:, :half], right[:, half:]
                pp = lr * rr
                qq = li * ri
                re = jnp.sum(pp + qq, axis=0, keepdims=True)
                im = jnp.sum(lr * ri - li * rr, axis=0, keepdims=True)
                p0 = jnp.sum(pp[:, :128], axis=0, keepdims=True)
                q0 = jnp.sum(qq[:, :128], axis=0, keepdims=True)
                cross[r:r + 1, 0:128] = jnp.where(lane == 0, p0, re[:, :128])
                cross[r:r + 1, 128:half] = re[:, 128:]
                cross[r:r + 1, half:half + 128] = jnp.where(lane == 0, q0, im[:, :128])
                cross[r:r + 1, half + 128:] = im[:, 128:]

            cb = cross[...].astype(jnp.bfloat16)
            corr = jnp.dot(cb, g_ref[...], preferred_element_type=jnp.float32)
            rows = lax.broadcasted_iota(jnp.int32, corr.shape, 0)
            slot_of = ((sid + rows // share) % groups) * share + rows % share
            out_ref[n] = jnp.where(slot_of < cnt_ref[q], corr, 0.0)

    return kernel


def rounds_call(pairs, counts, sid, own, partners, fwd, inv, rounds, events, chans, slots, groups, from_waves):
    length = fwd.shape[0]
    pad = 16
    share = slots // groups
    kernel = make_kernel(events, chans, pad, length, slots, groups, share, rounds, rounds[0], from_waves)
    smem = pl.BlockSpec(memory_space=pltpu.SMEM)
    vmem = pl.BlockSpec(memory_space=pltpu.VMEM)
    out_shape = [jax.ShapeDtypeStruct((len(rounds), slots, inv.shape[1]), jnp.float32)]
    out_specs = [vmem]
    if from_waves:
        out_shape.append(jax.ShapeDtypeStruct((events * pad, 2 * length), jnp.bfloat16))
        out_specs.append(vmem)
    res = pl.pallas_call(
        kernel,
        out_shape=tuple(out_shape),
        in_specs=[smem, smem, smem] + [vmem] * (3 + len(partners)),
        out_specs=tuple(out_specs),
        scratch_shapes=[
            pltpu.VMEM((events * chans, length), jnp.float32),
            pltpu.VMEM((events * pad, length), jnp.float32),
            pltpu.VMEM((events * pad, 2 * length), jnp.float32),
            pltpu.VMEM((events * pad, 2 * length), jnp.float32),
            pltpu.VMEM((slots, 2 * length), jnp.float32),
        ],
    )(pairs, counts, sid, own, *partners, fwd, inv)
    return res


def station_sum(block, groups):
    total = block[:, 0]
    for d in range(1, groups):
        perm = [(s, (s + d) % groups) for s in range(groups)]
        got = lax.ppermute(block[:, d].astype(jnp.bfloat16), "station", perm)
        total = total + got.astype(jnp.float32)
    return total


def shards(waveforms, pair_lists, pair_counts):
    events, stations, comps, length = waveforms.shape
    groups = lax.axis_size("station")
    rounds, slots, _ = pair_lists.shape
    chans = stations * comps
    share = slots // groups
    fwd_np, inv_np = half_tables(length, stations * groups * comps, LAGS)
    fwd = jnp.asarray(fwd_np)
    inv = jnp.asarray(inv_np)
    flat = waveforms.reshape(events * chans, length)
    sid = lax.axis_index("station").astype(jnp.int32).reshape(1)
    pairs = pair_lists.reshape(-1)
    counts = pair_counts.reshape(-1)
    partners = [swapped(flat, "region", q) for q in range(rounds)]
    early = list(range(rounds - 1))
    corr_a, spec = rounds_call(pairs, counts, sid, flat, [partners[q] for q in early], fwd, inv,
                               early, events, chans, slots, groups, True)
    sum_a = station_sum(corr_a.reshape(len(early), groups, share, LAGS), groups)
    (corr_b,) = rounds_call(pairs, counts, sid, spec, [partners[-1]], fwd, inv,
                            [rounds - 1], events, chans, slots, groups, False)
    sum_b = station_sum(corr_b.reshape(1, groups, share, LAGS), groups)
    return jnp.concatenate([sum_a, sum_b], axis=0)


def solution(mesh):
    return jax.shard_map(
        shards,
        mesh=mesh,
        in_specs=(P("region", "station", None, None), P(None, "region", None), P(None, "region")),
        out_specs=P(None, ("region", "station"), None),
        check_vma=False,
    )
```

time: 37.7 us -> 34.1 us (0.905)
  the two profiles are of different devices: /device:TPU:0 before, /device:TPU:1 now
where the time goes in v2:
time: 34.1 us; the launch traced here: 33.8 us
  starting transfers between devices  12.8 us (38%)
  Pallas kernels  8.84 us (26%)
  waiting for transfers between devices  6.6 us (19%)
  local copies, waits for them, and re-layouts  3.39 us (10%)
  other arithmetic  2.12 us (6%)
    pallas_call x2, Pallas kernels, rounds_call(): pl.pallas_call(kernel, out_shape=tuple(out_shape), in_specs=[smem, smem,...  8.84 us
    ppermute x6, starting transfers between devices, station_sum(): got = lax.ppermute(block[:, d].astype(jnp.bfloat16), 'station', perm)  7.08 us
    ppermute x3, starting transfers between devices, swapped(): return lax.ppermute(block, axis, route)  5.73 us
    ppermute x3, waiting for transfers between devices, swapped(): return lax.ppermute(block, axis, route)  4.23 us
    unnamed x14, local copies, waits for them, and re-layouts  2.51 us
    ppermute x6, waiting for transfers between devices, station_sum(): got = lax.ppermute(block[:, d].astype(jnp.bfloat16), 'station', perm)  2.37 us
    another operation x1, other arithmetic  0.79 us
    add x2, other arithmetic, station_sum(): total = total + got.astype(jnp.float32)  0.71 us
  transfers between devices with their start and end apart: 9, of which 5 were waited for; matrix products, arithmetic and copies ran while one was open for 4% of the time, Pallas kernels for 15%

profile of v2, /device:TPU:1, one launch (start us, length us, event | category | flops | bytes accessed | tf_op | source)
XLA Modules:
  0.0 33.8 jit_solution(10091986544185784267)
XLA Ops:
  0.0 1.0 %copy.10 = bf16[16,4,3,512]{3,2,1,0:T(4,128)(2,1)S(1)} copy(bf16[16,4,3,512]{3,1,2,0:T(4,128)(2,1)} %param.5) | data formatting | bytes 393216 | tf_op args[0]
  1.1 0.0 copy-start.5
  1.1 0.2 reshape.63.refs_3_
  1.2 0.0 copy-start
  1.2 2.1 %collective-permute-start = (bf16[192,512]{1,0:T(8,128)(2,1)S(1)}, bf16[192,512]{1,0:T(8,128)(2,1)S(1)}, u32[]{:S(2)}, u32[]{:S(2)}) collective-permute-start(bf16[192,512]{1,0:T(8,128)(2,1)S(1)} %reshape.63.refs_3_), channel_id=1, source_target_pairs={{0,4},{4,0},{8,12},{12,8},{16,20},{20,16},{24,28},{28,24},{1,5},{5... | collective-permute-start | bytes 589832 | tf_op jit(solution)/shard_map/ppermute | solution.py:24
  3.4 1.3 %collective-permute-start.1 = (bf16[192,512]{1,0:T(8,128)(2,1)S(1)}, bf16[192,512]{1,0:T(8,128)(2,1)S(1)}, u32[]{:S(2)}, u32[]{:S(2)}) collective-permute-start(bf16[192,512]{1,0:T(8,128)(2,1)S(1)} %reshape.63.refs_3_), channel_id=1, source_target_pairs={{0,8},{8,0},{4,12},{12,4},{16,24},{24,16},{20,28},{28,20},{1,9},{9... | collective-permute-start | bytes 589832 | tf_op jit(solution)/shard_map/ppermute | solution.py:24
  4.7 2.3 %collective-permute-start.5 = (bf16[192,512]{1,0:T(8,128)(2,1)S(1)}, bf16[192,512]{1,0:T(8,128)(2,1)S(1)}, u32[]{:S(2)}, u32[]{:S(2)}) collective-permute-start(bf16[192,512]{1,0:T(8,128)(2,1)S(1)} %reshape.63.refs_3_), channel_id=1, source_target_pairs={{0,16},{16,0},{4,20},{20,4},{8,24},{24,8},{12,28},{28,12},{1,17},{... | collective-permute-start | bytes 589832 | tf_op jit(solution)/shard_map/ppermute | solution.py:24
  7.0 0.0 copy-done.5
  7.0 0.1 copy.9
  7.1 0.7 %reshape.60.refs_0_ = s32[192]{0:T(256)} reshape(s32[3,32,2]{2,1,0:T(8,128)S(1)} %copy.9) | data formatting | bytes 1536 | tf_op jit(solution)/shard_map/reshape | solution.py:166
  7.8 0.2 collective-permute-done.refs_4_
  8.0 0.0 copy-start.2
  8.0 4.0 %collective-permute-done.1.refs_5_ = bf16[192,512]{1,0:T(8,128)(2,1)S(1)} collective-permute-done((bf16[192,512]{1,0:T(8,128)(2,1)S(1)}, bf16[192,512]{1,0:T(8,128)(2,1)S(1)}, u32[]{:S(2)}, u32[]{:S(2)}) %collective-permute-start.1) | collective-permute-done | bytes 196640 | tf_op jit(solution)/shard_map/ppermute | solution.py:24
  12.0 0.0 copy-start.3
  12.0 0.0 copy-done
  12.0 0.0 copy-done.2
  12.0 0.7 %copy-done.3 = bf16[192,512]{1,0:T(8,128)(2,1)} copy-done((bf16[192,512]{1,0:T(8,128)(2,1)}, bf16[192,512]{1,0:T(8,128)(2,1)S(1)}, u32[]{:S(2)}) %copy-start.3) | copy-done | bytes 196632
  12.7 5.1 %shard_map.55 = (f32[2,32,256]{2,1,0:T(8,128)}, bf16[256,1024]{1,0:T(8,128)(2,1)}) custom-call(s32[192]{0:T(256)} %reshape.60.refs_0_, s32[3]{0:T(128)} %bitcast.40, s32[1]{0:T(128)} %bitcast.1.refs_2_, bf16[192,512]{1,0:T(8,128)(2,1)} %copy-done, bf16[192,512]{1,0:T(8,128)(2,1)} %copy-done.2, bf16[192,512]{1,0:T(8,128)(2,1)} %copy-done.3, ...), custom_call_target="tpu_custom_call" | custom-call | tf_op jit(solution)/shard_map/pallas_call | solution.py:130
  17.8 0.0 collective-permute-done.5.refs_4_
  17.8 0.0 copy-start.4
  17.8 0.7 %copy-done.4 = bf16[192,512]{1,0:T(8,128)(2,1)} copy-done((bf16[192,512]{1,0:T(8,128)(2,1)}, bf16[192,512]{1,0:T(8,128)(2,1)S(1)}, u32[]{:S(2)}) %copy-start.4) | copy-done | bytes 196632
  18.5 3.7 %shard_map.56 = f32[1,32,256]{2,1,0:T(8,128)} custom-call(s32[192]{0:T(256)} %reshape.60.refs_0_, s32[3]{0:T(128)} %bitcast.41, s32[1]{0:T(128)} %bitcast.1.refs_2_, bf16[256,1024]{1,0:T(8,128)(2,1)} %get-tuple-element.8.refs_3_, bf16[192,512]{1,0:T(8,128)(2,1)} %copy-done.4, bf16[512,1024]{1,0:T(8,128)(2,1)} %constant.8.clone.refs_6_.refs_5_, ...), custom_call_target="tpu_custom_call" | custom-call | tf_op jit(solution)/shard_map/pallas_call | solution.py:130
  22.2 0.0 copy-start.1
  22.2 0.8 %bitcast_convert_fusion = bf16[1,4,8,256]{3,2,1,0:T(8,128)(2,1)S(1)} fusion(f32[1,32,256]{2,1,0:T(8,128)} %shard_map.56), kind=kLoop, calls=%fused_computation.15 | loop fusion | flops 8192 | bytes 49152 | tf_op jit(solution)/shard_map/convert.2
  23.0 3.9 %collective-permute-start.6 = (bf16[1,8,256]{2,1,0:T(8,128)(2,1)S(1)}, bf16[1,8,256]{2,1,0:T(8,128)(2,1)S(1)}, u32[]{:S(2)}, u32[]{:S(2)}) collective-permute-start(bf16[1,8,256]{2,1,0:T(8,128)(2,1)S(1)} %get-tuple-element.12), channel_id=1, source_target_pairs={{0,1},{1,2},{2,3},{3,0},{4,5},{5,6},{6,7},{7,4},{8,9},{9,10},{10,1... | collective-permute-start | bytes 12296 | tf_op jit(solution)/shard_map/ppermute | solution.py:150
  26.9 0.3 collective-permute-start.7
  27.1 0.2 collective-permute-start.8
  27.4 0.0 copy-done.1
  27.4 1.5 %collective-permute-start.2 = (bf16[2,8,256]{2,1,0:T(8,128)(2,1)S(1)}, bf16[2,8,256]{2,1,0:T(8,128)(2,1)S(1)}, u32[]{:S(2)}, u32[]{:S(2)}) collective-permute-start(bf16[2,8,256]{2,1,0:T(8,128)(2,1)S(1)} %get-tuple-element.9), channel_id=1, source_target_pairs={{0,1},{1,2},{2,3},{3,0},{4,5},{5,6},{6,7},{7,4},{8,9},{9,10},{10,1... | collective-permute-start | bytes 24584 | tf_op jit(solution)/shard_map/ppermute | solution.py:150
  28.9 1.2 %collective-permute-start.3 = (bf16[2,8,256]{2,1,0:T(8,128)(2,1)S(1)}, bf16[2,8,256]{2,1,0:T(8,128)(2,1)S(1)}, u32[]{:S(2)}, u32[]{:S(2)}) collective-permute-start(bf16[2,8,256]{2,1,0:T(8,128)(2,1)S(1)} %get-tuple-element.11), channel_id=1, source_target_pairs={{0,2},{1,3},{2,0},{3,1},{4,6},{5,7},{6,4},{7,5},{8,10},{9,11},{10,... | collective-permute-start | bytes 24584 | tf_op jit(solution)/shard_map/ppermute | solution.py:150
  30.1 0.0 collective-permute-done.6
  30.1 0.0 collective-permute-start.4
  30.1 0.0 collective-permute-done.7
  30.1 0.1 collective-permute-done.8
  30.2 0.7 %fusion.5 = f32[1,8,256]{2,1,0:T(8,128)S(1)} fusion(f32[1,4,8,256]{3,2,1,0:T(8,128)} %bitcast.39, bf16[1,8,256]{2,1,0:T(8,128)(2,1)S(1)} %collective-permute-done.8, bf16[1,8,256]{2,1,0:T(8,128)(2,1)S(1)} %collective-permute-done.7, bf16[1,8,256]{2,1,0:T(8,128)(2,1)S(1)} %collective-permute-done.6), kind=kLoop, calls=%fused_computation.8 | loop fusion | flops 12288 | bytes 28672 | tf_op jit(solution)/shard_map/add | solution.py:151
  30.9 0.0 collective-permute-done.2
  30.9 0.6 %collective-permute-done.3 = bf16[2,8,256]{2,1,0:T(8,128)(2,1)S(1)} collective-permute-done((bf16[2,8,256]{2,1,0:T(8,128)(2,1)S(1)}, bf16[2,8,256]{2,1,0:T(8,128)(2,1)S(1)}, u32[]{:S(2)}, u32[]{:S(2)}) %collective-permute-start.3) | collective-permute-done | bytes 8224 | tf_op jit(solution)/shard_map/ppermute | solution.py:150
  31.4 1.8 %collective-permute-done.4 = bf16[2,8,256]{2,1,0:T(8,128)(2,1)S(1)} collective-permute-done((bf16[2,8,256]{2,1,0:T(8,128)(2,1)S(1)}, bf16[2,8,256]{2,1,0:T(8,128)(2,1)S(1)}, u32[]{:S(2)}, u32[]{:S(2)}) %collective-permute-start.4) | collective-permute-done | bytes 8224 | tf_op jit(solution)/shard_map/ppermute | solution.py:150
  33.2 0.6 %pad_maximum_fusion = f32[3,8,256]{2,1,0:T(8,128)} fusion(f32[1,8,256]{2,1,0:T(8,128)S(1)} %fusion.5, f32[2,8,256]{2,1,0:T(8,128)S(1)} %fusion.2), kind=kLoop, calls=%fused_computation | loop fusion | flops 6144 | bytes 49152 | tf_op jit(solution)/shard_map/concatenate | solution.py:176
  (3 shorter events, 0.0 us)
Async XLA Ops:
  1.1 5.9 %copy-start.5 = (s32[3,32,2]{1,2,0:T(2,128)S(1)}, s32[3,32,2]{1,2,0:T(2,128)}, u32[]{:S(2)}) copy-start(s32[3,32,2]{1,2,0:T(2,128)} %param.6) | copy-start | bytes 2308
  1.2 10.8 %copy-start = (bf16[192,512]{1,0:T(8,128)(2,1)}, bf16[192,512]{1,0:T(8,128)(2,1)S(1)}, u32[]{:S(2)}) copy-start(bf16[192,512]{1,0:T(8,128)(2,1)S(1)} %reshape.63.refs_3_) | copy-start | bytes 589828
  1.2 6.7 %collective-permute-start = (bf16[192,512]{1,0:T(8,128)(2,1)S(1)}, bf16[192,512]{1,0:T(8,128)(2,1)S(1)}, u32[]{:S(2)}, u32[]{:S(2)}) collective-permute-start(bf16[192,512]{1,0:T(8,128)(2,1)S(1)} %reshape.63.refs_3_), channel_id=1, source_target_pairs={{0,4},{4,0},{8,12},{12,8},{16,20},{20,16},{24,28},{28,24},{1,5},{5... | collective-permute-start | bytes 589832 | tf_op jit(solution)/shard_map/ppermute | solution.py:24
  3.4 8.6 %collective-permute-start.1 = (bf16[192,512]{1,0:T(8,128)(2,1)S(1)}, bf16[192,512]{1,0:T(8,128)(2,1)S(1)}, u32[]{:S(2)}, u32[]{:S(2)}) collective-permute-start(bf16[192,512]{1,0:T(8,128)(2,1)S(1)} %reshape.63.refs_3_), channel_id=1, source_target_pairs={{0,8},{8,0},{4,12},{12,4},{16,24},{24,16},{20,28},{28,20},{1,9},{9... | collective-permute-start | bytes 589832 | tf_op jit(solution)/shard_map/ppermute | solution.py:24
  4.7 13.1 %collective-permute-start.5 = (bf16[192,512]{1,0:T(8,128)(2,1)S(1)}, bf16[192,512]{1,0:T(8,128)(2,1)S(1)}, u32[]{:S(2)}, u32[]{:S(2)}) collective-permute-start(bf16[192,512]{1,0:T(8,128)(2,1)S(1)} %reshape.63.refs_3_), channel_id=1, source_target_pairs={{0,16},{16,0},{4,20},{20,4},{8,24},{24,8},{12,28},{28,12},{1,17},{... | collective-permute-start | bytes 589832 | tf_op jit(solution)/shard_map/ppermute | solution.py:24
  8.0 4.0 %copy-start.2 = (bf16[192,512]{1,0:T(8,128)(2,1)}, bf16[192,512]{1,0:T(8,128)(2,1)S(1)}, u32[]{:S(2)}) copy-start(bf16[192,512]{1,0:T(8,128)(2,1)S(1)} %collective-permute-done.refs_4_) | copy-start | bytes 589828
  12.0 0.7 %copy-start.3 = (bf16[192,512]{1,0:T(8,128)(2,1)}, bf16[192,512]{1,0:T(8,128)(2,1)S(1)}, u32[]{:S(2)}) copy-start(bf16[192,512]{1,0:T(8,128)(2,1)S(1)} %collective-permute-done.1.refs_5_) | copy-start | bytes 589828
  17.8 0.7 %copy-start.4 = (bf16[192,512]{1,0:T(8,128)(2,1)}, bf16[192,512]{1,0:T(8,128)(2,1)S(1)}, u32[]{:S(2)}) copy-start(bf16[192,512]{1,0:T(8,128)(2,1)S(1)} %collective-permute-done.5.refs_4_) | copy-start | bytes 589828
  22.2 5.1 %copy-start.1 = (f32[2,32,256]{2,1,0:T(8,128)S(1)}, f32[2,32,256]{2,1,0:T(8,128)}, u32[]{:S(2)}) copy-start(f32[2,32,256]{2,1,0:T(8,128)} %get-tuple-element.7) | copy-start | bytes 196612
  23.0 7.1 %collective-permute-start.6 = (bf16[1,8,256]{2,1,0:T(8,128)(2,1)S(1)}, bf16[1,8,256]{2,1,0:T(8,128)(2,1)S(1)}, u32[]{:S(2)}, u32[]{:S(2)}) collective-permute-start(bf16[1,8,256]{2,1,0:T(8,128)(2,1)S(1)} %get-tuple-element.12), channel_id=1, source_target_pairs={{0,1},{1,2},{2,3},{3,0},{4,5},{5,6},{6,7},{7,4},{8,9},{9,10},{10,1... | collective-permute-start | bytes 12296 | tf_op jit(solution)/shard_map/ppermute | solution.py:150
  26.9 3.2 %collective-permute-start.7 = (bf16[1,8,256]{2,1,0:T(8,128)(2,1)S(1)}, bf16[1,8,256]{2,1,0:T(8,128)(2,1)S(1)}, u32[]{:S(2)}, u32[]{:S(2)}) collective-permute-start(bf16[1,8,256]{2,1,0:T(8,128)(2,1)S(1)} %get-tuple-element.14), channel_id=1, source_target_pairs={{0,2},{1,3},{2,0},{3,1},{4,6},{5,7},{6,4},{7,5},{8,10},{9,11},{10,... | collective-permute-start | bytes 12296 | tf_op jit(solution)/shard_map/ppermute | solution.py:150
  27.1 3.0 %collective-permute-start.8 = (bf16[1,8,256]{2,1,0:T(8,128)(2,1)S(1)}, bf16[1,8,256]{2,1,0:T(8,128)(2,1)S(1)}, u32[]{:S(2)}, u32[]{:S(2)}) collective-permute-start(bf16[1,8,256]{2,1,0:T(8,128)(2,1)S(1)} %get-tuple-element.13), channel_id=1, source_target_pairs={{0,3},{1,0},{2,1},{3,2},{4,7},{5,4},{6,5},{7,6},{8,11},{9,8},{10,9... | collective-permute-start | bytes 12296 | tf_op jit(solution)/shard_map/ppermute | solution.py:150
  27.4 3.5 %collective-permute-start.2 = (bf16[2,8,256]{2,1,0:T(8,128)(2,1)S(1)}, bf16[2,8,256]{2,1,0:T(8,128)(2,1)S(1)}, u32[]{:S(2)}, u32[]{:S(2)}) collective-permute-start(bf16[2,8,256]{2,1,0:T(8,128)(2,1)S(1)} %get-tuple-element.9), channel_id=1, source_target_pairs={{0,1},{1,2},{2,3},{3,0},{4,5},{5,6},{6,7},{7,4},{8,9},{9,10},{10,1... | collective-permute-start | bytes 24584 | tf_op jit(solution)/shard_map/ppermute | solution.py:150
  28.9 2.5 %collective-permute-start.3 = (bf16[2,8,256]{2,1,0:T(8,128)(2,1)S(1)}, bf16[2,8,256]{2,1,0:T(8,128)(2,1)S(1)}, u32[]{:S(2)}, u32[]{:S(2)}) collective-permute-start(bf16[2,8,256]{2,1,0:T(8,128)(2,1)S(1)} %get-tuple-element.11), channel_id=1, source_target_pairs={{0,2},{1,3},{2,0},{3,1},{4,6},{5,7},{6,4},{7,5},{8,10},{9,11},{10,... | collective-permute-start | bytes 24584 | tf_op jit(solution)/shard_map/ppermute | solution.py:150
  30.1 3.1 %collective-permute-start.4 = (bf16[2,8,256]{2,1,0:T(8,128)(2,1)S(1)}, bf16[2,8,256]{2,1,0:T(8,128)(2,1)S(1)}, u32[]{:S(2)}, u32[]{:S(2)}) collective-permute-start(bf16[2,8,256]{2,1,0:T(8,128)(2,1)S(1)} %get-tuple-element.10), channel_id=1, source_target_pairs={{0,3},{1,0},{2,1},{3,2},{4,7},{5,4},{6,5},{7,6},{8,11},{9,8},{10,9... | collective-permute-start | bytes 24584 | tf_op jit(solution)/shard_map/ppermute | solution.py:150

commit v3 on v2

--- a/solution.py
+++ b/solution.py
@@ -50,18 +50,22 @@
     return fwd, inv.astype(ml_dtypes.bfloat16)
 
 
-def make_kernel(events, chans, pad, length, slots, groups, share, rounds, first, from_waves):
+def make_kernel(events, chans, pad, length, slots, groups, share, rounds, n_prev, from_waves):
     half = length
     n_part = len(rounds)
 
     def kernel(*refs):
-        pl_ref, cnt_ref, sid_ref, own_ref = refs[:4]
-        part_refs = refs[4:4 + n_part]
-        f_ref, g_ref = refs[4 + n_part:6 + n_part]
-        outs = refs[6 + n_part:]
-        out_ref = outs[0]
-        spec_out = outs[1] if from_waves else None
-        nscr, xpad, specl, specp, cross = outs[1 + int(from_waves):]
+        pl_ref, cnt_ref, own_ref = refs[:3]
+        part_refs = refs[3:3 + n_part]
+        f_ref, g_ref = refs[3 + n_part:5 + n_part]
+        rest = refs[5 + n_part:]
+        if from_waves:
+            out_ref, spec_out = rest[:2]
+            rest = rest[2:]
+        else:
+            prev_ref, out_ref = rest[:2]
+            rest = rest[2:]
+        nscr, xpad, specl, specp, cross = rest
 
         def spectra(w_ref, spec_ref):
             x = w_ref[...].astype(jnp.float32)
@@ -80,17 +84,18 @@
             spec_out[...] = specl[...].astype(jnp.bfloat16)
         else:
             specl[...] = own_ref[...].astype(jnp.float32)
+            for n in range(n_prev):
+                prev = prev_ref[n]
+                for i in range(groups):
+                    out_ref[i, n] = prev[i * share:(i + 1) * share].astype(jnp.bfloat16)
 
-        sid = sid_ref[0]
         lane = lax.broadcasted_iota(jnp.int32, (1, 128), 1)
         for n, q in enumerate(rounds):
             spectra(part_refs[n], specp)
             base = q * slots * 2
             for r in range(slots):
-                d, ip = divmod(r, share)
-                slot = ((sid + d) % groups) * share + ip
-                a = jnp.minimum(jnp.maximum(pl_ref[base + 2 * slot], 0), events - 1)
-                b = jnp.minimum(jnp.maximum(pl_ref[base + 2 * slot + 1], 0), events - 1)
+                a = jnp.minimum(jnp.maximum(pl_ref[base + 2 * r], 0), events - 1)
+                b = jnp.minimum(jnp.maximum(pl_ref[base + 2 * r + 1], 0), events - 1)
                 left = specl[pl.ds(pl.multiple_of(a * pad, pad), pad), :]
                 right = specp[pl.ds(pl.multiple_of(b * pad, pad), pad), :]
                 lr, li = left[:, :half], left[:, half:]
@@ -109,29 +114,38 @@
             cb = cross[...].astype(jnp.bfloat16)
             corr = jnp.dot(cb, g_ref[...], preferred_element_type=jnp.float32)
             rows = lax.broadcasted_iota(jnp.int32, corr.shape, 0)
-            slot_of = ((sid + rows // share) % groups) * share + rows % share
-            out_ref[n] = jnp.where(slot_of < cnt_ref[q], corr, 0.0)
+            corr = jnp.where(rows < cnt_ref[q], corr, 0.0)
+            if from_waves:
+                out_ref[n] = corr
+            else:
+                for i in range(groups):
+                    out_ref[i, n_prev + n] = corr[i * share:(i + 1) * share].astype(jnp.bfloat16)
 
     return kernel
 
 
-def rounds_call(pairs, counts, sid, own, partners, fwd, inv, rounds, events, chans, slots, groups, from_waves):
+def rounds_call(pairs, counts, own, partners, fwd, inv, rounds, events, chans, slots, groups, prev=None):
     length = fwd.shape[0]
+    lags = inv.shape[1]
     pad = 16
     share = slots // groups
-    kernel = make_kernel(events, chans, pad, length, slots, groups, share, rounds, rounds[0], from_waves)
+    from_waves = prev is None
+    n_prev = 0 if from_waves else prev.shape[0]
+    kernel = make_kernel(events, chans, pad, length, slots, groups, share, rounds, n_prev, from_waves)
     smem = pl.BlockSpec(memory_space=pltpu.SMEM)
     vmem = pl.BlockSpec(memory_space=pltpu.VMEM)
-    out_shape = [jax.ShapeDtypeStruct((len(rounds), slots, inv.shape[1]), jnp.float32)]
-    out_specs = [vmem]
     if from_waves:
-        out_shape.append(jax.ShapeDtypeStruct((events * pad, 2 * length), jnp.bfloat16))
-        out_specs.append(vmem)
-    res = pl.pallas_call(
+        out_shape = (jax.ShapeDtypeStruct((len(rounds), slots, lags), jnp.float32),
+                     jax.ShapeDtypeStruct((events * pad, 2 * length), jnp.bfloat16))
+        extra = []
+    else:
+        out_shape = (jax.ShapeDtypeStruct((groups, n_prev + len(rounds), share, lags), jnp.bfloat16),)
+        extra = [prev]
+    return pl.pallas_call(
         kernel,
-        out_shape=tuple(out_shape),
-        in_specs=[smem, smem, smem] + [vmem] * (3 + len(partners)),
-        out_specs=tuple(out_specs),
+        out_shape=out_shape,
+        in_specs=[smem, smem] + [vmem] * (3 + len(partners) + len(extra)),
+        out_specs=tuple(vmem for _ in out_shape),
         scratch_shapes=[
             pltpu.VMEM((events * chans, length), jnp.float32),
             pltpu.VMEM((events * pad, length), jnp.float32),
@@ -139,17 +153,7 @@
             pltpu.VMEM((events * pad, 2 * length), jnp.float32),
             pltpu.VMEM((slots, 2 * length), jnp.float32),
         ],
-    )(pairs, counts, sid, own, *partners, fwd, inv)
-    return res
-
-
-def station_sum(block, groups):
-    total = block[:, 0]
-    for d in range(1, groups):
-        perm = [(s, (s + d) % groups) for s in range(groups)]
-        got = lax.ppermute(block[:, d].astype(jnp.bfloat16), "station", perm)
-        total = total + got.astype(jnp.float32)
-    return total
+    )(pairs, counts, own, *partners, fwd, inv, *extra)
 
 
 def shards(waveforms, pair_lists, pair_counts):
@@ -157,23 +161,20 @@
     groups = lax.axis_size("station")
     rounds, slots, _ = pair_lists.shape
     chans = stations * comps
-    share = slots // groups
     fwd_np, inv_np = half_tables(length, stations * groups * comps, LAGS)
     fwd = jnp.asarray(fwd_np)
     inv = jnp.asarray(inv_np)
     flat = waveforms.reshape(events * chans, length)
-    sid = lax.axis_index("station").astype(jnp.int32).reshape(1)
     pairs = pair_lists.reshape(-1)
     counts = pair_counts.reshape(-1)
     partners = [swapped(flat, "region", q) for q in range(rounds)]
     early = list(range(rounds - 1))
-    corr_a, spec = rounds_call(pairs, counts, sid, flat, [partners[q] for q in early], fwd, inv,
-                               early, events, chans, slots, groups, True)
-    sum_a = station_sum(corr_a.reshape(len(early), groups, share, LAGS), groups)
-    (corr_b,) = rounds_call(pairs, counts, sid, spec, [partners[-1]], fwd, inv,
-                            [rounds - 1], events, chans, slots, groups, False)
-    sum_b = station_sum(corr_b.reshape(1, groups, share, LAGS), groups)
-    return jnp.concatenate([sum_a, sum_b], axis=0)
+    corr_a, spec = rounds_call(pairs, counts, flat, [partners[q] for q in early], fwd, inv,
+                               early, events, chans, slots, groups)
+    (blocks,) = rounds_call(pairs, counts, spec, [partners[-1]], fwd, inv,
+                            [rounds - 1], events, chans, slots, groups, prev=corr_a)
+    got = lax.all_to_all(blocks, "station", 0, 0, tiled=True)
+    return jnp.sum(got.astype(jnp.float32), axis=0)
 
 
 def solution(mesh):

time: 34.1 us -> 33.2 us (0.974)
  the two profiles are of different devices: /device:TPU:1 before, /device:TPU:0 now
where the time goes in v3:
time: 33.2 us; the launch traced here: 32.9 us
  Pallas kernels  8.88 us (27%)
  blocking collectives  7.27 us (22%)
  starting transfers between devices  7.23 us (22%)
  waiting for transfers between devices  5.49 us (17%)
  local copies, waits for them, and re-layouts  3.36 us (10%)
  other arithmetic  0.62 us (2%)
    pallas_call x2, Pallas kernels, rounds_call(): pl.pallas_call(kernel, out_shape=out_shape, in_specs=[smem, smem] + [vmem...  8.88 us
    all_to_all x1, blocking collectives, shards(): got = lax.all_to_all(blocks, 'station', 0, 0, tiled=True)  7.27 us
    ppermute x3, starting transfers between devices, swapped(): return lax.ppermute(block, axis, route)  7.23 us
    ppermute x3, waiting for transfers between devices, swapped(): return lax.ppermute(block, axis, route)  5.49 us
    unnamed x12, local copies, waits for them, and re-layouts  2.49 us
    reshape x1, local copies, waits for them, and re-layouts, shards(): pairs = pair_lists.reshape(-1)  0.7 us
  transfers between devices with their start and end apart: 3, of which 1 were waited for; matrix products, arithmetic and copies ran while one was open for 2% of the time, Pallas kernels for 15%

profile of v3, /device:TPU:0, one launch (start us, length us, event | category | flops | bytes accessed | tf_op | source)
XLA Modules:
  0.0 32.9 jit_solution(9780184832349011084)
XLA Ops:
  0.0 1.0 %copy.8 = bf16[16,4,3,512]{3,2,1,0:T(4,128)(2,1)S(1)} copy(bf16[16,4,3,512]{3,1,2,0:T(4,128)(2,1)} %param.5) | data formatting | bytes 393216 | tf_op args[0]
  1.1 0.0 copy-start.4
  1.1 0.2 reshape.11.refs_2_
  1.2 0.0 copy-start
  1.2 3.1 %collective-permute-start = (bf16[192,512]{1,0:T(8,128)(2,1)S(1)}, bf16[192,512]{1,0:T(8,128)(2,1)S(1)}, u32[]{:S(2)}, u32[]{:S(2)}) collective-permute-start(bf16[192,512]{1,0:T(8,128)(2,1)S(1)} %reshape.11.refs_2_), channel_id=1, source_target_pairs={{0,4},{4,0},{8,12},{12,8},{16,20},{20,16},{24,28},{28,24},{1,5},{5... | collective-permute-start | bytes 589832 | tf_op jit(solution)/shard_map/ppermute | solution.py:24
  4.3 1.6 %collective-permute-start.1 = (bf16[192,512]{1,0:T(8,128)(2,1)S(1)}, bf16[192,512]{1,0:T(8,128)(2,1)S(1)}, u32[]{:S(2)}, u32[]{:S(2)}) collective-permute-start(bf16[192,512]{1,0:T(8,128)(2,1)S(1)} %reshape.11.refs_2_), channel_id=1, source_target_pairs={{0,8},{8,0},{4,12},{12,4},{16,24},{24,16},{20,28},{28,20},{1,9},{9... | collective-permute-start | bytes 589832 | tf_op jit(solution)/shard_map/ppermute | solution.py:24
  5.9 2.6 %collective-permute-start.2 = (bf16[192,512]{1,0:T(8,128)(2,1)S(1)}, bf16[192,512]{1,0:T(8,128)(2,1)S(1)}, u32[]{:S(2)}, u32[]{:S(2)}) collective-permute-start(bf16[192,512]{1,0:T(8,128)(2,1)S(1)} %reshape.11.refs_2_), channel_id=1, source_target_pairs={{0,16},{16,0},{4,20},{20,4},{8,24},{24,8},{12,28},{28,12},{1,17},{... | collective-permute-start | bytes 589832 | tf_op jit(solution)/shard_map/ppermute | solution.py:24
  8.5 0.0 copy-done.4
  8.5 0.1 copy.7
  8.6 0.7 %reshape.9.refs_0_ = s32[192]{0:T(256)} reshape(s32[3,32,2]{2,1,0:T(8,128)S(1)} %copy.7) | data formatting | bytes 1536 | tf_op jit(solution)/shard_map/reshape | solution.py:168
  9.3 0.0 collective-permute-done.refs_3_
  9.3 0.0 copy-start.2
  9.3 5.5 %collective-permute-done.1.refs_4_ = bf16[192,512]{1,0:T(8,128)(2,1)S(1)} collective-permute-done((bf16[192,512]{1,0:T(8,128)(2,1)S(1)}, bf16[192,512]{1,0:T(8,128)(2,1)S(1)}, u32[]{:S(2)}, u32[]{:S(2)}) %collective-permute-start.1) | collective-permute-done | bytes 196640 | tf_op jit(solution)/shard_map/ppermute | solution.py:24
  14.8 0.0 copy-start.3
  14.8 0.0 copy-done
  14.8 0.0 copy-done.2
  14.8 0.7 %copy-done.3 = bf16[192,512]{1,0:T(8,128)(2,1)} copy-done((bf16[192,512]{1,0:T(8,128)(2,1)}, bf16[192,512]{1,0:T(8,128)(2,1)S(1)}, u32[]{:S(2)}) %copy-start.3) | copy-done | bytes 196632
  15.4 5.1 %shard_map.55 = (f32[2,32,256]{2,1,0:T(8,128)}, bf16[256,1024]{1,0:T(8,128)(2,1)}) custom-call(s32[192]{0:T(256)} %reshape.9.refs_0_, s32[3]{0:T(128)} %bitcast.1, bf16[192,512]{1,0:T(8,128)(2,1)} %copy-done, bf16[192,512]{1,0:T(8,128)(2,1)} %copy-done.2, bf16[192,512]{1,0:T(8,128)(2,1)} %copy-done.3, bf16[512,1024]{1,0:T(8,128)(2,1)} %constant.6.clone.refs_5_.refs_4_, ...), custom_call_target="tpu_custom_call" | custom-call | tf_op jit(solution)/shard_map/pallas_call | solution.py:144
  20.5 0.0 collective-permute-done.2.refs_3_
  20.5 0.0 copy-start.1
  20.5 0.7 %copy-done.1 = bf16[192,512]{1,0:T(8,128)(2,1)} copy-done((bf16[192,512]{1,0:T(8,128)(2,1)}, bf16[192,512]{1,0:T(8,128)(2,1)S(1)}, u32[]{:S(2)}) %copy-start.1) | copy-done | bytes 196632
  21.2 3.8 %shard_map.56 = bf16[4,3,8,256]{3,2,1,0:T(8,128)(2,1)} custom-call(s32[192]{0:T(256)} %reshape.9.refs_0_, s32[3]{0:T(128)} %bitcast.2, bf16[256,1024]{1,0:T(8,128)(2,1)} %get-tuple-element.7.refs_2_, bf16[192,512]{1,0:T(8,128)(2,1)} %copy-done.1, bf16[512,1024]{1,0:T(8,128)(2,1)} %constant.6.clone.refs_5_.refs_4_, ...), custom_call_target="tpu_custom_call" | custom-call | tf_op jit(solution)/shard_map/pallas_call | solution.py:144
  25.0 7.3 %all_to_all.5 = bf16[4,3,8,256]{3,2,1,0:T(8,128)(2,1)S(1)} all-to-all(bf16[4,3,8,256]{3,2,1,0:T(8,128)(2,1)} %shard_map.56), channel_id=1, replica_groups=mesh['region'=8,'station'=4] {'station'}, dimensions={0} | all-to-all | bytes 98304 | tf_op jit(solution)/shard_map/all_to_all | solution.py:176
  32.3 0.6 %convert_reduce_fusion = f32[3,8,256]{2,1,0:T(8,128)} fusion(bf16[4,3,8,256]{3,2,1,0:T(8,128)(2,1)S(1)} %all_to_all.5), kind=kLoop, calls=%fused_computation | loop fusion | flops 43008 | bytes 73728 | tf_op jit(solution)/shard_map/reduce_sum | solution.py:177
Async XLA Ops:
  1.1 7.4 %copy-start.4 = (s32[3,32,2]{1,2,0:T(2,128)S(1)}, s32[3,32,2]{1,2,0:T(2,128)}, u32[]{:S(2)}) copy-start(s32[3,32,2]{1,2,0:T(2,128)} %param.6) | copy-start | bytes 2308
  1.2 13.5 %copy-start = (bf16[192,512]{1,0:T(8,128)(2,1)}, bf16[192,512]{1,0:T(8,128)(2,1)S(1)}, u32[]{:S(2)}) copy-start(bf16[192,512]{1,0:T(8,128)(2,1)S(1)} %reshape.11.refs_2_) | copy-start | bytes 589828
  1.2 8.0 %collective-permute-start = (bf16[192,512]{1,0:T(8,128)(2,1)S(1)}, bf16[192,512]{1,0:T(8,128)(2,1)S(1)}, u32[]{:S(2)}, u32[]{:S(2)}) collective-permute-start(bf16[192,512]{1,0:T(8,128)(2,1)S(1)} %reshape.11.refs_2_), channel_id=1, source_target_pairs={{0,4},{4,0},{8,12},{12,8},{16,20},{20,16},{24,28},{28,24},{1,5},{5... | collective-permute-start | bytes 589832 | tf_op jit(solution)/shard_map/ppermute | solution.py:24
  4.3 10.5 %collective-permute-start.1 = (bf16[192,512]{1,0:T(8,128)(2,1)S(1)}, bf16[192,512]{1,0:T(8,128)(2,1)S(1)}, u32[]{:S(2)}, u32[]{:S(2)}) collective-permute-start(bf16[192,512]{1,0:T(8,128)(2,1)S(1)} %reshape.11.refs_2_), channel_id=1, source_target_pairs={{0,8},{8,0},{4,12},{12,4},{16,24},{24,16},{20,28},{28,20},{1,9},{9... | collective-permute-start | bytes 589832 | tf_op jit(solution)/shard_map/ppermute | solution.py:24
  5.9 14.7 %collective-permute-start.2 = (bf16[192,512]{1,0:T(8,128)(2,1)S(1)}, bf16[192,512]{1,0:T(8,128)(2,1)S(1)}, u32[]{:S(2)}, u32[]{:S(2)}) collective-permute-start(bf16[192,512]{1,0:T(8,128)(2,1)S(1)} %reshape.11.refs_2_), channel_id=1, source_target_pairs={{0,16},{16,0},{4,20},{20,4},{8,24},{24,8},{12,28},{28,12},{1,17},{... | collective-permute-start | bytes 589832 | tf_op jit(solution)/shard_map/ppermute | solution.py:24
  9.3 5.5 %copy-start.2 = (bf16[192,512]{1,0:T(8,128)(2,1)}, bf16[192,512]{1,0:T(8,128)(2,1)S(1)}, u32[]{:S(2)}) copy-start(bf16[192,512]{1,0:T(8,128)(2,1)S(1)} %collective-permute-done.refs_3_) | copy-start | bytes 589828
  14.8 0.7 %copy-start.3 = (bf16[192,512]{1,0:T(8,128)(2,1)}, bf16[192,512]{1,0:T(8,128)(2,1)S(1)}, u32[]{:S(2)}) copy-start(bf16[192,512]{1,0:T(8,128)(2,1)S(1)} %collective-permute-done.1.refs_4_) | copy-start | bytes 589828
  20.5 0.7 %copy-start.1 = (bf16[192,512]{1,0:T(8,128)(2,1)}, bf16[192,512]{1,0:T(8,128)(2,1)S(1)}, u32[]{:S(2)}) copy-start(bf16[192,512]{1,0:T(8,128)(2,1)S(1)} %collective-permute-done.2.refs_3_) | copy-start | bytes 589828

commit v4 on v3

--- a/solution.py
+++ b/solution.py
@@ -55,10 +55,10 @@
     n_part = len(rounds)
 
     def kernel(*refs):
-        pl_ref, cnt_ref, own_ref = refs[:3]
-        part_refs = refs[3:3 + n_part]
-        f_ref, g_ref = refs[3 + n_part:5 + n_part]
-        rest = refs[5 + n_part:]
+        pl_ref, cnt_ref, sid_ref, own_ref = refs[:4]
+        part_refs = refs[4:4 + n_part]
+        f_ref, g_ref = refs[4 + n_part:6 + n_part]
+        rest = refs[6 + n_part:]
         if from_waves:
             out_ref, spec_out = rest[:2]
             rest = rest[2:]
@@ -85,17 +85,17 @@
         else:
             specl[...] = own_ref[...].astype(jnp.float32)
             for n in range(n_prev):
-                prev = prev_ref[n]
-                for i in range(groups):
-                    out_ref[i, n] = prev[i * share:(i + 1) * share].astype(jnp.bfloat16)
+                out_ref[n] = prev_ref[n]
 
+        sid = sid_ref[0]
         lane = lax.broadcasted_iota(jnp.int32, (1, 128), 1)
         for n, q in enumerate(rounds):
             spectra(part_refs[n], specp)
             base = q * slots * 2
             for r in range(slots):
-                a = jnp.minimum(jnp.maximum(pl_ref[base + 2 * r], 0), events - 1)
-                b = jnp.minimum(jnp.maximum(pl_ref[base + 2 * r + 1], 0), events - 1)
+                slot = (sid ^ (r // share)) * share + r % share
+                a = jnp.minimum(jnp.maximum(pl_ref[base + 2 * slot], 0), events - 1)
+                b = jnp.minimum(jnp.maximum(pl_ref[base + 2 * slot + 1], 0), events - 1)
                 left = specl[pl.ds(pl.multiple_of(a * pad, pad), pad), :]
                 right = specp[pl.ds(pl.multiple_of(b * pad, pad), pad), :]
                 lr, li = left[:, :half], left[:, half:]
@@ -114,17 +114,13 @@
             cb = cross[...].astype(jnp.bfloat16)
             corr = jnp.dot(cb, g_ref[...], preferred_element_type=jnp.float32)
             rows = lax.broadcasted_iota(jnp.int32, corr.shape, 0)
-            corr = jnp.where(rows < cnt_ref[q], corr, 0.0)
-            if from_waves:
-                out_ref[n] = corr
-            else:
-                for i in range(groups):
-                    out_ref[i, n_prev + n] = corr[i * share:(i + 1) * share].astype(jnp.bfloat16)
+            slot_of = (sid ^ (rows // share)) * share + rows % share
+            out_ref[n_prev + n] = jnp.where(slot_of < cnt_ref[q], corr, 0.0)
 
     return kernel
 
 
-def rounds_call(pairs, counts, own, partners, fwd, inv, rounds, events, chans, slots, groups, prev=None):
+def rounds_call(pairs, counts, sid, own, partners, fwd, inv, rounds, events, chans, slots, groups, prev=None):
     length = fwd.shape[0]
     lags = inv.shape[1]
     pad = 16
@@ -139,12 +135,12 @@
                      jax.ShapeDtypeStruct((events * pad, 2 * length), jnp.bfloat16))
         extra = []
     else:
-        out_shape = (jax.ShapeDtypeStruct((groups, n_prev + len(rounds), share, lags), jnp.bfloat16),)
+        out_shape = (jax.ShapeDtypeStruct((n_prev + len(rounds), slots, lags), jnp.float32),)
         extra = [prev]
     return pl.pallas_call(
         kernel,
         out_shape=out_shape,
-        in_specs=[smem, smem] + [vmem] * (3 + len(partners) + len(extra)),
+        in_specs=[smem, smem, smem] + [vmem] * (3 + len(partners) + len(extra)),
         out_specs=tuple(vmem for _ in out_shape),
         scratch_shapes=[
             pltpu.VMEM((events * chans, length), jnp.float32),
@@ -153,7 +149,19 @@
             pltpu.VMEM((events * pad, 2 * length), jnp.float32),
             pltpu.VMEM((slots, 2 * length), jnp.float32),
         ],
-    )(pairs, counts, own, *partners, fwd, inv, *extra)
+    )(pairs, counts, sid, own, *partners, fwd, inv, *extra)
+
+
+def station_sum(block, groups):
+    total = block
+    bit = groups // 2
+    while bit:
+        rows = total.shape[1] // 2
+        perm = [(s, s ^ bit) for s in range(groups)]
+        got = lax.ppermute(total[:, rows:].astype(jnp.bfloat16), "station", perm)
+        total = total[:, :rows] + got.astype(jnp.float32)
+        bit //= 2
+    return total
 
 
 def shards(waveforms, pair_lists, pair_counts):
@@ -165,16 +173,16 @@
     fwd = jnp.asarray(fwd_np)
     inv = jnp.asarray(inv_np)
     flat = waveforms.reshape(events * chans, length)
+    sid = lax.axis_index("station").astype(jnp.int32).reshape(1)
     pairs = pair_lists.reshape(-1)
     counts = pair_counts.reshape(-1)
-    partners = [swapped(flat, "region", q) for q in range(rounds)]
+    partners = {q: swapped(flat, "region", q) for q in reversed(range(rounds))}
     early = list(range(rounds - 1))
-    corr_a, spec = rounds_call(pairs, counts, flat, [partners[q] for q in early], fwd, inv,
+    corr_a, spec = rounds_call(pairs, counts, sid, flat, [partners[q] for q in early], fwd, inv,
                                early, events, chans, slots, groups)
-    (blocks,) = rounds_call(pairs, counts, spec, [partners[-1]], fwd, inv,
-                            [rounds - 1], events, chans, slots, groups, prev=corr_a)
-    got = lax.all_to_all(blocks, "station", 0, 0, tiled=True)
-    return jnp.sum(got.astype(jnp.float32), axis=0)
+    (corr,) = rounds_call(pairs, counts, sid, spec, [partners[rounds - 1]], fwd, inv,
+                          [rounds - 1], events, chans, slots, groups, prev=corr_a)
+    return station_sum(corr, groups)
 
 
 def solution(mesh):

time: 33.2 us -> 32.6 us (0.982)
  blocking collectives: 7.27 us -> 0 us
  waiting for transfers between devices: 5.49 us -> 8.99 us
  starting transfers between devices: 7.23 us -> 8.79 us
  local copies, waits for them, and re-layouts: 3.36 us -> 4.19 us
  other arithmetic: 0.62 us -> 1.42 us
    all_to_all x1 -> x0, blocking collectives: 7.27 us -> none  [shards(): got = lax.all_to_all(blocks, 'station', 0, 0, tiled=True)]
    ppermute x0 -> x2, waiting for transfers between devices: none -> 3.5 us  [station_sum(): got = lax.ppermute(total[:, rows:].astype(jnp.bfloat16), 'station', perm)]
    ppermute x0 -> x2, starting transfers between devices: none -> 1.56 us  [station_sum(): got = lax.ppermute(total[:, rows:].astype(jnp.bfloat16), 'station', perm)]
    add x0 -> x2, other arithmetic: none -> 1.42 us  [station_sum(): total = total[:, :rows] + got.astype(jnp.float32)]
    slice x0 -> x2, local copies, waits for them, and re-layouts: none -> 0.81 us  [station_sum(): got = lax.ppermute(total[:, rows:].astype(jnp.bfloat16), 'station', perm)]
    reduce_sum x1 -> x0, other arithmetic: 0.62 us -> none  [shards(): return jnp.sum(got.astype(jnp.float32), axis=0)]
  transfers between devices with their start and end apart: 3 -> 5, of which waited for: 1 -> 3; matrix products, arithmetic and copies ran while one was open for 2% -> 2% of each run, Pallas kernels for 15% -> 16%
where the time goes in v4:
time: 32.6 us; the launch traced here: 32.3 us
  waiting for transfers between devices  8.99 us (28%)
  Pallas kernels  8.9 us (27%)
  starting transfers between devices  8.79 us (27%)
  local copies, waits for them, and re-layouts  4.19 us (13%)
  other arithmetic  1.42 us (4%)
    pallas_call x2, Pallas kernels, rounds_call(): pl.pallas_call(kernel, out_shape=out_shape, in_specs=[smem, smem, smem] +...  8.9 us
    ppermute x3, starting transfers between devices, swapped(): return lax.ppermute(block, axis, route)  7.23 us
    ppermute x3, waiting for transfers between devices, swapped(): return lax.ppermute(block, axis, route)  5.49 us
    ppermute x2, waiting for transfers between devices, station_sum(): got = lax.ppermute(total[:, rows:].astype(jnp.bfloat16), 'station', perm)  3.5 us
    unnamed x12, local copies, waits for them, and re-layouts  2.51 us
    ppermute x2, starting transfers between devices, station_sum(): got = lax.ppermute(total[:, rows:].astype(jnp.bfloat16), 'station', perm)  1.56 us
    add x2, other arithmetic, station_sum(): total = total[:, :rows] + got.astype(jnp.float32)  1.42 us
    slice x2, local copies, waits for them, and re-layouts, station_sum(): got = lax.ppermute(total[:, rows:].astype(jnp.bfloat16), 'station', perm)  0.81 us
  transfers between devices with their start and end apart: 5, of which 3 were waited for; matrix products, arithmetic and copies ran while one was open for 2% of the time, Pallas kernels for 16%

profile of v4, /device:TPU:0, one launch (start us, length us, event | category | flops | bytes accessed | tf_op | source)
XLA Modules:
  0.0 32.3 jit_solution(8182069347542521184)
XLA Ops:
  0.0 1.0 %copy.8 = bf16[16,4,3,512]{3,2,1,0:T(4,128)(2,1)S(1)} copy(bf16[16,4,3,512]{3,1,2,0:T(4,128)(2,1)} %param.5) | data formatting | bytes 393216 | tf_op args[0]
  1.1 0.0 copy-start.4
  1.1 0.2 reshape.15.refs_3_
  1.2 0.0 copy-start
  1.2 3.1 %collective-permute-start = (bf16[192,512]{1,0:T(8,128)(2,1)S(1)}, bf16[192,512]{1,0:T(8,128)(2,1)S(1)}, u32[]{:S(2)}, u32[]{:S(2)}) collective-permute-start(bf16[192,512]{1,0:T(8,128)(2,1)S(1)} %reshape.15.refs_3_), channel_id=1, source_target_pairs={{0,4},{4,0},{8,12},{12,8},{16,20},{20,16},{24,28},{28,24},{1,5},{5... | collective-permute-start | bytes 589832 | tf_op jit(solution)/shard_map/ppermute | solution.py:24
  4.3 1.6 %collective-permute-start.1 = (bf16[192,512]{1,0:T(8,128)(2,1)S(1)}, bf16[192,512]{1,0:T(8,128)(2,1)S(1)}, u32[]{:S(2)}, u32[]{:S(2)}) collective-permute-start(bf16[192,512]{1,0:T(8,128)(2,1)S(1)} %reshape.15.refs_3_), channel_id=1, source_target_pairs={{0,8},{8,0},{4,12},{12,4},{16,24},{24,16},{20,28},{28,20},{1,9},{9... | collective-permute-start | bytes 589832 | tf_op jit(solution)/shard_map/ppermute | solution.py:24
  5.9 2.6 %collective-permute-start.2 = (bf16[192,512]{1,0:T(8,128)(2,1)S(1)}, bf16[192,512]{1,0:T(8,128)(2,1)S(1)}, u32[]{:S(2)}, u32[]{:S(2)}) collective-permute-start(bf16[192,512]{1,0:T(8,128)(2,1)S(1)} %reshape.15.refs_3_), channel_id=1, source_target_pairs={{0,16},{16,0},{4,20},{20,4},{8,24},{24,8},{12,28},{28,12},{1,17},{... | collective-permute-start | bytes 589832 | tf_op jit(solution)/shard_map/ppermute | solution.py:24
  8.5 0.0 copy-done.4
  8.5 0.1 copy.7
  8.6 0.7 %reshape.12.refs_0_ = s32[192]{0:T(256)} reshape(s32[3,32,2]{2,1,0:T(8,128)S(1)} %copy.7) | data formatting | bytes 1536 | tf_op jit(solution)/shard_map/reshape | solution.py:177
  9.3 0.0 collective-permute-done.refs_4_
  9.3 0.0 copy-start.1
  9.3 5.5 %collective-permute-done.1.refs_5_ = bf16[192,512]{1,0:T(8,128)(2,1)S(1)} collective-permute-done((bf16[192,512]{1,0:T(8,128)(2,1)S(1)}, bf16[192,512]{1,0:T(8,128)(2,1)S(1)}, u32[]{:S(2)}, u32[]{:S(2)}) %collective-permute-start.1) | collective-permute-done | bytes 196640 | tf_op jit(solution)/shard_map/ppermute | solution.py:24
  14.8 0.0 copy-start.2
  14.8 0.0 copy-done
  14.8 0.0 copy-done.1
  14.8 0.7 %copy-done.2 = bf16[192,512]{1,0:T(8,128)(2,1)} copy-done((bf16[192,512]{1,0:T(8,128)(2,1)}, bf16[192,512]{1,0:T(8,128)(2,1)S(1)}, u32[]{:S(2)}) %copy-start.2) | copy-done | bytes 196632
  15.5 5.1 %shard_map.55 = (f32[2,32,256]{2,1,0:T(8,128)}, bf16[256,1024]{1,0:T(8,128)(2,1)}) custom-call(s32[192]{0:T(256)} %reshape.12.refs_0_, s32[3]{0:T(128)} %bitcast.2, s32[1]{0:T(128)} %bitcast.1.refs_2_, bf16[192,512]{1,0:T(8,128)(2,1)} %copy-done, bf16[192,512]{1,0:T(8,128)(2,1)} %copy-done.1, bf16[192,512]{1,0:T(8,128)(2,1)} %copy-done.2, ...), custom_call_target="tpu_custom_call" | custom-call | tf_op jit(solution)/shard_map/pallas_call | solution.py:140
  20.5 0.0 collective-permute-done.2.refs_4_
  20.5 0.0 copy-start.3
  20.5 0.7 %copy-done.3 = bf16[192,512]{1,0:T(8,128)(2,1)} copy-done((bf16[192,512]{1,0:T(8,128)(2,1)}, bf16[192,512]{1,0:T(8,128)(2,1)S(1)}, u32[]{:S(2)}) %copy-start.3) | copy-done | bytes 196632
  21.2 3.8 %shard_map.56 = f32[3,32,256]{2,1,0:T(8,128)} custom-call(s32[192]{0:T(256)} %reshape.12.refs_0_, s32[3]{0:T(128)} %bitcast.3, s32[1]{0:T(128)} %bitcast.1.refs_2_, bf16[256,1024]{1,0:T(8,128)(2,1)} %get-tuple-element.7.refs_3_, bf16[192,512]{1,0:T(8,128)(2,1)} %copy-done.3, bf16[512,1024]{1,0:T(8,128)(2,1)} %constant.8.clone.refs_6_.refs_5_, ...), custom_call_target="tpu_custom_call" | custom-call | tf_op jit(solution)/shard_map/pallas_call | solution.py:140
  25.0 0.8 %slice.26 = bf16[3,16,256]{2,1,0:T(8,128)(2,1)S(1)} slice(f32[3,32,256]{2,1,0:T(8,128)} %shard_map.56), slice={[0:3], [16:32], [0:256]} | slice | bytes 49152 | tf_op jit(solution)/shard_map/slice | solution.py:161
  25.8 1.5 %collective-permute-start.3 = (bf16[3,16,256]{2,1,0:T(8,128)(2,1)S(1)}, bf16[3,16,256]{2,1,0:T(8,128)(2,1)S(1)}, u32[]{:S(2)}, u32[]{:S(2)}) collective-permute-start(bf16[3,16,256]{2,1,0:T(8,128)(2,1)S(1)} %slice.26), channel_id=1, source_target_pairs={{0,2},{1,3},{2,0},{3,1},{4,6},{5,7},{6,4},{7,5},{8,10},{9,11},{10,... | collective-permute-start | bytes 73736 | tf_op jit(solution)/shard_map/ppermute | solution.py:161
  27.3 2.3 %collective-permute-done.3 = bf16[3,16,256]{2,1,0:T(8,128)(2,1)S(1)} collective-permute-done((bf16[3,16,256]{2,1,0:T(8,128)(2,1)S(1)}, bf16[3,16,256]{2,1,0:T(8,128)(2,1)S(1)}, u32[]{:S(2)}, u32[]{:S(2)}) %collective-permute-start.3) | collective-permute-done | bytes 24608 | tf_op jit(solution)/shard_map/ppermute | solution.py:161
  29.7 0.8 %slice_add_fusion = f32[3,16,256]{2,1,0:T(8,128)S(1)} fusion(f32[3,32,256]{2,1,0:T(8,128)} %shard_map.56, bf16[3,16,256]{2,1,0:T(8,128)(2,1)S(1)} %collective-permute-done.3), kind=kLoop, calls=%fused_computation.1 | loop fusion | flops 24576 | bytes 122880 | tf_op jit(solution)/shard_map/add | solution.py:162
  30.5 0.1 collective-permute-start.4
  30.6 1.2 %collective-permute-done.4 = bf16[3,8,256]{2,1,0:T(8,128)(2,1)S(1)} collective-permute-done((bf16[3,8,256]{2,1,0:T(8,128)(2,1)S(1)}, bf16[3,8,256]{2,1,0:T(8,128)(2,1)S(1)}, u32[]{:S(2)}, u32[]{:S(2)}) %collective-permute-start.4) | collective-permute-done | bytes 12320 | tf_op jit(solution)/shard_map/ppermute | solution.py:161
  31.7 0.6 %slice_add_fusion.1 = f32[3,8,256]{2,1,0:T(8,128)} fusion(f32[3,16,256]{2,1,0:T(8,128)S(1)} %slice_add_fusion, bf16[3,8,256]{2,1,0:T(8,128)(2,1)S(1)} %collective-permute-done.4), kind=kLoop, calls=%fused_computation.3 | loop fusion | flops 12288 | bytes 61440 | tf_op jit(solution)/shard_map/add | solution.py:162
  (1 shorter events, 0.0 us)
Async XLA Ops:
  1.1 7.4 %copy-start.4 = (s32[3,32,2]{1,2,0:T(2,128)S(1)}, s32[3,32,2]{1,2,0:T(2,128)}, u32[]{:S(2)}) copy-start(s32[3,32,2]{1,2,0:T(2,128)} %param.6) | copy-start | bytes 2308
  1.2 13.5 %copy-start = (bf16[192,512]{1,0:T(8,128)(2,1)}, bf16[192,512]{1,0:T(8,128)(2,1)S(1)}, u32[]{:S(2)}) copy-start(bf16[192,512]{1,0:T(8,128)(2,1)S(1)} %reshape.15.refs_3_) | copy-start | bytes 589828
  1.2 8.0 %collective-permute-start = (bf16[192,512]{1,0:T(8,128)(2,1)S(1)}, bf16[192,512]{1,0:T(8,128)(2,1)S(1)}, u32[]{:S(2)}, u32[]{:S(2)}) collective-permute-start(bf16[192,512]{1,0:T(8,128)(2,1)S(1)} %reshape.15.refs_3_), channel_id=1, source_target_pairs={{0,4},{4,0},{8,12},{12,8},{16,20},{20,16},{24,28},{28,24},{1,5},{5... | collective-permute-start | bytes 589832 | tf_op jit(solution)/shard_map/ppermute | solution.py:24
  4.3 10.5 %collective-permute-start.1 = (bf16[192,512]{1,0:T(8,128)(2,1)S(1)}, bf16[192,512]{1,0:T(8,128)(2,1)S(1)}, u32[]{:S(2)}, u32[]{:S(2)}) collective-permute-start(bf16[192,512]{1,0:T(8,128)(2,1)S(1)} %reshape.15.refs_3_), channel_id=1, source_target_pairs={{0,8},{8,0},{4,12},{12,4},{16,24},{24,16},{20,28},{28,20},{1,9},{9... | collective-permute-start | bytes 589832 | tf_op jit(solution)/shard_map/ppermute | solution.py:24
  5.9 14.7 %collective-permute-start.2 = (bf16[192,512]{1,0:T(8,128)(2,1)S(1)}, bf16[192,512]{1,0:T(8,128)(2,1)S(1)}, u32[]{:S(2)}, u32[]{:S(2)}) collective-permute-start(bf16[192,512]{1,0:T(8,128)(2,1)S(1)} %reshape.15.refs_3_), channel_id=1, source_target_pairs={{0,16},{16,0},{4,20},{20,4},{8,24},{24,8},{12,28},{28,12},{1,17},{... | collective-permute-start | bytes 589832 | tf_op jit(solution)/shard_map/ppermute | solution.py:24
  9.3 5.5 %copy-start.1 = (bf16[192,512]{1,0:T(8,128)(2,1)}, bf16[192,512]{1,0:T(8,128)(2,1)S(1)}, u32[]{:S(2)}) copy-start(bf16[192,512]{1,0:T(8,128)(2,1)S(1)} %collective-permute-done.refs_4_) | copy-start | bytes 589828
  14.8 0.7 %copy-start.2 = (bf16[192,512]{1,0:T(8,128)(2,1)}, bf16[192,512]{1,0:T(8,128)(2,1)S(1)}, u32[]{:S(2)}) copy-start(bf16[192,512]{1,0:T(8,128)(2,1)S(1)} %collective-permute-done.1.refs_5_) | copy-start | bytes 589828
  20.5 0.7 %copy-start.3 = (bf16[192,512]{1,0:T(8,128)(2,1)}, bf16[192,512]{1,0:T(8,128)(2,1)S(1)}, u32[]{:S(2)}) copy-start(bf16[192,512]{1,0:T(8,128)(2,1)S(1)} %collective-permute-done.2.refs_4_) | copy-start | bytes 589828
  25.8 3.8 %collective-permute-start.3 = (bf16[3,16,256]{2,1,0:T(8,128)(2,1)S(1)}, bf16[3,16,256]{2,1,0:T(8,128)(2,1)S(1)}, u32[]{:S(2)}, u32[]{:S(2)}) collective-permute-start(bf16[3,16,256]{2,1,0:T(8,128)(2,1)S(1)} %slice.26), channel_id=1, source_target_pairs={{0,2},{1,3},{2,0},{3,1},{4,6},{5,7},{6,4},{7,5},{8,10},{9,11},{10,... | collective-permute-start | bytes 73736 | tf_op jit(solution)/shard_map/ppermute | solution.py:161
  30.5 1.2 %collective-permute-start.4 = (bf16[3,8,256]{2,1,0:T(8,128)(2,1)S(1)}, bf16[3,8,256]{2,1,0:T(8,128)(2,1)S(1)}, u32[]{:S(2)}, u32[]{:S(2)}) collective-permute-start(bf16[3,8,256]{2,1,0:T(8,128)(2,1)S(1)} %slice.27), channel_id=1, source_target_pairs={{0,1},{1,0},{2,3},{3,2},{4,5},{5,4},{6,7},{7,6},{8,9},{9,8},{10,11... | collective-permute-start | bytes 36872 | tf_op jit(solution)/shard_map/ppermute | solution.py:161

commit v5 on v4

--- a/solution.py
+++ b/solution.py
@@ -63,8 +63,8 @@
             out_ref, spec_out = rest[:2]
             rest = rest[2:]
         else:
-            prev_ref, out_ref = rest[:2]
-            rest = rest[2:]
+            prev_ref, keep_ref, send_ref = rest[:3]
+            rest = rest[3:]
         nscr, xpad, specl, specp, cross = rest
 
         def spectra(w_ref, spec_ref):
@@ -85,7 +85,9 @@
         else:
             specl[...] = own_ref[...].astype(jnp.float32)
             for n in range(n_prev):
-                out_ref[n] = prev_ref[n]
+                prev = prev_ref[n]
+                keep_ref[n] = prev[:slots // 2]
+                send_ref[n] = prev[slots // 2:].astype(jnp.bfloat16)
 
         sid = sid_ref[0]
         lane = lax.broadcasted_iota(jnp.int32, (1, 128), 1)
@@ -115,7 +117,12 @@
             corr = jnp.dot(cb, g_ref[...], preferred_element_type=jnp.float32)
             rows = lax.broadcasted_iota(jnp.int32, corr.shape, 0)
             slot_of = (sid ^ (rows // share)) * share + rows % share
-            out_ref[n_prev + n] = jnp.where(slot_of < cnt_ref[q], corr, 0.0)
+            corr = jnp.where(slot_of < cnt_ref[q], corr, 0.0)
+            if from_waves:
+                out_ref[n] = corr
+            else:
+                keep_ref[n_prev + n] = corr[:slots // 2]
+                send_ref[n_prev + n] = corr[slots // 2:].astype(jnp.bfloat16)
 
     return kernel
 
@@ -135,7 +142,8 @@
                      jax.ShapeDtypeStruct((events * pad, 2 * length), jnp.bfloat16))
         extra = []
     else:
-        out_shape = (jax.ShapeDtypeStruct((n_prev + len(rounds), slots, lags), jnp.float32),)
+        out_shape = (jax.ShapeDtypeStruct((n_prev + len(rounds), slots // 2, lags), jnp.float32),
+                     jax.ShapeDtypeStruct((n_prev + len(rounds), slots // 2, lags), jnp.bfloat16))
         extra = [prev]
     return pl.pallas_call(
         kernel,
@@ -152,16 +160,16 @@
     )(pairs, counts, sid, own, *partners, fwd, inv, *extra)
 
 
-def station_sum(block, groups):
-    total = block
+def station_sum(keep, send, groups):
     bit = groups // 2
-    while bit:
+    while True:
+        perm = [(s, s ^ bit) for s in range(groups)]
+        total = keep + lax.ppermute(send, "station", perm).astype(jnp.float32)
+        bit //= 2
+        if not bit:
+            return total
         rows = total.shape[1] // 2
-        perm = [(s, s ^ bit) for s in range(groups)]
-        got = lax.ppermute(total[:, rows:].astype(jnp.bfloat16), "station", perm)
-        total = total[:, :rows] + got.astype(jnp.float32)
-        bit //= 2
-    return total
+        keep, send = total[:, :rows], total[:, rows:].astype(jnp.bfloat16)
 
 
 def shards(waveforms, pair_lists, pair_counts):
@@ -180,9 +188,9 @@
     early = list(range(rounds - 1))
     corr_a, spec = rounds_call(pairs, counts, sid, flat, [partners[q] for q in early], fwd, inv,
                                early, events, chans, slots, groups)
-    (corr,) = rounds_call(pairs, counts, sid, spec, [partners[rounds - 1]], fwd, inv,
+    keep, send = rounds_call(pairs, counts, sid, spec, [partners[rounds - 1]], fwd, inv,
                           [rounds - 1], events, chans, slots, groups, prev=corr_a)
-    return station_sum(corr, groups)
+    return station_sum(keep, send, groups)
 
 
 def solution(mesh):

time: 32.6 us -> 32 us (0.982)
  local copies, waits for them, and re-layouts: 4.19 us -> 3.39 us
    slice x2 -> x1, local copies, waits for them, and re-layouts: 0.81 us -> 0.01 us  [station_sum(): keep, send = (total[:, :rows], total[:, rows:].astype(jnp.bfloat16))]
  transfers between devices with their start and end apart: 5 -> 5, of which waited for: 3 -> 3; matrix products, arithmetic and copies ran while one was open for 2% -> 3% of each run, Pallas kernels for 16% -> 16%
where the time goes in v5:
time: 32 us; the launch traced here: 31.7 us
  waiting for transfers between devices  9.18 us (29%)
  Pallas kernels  8.87 us (28%)
  starting transfers between devices  8.79 us (27%)
  local copies, waits for them, and re-layouts  3.39 us (11%)
  other arithmetic  1.42 us (4%)
    pallas_call x2, Pallas kernels, rounds_call(): pl.pallas_call(kernel, out_shape=out_shape, in_specs=[smem, smem, smem] +...  8.87 us
    ppermute x3, starting transfers between devices, swapped(): return lax.ppermute(block, axis, route)  7.23 us
    ppermute x3, waiting for transfers between devices, swapped(): return lax.ppermute(block, axis, route)  5.47 us
    ppermute x2, waiting for transfers between devices, station_sum(): total = keep + lax.ppermute(send, 'station', perm).astype(jnp.float32)  3.71 us
    unnamed x12, local copies, waits for them, and re-layouts  2.5 us
    ppermute x2, starting transfers between devices, station_sum(): total = keep + lax.ppermute(send, 'station', perm).astype(jnp.float32)  1.56 us
    add x2, other arithmetic, station_sum(): total = keep + lax.ppermute(send, 'station', perm).astype(jnp.float32)  1.42 us
    reshape x1, local copies, waits for them, and re-layouts, shards(): pairs = pair_lists.reshape(-1)  0.72 us
  transfers between devices with their start and end apart: 5, of which 3 were waited for; matrix products, arithmetic and copies ran while one was open for 3% of the time, Pallas kernels for 16%

profile of v5, /device:TPU:0, one launch (start us, length us, event | category | flops | bytes accessed | tf_op | source)
XLA Modules:
  0.0 31.7 jit_solution(9594043503335412852)
XLA Ops:
  0.0 1.0 %copy.8 = bf16[16,4,3,512]{3,2,1,0:T(4,128)(2,1)S(1)} copy(bf16[16,4,3,512]{3,1,2,0:T(4,128)(2,1)} %param.5) | data formatting | bytes 393216 | tf_op args[0]
  1.1 0.0 copy-start.4
  1.1 0.2 reshape.15.refs_3_
  1.2 0.0 copy-start
  1.2 3.1 %collective-permute-start = (bf16[192,512]{1,0:T(8,128)(2,1)S(1)}, bf16[192,512]{1,0:T(8,128)(2,1)S(1)}, u32[]{:S(2)}, u32[]{:S(2)}) collective-permute-start(bf16[192,512]{1,0:T(8,128)(2,1)S(1)} %reshape.15.refs_3_), channel_id=1, source_target_pairs={{0,4},{4,0},{8,12},{12,8},{16,20},{20,16},{24,28},{28,24},{1,5},{5... | collective-permute-start | bytes 589832 | tf_op jit(solution)/shard_map/ppermute | solution.py:24
  4.3 1.6 %collective-permute-start.1 = (bf16[192,512]{1,0:T(8,128)(2,1)S(1)}, bf16[192,512]{1,0:T(8,128)(2,1)S(1)}, u32[]{:S(2)}, u32[]{:S(2)}) collective-permute-start(bf16[192,512]{1,0:T(8,128)(2,1)S(1)} %reshape.15.refs_3_), channel_id=1, source_target_pairs={{0,8},{8,0},{4,12},{12,4},{16,24},{24,16},{20,28},{28,20},{1,9},{9... | collective-permute-start | bytes 589832 | tf_op jit(solution)/shard_map/ppermute | solution.py:24
  5.9 2.6 %collective-permute-start.2 = (bf16[192,512]{1,0:T(8,128)(2,1)S(1)}, bf16[192,512]{1,0:T(8,128)(2,1)S(1)}, u32[]{:S(2)}, u32[]{:S(2)}) collective-permute-start(bf16[192,512]{1,0:T(8,128)(2,1)S(1)} %reshape.15.refs_3_), channel_id=1, source_target_pairs={{0,16},{16,0},{4,20},{20,4},{8,24},{24,8},{12,28},{28,12},{1,17},{... | collective-permute-start | bytes 589832 | tf_op jit(solution)/shard_map/ppermute | solution.py:24
  8.5 0.0 copy-done.4
  8.5 0.1 copy.7
  8.6 0.7 %reshape.12.refs_0_ = s32[192]{0:T(256)} reshape(s32[3,32,2]{2,1,0:T(8,128)S(1)} %copy.7) | data formatting | bytes 1536 | tf_op jit(solution)/shard_map/reshape | solution.py:185
  9.3 0.0 collective-permute-done.refs_4_
  9.3 0.0 copy-start.1
  9.3 5.5 %collective-permute-done.1.refs_5_ = bf16[192,512]{1,0:T(8,128)(2,1)S(1)} collective-permute-done((bf16[192,512]{1,0:T(8,128)(2,1)S(1)}, bf16[192,512]{1,0:T(8,128)(2,1)S(1)}, u32[]{:S(2)}, u32[]{:S(2)}) %collective-permute-start.1) | collective-permute-done | bytes 196640 | tf_op jit(solution)/shard_map/ppermute | solution.py:24
  14.8 0.0 copy-start.2
  14.8 0.0 copy-done
  14.8 0.0 copy-done.1
  14.8 0.7 %copy-done.2 = bf16[192,512]{1,0:T(8,128)(2,1)} copy-done((bf16[192,512]{1,0:T(8,128)(2,1)}, bf16[192,512]{1,0:T(8,128)(2,1)S(1)}, u32[]{:S(2)}) %copy-start.2) | copy-done | bytes 196632
  15.4 5.1 %shard_map.55 = (f32[2,32,256]{2,1,0:T(8,128)}, bf16[256,1024]{1,0:T(8,128)(2,1)}) custom-call(s32[192]{0:T(256)} %reshape.12.refs_0_, s32[3]{0:T(128)} %bitcast.2, s32[1]{0:T(128)} %bitcast.1.refs_2_, bf16[192,512]{1,0:T(8,128)(2,1)} %copy-done, bf16[192,512]{1,0:T(8,128)(2,1)} %copy-done.1, bf16[192,512]{1,0:T(8,128)(2,1)} %copy-done.2, ...), custom_call_target="tpu_custom_call" | custom-call | tf_op jit(solution)/shard_map/pallas_call | solution.py:148
  20.5 0.0 collective-permute-done.2.refs_4_
  20.5 0.0 copy-start.3
  20.5 0.7 %copy-done.3 = bf16[192,512]{1,0:T(8,128)(2,1)} copy-done((bf16[192,512]{1,0:T(8,128)(2,1)}, bf16[192,512]{1,0:T(8,128)(2,1)S(1)}, u32[]{:S(2)}) %copy-start.3) | copy-done | bytes 196632
  21.2 3.8 %shard_map.56 = (f32[3,16,256]{2,1,0:T(8,128)}, bf16[3,16,256]{2,1,0:T(8,128)(2,1)}) custom-call(s32[192]{0:T(256)} %reshape.12.refs_0_, s32[3]{0:T(128)} %bitcast.3, s32[1]{0:T(128)} %bitcast.1.refs_2_, bf16[256,1024]{1,0:T(8,128)(2,1)} %get-tuple-element.9.refs_3_, bf16[192,512]{1,0:T(8,128)(2,1)} %copy-done.3, ...), custom_call_target="tpu_custom_call" | custom-call | tf_op jit(solution)/shard_map/pallas_call | solution.py:148
  25.0 1.5 %collective-permute-start.3 = (bf16[3,16,256]{2,1,0:T(8,128)(2,1)}, bf16[3,16,256]{2,1,0:T(8,128)(2,1)S(1)}, u32[]{:S(2)}, u32[]{:S(2)}) collective-permute-start(bf16[3,16,256]{2,1,0:T(8,128)(2,1)} %get-tuple-element.12), channel_id=1, source_target_pairs={{0,2},{1,3},{2,0},{3,1},{4,6},{5,7},{6,4},{7,5},{8,10},{9,11},{10,... | collective-permute-start | bytes 73736 | tf_op jit(solution)/shard_map/ppermute | solution.py:167
  26.5 2.5 %collective-permute-done.3 = bf16[3,16,256]{2,1,0:T(8,128)(2,1)S(1)} collective-permute-done((bf16[3,16,256]{2,1,0:T(8,128)(2,1)}, bf16[3,16,256]{2,1,0:T(8,128)(2,1)S(1)}, u32[]{:S(2)}, u32[]{:S(2)}) %collective-permute-start.3) | collective-permute-done | bytes 24608 | tf_op jit(solution)/shard_map/ppermute | solution.py:167
  29.0 0.8 %convert_add_fusion = f32[3,16,256]{2,1,0:T(8,128)S(1)} fusion(f32[3,16,256]{2,1,0:T(8,128)} %get-tuple-element.11, bf16[3,16,256]{2,1,0:T(8,128)(2,1)S(1)} %collective-permute-done.3), kind=kLoop, calls=%fused_computation | loop fusion | flops 24576 | bytes 122880 | tf_op jit(solution)/shard_map/add | solution.py:167
  29.8 0.1 collective-permute-start.4
  29.9 1.2 %collective-permute-done.4 = bf16[3,8,256]{2,1,0:T(8,128)(2,1)S(1)} collective-permute-done((bf16[3,8,256]{2,1,0:T(8,128)(2,1)S(1)}, bf16[3,8,256]{2,1,0:T(8,128)(2,1)S(1)}, u32[]{:S(2)}, u32[]{:S(2)}) %collective-permute-start.4) | collective-permute-done | bytes 12320 | tf_op jit(solution)/shard_map/ppermute | solution.py:167
  31.1 0.6 %slice_add_fusion = f32[3,8,256]{2,1,0:T(8,128)} fusion(f32[3,16,256]{2,1,0:T(8,128)S(1)} %convert_add_fusion, bf16[3,8,256]{2,1,0:T(8,128)(2,1)S(1)} %collective-permute-done.4), kind=kLoop, calls=%fused_computation.2 | loop fusion | flops 12288 | bytes 61440 | tf_op jit(solution)/shard_map/add | solution.py:167
  (1 shorter events, 0.0 us)
Async XLA Ops:
  1.1 7.4 %copy-start.4 = (s32[3,32,2]{1,2,0:T(2,128)S(1)}, s32[3,32,2]{1,2,0:T(2,128)}, u32[]{:S(2)}) copy-start(s32[3,32,2]{1,2,0:T(2,128)} %param.6) | copy-start | bytes 2308
  1.2 13.5 %copy-start = (bf16[192,512]{1,0:T(8,128)(2,1)}, bf16[192,512]{1,0:T(8,128)(2,1)S(1)}, u32[]{:S(2)}) copy-start(bf16[192,512]{1,0:T(8,128)(2,1)S(1)} %reshape.15.refs_3_) | copy-start | bytes 589828
  1.2 8.0 %collective-permute-start = (bf16[192,512]{1,0:T(8,128)(2,1)S(1)}, bf16[192,512]{1,0:T(8,128)(2,1)S(1)}, u32[]{:S(2)}, u32[]{:S(2)}) collective-permute-start(bf16[192,512]{1,0:T(8,128)(2,1)S(1)} %reshape.15.refs_3_), channel_id=1, source_target_pairs={{0,4},{4,0},{8,12},{12,8},{16,20},{20,16},{24,28},{28,24},{1,5},{5... | collective-permute-start | bytes 589832 | tf_op jit(solution)/shard_map/ppermute | solution.py:24
  4.3 10.5 %collective-permute-start.1 = (bf16[192,512]{1,0:T(8,128)(2,1)S(1)}, bf16[192,512]{1,0:T(8,128)(2,1)S(1)}, u32[]{:S(2)}, u32[]{:S(2)}) collective-permute-start(bf16[192,512]{1,0:T(8,128)(2,1)S(1)} %reshape.15.refs_3_), channel_id=1, source_target_pairs={{0,8},{8,0},{4,12},{12,4},{16,24},{24,16},{20,28},{28,20},{1,9},{9... | collective-permute-start | bytes 589832 | tf_op jit(solution)/shard_map/ppermute | solution.py:24
  5.9 14.6 %collective-permute-start.2 = (bf16[192,512]{1,0:T(8,128)(2,1)S(1)}, bf16[192,512]{1,0:T(8,128)(2,1)S(1)}, u32[]{:S(2)}, u32[]{:S(2)}) collective-permute-start(bf16[192,512]{1,0:T(8,128)(2,1)S(1)} %reshape.15.refs_3_), channel_id=1, source_target_pairs={{0,16},{16,0},{4,20},{20,4},{8,24},{24,8},{12,28},{28,12},{1,17},{... | collective-permute-start | bytes 589832 | tf_op jit(solution)/shard_map/ppermute | solution.py:24
  9.3 5.5 %copy-start.1 = (bf16[192,512]{1,0:T(8,128)(2,1)}, bf16[192,512]{1,0:T(8,128)(2,1)S(1)}, u32[]{:S(2)}) copy-start(bf16[192,512]{1,0:T(8,128)(2,1)S(1)} %collective-permute-done.refs_4_) | copy-start | bytes 589828
  14.8 0.7 %copy-start.2 = (bf16[192,512]{1,0:T(8,128)(2,1)}, bf16[192,512]{1,0:T(8,128)(2,1)S(1)}, u32[]{:S(2)}) copy-start(bf16[192,512]{1,0:T(8,128)(2,1)S(1)} %collective-permute-done.1.refs_5_) | copy-start | bytes 589828
  20.5 0.7 %copy-start.3 = (bf16[192,512]{1,0:T(8,128)(2,1)}, bf16[192,512]{1,0:T(8,128)(2,1)S(1)}, u32[]{:S(2)}) copy-start(bf16[192,512]{1,0:T(8,128)(2,1)S(1)} %collective-permute-done.2.refs_4_) | copy-start | bytes 589828
  25.0 4.0 %collective-permute-start.3 = (bf16[3,16,256]{2,1,0:T(8,128)(2,1)}, bf16[3,16,256]{2,1,0:T(8,128)(2,1)S(1)}, u32[]{:S(2)}, u32[]{:S(2)}) collective-permute-start(bf16[3,16,256]{2,1,0:T(8,128)(2,1)} %get-tuple-element.12), channel_id=1, source_target_pairs={{0,2},{1,3},{2,0},{3,1},{4,6},{5,7},{6,4},{7,5},{8,10},{9,11},{10,... | collective-permute-start | bytes 73736 | tf_op jit(solution)/shard_map/ppermute | solution.py:167
  29.8 1.2 %collective-permute-start.4 = (bf16[3,8,256]{2,1,0:T(8,128)(2,1)S(1)}, bf16[3,8,256]{2,1,0:T(8,128)(2,1)S(1)}, u32[]{:S(2)}, u32[]{:S(2)}) collective-permute-start(bf16[3,8,256]{2,1,0:T(8,128)(2,1)S(1)} %slice.13), channel_id=1, source_target_pairs={{0,1},{1,0},{2,3},{3,2},{4,5},{5,4},{6,7},{7,6},{8,9},{9,8},{10,11... | collective-permute-start | bytes 36872 | tf_op jit(solution)/shard_map/ppermute | solution.py:167

commit v6 on v5

--- a/solution.py
+++ b/solution.py
@@ -50,7 +50,7 @@
     return fwd, inv.astype(ml_dtypes.bfloat16)
 
 
-def make_kernel(events, chans, pad, length, slots, groups, share, rounds, n_prev, from_waves):
+def make_kernel(events, chans, pad, length, slots, groups, share, rounds, prev_rounds, from_waves):
     half = length
     n_part = len(rounds)
 
@@ -84,10 +84,10 @@
             spec_out[...] = specl[...].astype(jnp.bfloat16)
         else:
             specl[...] = own_ref[...].astype(jnp.float32)
-            for n in range(n_prev):
+            for n, q in enumerate(prev_rounds):
                 prev = prev_ref[n]
-                keep_ref[n] = prev[:slots // 2]
-                send_ref[n] = prev[slots // 2:].astype(jnp.bfloat16)
+                keep_ref[q] = prev[:slots // 2]
+                send_ref[q] = prev[slots // 2:].astype(jnp.bfloat16)
 
         sid = sid_ref[0]
         lane = lax.broadcasted_iota(jnp.int32, (1, 128), 1)
@@ -121,20 +121,21 @@
             if from_waves:
                 out_ref[n] = corr
             else:
-                keep_ref[n_prev + n] = corr[:slots // 2]
-                send_ref[n_prev + n] = corr[slots // 2:].astype(jnp.bfloat16)
+                keep_ref[q] = corr[:slots // 2]
+                send_ref[q] = corr[slots // 2:].astype(jnp.bfloat16)
 
     return kernel
 
 
-def rounds_call(pairs, counts, sid, own, partners, fwd, inv, rounds, events, chans, slots, groups, prev=None):
+def rounds_call(pairs, counts, sid, own, partners, fwd, inv, rounds, events, chans, slots, groups,
+                prev=None, prev_rounds=()):
     length = fwd.shape[0]
     lags = inv.shape[1]
     pad = 16
     share = slots // groups
     from_waves = prev is None
     n_prev = 0 if from_waves else prev.shape[0]
-    kernel = make_kernel(events, chans, pad, length, slots, groups, share, rounds, n_prev, from_waves)
+    kernel = make_kernel(events, chans, pad, length, slots, groups, share, rounds, list(prev_rounds), from_waves)
     smem = pl.BlockSpec(memory_space=pltpu.SMEM)
     vmem = pl.BlockSpec(memory_space=pltpu.VMEM)
     if from_waves:
@@ -185,11 +186,12 @@
     pairs = pair_lists.reshape(-1)
     counts = pair_counts.reshape(-1)
     partners = {q: swapped(flat, "region", q) for q in reversed(range(rounds))}
-    early = list(range(rounds - 1))
+    late = 1 if rounds > 2 else rounds - 1
+    early = [q for q in range(rounds) if q != late]
     corr_a, spec = rounds_call(pairs, counts, sid, flat, [partners[q] for q in early], fwd, inv,
                                early, events, chans, slots, groups)
-    keep, send = rounds_call(pairs, counts, sid, spec, [partners[rounds - 1]], fwd, inv,
-                          [rounds - 1], events, chans, slots, groups, prev=corr_a)
+    keep, send = rounds_call(pairs, counts, sid, spec, [partners[late]], fwd, inv,
+                             [late], events, chans, slots, groups, prev=corr_a, prev_rounds=early)
     return station_sum(keep, send, groups)
 
 

time: 32 us -> 33.1 us (1.034)
  waiting for transfers between devices: 9.18 us -> 10.3 us
    ppermute x3, waiting for transfers between devices: 5.47 us -> 6.59 us  [swapped(): return lax.ppermute(block, axis, route)]
  transfers between devices with their start and end apart: 5 -> 5, of which waited for: 3 -> 3; matrix products, arithmetic and copies ran while one was open for 3% -> 2% of each run, Pallas kernels for 16% -> 15%
where the time goes in v6:
time: 33.1 us; the launch traced here: 32.8 us
  waiting for transfers between devices  10.3 us (31%)
  Pallas kernels  8.87 us (27%)
  starting transfers between devices  8.79 us (27%)
  local copies, waits for them, and re-layouts  3.39 us (10%)
  other arithmetic  1.42 us (4%)
    pallas_call x2, Pallas kernels, rounds_call(): pl.pallas_call(kernel, out_shape=out_shape, in_specs=[smem, smem, smem] +...  8.87 us
    ppermute x3, starting transfers between devices, swapped(): return lax.ppermute(block, axis, route)  7.23 us
    ppermute x3, waiting for transfers between devices, swapped(): return lax.ppermute(block, axis, route)  6.59 us
    ppermute x2, waiting for transfers between devices, station_sum(): total = keep + lax.ppermute(send, 'station', perm).astype(jnp.float32)  3.71 us
    unnamed x12, local copies, waits for them, and re-layouts  2.5 us
    ppermute x2, starting transfers between devices, station_sum(): total = keep + lax.ppermute(send, 'station', perm).astype(jnp.float32)  1.56 us
    add x2, other arithmetic, station_sum(): total = keep + lax.ppermute(send, 'station', perm).astype(jnp.float32)  1.42 us
    reshape x1, local copies, waits for them, and re-layouts, shards(): pairs = pair_lists.reshape(-1)  0.72 us
  transfers between devices with their start and end apart: 5, of which 3 were waited for; matrix products, arithmetic and copies ran while one was open for 2% of the time, Pallas kernels for 15%

profile of v6, /device:TPU:0, one launch (start us, length us, event | category | flops | bytes accessed | tf_op | source)
XLA Modules:
  0.0 32.8 jit_solution(11401252568221019557)
XLA Ops:
  0.0 1.0 %copy.8 = bf16[16,4,3,512]{3,2,1,0:T(4,128)(2,1)S(1)} copy(bf16[16,4,3,512]{3,1,2,0:T(4,128)(2,1)} %param.5) | data formatting | bytes 393216 | tf_op args[0]
  1.1 0.0 copy-start.4
  1.1 0.2 reshape.15.refs_3_
  1.2 0.0 copy-start
  1.2 3.1 %collective-permute-start = (bf16[192,512]{1,0:T(8,128)(2,1)S(1)}, bf16[192,512]{1,0:T(8,128)(2,1)S(1)}, u32[]{:S(2)}, u32[]{:S(2)}) collective-permute-start(bf16[192,512]{1,0:T(8,128)(2,1)S(1)} %reshape.15.refs_3_), channel_id=1, source_target_pairs={{0,4},{4,0},{8,12},{12,8},{16,20},{20,16},{24,28},{28,24},{1,5},{5... | collective-permute-start | bytes 589832 | tf_op jit(solution)/shard_map/ppermute | solution.py:24
  4.3 2.6 %collective-permute-start.1 = (bf16[192,512]{1,0:T(8,128)(2,1)S(1)}, bf16[192,512]{1,0:T(8,128)(2,1)S(1)}, u32[]{:S(2)}, u32[]{:S(2)}) collective-permute-start(bf16[192,512]{1,0:T(8,128)(2,1)S(1)} %reshape.15.refs_3_), channel_id=1, source_target_pairs={{0,16},{16,0},{4,20},{20,4},{8,24},{24,8},{12,28},{28,12},{1,17},{... | collective-permute-start | bytes 589832 | tf_op jit(solution)/shard_map/ppermute | solution.py:24
  6.9 1.6 %collective-permute-start.2 = (bf16[192,512]{1,0:T(8,128)(2,1)S(1)}, bf16[192,512]{1,0:T(8,128)(2,1)S(1)}, u32[]{:S(2)}, u32[]{:S(2)}) collective-permute-start(bf16[192,512]{1,0:T(8,128)(2,1)S(1)} %reshape.15.refs_3_), channel_id=1, source_target_pairs={{0,8},{8,0},{4,12},{12,4},{16,24},{24,16},{20,28},{28,20},{1,9},{9... | collective-permute-start | bytes 589832 | tf_op jit(solution)/shard_map/ppermute | solution.py:24
  8.5 0.0 copy-done.4
  8.5 0.1 copy.7
  8.6 0.7 %reshape.12.refs_0_ = s32[192]{0:T(256)} reshape(s32[3,32,2]{2,1,0:T(8,128)S(1)} %copy.7) | data formatting | bytes 1536 | tf_op jit(solution)/shard_map/reshape | solution.py:186
  9.3 0.0 collective-permute-done.refs_4_
  9.3 0.0 copy-start.1
  9.3 6.6 %collective-permute-done.1.refs_5_ = bf16[192,512]{1,0:T(8,128)(2,1)S(1)} collective-permute-done((bf16[192,512]{1,0:T(8,128)(2,1)S(1)}, bf16[192,512]{1,0:T(8,128)(2,1)S(1)}, u32[]{:S(2)}, u32[]{:S(2)}) %collective-permute-start.1) | collective-permute-done | bytes 196640 | tf_op jit(solution)/shard_map/ppermute | solution.py:24
  15.9 0.0 copy-start.2
  15.9 0.0 copy-done
  15.9 0.0 copy-done.1
  15.9 0.7 %copy-done.2 = bf16[192,512]{1,0:T(8,128)(2,1)} copy-done((bf16[192,512]{1,0:T(8,128)(2,1)}, bf16[192,512]{1,0:T(8,128)(2,1)S(1)}, u32[]{:S(2)}) %copy-start.2) | copy-done | bytes 196632
  16.6 5.1 %shard_map.55 = (f32[2,32,256]{2,1,0:T(8,128)}, bf16[256,1024]{1,0:T(8,128)(2,1)}) custom-call(s32[192]{0:T(256)} %reshape.12.refs_0_, s32[3]{0:T(128)} %bitcast.2, s32[1]{0:T(128)} %bitcast.1.refs_2_, bf16[192,512]{1,0:T(8,128)(2,1)} %copy-done, bf16[192,512]{1,0:T(8,128)(2,1)} %copy-done.1, bf16[192,512]{1,0:T(8,128)(2,1)} %copy-done.2, ...), custom_call_target="tpu_custom_call" | custom-call | tf_op jit(solution)/shard_map/pallas_call | solution.py:149
  21.6 0.0 collective-permute-done.2.refs_4_
  21.6 0.0 copy-start.3
  21.6 0.7 %copy-done.3 = bf16[192,512]{1,0:T(8,128)(2,1)} copy-done((bf16[192,512]{1,0:T(8,128)(2,1)}, bf16[192,512]{1,0:T(8,128)(2,1)S(1)}, u32[]{:S(2)}) %copy-start.3) | copy-done | bytes 196632
  22.3 3.8 %shard_map.56 = (f32[3,16,256]{2,1,0:T(8,128)}, bf16[3,16,256]{2,1,0:T(8,128)(2,1)}) custom-call(s32[192]{0:T(256)} %reshape.12.refs_0_, s32[3]{0:T(128)} %bitcast.3, s32[1]{0:T(128)} %bitcast.1.refs_2_, bf16[256,1024]{1,0:T(8,128)(2,1)} %get-tuple-element.9.refs_3_, bf16[192,512]{1,0:T(8,128)(2,1)} %copy-done.3, ...), custom_call_target="tpu_custom_call" | custom-call | tf_op jit(solution)/shard_map/pallas_call | solution.py:149
  26.1 1.5 %collective-permute-start.3 = (bf16[3,16,256]{2,1,0:T(8,128)(2,1)}, bf16[3,16,256]{2,1,0:T(8,128)(2,1)S(1)}, u32[]{:S(2)}, u32[]{:S(2)}) collective-permute-start(bf16[3,16,256]{2,1,0:T(8,128)(2,1)} %get-tuple-element.12), channel_id=1, source_target_pairs={{0,2},{1,3},{2,0},{3,1},{4,6},{5,7},{6,4},{7,5},{8,10},{9,11},{10,... | collective-permute-start | bytes 73736 | tf_op jit(solution)/shard_map/ppermute | solution.py:168
  27.6 2.5 %collective-permute-done.3 = bf16[3,16,256]{2,1,0:T(8,128)(2,1)S(1)} collective-permute-done((bf16[3,16,256]{2,1,0:T(8,128)(2,1)}, bf16[3,16,256]{2,1,0:T(8,128)(2,1)S(1)}, u32[]{:S(2)}, u32[]{:S(2)}) %collective-permute-start.3) | collective-permute-done | bytes 24608 | tf_op jit(solution)/shard_map/ppermute | solution.py:168
  30.1 0.8 %convert_add_fusion = f32[3,16,256]{2,1,0:T(8,128)S(1)} fusion(f32[3,16,256]{2,1,0:T(8,128)} %get-tuple-element.11, bf16[3,16,256]{2,1,0:T(8,128)(2,1)S(1)} %collective-permute-done.3), kind=kLoop, calls=%fused_computation | loop fusion | flops 24576 | bytes 122880 | tf_op jit(solution)/shard_map/add | solution.py:168
  31.0 0.1 collective-permute-start.4
  31.0 1.2 %collective-permute-done.4 = bf16[3,8,256]{2,1,0:T(8,128)(2,1)S(1)} collective-permute-done((bf16[3,8,256]{2,1,0:T(8,128)(2,1)S(1)}, bf16[3,8,256]{2,1,0:T(8,128)(2,1)S(1)}, u32[]{:S(2)}, u32[]{:S(2)}) %collective-permute-start.4) | collective-permute-done | bytes 12320 | tf_op jit(solution)/shard_map/ppermute | solution.py:168
  32.2 0.6 %slice_add_fusion = f32[3,8,256]{2,1,0:T(8,128)} fusion(f32[3,16,256]{2,1,0:T(8,128)S(1)} %convert_add_fusion, bf16[3,8,256]{2,1,0:T(8,128)(2,1)S(1)} %collective-permute-done.4), kind=kLoop, calls=%fused_computation.2 | loop fusion | flops 12288 | bytes 61440 | tf_op jit(solution)/shard_map/add | solution.py:168
  (1 shorter events, 0.0 us)
Async XLA Ops:
  1.1 7.4 %copy-start.4 = (s32[3,32,2]{1,2,0:T(2,128)S(1)}, s32[3,32,2]{1,2,0:T(2,128)}, u32[]{:S(2)}) copy-start(s32[3,32,2]{1,2,0:T(2,128)} %param.6) | copy-start | bytes 2308
  1.2 14.6 %copy-start = (bf16[192,512]{1,0:T(8,128)(2,1)}, bf16[192,512]{1,0:T(8,128)(2,1)S(1)}, u32[]{:S(2)}) copy-start(bf16[192,512]{1,0:T(8,128)(2,1)S(1)} %reshape.15.refs_3_) | copy-start | bytes 589828
  1.2 8.0 %collective-permute-start = (bf16[192,512]{1,0:T(8,128)(2,1)S(1)}, bf16[192,512]{1,0:T(8,128)(2,1)S(1)}, u32[]{:S(2)}, u32[]{:S(2)}) collective-permute-start(bf16[192,512]{1,0:T(8,128)(2,1)S(1)} %reshape.15.refs_3_), channel_id=1, source_target_pairs={{0,4},{4,0},{8,12},{12,8},{16,20},{20,16},{24,28},{28,24},{1,5},{5... | collective-permute-start | bytes 589832 | tf_op jit(solution)/shard_map/ppermute | solution.py:24
  4.3 11.6 %collective-permute-start.1 = (bf16[192,512]{1,0:T(8,128)(2,1)S(1)}, bf16[192,512]{1,0:T(8,128)(2,1)S(1)}, u32[]{:S(2)}, u32[]{:S(2)}) collective-permute-start(bf16[192,512]{1,0:T(8,128)(2,1)S(1)} %reshape.15.refs_3_), channel_id=1, source_target_pairs={{0,16},{16,0},{4,20},{20,4},{8,24},{24,8},{12,28},{28,12},{1,17},{... | collective-permute-start | bytes 589832 | tf_op jit(solution)/shard_map/ppermute | solution.py:24
  6.9 14.7 %collective-permute-start.2 = (bf16[192,512]{1,0:T(8,128)(2,1)S(1)}, bf16[192,512]{1,0:T(8,128)(2,1)S(1)}, u32[]{:S(2)}, u32[]{:S(2)}) collective-permute-start(bf16[192,512]{1,0:T(8,128)(2,1)S(1)} %reshape.15.refs_3_), channel_id=1, source_target_pairs={{0,8},{8,0},{4,12},{12,4},{16,24},{24,16},{20,28},{28,20},{1,9},{9... | collective-permute-start | bytes 589832 | tf_op jit(solution)/shard_map/ppermute | solution.py:24
  9.3 6.6 %copy-start.1 = (bf16[192,512]{1,0:T(8,128)(2,1)}, bf16[192,512]{1,0:T(8,128)(2,1)S(1)}, u32[]{:S(2)}) copy-start(bf16[192,512]{1,0:T(8,128)(2,1)S(1)} %collective-permute-done.refs_4_) | copy-start | bytes 589828
  15.9 0.7 %copy-start.2 = (bf16[192,512]{1,0:T(8,128)(2,1)}, bf16[192,512]{1,0:T(8,128)(2,1)S(1)}, u32[]{:S(2)}) copy-start(bf16[192,512]{1,0:T(8,128)(2,1)S(1)} %collective-permute-done.1.refs_5_) | copy-start | bytes 589828
  21.6 0.7 %copy-start.3 = (bf16[192,512]{1,0:T(8,128)(2,1)}, bf16[192,512]{1,0:T(8,128)(2,1)S(1)}, u32[]{:S(2)}) copy-start(bf16[192,512]{1,0:T(8,128)(2,1)S(1)} %collective-permute-done.2.refs_4_) | copy-start | bytes 589828
  26.1 4.0 %collective-permute-start.3 = (bf16[3,16,256]{2,1,0:T(8,128)(2,1)}, bf16[3,16,256]{2,1,0:T(8,128)(2,1)S(1)}, u32[]{:S(2)}, u32[]{:S(2)}) collective-permute-start(bf16[3,16,256]{2,1,0:T(8,128)(2,1)} %get-tuple-element.12), channel_id=1, source_target_pairs={{0,2},{1,3},{2,0},{3,1},{4,6},{5,7},{6,4},{7,5},{8,10},{9,11},{10,... | collective-permute-start | bytes 73736 | tf_op jit(solution)/shard_map/ppermute | solution.py:168
  31.0 1.2 %collective-permute-start.4 = (bf16[3,8,256]{2,1,0:T(8,128)(2,1)S(1)}, bf16[3,8,256]{2,1,0:T(8,128)(2,1)S(1)}, u32[]{:S(2)}, u32[]{:S(2)}) collective-permute-start(bf16[3,8,256]{2,1,0:T(8,128)(2,1)S(1)} %slice.13), channel_id=1, source_target_pairs={{0,1},{1,0},{2,3},{3,2},{4,5},{5,4},{6,7},{7,6},{8,9},{9,8},{10,11... | collective-permute-start | bytes 36872 | tf_op jit(solution)/shard_map/ppermute | solution.py:168

commit v7 on v5

--- a/solution.py
+++ b/solution.py
@@ -50,7 +50,7 @@
     return fwd, inv.astype(ml_dtypes.bfloat16)
 
 
-def make_kernel(events, chans, pad, length, slots, groups, share, rounds, n_prev, from_waves):
+def make_kernel(events, chans, pad, length, slots, groups, share, rounds, n_prev, from_waves, final):
     half = length
     n_part = len(rounds)
 
@@ -62,9 +62,12 @@
         if from_waves:
             out_ref, spec_out = rest[:2]
             rest = rest[2:]
-        else:
+        elif final:
             prev_ref, keep_ref, send_ref = rest[:3]
             rest = rest[3:]
+        else:
+            prev_ref, out_ref = rest[:2]
+            rest = rest[2:]
         nscr, xpad, specl, specp, cross = rest
 
         def spectra(w_ref, spec_ref):
@@ -86,8 +89,11 @@
             specl[...] = own_ref[...].astype(jnp.float32)
             for n in range(n_prev):
                 prev = prev_ref[n]
-                keep_ref[n] = prev[:slots // 2]
-                send_ref[n] = prev[slots // 2:].astype(jnp.bfloat16)
+                if final:
+                    keep_ref[n] = prev[:slots // 2]
+                    send_ref[n] = prev[slots // 2:].astype(jnp.bfloat16)
+                else:
+                    out_ref[n] = prev
 
         sid = sid_ref[0]
         lane = lax.broadcasted_iota(jnp.int32, (1, 128), 1)
@@ -118,8 +124,8 @@
             rows = lax.broadcasted_iota(jnp.int32, corr.shape, 0)
             slot_of = (sid ^ (rows // share)) * share + rows % share
             corr = jnp.where(slot_of < cnt_ref[q], corr, 0.0)
-            if from_waves:
-                out_ref[n] = corr
+            if not final:
+                out_ref[n_prev + n] = corr
             else:
                 keep_ref[n_prev + n] = corr[:slots // 2]
                 send_ref[n_prev + n] = corr[slots // 2:].astype(jnp.bfloat16)
@@ -127,20 +133,24 @@
     return kernel
 
 
-def rounds_call(pairs, counts, sid, own, partners, fwd, inv, rounds, events, chans, slots, groups, prev=None):
+def rounds_call(pairs, counts, sid, own, partners, fwd, inv, rounds, events, chans, slots, groups,
+                prev=None, final=False):
     length = fwd.shape[0]
     lags = inv.shape[1]
     pad = 16
     share = slots // groups
     from_waves = prev is None
     n_prev = 0 if from_waves else prev.shape[0]
-    kernel = make_kernel(events, chans, pad, length, slots, groups, share, rounds, n_prev, from_waves)
+    kernel = make_kernel(events, chans, pad, length, slots, groups, share, rounds, n_prev, from_waves, final)
     smem = pl.BlockSpec(memory_space=pltpu.SMEM)
     vmem = pl.BlockSpec(memory_space=pltpu.VMEM)
     if from_waves:
         out_shape = (jax.ShapeDtypeStruct((len(rounds), slots, lags), jnp.float32),
                      jax.ShapeDtypeStruct((events * pad, 2 * length), jnp.bfloat16))
         extra = []
+    elif not final:
+        out_shape = (jax.ShapeDtypeStruct((n_prev + len(rounds), slots, lags), jnp.float32),)
+        extra = [prev]
     else:
         out_shape = (jax.ShapeDtypeStruct((n_prev + len(rounds), slots // 2, lags), jnp.float32),
                      jax.ShapeDtypeStruct((n_prev + len(rounds), slots // 2, lags), jnp.bfloat16))
@@ -185,11 +195,13 @@
     pairs = pair_lists.reshape(-1)
     counts = pair_counts.reshape(-1)
     partners = {q: swapped(flat, "region", q) for q in reversed(range(rounds))}
-    early = list(range(rounds - 1))
-    corr_a, spec = rounds_call(pairs, counts, sid, flat, [partners[q] for q in early], fwd, inv,
-                               early, events, chans, slots, groups)
+    corr, spec = rounds_call(pairs, counts, sid, flat, [partners[0]], fwd, inv,
+                             [0], events, chans, slots, groups)
+    for q in range(1, rounds - 1):
+        (corr,) = rounds_call(pairs, counts, sid, spec, [partners[q]], fwd, inv,
+                              [q], events, chans, slots, groups, prev=corr)
     keep, send = rounds_call(pairs, counts, sid, spec, [partners[rounds - 1]], fwd, inv,
-                          [rounds - 1], events, chans, slots, groups, prev=corr_a)
+                             [rounds - 1], events, chans, slots, groups, prev=corr, final=True)
     return station_sum(keep, send, groups)
 
 

time: 32 us -> 30.7 us (0.959)
  waiting for transfers between devices: 9.18 us -> 4.4 us
  Pallas kernels: 8.87 us -> 11.7 us
  local copies, waits for them, and re-layouts: 3.39 us -> 4.05 us
    ppermute x3, waiting for transfers between devices: 5.47 us -> 0.69 us  [swapped(): return lax.ppermute(block, axis, route)]
    pallas_call x2 -> x3, Pallas kernels: 8.87 us -> 11.7 us  [rounds_call(): pl.pallas_call(kernel, out_shape=out_shape, in_specs=[smem, smem, smem] +...]
    unnamed x12, local copies, waits for them, and re-layouts: 2.5 us -> 3.17 us
  transfers between devices with their start and end apart: 5 -> 5, of which waited for: 3 -> 3; matrix products, arithmetic and copies ran while one was open for 3% -> 3% of each run, Pallas kernels for 16% -> 26%
where the time goes in v7:
time: 30.7 us; the launch traced here: 30.4 us
  Pallas kernels  11.7 us (38%)
  starting transfers between devices  8.79 us (29%)
  waiting for transfers between devices  4.4 us (14%)
  local copies, waits for them, and re-layouts  4.05 us (13%)
  other arithmetic  1.42 us (5%)
    pallas_call x3, Pallas kernels, rounds_call(): pl.pallas_call(kernel, out_shape=out_shape, in_specs=[smem, smem, smem] +...  11.7 us
    ppermute x3, starting transfers between devices, swapped(): return lax.ppermute(block, axis, route)  7.23 us
    ppermute x2, waiting for transfers between devices, station_sum(): total = keep + lax.ppermute(send, 'station', perm).astype(jnp.float32)  3.71 us
    unnamed x12, local copies, waits for them, and re-layouts  3.17 us
    ppermute x2, starting transfers between devices, station_sum(): total = keep + lax.ppermute(send, 'station', perm).astype(jnp.float32)  1.56 us
    add x2, other arithmetic, station_sum(): total = keep + lax.ppermute(send, 'station', perm).astype(jnp.float32)  1.42 us
    reshape x1, local copies, waits for them, and re-layouts, shards(): pairs = pair_lists.reshape(-1)  0.71 us
    ppermute x3, waiting for transfers between devices, swapped(): return lax.ppermute(block, axis, route)  0.69 us
  transfers between devices with their start and end apart: 5, of which 3 were waited for; matrix products, arithmetic and copies ran while one was open for 3% of the time, Pallas kernels for 26%

profile of v7, /device:TPU:0, one launch (start us, length us, event | category | flops | bytes accessed | tf_op | source)
XLA Modules:
  0.0 30.4 jit_solution(4850312818580447762)
XLA Ops:
  0.0 1.0 %copy.8 = bf16[16,4,3,512]{3,2,1,0:T(4,128)(2,1)S(1)} copy(bf16[16,4,3,512]{3,1,2,0:T(4,128)(2,1)} %param.5) | data formatting | bytes 393216 | tf_op args[0]
  1.1 0.0 copy-start.4
  1.1 0.2 reshape.15.refs_3_
  1.2 0.0 copy-start
  1.2 3.1 %collective-permute-start = (bf16[192,512]{1,0:T(8,128)(2,1)S(1)}, bf16[192,512]{1,0:T(8,128)(2,1)S(1)}, u32[]{:S(2)}, u32[]{:S(2)}) collective-permute-start(bf16[192,512]{1,0:T(8,128)(2,1)S(1)} %reshape.15.refs_3_), channel_id=1, source_target_pairs={{0,4},{4,0},{8,12},{12,8},{16,20},{20,16},{24,28},{28,24},{1,5},{5... | collective-permute-start | bytes 589832 | tf_op jit(solution)/shard_map/ppermute | solution.py:24
  4.3 1.6 %collective-permute-start.2 = (bf16[192,512]{1,0:T(8,128)(2,1)S(1)}, bf16[192,512]{1,0:T(8,128)(2,1)S(1)}, u32[]{:S(2)}, u32[]{:S(2)}) collective-permute-start(bf16[192,512]{1,0:T(8,128)(2,1)S(1)} %reshape.15.refs_3_), channel_id=1, source_target_pairs={{0,8},{8,0},{4,12},{12,4},{16,24},{24,16},{20,28},{28,20},{1,9},{9... | collective-permute-start | bytes 589832 | tf_op jit(solution)/shard_map/ppermute | solution.py:24
  5.9 2.6 %collective-permute-start.1 = (bf16[192,512]{1,0:T(8,128)(2,1)S(1)}, bf16[192,512]{1,0:T(8,128)(2,1)S(1)}, u32[]{:S(2)}, u32[]{:S(2)}) collective-permute-start(bf16[192,512]{1,0:T(8,128)(2,1)S(1)} %reshape.15.refs_3_), channel_id=1, source_target_pairs={{0,16},{16,0},{4,20},{20,4},{8,24},{24,8},{12,28},{28,12},{1,17},{... | collective-permute-start | bytes 589832 | tf_op jit(solution)/shard_map/ppermute | solution.py:24
  8.5 0.0 copy-done.4
  8.5 0.1 copy.7
  8.6 0.7 %reshape.12.refs_0_ = s32[192]{0:T(256)} reshape(s32[3,32,2]{2,1,0:T(8,128)S(1)} %copy.7) | data formatting | bytes 1536 | tf_op jit(solution)/shard_map/reshape | solution.py:195
  9.3 0.0 collective-permute-done.refs_4_
  9.3 0.0 copy-start.1
  9.3 0.0 copy-done
  9.3 0.7 %copy-done.1 = bf16[192,512]{1,0:T(8,128)(2,1)} copy-done((bf16[192,512]{1,0:T(8,128)(2,1)}, bf16[192,512]{1,0:T(8,128)(2,1)S(1)}, u32[]{:S(2)}) %copy-start.1) | copy-done | bytes 196632
  10.0 4.1 %shard_map.55 = (f32[1,32,256]{2,1,0:T(8,128)}, bf16[256,1024]{1,0:T(8,128)(2,1)}) custom-call(s32[192]{0:T(256)} %reshape.12.refs_0_, s32[3]{0:T(128)} %bitcast.2, s32[1]{0:T(128)} %bitcast.1.refs_2_, bf16[192,512]{1,0:T(8,128)(2,1)} %copy-done, bf16[192,512]{1,0:T(8,128)(2,1)} %copy-done.1, bf16[512,1024]{1,0:T(8,128)(2,1)} %constant.8.clone.refs_5_, ...), custom_call_target="tpu_custom_call" | custom-call | tf_op jit(solution)/shard_map/pallas_call | solution.py:158
  14.1 0.7 %collective-permute-done.2.refs_4_ = bf16[192,512]{1,0:T(8,128)(2,1)S(1)} collective-permute-done((bf16[192,512]{1,0:T(8,128)(2,1)S(1)}, bf16[192,512]{1,0:T(8,128)(2,1)S(1)}, u32[]{:S(2)}, u32[]{:S(2)}) %collective-permute-start.2) | collective-permute-done | bytes 196640 | tf_op jit(solution)/shard_map/ppermute | solution.py:24
  14.8 0.0 copy-start.3
  14.8 0.7 %copy-done.3 = bf16[192,512]{1,0:T(8,128)(2,1)} copy-done((bf16[192,512]{1,0:T(8,128)(2,1)}, bf16[192,512]{1,0:T(8,128)(2,1)S(1)}, u32[]{:S(2)}) %copy-start.3) | copy-done | bytes 196632
  15.4 3.8 %shard_map.56.refs_7_ = f32[2,32,256]{2,1,0:T(8,128)} custom-call(s32[192]{0:T(256)} %reshape.12.refs_0_, s32[3]{0:T(128)} %bitcast.3, s32[1]{0:T(128)} %bitcast.1.refs_2_, bf16[256,1024]{1,0:T(8,128)(2,1)} %get-tuple-element.9.refs_3_, bf16[192,512]{1,0:T(8,128)(2,1)} %copy-done.3, bf16[512,1024]{1,0:T(8,128)(2,1)} %constant.8.clone.refs_5_, ...), custom_call_target="tpu_custom_call" | custom-call | tf_op jit(solution)/shard_map/pallas_call | solution.py:158
  19.2 0.0 collective-permute-done.1.refs_4_
  19.2 0.0 copy-start.2
  19.2 0.7 %copy-done.2 = bf16[192,512]{1,0:T(8,128)(2,1)} copy-done((bf16[192,512]{1,0:T(8,128)(2,1)}, bf16[192,512]{1,0:T(8,128)(2,1)S(1)}, u32[]{:S(2)}) %copy-start.2) | copy-done | bytes 196632
  19.9 3.8 %shard_map.57 = (f32[3,16,256]{2,1,0:T(8,128)}, bf16[3,16,256]{2,1,0:T(8,128)(2,1)}) custom-call(s32[192]{0:T(256)} %reshape.12.refs_0_, s32[3]{0:T(128)} %bitcast.4, s32[1]{0:T(128)} %bitcast.1.refs_2_, bf16[256,1024]{1,0:T(8,128)(2,1)} %get-tuple-element.9.refs_3_, bf16[192,512]{1,0:T(8,128)(2,1)} %copy-done.2, bf16[512,1024]{1,0:T(8,128)(2,1)} %constant.8.clone.refs_5_, ...), custom_call_target="tpu_custom_call" | custom-call | tf_op jit(solution)/shard_map/pallas_call | solution.py:158
  23.7 1.5 %collective-permute-start.3 = (bf16[3,16,256]{2,1,0:T(8,128)(2,1)}, bf16[3,16,256]{2,1,0:T(8,128)(2,1)S(1)}, u32[]{:S(2)}, u32[]{:S(2)}) collective-permute-start(bf16[3,16,256]{2,1,0:T(8,128)(2,1)} %get-tuple-element.12), channel_id=1, source_target_pairs={{0,2},{1,3},{2,0},{3,1},{4,6},{5,7},{6,4},{7,5},{8,10},{9,11},{10,... | collective-permute-start | bytes 73736 | tf_op jit(solution)/shard_map/ppermute | solution.py:177
  25.2 2.5 %collective-permute-done.3 = bf16[3,16,256]{2,1,0:T(8,128)(2,1)S(1)} collective-permute-done((bf16[3,16,256]{2,1,0:T(8,128)(2,1)}, bf16[3,16,256]{2,1,0:T(8,128)(2,1)S(1)}, u32[]{:S(2)}, u32[]{:S(2)}) %collective-permute-start.3) | collective-permute-done | bytes 24608 | tf_op jit(solution)/shard_map/ppermute | solution.py:177
  27.7 0.8 %convert_add_fusion = f32[3,16,256]{2,1,0:T(8,128)S(1)} fusion(f32[3,16,256]{2,1,0:T(8,128)} %get-tuple-element.11, bf16[3,16,256]{2,1,0:T(8,128)(2,1)S(1)} %collective-permute-done.3), kind=kLoop, calls=%fused_computation | loop fusion | flops 24576 | bytes 122880 | tf_op jit(solution)/shard_map/add | solution.py:177
  28.6 0.1 collective-permute-start.4
  28.6 1.2 %collective-permute-done.4 = bf16[3,8,256]{2,1,0:T(8,128)(2,1)S(1)} collective-permute-done((bf16[3,8,256]{2,1,0:T(8,128)(2,1)S(1)}, bf16[3,8,256]{2,1,0:T(8,128)(2,1)S(1)}, u32[]{:S(2)}, u32[]{:S(2)}) %collective-permute-start.4) | collective-permute-done | bytes 12320 | tf_op jit(solution)/shard_map/ppermute | solution.py:177
  29.8 0.6 %slice_add_fusion = f32[3,8,256]{2,1,0:T(8,128)} fusion(f32[3,16,256]{2,1,0:T(8,128)S(1)} %convert_add_fusion, bf16[3,8,256]{2,1,0:T(8,128)(2,1)S(1)} %collective-permute-done.4), kind=kLoop, calls=%fused_computation.2 | loop fusion | flops 12288 | bytes 61440 | tf_op jit(solution)/shard_map/add | solution.py:177
  (1 shorter events, 0.0 us)
Async XLA Ops:
  1.1 7.4 %copy-start.4 = (s32[3,32,2]{1,2,0:T(2,128)S(1)}, s32[3,32,2]{1,2,0:T(2,128)}, u32[]{:S(2)}) copy-start(s32[3,32,2]{1,2,0:T(2,128)} %param.6) | copy-start | bytes 2308
  1.2 8.1 %copy-start = (bf16[192,512]{1,0:T(8,128)(2,1)}, bf16[192,512]{1,0:T(8,128)(2,1)S(1)}, u32[]{:S(2)}) copy-start(bf16[192,512]{1,0:T(8,128)(2,1)S(1)} %reshape.15.refs_3_) | copy-start | bytes 589828
  1.2 8.0 %collective-permute-start = (bf16[192,512]{1,0:T(8,128)(2,1)S(1)}, bf16[192,512]{1,0:T(8,128)(2,1)S(1)}, u32[]{:S(2)}, u32[]{:S(2)}) collective-permute-start(bf16[192,512]{1,0:T(8,128)(2,1)S(1)} %reshape.15.refs_3_), channel_id=1, source_target_pairs={{0,4},{4,0},{8,12},{12,8},{16,20},{20,16},{24,28},{28,24},{1,5},{5... | collective-permute-start | bytes 589832 | tf_op jit(solution)/shard_map/ppermute | solution.py:24
  4.3 10.5 %collective-permute-start.2 = (bf16[192,512]{1,0:T(8,128)(2,1)S(1)}, bf16[192,512]{1,0:T(8,128)(2,1)S(1)}, u32[]{:S(2)}, u32[]{:S(2)}) collective-permute-start(bf16[192,512]{1,0:T(8,128)(2,1)S(1)} %reshape.15.refs_3_), channel_id=1, source_target_pairs={{0,8},{8,0},{4,12},{12,4},{16,24},{24,16},{20,28},{28,20},{1,9},{9... | collective-permute-start | bytes 589832 | tf_op jit(solution)/shard_map/ppermute | solution.py:24
  5.9 13.4 %collective-permute-start.1 = (bf16[192,512]{1,0:T(8,128)(2,1)S(1)}, bf16[192,512]{1,0:T(8,128)(2,1)S(1)}, u32[]{:S(2)}, u32[]{:S(2)}) collective-permute-start(bf16[192,512]{1,0:T(8,128)(2,1)S(1)} %reshape.15.refs_3_), channel_id=1, source_target_pairs={{0,16},{16,0},{4,20},{20,4},{8,24},{24,8},{12,28},{28,12},{1,17},{... | collective-permute-start | bytes 589832 | tf_op jit(solution)/shard_map/ppermute | solution.py:24
  9.3 0.7 %copy-start.1 = (bf16[192,512]{1,0:T(8,128)(2,1)}, bf16[192,512]{1,0:T(8,128)(2,1)S(1)}, u32[]{:S(2)}) copy-start(bf16[192,512]{1,0:T(8,128)(2,1)S(1)} %collective-permute-done.refs_4_) | copy-start | bytes 589828
  14.8 0.7 %copy-start.3 = (bf16[192,512]{1,0:T(8,128)(2,1)}, bf16[192,512]{1,0:T(8,128)(2,1)S(1)}, u32[]{:S(2)}) copy-start(bf16[192,512]{1,0:T(8,128)(2,1)S(1)} %collective-permute-done.2.refs_4_) | copy-start | bytes 589828
  19.2 0.7 %copy-start.2 = (bf16[192,512]{1,0:T(8,128)(2,1)}, bf16[192,512]{1,0:T(8,128)(2,1)S(1)}, u32[]{:S(2)}) copy-start(bf16[192,512]{1,0:T(8,128)(2,1)S(1)} %collective-permute-done.1.refs_4_) | copy-start | bytes 589828
  23.7 4.0 %collective-permute-start.3 = (bf16[3,16,256]{2,1,0:T(8,128)(2,1)}, bf16[3,16,256]{2,1,0:T(8,128)(2,1)S(1)}, u32[]{:S(2)}, u32[]{:S(2)}) collective-permute-start(bf16[3,16,256]{2,1,0:T(8,128)(2,1)} %get-tuple-element.12), channel_id=1, source_target_pairs={{0,2},{1,3},{2,0},{3,1},{4,6},{5,7},{6,4},{7,5},{8,10},{9,11},{10,... | collective-permute-start | bytes 73736 | tf_op jit(solution)/shard_map/ppermute | solution.py:177
  28.6 1.2 %collective-permute-start.4 = (bf16[3,8,256]{2,1,0:T(8,128)(2,1)S(1)}, bf16[3,8,256]{2,1,0:T(8,128)(2,1)S(1)}, u32[]{:S(2)}, u32[]{:S(2)}) collective-permute-start(bf16[3,8,256]{2,1,0:T(8,128)(2,1)S(1)} %slice.13), channel_id=1, source_target_pairs={{0,1},{1,0},{2,3},{3,2},{4,5},{5,4},{6,7},{7,6},{8,9},{9,8},{10,11... | collective-permute-start | bytes 36872 | tf_op jit(solution)/shard_map/ppermute | solution.py:177

commit v8 on v7

--- a/solution.py
+++ b/solution.py
@@ -68,7 +68,10 @@
         else:
             prev_ref, out_ref = rest[:2]
             rest = rest[2:]
-        nscr, xpad, specl, specp, cross = rest
+        nscr, xpad, specl, specp, cross, wbuf, sems = rest
+        copies = [pltpu.make_async_copy(part_refs[n], wbuf.at[n], sems.at[n]) for n in range(n_part)]
+        for c in copies:
+            c.start()
 
         def spectra(w_ref, spec_ref):
             x = w_ref[...].astype(jnp.float32)
@@ -98,7 +101,8 @@
         sid = sid_ref[0]
         lane = lax.broadcasted_iota(jnp.int32, (1, 128), 1)
         for n, q in enumerate(rounds):
-            spectra(part_refs[n], specp)
+            copies[n].wait()
+            spectra(wbuf.at[n], specp)
             base = q * slots * 2
             for r in range(slots):
                 slot = (sid ^ (r // share)) * share + r % share
@@ -144,6 +148,7 @@
     kernel = make_kernel(events, chans, pad, length, slots, groups, share, rounds, n_prev, from_waves, final)
     smem = pl.BlockSpec(memory_space=pltpu.SMEM)
     vmem = pl.BlockSpec(memory_space=pltpu.VMEM)
+    anyspace = pl.BlockSpec(memory_space=pl.ANY)
     if from_waves:
         out_shape = (jax.ShapeDtypeStruct((len(rounds), slots, lags), jnp.float32),
                      jax.ShapeDtypeStruct((events * pad, 2 * length), jnp.bfloat16))
@@ -158,7 +163,7 @@
     return pl.pallas_call(
         kernel,
         out_shape=out_shape,
-        in_specs=[smem, smem, smem] + [vmem] * (3 + len(partners) + len(extra)),
+        in_specs=[smem, smem, smem, vmem] + [anyspace] * len(partners) + [vmem] * (2 + len(extra)),
         out_specs=tuple(vmem for _ in out_shape),
         scratch_shapes=[
             pltpu.VMEM((events * chans, length), jnp.float32),
@@ -166,6 +171,8 @@
             pltpu.VMEM((events * pad, 2 * length), jnp.float32),
             pltpu.VMEM((events * pad, 2 * length), jnp.float32),
             pltpu.VMEM((slots, 2 * length), jnp.float32),
+            pltpu.VMEM((len(partners),) + partners[0].shape, partners[0].dtype),
+            pltpu.SemaphoreType.DMA((len(partners),)),
         ],
     )(pairs, counts, sid, own, *partners, fwd, inv, *extra)
 

time: 30.7 us -> 32.4 us (1.055)
  Pallas kernels: 11.7 us -> 13.6 us
    pallas_call x3, Pallas kernels: 11.7 us -> 13.6 us  [rounds_call(): pl.pallas_call(kernel, out_shape=out_shape, in_specs=[smem, smem, smem, v...]
  transfers between devices with their start and end apart: 5 -> 5, of which waited for: 3 -> 3; matrix products, arithmetic and copies ran while one was open for 3% -> 3% of each run, Pallas kernels for 26% -> 28%
where the time goes in v8:
time: 32.4 us; the launch traced here: 32.1 us
  Pallas kernels  13.6 us (42%)
  starting transfers between devices  8.85 us (27%)
  waiting for transfers between devices  4.1 us (13%)
  local copies, waits for them, and re-layouts  4.05 us (12%)
  other arithmetic  1.42 us (4%)
    pallas_call x3, Pallas kernels, rounds_call(): pl.pallas_call(kernel, out_shape=out_shape, in_specs=[smem, smem, smem, v...  13.6 us
    ppermute x3, starting transfers between devices, swapped(): return lax.ppermute(block, axis, route)  7.23 us
    ppermute x2, waiting for transfers between devices, station_sum(): total = keep + lax.ppermute(send, 'station', perm).astype(jnp.float32)  3.71 us
    unnamed x12, local copies, waits for them, and re-layouts  3.16 us
    ppermute x2, starting transfers between devices, station_sum(): total = keep + lax.ppermute(send, 'station', perm).astype(jnp.float32)  1.62 us
    add x2, other arithmetic, station_sum(): total = keep + lax.ppermute(send, 'station', perm).astype(jnp.float32)  1.42 us
    reshape x1, local copies, waits for them, and re-layouts, shards(): pairs = pair_lists.reshape(-1)  0.71 us
  transfers between devices with their start and end apart: 5, of which 3 were waited for; matrix products, arithmetic and copies ran while one was open for 3% of the time, Pallas kernels for 28%

profile of v8, /device:TPU:0, one launch (start us, length us, event | category | flops | bytes accessed | tf_op | source)
XLA Modules:
  0.0 32.1 jit_solution(15017710600729287115)
XLA Ops:
  0.0 1.0 %copy.8 = bf16[16,4,3,512]{3,2,1,0:T(4,128)(2,1)S(1)} copy(bf16[16,4,3,512]{3,1,2,0:T(4,128)(2,1)} %param.5) | data formatting | bytes 393216 | tf_op args[0]
  1.1 0.0 copy-start.4
  1.1 0.2 reshape.15.refs_3_
  1.2 0.0 copy-start
  1.2 3.1 %collective-permute-start = (bf16[192,512]{1,0:T(8,128)(2,1)S(1)}, bf16[192,512]{1,0:T(8,128)(2,1)S(1)}, u32[]{:S(2)}, u32[]{:S(2)}) collective-permute-start(bf16[192,512]{1,0:T(8,128)(2,1)S(1)} %reshape.15.refs_3_), channel_id=1, source_target_pairs={{0,4},{4,0},{8,12},{12,8},{16,20},{20,16},{24,28},{28,24},{1,5},{5... | collective-permute-start | bytes 589832 | tf_op jit(solution)/shard_map/ppermute | solution.py:24
  4.3 1.6 %collective-permute-start.2 = (bf16[192,512]{1,0:T(8,128)(2,1)S(1)}, bf16[192,512]{1,0:T(8,128)(2,1)S(1)}, u32[]{:S(2)}, u32[]{:S(2)}) collective-permute-start(bf16[192,512]{1,0:T(8,128)(2,1)S(1)} %reshape.15.refs_3_), channel_id=1, source_target_pairs={{0,8},{8,0},{4,12},{12,4},{16,24},{24,16},{20,28},{28,20},{1,9},{9... | collective-permute-start | bytes 589832 | tf_op jit(solution)/shard_map/ppermute | solution.py:24
  5.9 2.6 %collective-permute-start.1 = (bf16[192,512]{1,0:T(8,128)(2,1)S(1)}, bf16[192,512]{1,0:T(8,128)(2,1)S(1)}, u32[]{:S(2)}, u32[]{:S(2)}) collective-permute-start(bf16[192,512]{1,0:T(8,128)(2,1)S(1)} %reshape.15.refs_3_), channel_id=1, source_target_pairs={{0,16},{16,0},{4,20},{20,4},{8,24},{24,8},{12,28},{28,12},{1,17},{... | collective-permute-start | bytes 589832 | tf_op jit(solution)/shard_map/ppermute | solution.py:24
  8.5 0.0 copy-done.4
  8.5 0.1 copy.7
  8.6 0.7 %reshape.12.refs_0_ = s32[192]{0:T(256)} reshape(s32[3,32,2]{2,1,0:T(8,128)S(1)} %copy.7) | data formatting | bytes 1536 | tf_op jit(solution)/shard_map/reshape | solution.py:202
  9.3 0.0 collective-permute-done.refs_4_
  9.3 0.0 copy-start.1
  9.3 0.0 copy-done
  9.3 0.7 %copy-done.1 = bf16[192,512]{1,0:T(8,128)(2,1)} copy-done((bf16[192,512]{1,0:T(8,128)(2,1)}, bf16[192,512]{1,0:T(8,128)(2,1)S(1)}, u32[]{:S(2)}) %copy-start.1) | copy-done | bytes 196632
  10.0 4.4 %shard_map.55 = (f32[1,32,256]{2,1,0:T(8,128)}, bf16[256,1024]{1,0:T(8,128)(2,1)}) custom-call(s32[192]{0:T(256)} %reshape.12.refs_0_, s32[3]{0:T(128)} %bitcast.2, s32[1]{0:T(128)} %bitcast.1.refs_2_, bf16[192,512]{1,0:T(8,128)(2,1)} %copy-done, bf16[192,512]{1,0:T(8,128)(2,1)} %copy-done.1, bf16[512,1024]{1,0:T(8,128)(2,1)} %constant.8.clone.refs_5_, ...), custom_call_target="tpu_custom_call" | custom-call | tf_op jit(solution)/shard_map/pallas_call | solution.py:163
  14.4 0.4 %collective-permute-done.2.refs_4_ = bf16[192,512]{1,0:T(8,128)(2,1)S(1)} collective-permute-done((bf16[192,512]{1,0:T(8,128)(2,1)S(1)}, bf16[192,512]{1,0:T(8,128)(2,1)S(1)}, u32[]{:S(2)}, u32[]{:S(2)}) %collective-permute-start.2) | collective-permute-done | bytes 196640 | tf_op jit(solution)/shard_map/ppermute | solution.py:24
  14.8 0.0 copy-start.3
  14.8 0.7 %copy-done.3 = bf16[192,512]{1,0:T(8,128)(2,1)} copy-done((bf16[192,512]{1,0:T(8,128)(2,1)}, bf16[192,512]{1,0:T(8,128)(2,1)S(1)}, u32[]{:S(2)}) %copy-start.3) | copy-done | bytes 196632
  15.4 4.6 %shard_map.56.refs_7_ = f32[2,32,256]{2,1,0:T(8,128)} custom-call(s32[192]{0:T(256)} %reshape.12.refs_0_, s32[3]{0:T(128)} %bitcast.3, s32[1]{0:T(128)} %bitcast.1.refs_2_, bf16[256,1024]{1,0:T(8,128)(2,1)} %get-tuple-element.9.refs_3_, bf16[192,512]{1,0:T(8,128)(2,1)} %copy-done.3, bf16[512,1024]{1,0:T(8,128)(2,1)} %constant.8.clone.refs_5_, ...), custom_call_target="tpu_custom_call" | custom-call | tf_op jit(solution)/shard_map/pallas_call | solution.py:163
  20.0 0.0 collective-permute-done.1.refs_4_
  20.0 0.0 copy-start.2
  20.1 0.7 %copy-done.2 = bf16[192,512]{1,0:T(8,128)(2,1)} copy-done((bf16[192,512]{1,0:T(8,128)(2,1)}, bf16[192,512]{1,0:T(8,128)(2,1)S(1)}, u32[]{:S(2)}) %copy-start.2) | copy-done | bytes 196632
  20.7 4.6 %shard_map.57 = (f32[3,16,256]{2,1,0:T(8,128)}, bf16[3,16,256]{2,1,0:T(8,128)(2,1)}) custom-call(s32[192]{0:T(256)} %reshape.12.refs_0_, s32[3]{0:T(128)} %bitcast.4, s32[1]{0:T(128)} %bitcast.1.refs_2_, bf16[256,1024]{1,0:T(8,128)(2,1)} %get-tuple-element.9.refs_3_, bf16[192,512]{1,0:T(8,128)(2,1)} %copy-done.2, bf16[512,1024]{1,0:T(8,128)(2,1)} %constant.8.clone.refs_5_, ...), custom_call_target="tpu_custom_call" | custom-call | tf_op jit(solution)/shard_map/pallas_call | solution.py:163
  25.3 1.6 %collective-permute-start.3 = (bf16[3,16,256]{2,1,0:T(8,128)(2,1)}, bf16[3,16,256]{2,1,0:T(8,128)(2,1)S(1)}, u32[]{:S(2)}, u32[]{:S(2)}) collective-permute-start(bf16[3,16,256]{2,1,0:T(8,128)(2,1)} %get-tuple-element.12), channel_id=1, source_target_pairs={{0,2},{1,3},{2,0},{3,1},{4,6},{5,7},{6,4},{7,5},{8,10},{9,11},{10,... | collective-permute-start | bytes 73736 | tf_op jit(solution)/shard_map/ppermute | solution.py:184
  26.9 2.5 %collective-permute-done.3 = bf16[3,16,256]{2,1,0:T(8,128)(2,1)S(1)} collective-permute-done((bf16[3,16,256]{2,1,0:T(8,128)(2,1)}, bf16[3,16,256]{2,1,0:T(8,128)(2,1)S(1)}, u32[]{:S(2)}, u32[]{:S(2)}) %collective-permute-start.3) | collective-permute-done | bytes 24608 | tf_op jit(solution)/shard_map/ppermute | solution.py:184
  29.4 0.8 %convert_add_fusion = f32[3,16,256]{2,1,0:T(8,128)S(1)} fusion(f32[3,16,256]{2,1,0:T(8,128)} %get-tuple-element.11, bf16[3,16,256]{2,1,0:T(8,128)(2,1)S(1)} %collective-permute-done.3), kind=kLoop, calls=%fused_computation | loop fusion | flops 24576 | bytes 122880 | tf_op jit(solution)/shard_map/add | solution.py:184
  30.2 0.1 collective-permute-start.4
  30.3 1.2 %collective-permute-done.4 = bf16[3,8,256]{2,1,0:T(8,128)(2,1)S(1)} collective-permute-done((bf16[3,8,256]{2,1,0:T(8,128)(2,1)S(1)}, bf16[3,8,256]{2,1,0:T(8,128)(2,1)S(1)}, u32[]{:S(2)}, u32[]{:S(2)}) %collective-permute-start.4) | collective-permute-done | bytes 12320 | tf_op jit(solution)/shard_map/ppermute | solution.py:184
  31.5 0.6 %slice_add_fusion = f32[3,8,256]{2,1,0:T(8,128)} fusion(f32[3,16,256]{2,1,0:T(8,128)S(1)} %convert_add_fusion, bf16[3,8,256]{2,1,0:T(8,128)(2,1)S(1)} %collective-permute-done.4), kind=kLoop, calls=%fused_computation.2 | loop fusion | flops 12288 | bytes 61440 | tf_op jit(solution)/shard_map/add | solution.py:184
  (1 shorter events, 0.0 us)
Async XLA Ops:
  1.1 7.4 %copy-start.4 = (s32[3,32,2]{1,2,0:T(2,128)S(1)}, s32[3,32,2]{1,2,0:T(2,128)}, u32[]{:S(2)}) copy-start(s32[3,32,2]{1,2,0:T(2,128)} %param.6) | copy-start | bytes 2308
  1.2 8.1 %copy-start = (bf16[192,512]{1,0:T(8,128)(2,1)}, bf16[192,512]{1,0:T(8,128)(2,1)S(1)}, u32[]{:S(2)}) copy-start(bf16[192,512]{1,0:T(8,128)(2,1)S(1)} %reshape.15.refs_3_) | copy-start | bytes 589828
  1.2 8.0 %collective-permute-start = (bf16[192,512]{1,0:T(8,128)(2,1)S(1)}, bf16[192,512]{1,0:T(8,128)(2,1)S(1)}, u32[]{:S(2)}, u32[]{:S(2)}) collective-permute-start(bf16[192,512]{1,0:T(8,128)(2,1)S(1)} %reshape.15.refs_3_), channel_id=1, source_target_pairs={{0,4},{4,0},{8,12},{12,8},{16,20},{20,16},{24,28},{28,24},{1,5},{5... | collective-permute-start | bytes 589832 | tf_op jit(solution)/shard_map/ppermute | solution.py:24
  4.3 10.5 %collective-permute-start.2 = (bf16[192,512]{1,0:T(8,128)(2,1)S(1)}, bf16[192,512]{1,0:T(8,128)(2,1)S(1)}, u32[]{:S(2)}, u32[]{:S(2)}) collective-permute-start(bf16[192,512]{1,0:T(8,128)(2,1)S(1)} %reshape.15.refs_3_), channel_id=1, source_target_pairs={{0,8},{8,0},{4,12},{12,4},{16,24},{24,16},{20,28},{28,20},{1,9},{9... | collective-permute-start | bytes 589832 | tf_op jit(solution)/shard_map/ppermute | solution.py:24
  5.9 14.2 %collective-permute-start.1 = (bf16[192,512]{1,0:T(8,128)(2,1)S(1)}, bf16[192,512]{1,0:T(8,128)(2,1)S(1)}, u32[]{:S(2)}, u32[]{:S(2)}) collective-permute-start(bf16[192,512]{1,0:T(8,128)(2,1)S(1)} %reshape.15.refs_3_), channel_id=1, source_target_pairs={{0,16},{16,0},{4,20},{20,4},{8,24},{24,8},{12,28},{28,12},{1,17},{... | collective-permute-start | bytes 589832 | tf_op jit(solution)/shard_map/ppermute | solution.py:24
  9.3 0.7 %copy-start.1 = (bf16[192,512]{1,0:T(8,128)(2,1)}, bf16[192,512]{1,0:T(8,128)(2,1)S(1)}, u32[]{:S(2)}) copy-start(bf16[192,512]{1,0:T(8,128)(2,1)S(1)} %collective-permute-done.refs_4_) | copy-start | bytes 589828
  14.8 0.7 %copy-start.3 = (bf16[192,512]{1,0:T(8,128)(2,1)}, bf16[192,512]{1,0:T(8,128)(2,1)S(1)}, u32[]{:S(2)}) copy-start(bf16[192,512]{1,0:T(8,128)(2,1)S(1)} %collective-permute-done.2.refs_4_) | copy-start | bytes 589828
  20.0 0.7 %copy-start.2 = (bf16[192,512]{1,0:T(8,128)(2,1)}, bf16[192,512]{1,0:T(8,128)(2,1)S(1)}, u32[]{:S(2)}) copy-start(bf16[192,512]{1,0:T(8,128)(2,1)S(1)} %collective-permute-done.1.refs_4_) | copy-start | bytes 589828
  25.3 4.1 %collective-permute-start.3 = (bf16[3,16,256]{2,1,0:T(8,128)(2,1)}, bf16[3,16,256]{2,1,0:T(8,128)(2,1)S(1)}, u32[]{:S(2)}, u32[]{:S(2)}) collective-permute-start(bf16[3,16,256]{2,1,0:T(8,128)(2,1)} %get-tuple-element.12), channel_id=1, source_target_pairs={{0,2},{1,3},{2,0},{3,1},{4,6},{5,7},{6,4},{7,5},{8,10},{9,11},{10,... | collective-permute-start | bytes 73736 | tf_op jit(solution)/shard_map/ppermute | solution.py:184
  30.2 1.2 %collective-permute-start.4 = (bf16[3,8,256]{2,1,0:T(8,128)(2,1)S(1)}, bf16[3,8,256]{2,1,0:T(8,128)(2,1)S(1)}, u32[]{:S(2)}, u32[]{:S(2)}) collective-permute-start(bf16[3,8,256]{2,1,0:T(8,128)(2,1)S(1)} %slice.13), channel_id=1, source_target_pairs={{0,1},{1,0},{2,3},{3,2},{4,5},{5,4},{6,7},{7,6},{8,9},{9,8},{10,11... | collective-permute-start | bytes 36872 | tf_op jit(solution)/shard_map/ppermute | solution.py:184

commit v9 on v7

--- a/solution.py
+++ b/solution.py
@@ -90,8 +90,9 @@
             for n in range(n_prev):
                 prev = prev_ref[n]
                 if final:
-                    keep_ref[n] = prev[:slots // 2]
-                    send_ref[n] = prev[slots // 2:].astype(jnp.bfloat16)
+                    keep_ref[n] = prev[:share]
+                    for j in range(1, groups):
+                        send_ref[j - 1, n] = prev[j * share:(j + 1) * share].astype(jnp.bfloat16)
                 else:
                     out_ref[n] = prev
 
@@ -127,8 +128,9 @@
             if not final:
                 out_ref[n_prev + n] = corr
             else:
-                keep_ref[n_prev + n] = corr[:slots // 2]
-                send_ref[n_prev + n] = corr[slots // 2:].astype(jnp.bfloat16)
+                keep_ref[n_prev + n] = corr[:share]
+                for j in range(1, groups):
+                    send_ref[j - 1, n_prev + n] = corr[j * share:(j + 1) * share].astype(jnp.bfloat16)
 
     return kernel
 
@@ -152,8 +154,8 @@
         out_shape = (jax.ShapeDtypeStruct((n_prev + len(rounds), slots, lags), jnp.float32),)
         extra = [prev]
     else:
-        out_shape = (jax.ShapeDtypeStruct((n_prev + len(rounds), slots // 2, lags), jnp.float32),
-                     jax.ShapeDtypeStruct((n_prev + len(rounds), slots // 2, lags), jnp.bfloat16))
+        out_shape = (jax.ShapeDtypeStruct((n_prev + len(rounds), share, lags), jnp.float32),
+                     jax.ShapeDtypeStruct((groups - 1, n_prev + len(rounds), share, lags), jnp.bfloat16))
         extra = [prev]
     return pl.pallas_call(
         kernel,
@@ -171,15 +173,11 @@
 
 
 def station_sum(keep, send, groups):
-    bit = groups // 2
-    while True:
-        perm = [(s, s ^ bit) for s in range(groups)]
-        total = keep + lax.ppermute(send, "station", perm).astype(jnp.float32)
-        bit //= 2
-        if not bit:
-            return total
-        rows = total.shape[1] // 2
-        keep, send = total[:, :rows], total[:, rows:].astype(jnp.bfloat16)
+    total = keep
+    for j in range(1, groups):
+        perm = [(s, s ^ j) for s in range(groups)]
+        total = total + lax.ppermute(send[j - 1], "station", perm).astype(jnp.float32)
+    return total
 
 
 def shards(waveforms, pair_lists, pair_counts):

time: 30.7 us -> 30 us (0.977)
  waiting for transfers between devices: 4.4 us -> 3.44 us
  other arithmetic: 1.42 us -> 0.62 us
  local copies, waits for them, and re-layouts: 4.05 us -> 4.8 us
    ppermute x2 -> x3, waiting for transfers between devices: 3.71 us -> 2.75 us  [station_sum(): lax.ppermute(send[j - 1], 'station', perm).astype(jnp.float32)]
    add x2 -> x1, other arithmetic: 1.42 us -> 0.62 us  [station_sum(): total + lax.ppermute(send[j - 1], 'station', perm).astype(jnp.float32)]
    squeeze x0 -> x1, local copies, waits for them, and re-layouts: none -> 0.75 us  [station_sum(): send[j - 1]]
    ppermute x2 -> x3, starting transfers between devices: 1.56 us -> 1.86 us  [station_sum(): lax.ppermute(send[j - 1], 'station', perm).astype(jnp.float32)]
    unnamed x12 -> x14, local copies, waits for them, and re-layouts: 3.17 us -> 3.18 us
  transfers between devices with their start and end apart: 5 -> 6, of which waited for: 3 -> 3; matrix products, arithmetic and copies ran while one was open for 3% -> 3% of each run, Pallas kernels for 26% -> 27%
where the time goes in v9:
time: 30 us; the launch traced here: 29.7 us
  Pallas kernels  11.7 us (39%)
  starting transfers between devices  9.09 us (30%)
  local copies, waits for them, and re-layouts  4.8 us (16%)
  waiting for transfers between devices  3.44 us (11%)
  other arithmetic  0.62 us (2%)
    pallas_call x3, Pallas kernels, rounds_call(): pl.pallas_call(kernel, out_shape=out_shape, in_specs=[smem, smem, smem] +...  11.7 us
    ppermute x3, starting transfers between devices, swapped(): return lax.ppermute(block, axis, route)  7.23 us
    unnamed x14, local copies, waits for them, and re-layouts  3.18 us
    ppermute x3, waiting for transfers between devices, station_sum(): lax.ppermute(send[j - 1], 'station', perm).astype(jnp.float32)  2.75 us
    ppermute x3, starting transfers between devices, station_sum(): lax.ppermute(send[j - 1], 'station', perm).astype(jnp.float32)  1.86 us
    squeeze x1, local copies, waits for them, and re-layouts, station_sum(): send[j - 1]  0.75 us
    reshape x1, local copies, waits for them, and re-layouts, shards(): pairs = pair_lists.reshape(-1)  0.71 us
    ppermute x3, waiting for transfers between devices, swapped(): return lax.ppermute(block, axis, route)  0.69 us
  transfers between devices with their start and end apart: 6, of which 3 were waited for; matrix products, arithmetic and copies ran while one was open for 3% of the time, Pallas kernels for 27%

profile of v9, /device:TPU:0, one launch (start us, length us, event | category | flops | bytes accessed | tf_op | source)
XLA Modules:
  0.0 29.7 jit_solution(17088412382038769915)
XLA Ops:
  0.0 1.0 %copy.8 = bf16[16,4,3,512]{3,2,1,0:T(4,128)(2,1)S(1)} copy(bf16[16,4,3,512]{3,1,2,0:T(4,128)(2,1)} %param.5) | data formatting | bytes 393216 | tf_op args[0]
  1.1 0.0 copy-start.5
  1.1 0.2 reshape.15.refs_3_
  1.2 0.0 copy-start
  1.2 3.1 %collective-permute-start = (bf16[192,512]{1,0:T(8,128)(2,1)S(1)}, bf16[192,512]{1,0:T(8,128)(2,1)S(1)}, u32[]{:S(2)}, u32[]{:S(2)}) collective-permute-start(bf16[192,512]{1,0:T(8,128)(2,1)S(1)} %reshape.15.refs_3_), channel_id=1, source_target_pairs={{0,4},{4,0},{8,12},{12,8},{16,20},{20,16},{24,28},{28,24},{1,5},{5... | collective-permute-start | bytes 589832 | tf_op jit(solution)/shard_map/ppermute | solution.py:24
  4.3 1.6 %collective-permute-start.2 = (bf16[192,512]{1,0:T(8,128)(2,1)S(1)}, bf16[192,512]{1,0:T(8,128)(2,1)S(1)}, u32[]{:S(2)}, u32[]{:S(2)}) collective-permute-start(bf16[192,512]{1,0:T(8,128)(2,1)S(1)} %reshape.15.refs_3_), channel_id=1, source_target_pairs={{0,8},{8,0},{4,12},{12,4},{16,24},{24,16},{20,28},{28,20},{1,9},{9... | collective-permute-start | bytes 589832 | tf_op jit(solution)/shard_map/ppermute | solution.py:24
  5.9 2.6 %collective-permute-start.1 = (bf16[192,512]{1,0:T(8,128)(2,1)S(1)}, bf16[192,512]{1,0:T(8,128)(2,1)S(1)}, u32[]{:S(2)}, u32[]{:S(2)}) collective-permute-start(bf16[192,512]{1,0:T(8,128)(2,1)S(1)} %reshape.15.refs_3_), channel_id=1, source_target_pairs={{0,16},{16,0},{4,20},{20,4},{8,24},{24,8},{12,28},{28,12},{1,17},{... | collective-permute-start | bytes 589832 | tf_op jit(solution)/shard_map/ppermute | solution.py:24
  8.5 0.0 copy-done.5
  8.5 0.1 copy.7
  8.6 0.7 %reshape.12.refs_0_ = s32[192]{0:T(256)} reshape(s32[3,32,2]{2,1,0:T(8,128)S(1)} %copy.7) | data formatting | bytes 1536 | tf_op jit(solution)/shard_map/reshape | solution.py:193
  9.3 0.0 collective-permute-done.refs_4_
  9.3 0.0 copy-start.1
  9.3 0.0 copy-done
  9.3 0.7 %copy-done.1 = bf16[192,512]{1,0:T(8,128)(2,1)} copy-done((bf16[192,512]{1,0:T(8,128)(2,1)}, bf16[192,512]{1,0:T(8,128)(2,1)S(1)}, u32[]{:S(2)}) %copy-start.1) | copy-done | bytes 196632
  10.0 4.1 %shard_map.55 = (f32[1,32,256]{2,1,0:T(8,128)}, bf16[256,1024]{1,0:T(8,128)(2,1)}) custom-call(s32[192]{0:T(256)} %reshape.12.refs_0_, s32[3]{0:T(128)} %bitcast.8, s32[1]{0:T(128)} %bitcast.1.refs_2_, bf16[192,512]{1,0:T(8,128)(2,1)} %copy-done, bf16[192,512]{1,0:T(8,128)(2,1)} %copy-done.1, bf16[512,1024]{1,0:T(8,128)(2,1)} %constant.8.clone.refs_5_, ...), custom_call_target="tpu_custom_call" | custom-call | tf_op jit(solution)/shard_map/pallas_call | solution.py:160
  14.1 0.7 %collective-permute-done.2.refs_4_ = bf16[192,512]{1,0:T(8,128)(2,1)S(1)} collective-permute-done((bf16[192,512]{1,0:T(8,128)(2,1)S(1)}, bf16[192,512]{1,0:T(8,128)(2,1)S(1)}, u32[]{:S(2)}, u32[]{:S(2)}) %collective-permute-start.2) | collective-permute-done | bytes 196640 | tf_op jit(solution)/shard_map/ppermute | solution.py:24
  14.8 0.0 copy-start.3
  14.8 0.7 %copy-done.3 = bf16[192,512]{1,0:T(8,128)(2,1)} copy-done((bf16[192,512]{1,0:T(8,128)(2,1)}, bf16[192,512]{1,0:T(8,128)(2,1)S(1)}, u32[]{:S(2)}) %copy-start.3) | copy-done | bytes 196632
  15.4 3.8 %shard_map.56.refs_7_ = f32[2,32,256]{2,1,0:T(8,128)} custom-call(s32[192]{0:T(256)} %reshape.12.refs_0_, s32[3]{0:T(128)} %bitcast.9, s32[1]{0:T(128)} %bitcast.1.refs_2_, bf16[256,1024]{1,0:T(8,128)(2,1)} %get-tuple-element.9.refs_3_, bf16[192,512]{1,0:T(8,128)(2,1)} %copy-done.3, bf16[512,1024]{1,0:T(8,128)(2,1)} %constant.8.clone.refs_5_, ...), custom_call_target="tpu_custom_call" | custom-call | tf_op jit(solution)/shard_map/pallas_call | solution.py:160
  19.2 0.0 collective-permute-done.1.refs_4_
  19.3 0.0 copy-start.2
  19.3 0.7 %copy-done.2 = bf16[192,512]{1,0:T(8,128)(2,1)} copy-done((bf16[192,512]{1,0:T(8,128)(2,1)}, bf16[192,512]{1,0:T(8,128)(2,1)S(1)}, u32[]{:S(2)}) %copy-start.2) | copy-done | bytes 196632
  19.9 3.8 %shard_map.57 = (f32[3,8,256]{2,1,0:T(8,128)}, bf16[3,3,8,256]{3,2,1,0:T(8,128)(2,1)}) custom-call(s32[192]{0:T(256)} %reshape.12.refs_0_, s32[3]{0:T(128)} %bitcast.10, s32[1]{0:T(128)} %bitcast.1.refs_2_, bf16[256,1024]{1,0:T(8,128)(2,1)} %get-tuple-element.9.refs_3_, bf16[192,512]{1,0:T(8,128)(2,1)} %copy-done.2, ...), custom_call_target="tpu_custom_call" | custom-call | tf_op jit(solution)/shard_map/pallas_call | solution.py:160
  23.7 0.0 copy-start.4
  23.7 0.7 %slice_bitcast_fusion.2 = (bf16[3,8,256]{2,1,0:T(8,128)(2,1)S(1)}, bf16[3,8,256]{2,1,0:T(8,128)(2,1)S(1)}, bf16[3,8,256]{2,1,0:T(8,128)(2,1)S(1)}) fusion(bf16[3,3,8,256]{3,2,1,0:T(8,128)(2,1)} %get-tuple-element.12), kind=kLoop, calls=%fused_computation.3 | loop fusion | bytes 73728 | tf_op jit(solution)/shard_map/squeeze | solution.py:179
  24.5 0.0 collective-permute-start.3
  24.5 1.5 %collective-permute-start.4 = (bf16[3,8,256]{2,1,0:T(8,128)(2,1)S(1)}, bf16[3,8,256]{2,1,0:T(8,128)(2,1)S(1)}, u32[]{:S(2)}, u32[]{:S(2)}) collective-permute-start(bf16[3,8,256]{2,1,0:T(8,128)(2,1)S(1)} %get-tuple-element.15), channel_id=1, source_target_pairs={{0,2},{1,3},{2,0},{3,1},{4,6},{5,7},{6,4},{7,5},{8,10},{9,11},{10,... | collective-permute-start | bytes 36872 | tf_op jit(solution)/shard_map/ppermute | solution.py:179
  26.0 0.4 %collective-permute-start.5 = (bf16[3,8,256]{2,1,0:T(8,128)(2,1)S(1)}, bf16[3,8,256]{2,1,0:T(8,128)(2,1)S(1)}, u32[]{:S(2)}, u32[]{:S(2)}) collective-permute-start(bf16[3,8,256]{2,1,0:T(8,128)(2,1)S(1)} %get-tuple-element.14), channel_id=1, source_target_pairs={{0,3},{1,2},{2,1},{3,0},{4,7},{5,6},{6,5},{7,4},{8,11},{9,10},{10,... | collective-permute-start | bytes 36872 | tf_op jit(solution)/shard_map/ppermute | solution.py:179
  26.3 0.0 collective-permute-done.3
  26.3 1.8 %collective-permute-done.4 = bf16[3,8,256]{2,1,0:T(8,128)(2,1)S(1)} collective-permute-done((bf16[3,8,256]{2,1,0:T(8,128)(2,1)S(1)}, bf16[3,8,256]{2,1,0:T(8,128)(2,1)S(1)}, u32[]{:S(2)}, u32[]{:S(2)}) %collective-permute-start.4) | collective-permute-done | bytes 12320 | tf_op jit(solution)/shard_map/ppermute | solution.py:179
  28.2 0.9 %collective-permute-done.5 = bf16[3,8,256]{2,1,0:T(8,128)(2,1)S(1)} collective-permute-done((bf16[3,8,256]{2,1,0:T(8,128)(2,1)S(1)}, bf16[3,8,256]{2,1,0:T(8,128)(2,1)S(1)}, u32[]{:S(2)}, u32[]{:S(2)}) %collective-permute-start.5) | collective-permute-done | bytes 12320 | tf_op jit(solution)/shard_map/ppermute | solution.py:179
  29.1 0.0 copy-done.4
  29.1 0.6 %convert_add_fusion = f32[3,8,256]{2,1,0:T(8,128)} fusion(bf16[3,8,256]{2,1,0:T(8,128)(2,1)S(1)} %collective-permute-done.5, bf16[3,8,256]{2,1,0:T(8,128)(2,1)S(1)} %collective-permute-done.4, f32[3,8,256]{2,1,0:T(8,128)S(1)} %copy-done.4, bf16[3,8,256]{2,1,0:T(8,128)(2,1)S(1)} %collective-permute-done.3), kind=kLoop, calls=%fused_computation | loop fusion | flops 36864 | bytes 86016 | tf_op jit(solution)/shard_map/add | solution.py:179
Async XLA Ops:
  1.1 7.4 %copy-start.5 = (s32[3,32,2]{1,2,0:T(2,128)S(1)}, s32[3,32,2]{1,2,0:T(2,128)}, u32[]{:S(2)}) copy-start(s32[3,32,2]{1,2,0:T(2,128)} %param.6) | copy-start | bytes 2308
  1.2 8.1 %copy-start = (bf16[192,512]{1,0:T(8,128)(2,1)}, bf16[192,512]{1,0:T(8,128)(2,1)S(1)}, u32[]{:S(2)}) copy-start(bf16[192,512]{1,0:T(8,128)(2,1)S(1)} %reshape.15.refs_3_) | copy-start | bytes 589828
  1.2 8.0 %collective-permute-start = (bf16[192,512]{1,0:T(8,128)(2,1)S(1)}, bf16[192,512]{1,0:T(8,128)(2,1)S(1)}, u32[]{:S(2)}, u32[]{:S(2)}) collective-permute-start(bf16[192,512]{1,0:T(8,128)(2,1)S(1)} %reshape.15.refs_3_), channel_id=1, source_target_pairs={{0,4},{4,0},{8,12},{12,8},{16,20},{20,16},{24,28},{28,24},{1,5},{5... | collective-permute-start | bytes 589832 | tf_op jit(solution)/shard_map/ppermute | solution.py:24
  4.3 10.5 %collective-permute-start.2 = (bf16[192,512]{1,0:T(8,128)(2,1)S(1)}, bf16[192,512]{1,0:T(8,128)(2,1)S(1)}, u32[]{:S(2)}, u32[]{:S(2)}) collective-permute-start(bf16[192,512]{1,0:T(8,128)(2,1)S(1)} %reshape.15.refs_3_), channel_id=1, source_target_pairs={{0,8},{8,0},{4,12},{12,4},{16,24},{24,16},{20,28},{28,20},{1,9},{9... | collective-permute-start | bytes 589832 | tf_op jit(solution)/shard_map/ppermute | solution.py:24
  5.9 13.4 %collective-permute-start.1 = (bf16[192,512]{1,0:T(8,128)(2,1)S(1)}, bf16[192,512]{1,0:T(8,128)(2,1)S(1)}, u32[]{:S(2)}, u32[]{:S(2)}) collective-permute-start(bf16[192,512]{1,0:T(8,128)(2,1)S(1)} %reshape.15.refs_3_), channel_id=1, source_target_pairs={{0,16},{16,0},{4,20},{20,4},{8,24},{24,8},{12,28},{28,12},{1,17},{... | collective-permute-start | bytes 589832 | tf_op jit(solution)/shard_map/ppermute | solution.py:24
  9.3 0.7 %copy-start.1 = (bf16[192,512]{1,0:T(8,128)(2,1)}, bf16[192,512]{1,0:T(8,128)(2,1)S(1)}, u32[]{:S(2)}) copy-start(bf16[192,512]{1,0:T(8,128)(2,1)S(1)} %collective-permute-done.refs_4_) | copy-start | bytes 589828
  14.8 0.7 %copy-start.3 = (bf16[192,512]{1,0:T(8,128)(2,1)}, bf16[192,512]{1,0:T(8,128)(2,1)S(1)}, u32[]{:S(2)}) copy-start(bf16[192,512]{1,0:T(8,128)(2,1)S(1)} %collective-permute-done.2.refs_4_) | copy-start | bytes 589828
  19.3 0.7 %copy-start.2 = (bf16[192,512]{1,0:T(8,128)(2,1)}, bf16[192,512]{1,0:T(8,128)(2,1)S(1)}, u32[]{:S(2)}) copy-start(bf16[192,512]{1,0:T(8,128)(2,1)S(1)} %collective-permute-done.1.refs_4_) | copy-start | bytes 589828
  23.7 5.4 %copy-start.4 = (f32[3,8,256]{2,1,0:T(8,128)S(1)}, f32[3,8,256]{2,1,0:T(8,128)}, u32[]{:S(2)}) copy-start(f32[3,8,256]{2,1,0:T(8,128)} %get-tuple-element.11) | copy-start | bytes 73732
  24.5 1.9 %collective-permute-start.3 = (bf16[3,8,256]{2,1,0:T(8,128)(2,1)S(1)}, bf16[3,8,256]{2,1,0:T(8,128)(2,1)S(1)}, u32[]{:S(2)}, u32[]{:S(2)}) collective-permute-start(bf16[3,8,256]{2,1,0:T(8,128)(2,1)S(1)} %get-tuple-element.13), channel_id=1, source_target_pairs={{0,1},{1,0},{2,3},{3,2},{4,5},{5,4},{6,7},{7,6},{8,9},{9,8},{10,11... | collective-permute-start | bytes 36872 | tf_op jit(solution)/shard_map/ppermute | solution.py:179
  24.5 3.7 %collective-permute-start.4 = (bf16[3,8,256]{2,1,0:T(8,128)(2,1)S(1)}, bf16[3,8,256]{2,1,0:T(8,128)(2,1)S(1)}, u32[]{:S(2)}, u32[]{:S(2)}) collective-permute-start(bf16[3,8,256]{2,1,0:T(8,128)(2,1)S(1)} %get-tuple-element.15), channel_id=1, source_target_pairs={{0,2},{1,3},{2,0},{3,1},{4,6},{5,7},{6,4},{7,5},{8,10},{9,11},{10,... | collective-permute-start | bytes 36872 | tf_op jit(solution)/shard_map/ppermute | solution.py:179
  26.0 3.1 %collective-permute-start.5 = (bf16[3,8,256]{2,1,0:T(8,128)(2,1)S(1)}, bf16[3,8,256]{2,1,0:T(8,128)(2,1)S(1)}, u32[]{:S(2)}, u32[]{:S(2)}) collective-permute-start(bf16[3,8,256]{2,1,0:T(8,128)(2,1)S(1)} %get-tuple-element.14), channel_id=1, source_target_pairs={{0,3},{1,2},{2,1},{3,0},{4,7},{5,6},{6,5},{7,4},{8,11},{9,10},{10,... | collective-permute-start | bytes 36872 | tf_op jit(solution)/shard_map/ppermute | solution.py:179

commit v10 on v9

--- a/solution.py
+++ b/solution.py
@@ -63,8 +63,9 @@
             out_ref, spec_out = rest[:2]
             rest = rest[2:]
         elif final:
-            prev_ref, keep_ref, send_ref = rest[:3]
-            rest = rest[3:]
+            prev_ref, keep_ref = rest[:2]
+            send_refs = rest[2:2 + groups - 1]
+            rest = rest[2 + groups - 1:]
         else:
             prev_ref, out_ref = rest[:2]
             rest = rest[2:]
@@ -92,7 +93,7 @@
                 if final:
                     keep_ref[n] = prev[:share]
                     for j in range(1, groups):
-                        send_ref[j - 1, n] = prev[j * share:(j + 1) * share].astype(jnp.bfloat16)
+                        send_refs[j - 1][n] = prev[j * share:(j + 1) * share].astype(jnp.bfloat16)
                 else:
                     out_ref[n] = prev
 
@@ -130,7 +131,7 @@
             else:
                 keep_ref[n_prev + n] = corr[:share]
                 for j in range(1, groups):
-                    send_ref[j - 1, n_prev + n] = corr[j * share:(j + 1) * share].astype(jnp.bfloat16)
+                    send_refs[j - 1][n_prev + n] = corr[j * share:(j + 1) * share].astype(jnp.bfloat16)
 
     return kernel
 
@@ -155,7 +156,8 @@
         extra = [prev]
     else:
         out_shape = (jax.ShapeDtypeStruct((n_prev + len(rounds), share, lags), jnp.float32),
-                     jax.ShapeDtypeStruct((groups - 1, n_prev + len(rounds), share, lags), jnp.bfloat16))
+                     ) + tuple(jax.ShapeDtypeStruct((n_prev + len(rounds), share, lags), jnp.bfloat16)
+                               for _ in range(groups - 1))
         extra = [prev]
     return pl.pallas_call(
         kernel,
@@ -198,7 +200,7 @@
     for q in range(1, rounds - 1):
         (corr,) = rounds_call(pairs, counts, sid, spec, [partners[q]], fwd, inv,
                               [q], events, chans, slots, groups, prev=corr)
-    keep, send = rounds_call(pairs, counts, sid, spec, [partners[rounds - 1]], fwd, inv,
+    keep, *send = rounds_call(pairs, counts, sid, spec, [partners[rounds - 1]], fwd, inv,
                              [rounds - 1], events, chans, slots, groups, prev=corr, final=True)
     return station_sum(keep, send, groups)
 

time: 30 us -> 30.3 us (1.010)
  other arithmetic: 0.62 us -> 1.35 us
  local copies, waits for them, and re-layouts: 4.8 us -> 4.09 us
    squeeze x1 -> x0, local copies, waits for them, and re-layouts: 0.75 us -> none  [station_sum(): send[j - 1]]
    add x1, other arithmetic: 0.62 us -> 1.35 us  [station_sum(): total + lax.ppermute(send[j - 1], 'station', perm).astype(jnp.float32)]
    unnamed x14 -> x12, local copies, waits for them, and re-layouts: 3.18 us -> 3.2 us
  transfers between devices with their start and end apart: 6 -> 6, of which waited for: 3 -> 3; matrix products, arithmetic and copies ran while one was open for 3% -> 3% of each run, Pallas kernels for 27% -> 26%
where the time goes in v10:
time: 30.3 us; the launch traced here: 30 us
  Pallas kernels  11.7 us (39%)
  starting transfers between devices  9.09 us (30%)
  local copies, waits for them, and re-layouts  4.09 us (13%)
  waiting for transfers between devices  3.68 us (12%)
  other arithmetic  1.35 us (4%)
    pallas_call x3, Pallas kernels, rounds_call(): pl.pallas_call(kernel, out_shape=out_shape, in_specs=[smem, smem, smem] +...  11.7 us
    ppermute x3, starting transfers between devices, swapped(): return lax.ppermute(block, axis, route)  7.23 us
    unnamed x12, local copies, waits for them, and re-layouts  3.2 us
    ppermute x3, waiting for transfers between devices, station_sum(): lax.ppermute(send[j - 1], 'station', perm).astype(jnp.float32)  3.03 us
    ppermute x3, starting transfers between devices, station_sum(): lax.ppermute(send[j - 1], 'station', perm).astype(jnp.float32)  1.86 us
    add x1, other arithmetic, station_sum(): total + lax.ppermute(send[j - 1], 'station', perm).astype(jnp.float32)  1.35 us
    reshape x1, local copies, waits for them, and re-layouts, shards(): pairs = pair_lists.reshape(-1)  0.72 us
    ppermute x3, waiting for transfers between devices, swapped(): return lax.ppermute(block, axis, route)  0.66 us
  transfers between devices with their start and end apart: 6, of which 3 were waited for; matrix products, arithmetic and copies ran while one was open for 3% of the time, Pallas kernels for 26%

profile of v10, /device:TPU:0, one launch (start us, length us, event | category | flops | bytes accessed | tf_op | source)
XLA Modules:
  0.0 30.0 jit_solution(9221445676766801146)
XLA Ops:
  0.0 1.0 %copy.8 = bf16[16,4,3,512]{3,2,1,0:T(4,128)(2,1)S(1)} copy(bf16[16,4,3,512]{3,1,2,0:T(4,128)(2,1)} %param.5) | data formatting | bytes 393216 | tf_op args[0]
  1.1 0.0 copy-start.4
  1.1 0.2 reshape.15.refs_3_
  1.2 0.0 copy-start
  1.2 3.1 %collective-permute-start = (bf16[192,512]{1,0:T(8,128)(2,1)S(1)}, bf16[192,512]{1,0:T(8,128)(2,1)S(1)}, u32[]{:S(2)}, u32[]{:S(2)}) collective-permute-start(bf16[192,512]{1,0:T(8,128)(2,1)S(1)} %reshape.15.refs_3_), channel_id=1, source_target_pairs={{0,4},{4,0},{8,12},{12,8},{16,20},{20,16},{24,28},{28,24},{1,5},{5... | collective-permute-start | bytes 589832 | tf_op jit(solution)/shard_map/ppermute | solution.py:24
  4.3 1.6 %collective-permute-start.2 = (bf16[192,512]{1,0:T(8,128)(2,1)S(1)}, bf16[192,512]{1,0:T(8,128)(2,1)S(1)}, u32[]{:S(2)}, u32[]{:S(2)}) collective-permute-start(bf16[192,512]{1,0:T(8,128)(2,1)S(1)} %reshape.15.refs_3_), channel_id=1, source_target_pairs={{0,8},{8,0},{4,12},{12,4},{16,24},{24,16},{20,28},{28,20},{1,9},{9... | collective-permute-start | bytes 589832 | tf_op jit(solution)/shard_map/ppermute | solution.py:24
  5.9 2.6 %collective-permute-start.1 = (bf16[192,512]{1,0:T(8,128)(2,1)S(1)}, bf16[192,512]{1,0:T(8,128)(2,1)S(1)}, u32[]{:S(2)}, u32[]{:S(2)}) collective-permute-start(bf16[192,512]{1,0:T(8,128)(2,1)S(1)} %reshape.15.refs_3_), channel_id=1, source_target_pairs={{0,16},{16,0},{4,20},{20,4},{8,24},{24,8},{12,28},{28,12},{1,17},{... | collective-permute-start | bytes 589832 | tf_op jit(solution)/shard_map/ppermute | solution.py:24
  8.5 0.0 copy-done.4
  8.5 0.1 copy.7
  8.6 0.7 %reshape.12.refs_0_ = s32[192]{0:T(256)} reshape(s32[3,32,2]{2,1,0:T(8,128)S(1)} %copy.7) | data formatting | bytes 1536 | tf_op jit(solution)/shard_map/reshape | solution.py:195
  9.3 0.0 collective-permute-done.refs_4_
  9.3 0.0 copy-start.1
  9.3 0.0 copy-done
  9.3 0.7 %copy-done.1 = bf16[192,512]{1,0:T(8,128)(2,1)} copy-done((bf16[192,512]{1,0:T(8,128)(2,1)}, bf16[192,512]{1,0:T(8,128)(2,1)S(1)}, u32[]{:S(2)}) %copy-start.1) | copy-done | bytes 196632
  10.0 4.1 %shard_map.55 = (f32[1,32,256]{2,1,0:T(8,128)}, bf16[256,1024]{1,0:T(8,128)(2,1)}) custom-call(s32[192]{0:T(256)} %reshape.12.refs_0_, s32[3]{0:T(128)} %bitcast.2, s32[1]{0:T(128)} %bitcast.1.refs_2_, bf16[192,512]{1,0:T(8,128)(2,1)} %copy-done, bf16[192,512]{1,0:T(8,128)(2,1)} %copy-done.1, bf16[512,1024]{1,0:T(8,128)(2,1)} %constant.8.clone.refs_5_, ...), custom_call_target="tpu_custom_call" | custom-call | tf_op jit(solution)/shard_map/pallas_call | solution.py:162
  14.1 0.7 %collective-permute-done.2.refs_4_ = bf16[192,512]{1,0:T(8,128)(2,1)S(1)} collective-permute-done((bf16[192,512]{1,0:T(8,128)(2,1)S(1)}, bf16[192,512]{1,0:T(8,128)(2,1)S(1)}, u32[]{:S(2)}, u32[]{:S(2)}) %collective-permute-start.2) | collective-permute-done | bytes 196640 | tf_op jit(solution)/shard_map/ppermute | solution.py:24
  14.8 0.0 copy-start.3
  14.8 0.7 %copy-done.3 = bf16[192,512]{1,0:T(8,128)(2,1)} copy-done((bf16[192,512]{1,0:T(8,128)(2,1)}, bf16[192,512]{1,0:T(8,128)(2,1)S(1)}, u32[]{:S(2)}) %copy-start.3) | copy-done | bytes 196632
  15.4 3.8 %shard_map.56.refs_7_ = f32[2,32,256]{2,1,0:T(8,128)} custom-call(s32[192]{0:T(256)} %reshape.12.refs_0_, s32[3]{0:T(128)} %bitcast.3, s32[1]{0:T(128)} %bitcast.1.refs_2_, bf16[256,1024]{1,0:T(8,128)(2,1)} %get-tuple-element.11.refs_3_, bf16[192,512]{1,0:T(8,128)(2,1)} %copy-done.3, bf16[512,1024]{1,0:T(8,128)(2,1)} %constant.8.clone.refs_5_, ...), custom_call_target="tpu_custom_call" | custom-call | tf_op jit(solution)/shard_map/pallas_call | solution.py:162
  19.3 0.0 collective-permute-done.1.refs_4_
  19.3 0.0 copy-start.2
  19.3 0.7 %copy-done.2 = bf16[192,512]{1,0:T(8,128)(2,1)} copy-done((bf16[192,512]{1,0:T(8,128)(2,1)}, bf16[192,512]{1,0:T(8,128)(2,1)S(1)}, u32[]{:S(2)}) %copy-start.2) | copy-done | bytes 196632
  19.9 3.8 %shard_map.57 = (f32[3,8,256]{2,1,0:T(8,128)}, bf16[3,8,256]{2,1,0:T(8,128)(2,1)}, bf16[3,8,256]{2,1,0:T(8,128)(2,1)}, bf16[3,8,256]{2,1,0:T(8,128)(2,1)}) custom-call(s32[192]{0:T(256)} %reshape.12.refs_0_, s32[3]{0:T(128)} %bitcast.4, s32[1]{0:T(128)} %bitcast.1.refs_2_, bf16[256,1024]{1,0:T(8,128)(2,1)} %get-tuple-element.11.refs_3_, ...), custom_call_target="tpu_custom_call" | custom-call | tf_op jit(solution)/shard_map/pallas_call | solution.py:162
  23.7 0.0 collective-permute-start.3
  23.7 1.6 %collective-permute-start.4 = (bf16[3,8,256]{2,1,0:T(8,128)(2,1)}, bf16[3,8,256]{2,1,0:T(8,128)(2,1)S(1)}, u32[]{:S(2)}, u32[]{:S(2)}) collective-permute-start(bf16[3,8,256]{2,1,0:T(8,128)(2,1)} %get-tuple-element.15), channel_id=1, source_target_pairs={{0,2},{1,3},{2,0},{3,1},{4,6},{5,7},{6,4},{7,5},{8,10},{9,11},{10,... | collective-permute-start | bytes 36872 | tf_op jit(solution)/shard_map/ppermute | solution.py:181
  25.3 0.3 %collective-permute-start.5 = (bf16[3,8,256]{2,1,0:T(8,128)(2,1)}, bf16[3,8,256]{2,1,0:T(8,128)(2,1)S(1)}, u32[]{:S(2)}, u32[]{:S(2)}) collective-permute-start(bf16[3,8,256]{2,1,0:T(8,128)(2,1)} %get-tuple-element.16), channel_id=1, source_target_pairs={{0,3},{1,2},{2,1},{3,0},{4,7},{5,6},{6,5},{7,4},{8,11},{9,10},{10,... | collective-permute-start | bytes 36872 | tf_op jit(solution)/shard_map/ppermute | solution.py:181
  25.6 0.0 collective-permute-done.3
  25.6 2.1 %collective-permute-done.4 = bf16[3,8,256]{2,1,0:T(8,128)(2,1)S(1)} collective-permute-done((bf16[3,8,256]{2,1,0:T(8,128)(2,1)}, bf16[3,8,256]{2,1,0:T(8,128)(2,1)S(1)}, u32[]{:S(2)}, u32[]{:S(2)}) %collective-permute-start.4) | collective-permute-done | bytes 12320 | tf_op jit(solution)/shard_map/ppermute | solution.py:181
  27.7 0.9 %collective-permute-done.5 = bf16[3,8,256]{2,1,0:T(8,128)(2,1)S(1)} collective-permute-done((bf16[3,8,256]{2,1,0:T(8,128)(2,1)}, bf16[3,8,256]{2,1,0:T(8,128)(2,1)S(1)}, u32[]{:S(2)}, u32[]{:S(2)}) %collective-permute-start.5) | collective-permute-done | bytes 12320 | tf_op jit(solution)/shard_map/ppermute | solution.py:181
  28.6 1.4 %convert_add_fusion = f32[3,8,256]{2,1,0:T(8,128)} fusion(bf16[3,8,256]{2,1,0:T(8,128)(2,1)S(1)} %collective-permute-done.5, bf16[3,8,256]{2,1,0:T(8,128)(2,1)S(1)} %collective-permute-done.4, f32[3,8,256]{2,1,0:T(8,128)} %get-tuple-element.13, bf16[3,8,256]{2,1,0:T(8,128)(2,1)S(1)} %collective-permute-done.3), kind=kLoop, calls=%fused_computation | loop fusion | flops 36864 | bytes 86016 | tf_op jit(solution)/shard_map/add | solution.py:181
Async XLA Ops:
  1.1 7.4 %copy-start.4 = (s32[3,32,2]{1,2,0:T(2,128)S(1)}, s32[3,32,2]{1,2,0:T(2,128)}, u32[]{:S(2)}) copy-start(s32[3,32,2]{1,2,0:T(2,128)} %param.6) | copy-start | bytes 2308
  1.2 8.1 %copy-start = (bf16[192,512]{1,0:T(8,128)(2,1)}, bf16[192,512]{1,0:T(8,128)(2,1)S(1)}, u32[]{:S(2)}) copy-start(bf16[192,512]{1,0:T(8,128)(2,1)S(1)} %reshape.15.refs_3_) | copy-start | bytes 589828
  1.2 8.1 %collective-permute-start = (bf16[192,512]{1,0:T(8,128)(2,1)S(1)}, bf16[192,512]{1,0:T(8,128)(2,1)S(1)}, u32[]{:S(2)}, u32[]{:S(2)}) collective-permute-start(bf16[192,512]{1,0:T(8,128)(2,1)S(1)} %reshape.15.refs_3_), channel_id=1, source_target_pairs={{0,4},{4,0},{8,12},{12,8},{16,20},{20,16},{24,28},{28,24},{1,5},{5... | collective-permute-start | bytes 589832 | tf_op jit(solution)/shard_map/ppermute | solution.py:24
  4.3 10.5 %collective-permute-start.2 = (bf16[192,512]{1,0:T(8,128)(2,1)S(1)}, bf16[192,512]{1,0:T(8,128)(2,1)S(1)}, u32[]{:S(2)}, u32[]{:S(2)}) collective-permute-start(bf16[192,512]{1,0:T(8,128)(2,1)S(1)} %reshape.15.refs_3_), channel_id=1, source_target_pairs={{0,8},{8,0},{4,12},{12,4},{16,24},{24,16},{20,28},{28,20},{1,9},{9... | collective-permute-start | bytes 589832 | tf_op jit(solution)/shard_map/ppermute | solution.py:24
  5.9 13.4 %collective-permute-start.1 = (bf16[192,512]{1,0:T(8,128)(2,1)S(1)}, bf16[192,512]{1,0:T(8,128)(2,1)S(1)}, u32[]{:S(2)}, u32[]{:S(2)}) collective-permute-start(bf16[192,512]{1,0:T(8,128)(2,1)S(1)} %reshape.15.refs_3_), channel_id=1, source_target_pairs={{0,16},{16,0},{4,20},{20,4},{8,24},{24,8},{12,28},{28,12},{1,17},{... | collective-permute-start | bytes 589832 | tf_op jit(solution)/shard_map/ppermute | solution.py:24
  9.3 0.7 %copy-start.1 = (bf16[192,512]{1,0:T(8,128)(2,1)}, bf16[192,512]{1,0:T(8,128)(2,1)S(1)}, u32[]{:S(2)}) copy-start(bf16[192,512]{1,0:T(8,128)(2,1)S(1)} %collective-permute-done.refs_4_) | copy-start | bytes 589828
  14.8 0.7 %copy-start.3 = (bf16[192,512]{1,0:T(8,128)(2,1)}, bf16[192,512]{1,0:T(8,128)(2,1)S(1)}, u32[]{:S(2)}) copy-start(bf16[192,512]{1,0:T(8,128)(2,1)S(1)} %collective-permute-done.2.refs_4_) | copy-start | bytes 589828
  19.3 0.7 %copy-start.2 = (bf16[192,512]{1,0:T(8,128)(2,1)}, bf16[192,512]{1,0:T(8,128)(2,1)S(1)}, u32[]{:S(2)}) copy-start(bf16[192,512]{1,0:T(8,128)(2,1)S(1)} %collective-permute-done.1.refs_4_) | copy-start | bytes 589828
  23.7 1.9 %collective-permute-start.3 = (bf16[3,8,256]{2,1,0:T(8,128)(2,1)}, bf16[3,8,256]{2,1,0:T(8,128)(2,1)S(1)}, u32[]{:S(2)}, u32[]{:S(2)}) collective-permute-start(bf16[3,8,256]{2,1,0:T(8,128)(2,1)} %get-tuple-element.14), channel_id=1, source_target_pairs={{0,1},{1,0},{2,3},{3,2},{4,5},{5,4},{6,7},{7,6},{8,9},{9,8},{10,11... | collective-permute-start | bytes 36872 | tf_op jit(solution)/shard_map/ppermute | solution.py:181
  23.7 4.0 %collective-permute-start.4 = (bf16[3,8,256]{2,1,0:T(8,128)(2,1)}, bf16[3,8,256]{2,1,0:T(8,128)(2,1)S(1)}, u32[]{:S(2)}, u32[]{:S(2)}) collective-permute-start(bf16[3,8,256]{2,1,0:T(8,128)(2,1)} %get-tuple-element.15), channel_id=1, source_target_pairs={{0,2},{1,3},{2,0},{3,1},{4,6},{5,7},{6,4},{7,5},{8,10},{9,11},{10,... | collective-permute-start | bytes 36872 | tf_op jit(solution)/shard_map/ppermute | solution.py:181
  25.3 3.3 %collective-permute-start.5 = (bf16[3,8,256]{2,1,0:T(8,128)(2,1)}, bf16[3,8,256]{2,1,0:T(8,128)(2,1)S(1)}, u32[]{:S(2)}, u32[]{:S(2)}) collective-permute-start(bf16[3,8,256]{2,1,0:T(8,128)(2,1)} %get-tuple-element.16), channel_id=1, source_target_pairs={{0,3},{1,2},{2,1},{3,0},{4,7},{5,6},{6,5},{7,4},{8,11},{9,10},{10,... | collective-permute-start | bytes 36872 | tf_op jit(solution)/shard_map/ppermute | solution.py:181

commit v11 on v9

--- a/solution.py
+++ b/solution.py
@@ -68,7 +68,17 @@
         else:
             prev_ref, out_ref = rest[:2]
             rest = rest[2:]
-        nscr, xpad, specl, specp, cross = rest
+        nscr, xpad, specl, specp, cross, fbuf, gbuf, sems = rest
+        f_copy = pltpu.make_async_copy(f_ref, fbuf, sems.at[0])
+        g_copy = pltpu.make_async_copy(g_ref, gbuf, sems.at[1])
+        f_copy.start()
+        g_copy.start()
+        pending = {"f": f_copy, "g": g_copy}
+
+        def table(name, buf):
+            if name in pending:
+                pending.pop(name).wait()
+            return buf[...]
 
         def spectra(w_ref, spec_ref):
             x = w_ref[...].astype(jnp.float32)
@@ -78,7 +88,7 @@
             for e in range(events):
                 xpad[e * pad:e * pad + chans, :] = nscr[e * chans:(e + 1) * chans, :]
             xb = xpad[...].astype(jnp.bfloat16)
-            spec = jnp.dot(xb, f_ref[...], preferred_element_type=jnp.float32)
+            spec = jnp.dot(xb, table("f", fbuf), preferred_element_type=jnp.float32)
             spec_ref[...] = spec.astype(jnp.bfloat16).astype(jnp.float32)
 
         xpad[...] = jnp.zeros(xpad.shape, jnp.float32)
@@ -121,7 +131,7 @@
                 cross[r:r + 1, half + 128:] = im[:, 128:]
 
             cb = cross[...].astype(jnp.bfloat16)
-            corr = jnp.dot(cb, g_ref[...], preferred_element_type=jnp.float32)
+            corr = jnp.dot(cb, table("g", gbuf), preferred_element_type=jnp.float32)
             rows = lax.broadcasted_iota(jnp.int32, corr.shape, 0)
             slot_of = (sid ^ (rows // share)) * share + rows % share
             corr = jnp.where(slot_of < cnt_ref[q], corr, 0.0)
@@ -146,6 +156,7 @@
     kernel = make_kernel(events, chans, pad, length, slots, groups, share, rounds, n_prev, from_waves, final)
     smem = pl.BlockSpec(memory_space=pltpu.SMEM)
     vmem = pl.BlockSpec(memory_space=pltpu.VMEM)
+    anyspace = pl.BlockSpec(memory_space=pl.ANY)
     if from_waves:
         out_shape = (jax.ShapeDtypeStruct((len(rounds), slots, lags), jnp.float32),
                      jax.ShapeDtypeStruct((events * pad, 2 * length), jnp.bfloat16))
@@ -160,7 +171,7 @@
     return pl.pallas_call(
         kernel,
         out_shape=out_shape,
-        in_specs=[smem, smem, smem] + [vmem] * (3 + len(partners) + len(extra)),
+        in_specs=[smem, smem, smem] + [vmem] * (1 + len(partners)) + [anyspace] * 2 + [vmem] * len(extra),
         out_specs=tuple(vmem for _ in out_shape),
         scratch_shapes=[
             pltpu.VMEM((events * chans, length), jnp.float32),
@@ -168,6 +179,9 @@
             pltpu.VMEM((events * pad, 2 * length), jnp.float32),
             pltpu.VMEM((events * pad, 2 * length), jnp.float32),
             pltpu.VMEM((slots, 2 * length), jnp.float32),
+            pltpu.VMEM(fwd.shape, fwd.dtype),
+            pltpu.VMEM(inv.shape, inv.dtype),
+            pltpu.SemaphoreType.DMA((2,)),
         ],
     )(pairs, counts, sid, own, *partners, fwd, inv, *extra)
 

time: 30 us -> 31.2 us (1.040)
  Pallas kernels: 11.7 us -> 13.3 us
  waiting for transfers between devices: 3.44 us -> 2.93 us
    pallas_call x3, Pallas kernels: 11.7 us -> 13.3 us  [rounds_call(): pl.pallas_call(kernel, out_shape=out_shape, in_specs=[smem, smem, smem] +...]
    ppermute x3, waiting for transfers between devices: 0.69 us -> 0.18 us  [swapped(): return lax.ppermute(block, axis, route)]
  transfers between devices with their start and end apart: 6 -> 6, of which waited for: 3 -> 3; matrix products, arithmetic and copies ran while one was open for 3% -> 3% of each run, Pallas kernels for 27% -> 29%
where the time goes in v11:
time: 31.2 us; the launch traced here: 30.8 us
  Pallas kernels  13.3 us (43%)
  starting transfers between devices  9.09 us (29%)
  local copies, waits for them, and re-layouts  4.8 us (15%)
  waiting for transfers between devices  2.93 us (9%)
  other arithmetic  0.62 us (2%)
    pallas_call x3, Pallas kernels, rounds_call(): pl.pallas_call(kernel, out_shape=out_shape, in_specs=[smem, smem, smem] +...  13.3 us
    ppermute x3, starting transfers between devices, swapped(): return lax.ppermute(block, axis, route)  7.23 us
    unnamed x14, local copies, waits for them, and re-layouts  3.17 us
    ppermute x3, waiting for transfers between devices, station_sum(): lax.ppermute(send[j - 1], 'station', perm).astype(jnp.float32)  2.75 us
    ppermute x3, starting transfers between devices, station_sum(): lax.ppermute(send[j - 1], 'station', perm).astype(jnp.float32)  1.86 us
    squeeze x1, local copies, waits for them, and re-layouts, station_sum(): send[j - 1]  0.75 us
    reshape x1, local copies, waits for them, and re-layouts, shards(): pairs = pair_lists.reshape(-1)  0.71 us
  transfers between devices with their start and end apart: 6, of which 3 were waited for; matrix products, arithmetic and copies ran while one was open for 3% of the time, Pallas kernels for 29%

profile of v11, /device:TPU:0, one launch (start us, length us, event | category | flops | bytes accessed | tf_op | source)
XLA Modules:
  0.0 30.8 jit_solution(3069579552798259983)
XLA Ops:
  0.0 1.0 %copy.8 = bf16[16,4,3,512]{3,2,1,0:T(4,128)(2,1)S(1)} copy(bf16[16,4,3,512]{3,1,2,0:T(4,128)(2,1)} %param.5) | data formatting | bytes 393216 | tf_op args[0]
  1.1 0.0 copy-start.5
  1.1 0.2 reshape.15.refs_3_
  1.2 0.0 copy-start
  1.2 3.1 %collective-permute-start = (bf16[192,512]{1,0:T(8,128)(2,1)S(1)}, bf16[192,512]{1,0:T(8,128)(2,1)S(1)}, u32[]{:S(2)}, u32[]{:S(2)}) collective-permute-start(bf16[192,512]{1,0:T(8,128)(2,1)S(1)} %reshape.15.refs_3_), channel_id=1, source_target_pairs={{0,4},{4,0},{8,12},{12,8},{16,20},{20,16},{24,28},{28,24},{1,5},{5... | collective-permute-start | bytes 589832 | tf_op jit(solution)/shard_map/ppermute | solution.py:24
  4.3 1.6 %collective-permute-start.2 = (bf16[192,512]{1,0:T(8,128)(2,1)S(1)}, bf16[192,512]{1,0:T(8,128)(2,1)S(1)}, u32[]{:S(2)}, u32[]{:S(2)}) collective-permute-start(bf16[192,512]{1,0:T(8,128)(2,1)S(1)} %reshape.15.refs_3_), channel_id=1, source_target_pairs={{0,8},{8,0},{4,12},{12,4},{16,24},{24,16},{20,28},{28,20},{1,9},{9... | collective-permute-start | bytes 589832 | tf_op jit(solution)/shard_map/ppermute | solution.py:24
  5.9 2.6 %collective-permute-start.1 = (bf16[192,512]{1,0:T(8,128)(2,1)S(1)}, bf16[192,512]{1,0:T(8,128)(2,1)S(1)}, u32[]{:S(2)}, u32[]{:S(2)}) collective-permute-start(bf16[192,512]{1,0:T(8,128)(2,1)S(1)} %reshape.15.refs_3_), channel_id=1, source_target_pairs={{0,16},{16,0},{4,20},{20,4},{8,24},{24,8},{12,28},{28,12},{1,17},{... | collective-permute-start | bytes 589832 | tf_op jit(solution)/shard_map/ppermute | solution.py:24
  8.5 0.0 copy-done.5
  8.5 0.1 copy.7
  8.6 0.7 %reshape.12.refs_0_ = s32[192]{0:T(256)} reshape(s32[3,32,2]{2,1,0:T(8,128)S(1)} %copy.7) | data formatting | bytes 1536 | tf_op jit(solution)/shard_map/reshape | solution.py:207
  9.3 0.0 collective-permute-done.refs_4_
  9.3 0.0 copy-start.1
  9.3 0.0 copy-done
  9.3 0.7 %copy-done.1 = bf16[192,512]{1,0:T(8,128)(2,1)} copy-done((bf16[192,512]{1,0:T(8,128)(2,1)}, bf16[192,512]{1,0:T(8,128)(2,1)S(1)}, u32[]{:S(2)}) %copy-start.1) | copy-done | bytes 196632
  10.0 4.6 %shard_map.55 = (f32[1,32,256]{2,1,0:T(8,128)}, bf16[256,1024]{1,0:T(8,128)(2,1)}) custom-call(s32[192]{0:T(256)} %reshape.12.refs_0_, s32[3]{0:T(128)} %bitcast.8, s32[1]{0:T(128)} %bitcast.1.refs_2_, bf16[192,512]{1,0:T(8,128)(2,1)} %copy-done, bf16[192,512]{1,0:T(8,128)(2,1)} %copy-done.1, bf16[512,1024]{1,0:T(8,128)(2,1)} %constant.8.clone.refs_5_, ...), custom_call_target="tpu_custom_call" | custom-call | tf_op jit(solution)/shard_map/pallas_call | solution.py:171
  14.6 0.2 collective-permute-done.2.refs_4_
  14.8 0.0 copy-start.3
  14.8 0.7 %copy-done.3 = bf16[192,512]{1,0:T(8,128)(2,1)} copy-done((bf16[192,512]{1,0:T(8,128)(2,1)}, bf16[192,512]{1,0:T(8,128)(2,1)S(1)}, u32[]{:S(2)}) %copy-start.3) | copy-done | bytes 196632
  15.4 4.4 %shard_map.56.refs_7_ = f32[2,32,256]{2,1,0:T(8,128)} custom-call(s32[192]{0:T(256)} %reshape.12.refs_0_, s32[3]{0:T(128)} %bitcast.9, s32[1]{0:T(128)} %bitcast.1.refs_2_, bf16[256,1024]{1,0:T(8,128)(2,1)} %get-tuple-element.9.refs_3_, bf16[192,512]{1,0:T(8,128)(2,1)} %copy-done.3, bf16[512,1024]{1,0:T(8,128)(2,1)} %constant.8.clone.refs_5_, ...), custom_call_target="tpu_custom_call" | custom-call | tf_op jit(solution)/shard_map/pallas_call | solution.py:171
  19.8 0.0 collective-permute-done.1.refs_4_
  19.8 0.0 copy-start.2
  19.8 0.7 %copy-done.2 = bf16[192,512]{1,0:T(8,128)(2,1)} copy-done((bf16[192,512]{1,0:T(8,128)(2,1)}, bf16[192,512]{1,0:T(8,128)(2,1)S(1)}, u32[]{:S(2)}) %copy-start.2) | copy-done | bytes 196632
  20.5 4.3 %shard_map.57 = (f32[3,8,256]{2,1,0:T(8,128)}, bf16[3,3,8,256]{3,2,1,0:T(8,128)(2,1)}) custom-call(s32[192]{0:T(256)} %reshape.12.refs_0_, s32[3]{0:T(128)} %bitcast.10, s32[1]{0:T(128)} %bitcast.1.refs_2_, bf16[256,1024]{1,0:T(8,128)(2,1)} %get-tuple-element.9.refs_3_, bf16[192,512]{1,0:T(8,128)(2,1)} %copy-done.2, ...), custom_call_target="tpu_custom_call" | custom-call | tf_op jit(solution)/shard_map/pallas_call | solution.py:171
  24.9 0.0 copy-start.4
  24.9 0.7 %slice_bitcast_fusion.2 = (bf16[3,8,256]{2,1,0:T(8,128)(2,1)S(1)}, bf16[3,8,256]{2,1,0:T(8,128)(2,1)S(1)}, bf16[3,8,256]{2,1,0:T(8,128)(2,1)S(1)}) fusion(bf16[3,3,8,256]{3,2,1,0:T(8,128)(2,1)} %get-tuple-element.12), kind=kLoop, calls=%fused_computation.3 | loop fusion | bytes 73728 | tf_op jit(solution)/shard_map/squeeze | solution.py:193
  25.6 0.0 collective-permute-start.3
  25.6 1.5 %collective-permute-start.4 = (bf16[3,8,256]{2,1,0:T(8,128)(2,1)S(1)}, bf16[3,8,256]{2,1,0:T(8,128)(2,1)S(1)}, u32[]{:S(2)}, u32[]{:S(2)}) collective-permute-start(bf16[3,8,256]{2,1,0:T(8,128)(2,1)S(1)} %get-tuple-element.15), channel_id=1, source_target_pairs={{0,2},{1,3},{2,0},{3,1},{4,6},{5,7},{6,4},{7,5},{8,10},{9,11},{10,... | collective-permute-start | bytes 36872 | tf_op jit(solution)/shard_map/ppermute | solution.py:193
  27.1 0.4 %collective-permute-start.5 = (bf16[3,8,256]{2,1,0:T(8,128)(2,1)S(1)}, bf16[3,8,256]{2,1,0:T(8,128)(2,1)S(1)}, u32[]{:S(2)}, u32[]{:S(2)}) collective-permute-start(bf16[3,8,256]{2,1,0:T(8,128)(2,1)S(1)} %get-tuple-element.14), channel_id=1, source_target_pairs={{0,3},{1,2},{2,1},{3,0},{4,7},{5,6},{6,5},{7,4},{8,11},{9,10},{10,... | collective-permute-start | bytes 36872 | tf_op jit(solution)/shard_map/ppermute | solution.py:193
  27.5 0.0 collective-permute-done.3
  27.5 1.8 %collective-permute-done.4 = bf16[3,8,256]{2,1,0:T(8,128)(2,1)S(1)} collective-permute-done((bf16[3,8,256]{2,1,0:T(8,128)(2,1)S(1)}, bf16[3,8,256]{2,1,0:T(8,128)(2,1)S(1)}, u32[]{:S(2)}, u32[]{:S(2)}) %collective-permute-start.4) | collective-permute-done | bytes 12320 | tf_op jit(solution)/shard_map/ppermute | solution.py:193
  29.3 0.9 %collective-permute-done.5 = bf16[3,8,256]{2,1,0:T(8,128)(2,1)S(1)} collective-permute-done((bf16[3,8,256]{2,1,0:T(8,128)(2,1)S(1)}, bf16[3,8,256]{2,1,0:T(8,128)(2,1)S(1)}, u32[]{:S(2)}, u32[]{:S(2)}) %collective-permute-start.5) | collective-permute-done | bytes 12320 | tf_op jit(solution)/shard_map/ppermute | solution.py:193
  30.2 0.0 copy-done.4
  30.2 0.6 %convert_add_fusion = f32[3,8,256]{2,1,0:T(8,128)} fusion(bf16[3,8,256]{2,1,0:T(8,128)(2,1)S(1)} %collective-permute-done.5, bf16[3,8,256]{2,1,0:T(8,128)(2,1)S(1)} %collective-permute-done.4, f32[3,8,256]{2,1,0:T(8,128)S(1)} %copy-done.4, bf16[3,8,256]{2,1,0:T(8,128)(2,1)S(1)} %collective-permute-done.3), kind=kLoop, calls=%fused_computation | loop fusion | flops 36864 | bytes 86016 | tf_op jit(solution)/shard_map/add | solution.py:193
Async XLA Ops:
  1.1 7.4 %copy-start.5 = (s32[3,32,2]{1,2,0:T(2,128)S(1)}, s32[3,32,2]{1,2,0:T(2,128)}, u32[]{:S(2)}) copy-start(s32[3,32,2]{1,2,0:T(2,128)} %param.6) | copy-start | bytes 2308
  1.2 8.1 %copy-start = (bf16[192,512]{1,0:T(8,128)(2,1)}, bf16[192,512]{1,0:T(8,128)(2,1)S(1)}, u32[]{:S(2)}) copy-start(bf16[192,512]{1,0:T(8,128)(2,1)S(1)} %reshape.15.refs_3_) | copy-start | bytes 589828
  1.2 8.0 %collective-permute-start = (bf16[192,512]{1,0:T(8,128)(2,1)S(1)}, bf16[192,512]{1,0:T(8,128)(2,1)S(1)}, u32[]{:S(2)}, u32[]{:S(2)}) collective-permute-start(bf16[192,512]{1,0:T(8,128)(2,1)S(1)} %reshape.15.refs_3_), channel_id=1, source_target_pairs={{0,4},{4,0},{8,12},{12,8},{16,20},{20,16},{24,28},{28,24},{1,5},{5... | collective-permute-start | bytes 589832 | tf_op jit(solution)/shard_map/ppermute | solution.py:24
  4.3 10.5 %collective-permute-start.2 = (bf16[192,512]{1,0:T(8,128)(2,1)S(1)}, bf16[192,512]{1,0:T(8,128)(2,1)S(1)}, u32[]{:S(2)}, u32[]{:S(2)}) collective-permute-start(bf16[192,512]{1,0:T(8,128)(2,1)S(1)} %reshape.15.refs_3_), channel_id=1, source_target_pairs={{0,8},{8,0},{4,12},{12,4},{16,24},{24,16},{20,28},{28,20},{1,9},{9... | collective-permute-start | bytes 589832 | tf_op jit(solution)/shard_map/ppermute | solution.py:24
  5.9 13.9 %collective-permute-start.1 = (bf16[192,512]{1,0:T(8,128)(2,1)S(1)}, bf16[192,512]{1,0:T(8,128)(2,1)S(1)}, u32[]{:S(2)}, u32[]{:S(2)}) collective-permute-start(bf16[192,512]{1,0:T(8,128)(2,1)S(1)} %reshape.15.refs_3_), channel_id=1, source_target_pairs={{0,16},{16,0},{4,20},{20,4},{8,24},{24,8},{12,28},{28,12},{1,17},{... | collective-permute-start | bytes 589832 | tf_op jit(solution)/shard_map/ppermute | solution.py:24
  9.3 0.7 %copy-start.1 = (bf16[192,512]{1,0:T(8,128)(2,1)}, bf16[192,512]{1,0:T(8,128)(2,1)S(1)}, u32[]{:S(2)}) copy-start(bf16[192,512]{1,0:T(8,128)(2,1)S(1)} %collective-permute-done.refs_4_) | copy-start | bytes 589828
  14.8 0.7 %copy-start.3 = (bf16[192,512]{1,0:T(8,128)(2,1)}, bf16[192,512]{1,0:T(8,128)(2,1)S(1)}, u32[]{:S(2)}) copy-start(bf16[192,512]{1,0:T(8,128)(2,1)S(1)} %collective-permute-done.2.refs_4_) | copy-start | bytes 589828
  19.8 0.7 %copy-start.2 = (bf16[192,512]{1,0:T(8,128)(2,1)}, bf16[192,512]{1,0:T(8,128)(2,1)S(1)}, u32[]{:S(2)}) copy-start(bf16[192,512]{1,0:T(8,128)(2,1)S(1)} %collective-permute-done.1.refs_4_) | copy-start | bytes 589828
  24.9 5.4 %copy-start.4 = (f32[3,8,256]{2,1,0:T(8,128)S(1)}, f32[3,8,256]{2,1,0:T(8,128)}, u32[]{:S(2)}) copy-start(f32[3,8,256]{2,1,0:T(8,128)} %get-tuple-element.11) | copy-start | bytes 73732
  25.6 1.9 %collective-permute-start.3 = (bf16[3,8,256]{2,1,0:T(8,128)(2,1)S(1)}, bf16[3,8,256]{2,1,0:T(8,128)(2,1)S(1)}, u32[]{:S(2)}, u32[]{:S(2)}) collective-permute-start(bf16[3,8,256]{2,1,0:T(8,128)(2,1)S(1)} %get-tuple-element.13), channel_id=1, source_target_pairs={{0,1},{1,0},{2,3},{3,2},{4,5},{5,4},{6,7},{7,6},{8,9},{9,8},{10,11... | collective-permute-start | bytes 36872 | tf_op jit(solution)/shard_map/ppermute | solution.py:193
  25.6 3.7 %collective-permute-start.4 = (bf16[3,8,256]{2,1,0:T(8,128)(2,1)S(1)}, bf16[3,8,256]{2,1,0:T(8,128)(2,1)S(1)}, u32[]{:S(2)}, u32[]{:S(2)}) collective-permute-start(bf16[3,8,256]{2,1,0:T(8,128)(2,1)S(1)} %get-tuple-element.15), channel_id=1, source_target_pairs={{0,2},{1,3},{2,0},{3,1},{4,6},{5,7},{6,4},{7,5},{8,10},{9,11},{10,... | collective-permute-start | bytes 36872 | tf_op jit(solution)/shard_map/ppermute | solution.py:193
  27.1 3.1 %collective-permute-start.5 = (bf16[3,8,256]{2,1,0:T(8,128)(2,1)S(1)}, bf16[3,8,256]{2,1,0:T(8,128)(2,1)S(1)}, u32[]{:S(2)}, u32[]{:S(2)}) collective-permute-start(bf16[3,8,256]{2,1,0:T(8,128)(2,1)S(1)} %get-tuple-element.14), channel_id=1, source_target_pairs={{0,3},{1,2},{2,1},{3,0},{4,7},{5,6},{6,5},{7,4},{8,11},{9,10},{10,... | collective-permute-start | bytes 36872 | tf_op jit(solution)/shard_map/ppermute | solution.py:193

commit v12 on v9

--- a/solution.py
+++ b/solution.py
@@ -53,22 +53,22 @@
 def make_kernel(events, chans, pad, length, slots, groups, share, rounds, n_prev, from_waves, final):
     half = length
     n_part = len(rounds)
+    total_rounds = n_prev + n_part
 
     def kernel(*refs):
         pl_ref, cnt_ref, sid_ref, own_ref = refs[:4]
         part_refs = refs[4:4 + n_part]
-        f_ref, g_ref = refs[4 + n_part:6 + n_part]
-        rest = refs[6 + n_part:]
-        if from_waves:
-            out_ref, spec_out = rest[:2]
-            rest = rest[2:]
-        elif final:
-            prev_ref, keep_ref, send_ref = rest[:3]
-            rest = rest[3:]
+        rest = list(refs[4 + n_part:])
+        f_ref = rest.pop(0)
+        g_ref = rest.pop(0) if final else None
+        prev_ref = rest.pop(0) if n_prev else None
+        if final:
+            keep_ref, send_ref = rest.pop(0), rest.pop(0)
         else:
-            prev_ref, out_ref = rest[:2]
-            rest = rest[2:]
-        nscr, xpad, specl, specp, cross = rest
+            xout = rest.pop(0)
+            spec_out = rest.pop(0) if from_waves else None
+        nscr, xpad, specl, specp, cross = rest[:5]
+        allx = rest[5] if final else None
 
         def spectra(w_ref, spec_ref):
             x = w_ref[...].astype(jnp.float32)
@@ -88,13 +88,10 @@
         else:
             specl[...] = own_ref[...].astype(jnp.float32)
             for n in range(n_prev):
-                prev = prev_ref[n]
                 if final:
-                    keep_ref[n] = prev[:share]
-                    for j in range(1, groups):
-                        send_ref[j - 1, n] = prev[j * share:(j + 1) * share].astype(jnp.bfloat16)
+                    allx[n * slots:(n + 1) * slots, :] = prev_ref[n]
                 else:
-                    out_ref[n] = prev
+                    xout[n] = prev_ref[n]
 
         sid = sid_ref[0]
         lane = lax.broadcasted_iota(jnp.int32, (1, 128), 1)
@@ -119,18 +116,27 @@
                 cross[r:r + 1, 128:half] = re[:, 128:]
                 cross[r:r + 1, half:half + 128] = jnp.where(lane == 0, q0, im[:, :128])
                 cross[r:r + 1, half + 128:] = im[:, 128:]
-
             cb = cross[...].astype(jnp.bfloat16)
-            corr = jnp.dot(cb, g_ref[...], preferred_element_type=jnp.float32)
+            if final:
+                allx[(n_prev + n) * slots:(n_prev + n + 1) * slots, :] = cb
+            else:
+                xout[n_prev + n] = cb
+
+        if final:
+            corr = jnp.dot(allx[...], g_ref[...], preferred_element_type=jnp.float32)
             rows = lax.broadcasted_iota(jnp.int32, corr.shape, 0)
-            slot_of = (sid ^ (rows // share)) * share + rows % share
-            corr = jnp.where(slot_of < cnt_ref[q], corr, 0.0)
-            if not final:
-                out_ref[n_prev + n] = corr
-            else:
-                keep_ref[n_prev + n] = corr[:share]
+            rnd = rows // slots
+            rr_ = rows % slots
+            slot_of = (sid ^ (rr_ // share)) * share + rr_ % share
+            limit = jnp.zeros(corr.shape, jnp.int32)
+            for q in range(total_rounds):
+                limit = jnp.where(rnd == q, cnt_ref[q], limit)
+            corr = jnp.where(slot_of < limit, corr, 0.0)
+            for q in range(total_rounds):
+                keep_ref[q] = corr[q * slots:q * slots + share]
                 for j in range(1, groups):
-                    send_ref[j - 1, n_prev + n] = corr[j * share:(j + 1) * share].astype(jnp.bfloat16)
+                    lo = q * slots + j * share
+                    send_ref[j - 1, q] = corr[lo:lo + share].astype(jnp.bfloat16)
 
     return kernel
 
@@ -141,35 +147,39 @@
     lags = inv.shape[1]
     pad = 16
     share = slots // groups
-    from_waves = prev is None
-    n_prev = 0 if from_waves else prev.shape[0]
+    from_waves = prev is None and own.shape[0] == events * chans
+    n_prev = 0 if prev is None else prev.shape[0]
+    total = n_prev + len(rounds)
     kernel = make_kernel(events, chans, pad, length, slots, groups, share, rounds, n_prev, from_waves, final)
     smem = pl.BlockSpec(memory_space=pltpu.SMEM)
     vmem = pl.BlockSpec(memory_space=pltpu.VMEM)
-    if from_waves:
-        out_shape = (jax.ShapeDtypeStruct((len(rounds), slots, lags), jnp.float32),
-                     jax.ShapeDtypeStruct((events * pad, 2 * length), jnp.bfloat16))
-        extra = []
-    elif not final:
-        out_shape = (jax.ShapeDtypeStruct((n_prev + len(rounds), slots, lags), jnp.float32),)
-        extra = [prev]
+    inputs = [pairs, counts, sid, own, *partners, fwd]
+    if final:
+        inputs.append(inv)
+        out_shape = (jax.ShapeDtypeStruct((total, share, lags), jnp.float32),
+                     jax.ShapeDtypeStruct((groups - 1, total, share, lags), jnp.bfloat16))
     else:
-        out_shape = (jax.ShapeDtypeStruct((n_prev + len(rounds), share, lags), jnp.float32),
-                     jax.ShapeDtypeStruct((groups - 1, n_prev + len(rounds), share, lags), jnp.bfloat16))
-        extra = [prev]
+        out_shape = (jax.ShapeDtypeStruct((total, slots, 2 * length), jnp.bfloat16),)
+        if from_waves:
+            out_shape += (jax.ShapeDtypeStruct((events * pad, 2 * length), jnp.bfloat16),)
+    if prev is not None:
+        inputs.append(prev)
+    scratch = [
+        pltpu.VMEM((events * chans, length), jnp.float32),
+        pltpu.VMEM((events * pad, length), jnp.float32),
+        pltpu.VMEM((events * pad, 2 * length), jnp.float32),
+        pltpu.VMEM((events * pad, 2 * length), jnp.float32),
+        pltpu.VMEM((slots, 2 * length), jnp.float32),
+    ]
+    if final:
+        scratch.append(pltpu.VMEM((total * slots, 2 * length), jnp.bfloat16))
     return pl.pallas_call(
         kernel,
         out_shape=out_shape,
-        in_specs=[smem, smem, smem] + [vmem] * (3 + len(partners) + len(extra)),
+        in_specs=[smem, smem, smem] + [vmem] * (len(inputs) - 3),
         out_specs=tuple(vmem for _ in out_shape),
-        scratch_shapes=[
-            pltpu.VMEM((events * chans, length), jnp.float32),
-            pltpu.VMEM((events * pad, length), jnp.float32),
-            pltpu.VMEM((events * pad, 2 * length), jnp.float32),
-            pltpu.VMEM((events * pad, 2 * length), jnp.float32),
-            pltpu.VMEM((slots, 2 * length), jnp.float32),
-        ],
-    )(pairs, counts, sid, own, *partners, fwd, inv, *extra)
+        scratch_shapes=scratch,
+    )(*inputs)
 
 
 def station_sum(keep, send, groups):
@@ -193,13 +203,13 @@
     pairs = pair_lists.reshape(-1)
     counts = pair_counts.reshape(-1)
     partners = {q: swapped(flat, "region", q) for q in reversed(range(rounds))}
-    corr, spec = rounds_call(pairs, counts, sid, flat, [partners[0]], fwd, inv,
-                             [0], events, chans, slots, groups)
+    crosses, spec = rounds_call(pairs, counts, sid, flat, [partners[0]], fwd, inv,
+                                [0], events, chans, slots, groups)
     for q in range(1, rounds - 1):
-        (corr,) = rounds_call(pairs, counts, sid, spec, [partners[q]], fwd, inv,
-                              [q], events, chans, slots, groups, prev=corr)
+        (crosses,) = rounds_call(pairs, counts, sid, spec, [partners[q]], fwd, inv,
+                                 [q], events, chans, slots, groups, prev=crosses)
     keep, send = rounds_call(pairs, counts, sid, spec, [partners[rounds - 1]], fwd, inv,
-                             [rounds - 1], events, chans, slots, groups, prev=corr, final=True)
+                             [rounds - 1], events, chans, slots, groups, prev=crosses, final=True)
     return station_sum(keep, send, groups)
 
 

time: 30 us -> 29.7 us (0.990)
  Pallas kernels: 11.7 us -> 11.1 us
  waiting for transfers between devices: 3.44 us -> 3.75 us
    pallas_call x3, Pallas kernels: 11.7 us -> 11.1 us  [rounds_call(): pl.pallas_call(kernel, out_shape=out_shape, in_specs=[smem, smem, smem] +...]
    ppermute x3, waiting for transfers between devices: 0.69 us -> 1 us  [swapped(): return lax.ppermute(block, axis, route)]
  transfers between devices with their start and end apart: 6 -> 6, of which waited for: 3 -> 3; matrix products, arithmetic and copies ran while one was open for 3% -> 3% of each run, Pallas kernels for 27% -> 25%
where the time goes in v12:
time: 29.7 us; the launch traced here: 29.4 us
  Pallas kernels  11.1 us (37%)
  starting transfers between devices  9.09 us (31%)
  local copies, waits for them, and re-layouts  4.81 us (16%)
  waiting for transfers between devices  3.75 us (13%)
  other arithmetic  0.62 us (2%)
    pallas_call x3, Pallas kernels, rounds_call(): pl.pallas_call(kernel, out_shape=out_shape, in_specs=[smem, smem, smem] +...  11.1 us
    ppermute x3, starting transfers between devices, swapped(): return lax.ppermute(block, axis, route)  7.23 us
    unnamed x14, local copies, waits for them, and re-layouts  3.18 us
    ppermute x3, waiting for transfers between devices, station_sum(): lax.ppermute(send[j - 1], 'station', perm).astype(jnp.float32)  2.75 us
    ppermute x3, starting transfers between devices, station_sum(): lax.ppermute(send[j - 1], 'station', perm).astype(jnp.float32)  1.86 us
    ppermute x3, waiting for transfers between devices, swapped(): return lax.ppermute(block, axis, route)  1 us
    squeeze x1, local copies, waits for them, and re-layouts, station_sum(): send[j - 1]  0.75 us
    reshape x1, local copies, waits for them, and re-layouts, shards(): pairs = pair_lists.reshape(-1)  0.72 us
  transfers between devices with their start and end apart: 6, of which 3 were waited for; matrix products, arithmetic and copies ran while one was open for 3% of the time, Pallas kernels for 25%

profile of v12, /device:TPU:0, one launch (start us, length us, event | category | flops | bytes accessed | tf_op | source)
XLA Modules:
  0.0 29.4 jit_solution(5211583461689973331)
XLA Ops:
  0.0 1.0 %copy.8 = bf16[16,4,3,512]{3,2,1,0:T(4,128)(2,1)S(1)} copy(bf16[16,4,3,512]{3,1,2,0:T(4,128)(2,1)} %param.5) | data formatting | bytes 393216 | tf_op args[0]
  1.1 0.0 copy-start.5
  1.1 0.2 reshape.15.refs_3_
  1.2 0.0 copy-start
  1.2 3.1 %collective-permute-start = (bf16[192,512]{1,0:T(8,128)(2,1)S(1)}, bf16[192,512]{1,0:T(8,128)(2,1)S(1)}, u32[]{:S(2)}, u32[]{:S(2)}) collective-permute-start(bf16[192,512]{1,0:T(8,128)(2,1)S(1)} %reshape.15.refs_3_), channel_id=1, source_target_pairs={{0,4},{4,0},{8,12},{12,8},{16,20},{20,16},{24,28},{28,24},{1,5},{5... | collective-permute-start | bytes 589832 | tf_op jit(solution)/shard_map/ppermute | solution.py:24
  4.3 1.6 %collective-permute-start.2 = (bf16[192,512]{1,0:T(8,128)(2,1)S(1)}, bf16[192,512]{1,0:T(8,128)(2,1)S(1)}, u32[]{:S(2)}, u32[]{:S(2)}) collective-permute-start(bf16[192,512]{1,0:T(8,128)(2,1)S(1)} %reshape.15.refs_3_), channel_id=1, source_target_pairs={{0,8},{8,0},{4,12},{12,4},{16,24},{24,16},{20,28},{28,20},{1,9},{9... | collective-permute-start | bytes 589832 | tf_op jit(solution)/shard_map/ppermute | solution.py:24
  5.9 2.6 %collective-permute-start.1 = (bf16[192,512]{1,0:T(8,128)(2,1)S(1)}, bf16[192,512]{1,0:T(8,128)(2,1)S(1)}, u32[]{:S(2)}, u32[]{:S(2)}) collective-permute-start(bf16[192,512]{1,0:T(8,128)(2,1)S(1)} %reshape.15.refs_3_), channel_id=1, source_target_pairs={{0,16},{16,0},{4,20},{20,4},{8,24},{24,8},{12,28},{28,12},{1,17},{... | collective-permute-start | bytes 589832 | tf_op jit(solution)/shard_map/ppermute | solution.py:24
  8.5 0.0 copy-done.5
  8.5 0.1 copy.7
  8.6 0.7 %reshape.12.refs_0_ = s32[192]{0:T(256)} reshape(s32[3,32,2]{2,1,0:T(8,128)S(1)} %copy.7) | data formatting | bytes 1536 | tf_op jit(solution)/shard_map/reshape | solution.py:203
  9.3 0.0 collective-permute-done.refs_4_
  9.3 0.0 copy-start.2
  9.3 0.0 copy-done
  9.3 0.7 %copy-done.2 = bf16[192,512]{1,0:T(8,128)(2,1)} copy-done((bf16[192,512]{1,0:T(8,128)(2,1)}, bf16[192,512]{1,0:T(8,128)(2,1)S(1)}, u32[]{:S(2)}) %copy-start.2) | copy-done | bytes 196632
  10.0 3.8 %shard_map.55 = (bf16[1,32,1024]{2,1,0:T(8,128)(2,1)}, bf16[256,1024]{1,0:T(8,128)(2,1)}) custom-call(s32[192]{0:T(256)} %reshape.12.refs_0_, s32[3]{0:T(128)} %bitcast.8, s32[1]{0:T(128)} %bitcast.1.refs_2_, bf16[192,512]{1,0:T(8,128)(2,1)} %copy-done, bf16[192,512]{1,0:T(8,128)(2,1)} %copy-done.2, bf16[512,1024]{1,0:T(8,128)(2,1)} %constant.8.clone.refs_5_), custom_call_target="tpu_custom_call" | custom-call | tf_op jit(solution)/shard_map/pallas_call | solution.py:176
  13.8 1.0 %collective-permute-done.2.refs_4_ = bf16[192,512]{1,0:T(8,128)(2,1)S(1)} collective-permute-done((bf16[192,512]{1,0:T(8,128)(2,1)S(1)}, bf16[192,512]{1,0:T(8,128)(2,1)S(1)}, u32[]{:S(2)}, u32[]{:S(2)}) %collective-permute-start.2) | collective-permute-done | bytes 196640 | tf_op jit(solution)/shard_map/ppermute | solution.py:24
  14.8 0.0 copy-start.1
  14.8 0.7 %copy-done.1 = bf16[192,512]{1,0:T(8,128)(2,1)} copy-done((bf16[192,512]{1,0:T(8,128)(2,1)}, bf16[192,512]{1,0:T(8,128)(2,1)S(1)}, u32[]{:S(2)}) %copy-start.1) | copy-done | bytes 196632
  15.4 3.4 %shard_map.56.refs_7_ = bf16[2,32,1024]{2,1,0:T(8,128)(2,1)} custom-call(s32[192]{0:T(256)} %reshape.12.refs_0_, s32[3]{0:T(128)} %bitcast.9, s32[1]{0:T(128)} %bitcast.1.refs_2_, bf16[256,1024]{1,0:T(8,128)(2,1)} %get-tuple-element.9.refs_3_, bf16[192,512]{1,0:T(8,128)(2,1)} %copy-done.1, bf16[512,1024]{1,0:T(8,128)(2,1)} %constant.8.clone.refs_5_, ...), custom_call_target="tpu_custom_call" | custom-call | tf_op jit(solution)/shard_map/pallas_call | solution.py:176
  18.9 0.0 collective-permute-done.1.refs_4_
  18.9 0.0 copy-start.3
  18.9 0.7 %copy-done.3 = bf16[192,512]{1,0:T(8,128)(2,1)} copy-done((bf16[192,512]{1,0:T(8,128)(2,1)}, bf16[192,512]{1,0:T(8,128)(2,1)S(1)}, u32[]{:S(2)}) %copy-start.3) | copy-done | bytes 196632
  19.5 3.8 %shard_map.57 = (f32[3,8,256]{2,1,0:T(8,128)}, bf16[3,3,8,256]{3,2,1,0:T(8,128)(2,1)}) custom-call(s32[192]{0:T(256)} %reshape.12.refs_0_, s32[3]{0:T(128)} %bitcast.10, s32[1]{0:T(128)} %bitcast.1.refs_2_, bf16[256,1024]{1,0:T(8,128)(2,1)} %get-tuple-element.9.refs_3_, bf16[192,512]{1,0:T(8,128)(2,1)} %copy-done.3, ...), custom_call_target="tpu_custom_call" | custom-call | tf_op jit(solution)/shard_map/pallas_call | solution.py:176
  23.4 0.0 copy-start.4
  23.4 0.7 %slice_bitcast_fusion.2 = (bf16[3,8,256]{2,1,0:T(8,128)(2,1)S(1)}, bf16[3,8,256]{2,1,0:T(8,128)(2,1)S(1)}, bf16[3,8,256]{2,1,0:T(8,128)(2,1)S(1)}) fusion(bf16[3,3,8,256]{3,2,1,0:T(8,128)(2,1)} %get-tuple-element.12), kind=kLoop, calls=%fused_computation.3 | loop fusion | bytes 73728 | tf_op jit(solution)/shard_map/squeeze | solution.py:189
  24.1 0.0 collective-permute-start.3
  24.1 1.5 %collective-permute-start.4 = (bf16[3,8,256]{2,1,0:T(8,128)(2,1)S(1)}, bf16[3,8,256]{2,1,0:T(8,128)(2,1)S(1)}, u32[]{:S(2)}, u32[]{:S(2)}) collective-permute-start(bf16[3,8,256]{2,1,0:T(8,128)(2,1)S(1)} %get-tuple-element.15), channel_id=1, source_target_pairs={{0,2},{1,3},{2,0},{3,1},{4,6},{5,7},{6,4},{7,5},{8,10},{9,11},{10,... | collective-permute-start | bytes 36872 | tf_op jit(solution)/shard_map/ppermute | solution.py:189
  25.6 0.4 %collective-permute-start.5 = (bf16[3,8,256]{2,1,0:T(8,128)(2,1)S(1)}, bf16[3,8,256]{2,1,0:T(8,128)(2,1)S(1)}, u32[]{:S(2)}, u32[]{:S(2)}) collective-permute-start(bf16[3,8,256]{2,1,0:T(8,128)(2,1)S(1)} %get-tuple-element.14), channel_id=1, source_target_pairs={{0,3},{1,2},{2,1},{3,0},{4,7},{5,6},{6,5},{7,4},{8,11},{9,10},{10,... | collective-permute-start | bytes 36872 | tf_op jit(solution)/shard_map/ppermute | solution.py:189
  26.0 0.0 collective-permute-done.3
  26.0 1.8 %collective-permute-done.4 = bf16[3,8,256]{2,1,0:T(8,128)(2,1)S(1)} collective-permute-done((bf16[3,8,256]{2,1,0:T(8,128)(2,1)S(1)}, bf16[3,8,256]{2,1,0:T(8,128)(2,1)S(1)}, u32[]{:S(2)}, u32[]{:S(2)}) %collective-permute-start.4) | collective-permute-done | bytes 12320 | tf_op jit(solution)/shard_map/ppermute | solution.py:189
  27.8 0.9 %collective-permute-done.5 = bf16[3,8,256]{2,1,0:T(8,128)(2,1)S(1)} collective-permute-done((bf16[3,8,256]{2,1,0:T(8,128)(2,1)S(1)}, bf16[3,8,256]{2,1,0:T(8,128)(2,1)S(1)}, u32[]{:S(2)}, u32[]{:S(2)}) %collective-permute-start.5) | collective-permute-done | bytes 12320 | tf_op jit(solution)/shard_map/ppermute | solution.py:189
  28.7 0.0 copy-done.4
  28.7 0.6 %convert_add_fusion = f32[3,8,256]{2,1,0:T(8,128)} fusion(bf16[3,8,256]{2,1,0:T(8,128)(2,1)S(1)} %collective-permute-done.5, bf16[3,8,256]{2,1,0:T(8,128)(2,1)S(1)} %collective-permute-done.4, f32[3,8,256]{2,1,0:T(8,128)S(1)} %copy-done.4, bf16[3,8,256]{2,1,0:T(8,128)(2,1)S(1)} %collective-permute-done.3), kind=kLoop, calls=%fused_computation | loop fusion | flops 36864 | bytes 86016 | tf_op jit(solution)/shard_map/add | solution.py:189
Async XLA Ops:
  1.1 7.4 %copy-start.5 = (s32[3,32,2]{1,2,0:T(2,128)S(1)}, s32[3,32,2]{1,2,0:T(2,128)}, u32[]{:S(2)}) copy-start(s32[3,32,2]{1,2,0:T(2,128)} %param.6) | copy-start | bytes 2308
  1.2 8.1 %copy-start = (bf16[192,512]{1,0:T(8,128)(2,1)}, bf16[192,512]{1,0:T(8,128)(2,1)S(1)}, u32[]{:S(2)}) copy-start(bf16[192,512]{1,0:T(8,128)(2,1)S(1)} %reshape.15.refs_3_) | copy-start | bytes 589828
  1.2 8.0 %collective-permute-start = (bf16[192,512]{1,0:T(8,128)(2,1)S(1)}, bf16[192,512]{1,0:T(8,128)(2,1)S(1)}, u32[]{:S(2)}, u32[]{:S(2)}) collective-permute-start(bf16[192,512]{1,0:T(8,128)(2,1)S(1)} %reshape.15.refs_3_), channel_id=1, source_target_pairs={{0,4},{4,0},{8,12},{12,8},{16,20},{20,16},{24,28},{28,24},{1,5},{5... | collective-permute-start | bytes 589832 | tf_op jit(solution)/shard_map/ppermute | solution.py:24
  4.3 10.5 %collective-permute-start.2 = (bf16[192,512]{1,0:T(8,128)(2,1)S(1)}, bf16[192,512]{1,0:T(8,128)(2,1)S(1)}, u32[]{:S(2)}, u32[]{:S(2)}) collective-permute-start(bf16[192,512]{1,0:T(8,128)(2,1)S(1)} %reshape.15.refs_3_), channel_id=1, source_target_pairs={{0,8},{8,0},{4,12},{12,4},{16,24},{24,16},{20,28},{28,20},{1,9},{9... | collective-permute-start | bytes 589832 | tf_op jit(solution)/shard_map/ppermute | solution.py:24
  5.9 13.0 %collective-permute-start.1 = (bf16[192,512]{1,0:T(8,128)(2,1)S(1)}, bf16[192,512]{1,0:T(8,128)(2,1)S(1)}, u32[]{:S(2)}, u32[]{:S(2)}) collective-permute-start(bf16[192,512]{1,0:T(8,128)(2,1)S(1)} %reshape.15.refs_3_), channel_id=1, source_target_pairs={{0,16},{16,0},{4,20},{20,4},{8,24},{24,8},{12,28},{28,12},{1,17},{... | collective-permute-start | bytes 589832 | tf_op jit(solution)/shard_map/ppermute | solution.py:24
  9.3 0.7 %copy-start.2 = (bf16[192,512]{1,0:T(8,128)(2,1)}, bf16[192,512]{1,0:T(8,128)(2,1)S(1)}, u32[]{:S(2)}) copy-start(bf16[192,512]{1,0:T(8,128)(2,1)S(1)} %collective-permute-done.refs_4_) | copy-start | bytes 589828
  14.8 0.7 %copy-start.1 = (bf16[192,512]{1,0:T(8,128)(2,1)}, bf16[192,512]{1,0:T(8,128)(2,1)S(1)}, u32[]{:S(2)}) copy-start(bf16[192,512]{1,0:T(8,128)(2,1)S(1)} %collective-permute-done.2.refs_4_) | copy-start | bytes 589828
  18.9 0.7 %copy-start.3 = (bf16[192,512]{1,0:T(8,128)(2,1)}, bf16[192,512]{1,0:T(8,128)(2,1)S(1)}, u32[]{:S(2)}) copy-start(bf16[192,512]{1,0:T(8,128)(2,1)S(1)} %collective-permute-done.1.refs_4_) | copy-start | bytes 589828
  23.4 5.4 %copy-start.4 = (f32[3,8,256]{2,1,0:T(8,128)S(1)}, f32[3,8,256]{2,1,0:T(8,128)}, u32[]{:S(2)}) copy-start(f32[3,8,256]{2,1,0:T(8,128)} %get-tuple-element.11) | copy-start | bytes 73732
  24.1 1.9 %collective-permute-start.3 = (bf16[3,8,256]{2,1,0:T(8,128)(2,1)S(1)}, bf16[3,8,256]{2,1,0:T(8,128)(2,1)S(1)}, u32[]{:S(2)}, u32[]{:S(2)}) collective-permute-start(bf16[3,8,256]{2,1,0:T(8,128)(2,1)S(1)} %get-tuple-element.13), channel_id=1, source_target_pairs={{0,1},{1,0},{2,3},{3,2},{4,5},{5,4},{6,7},{7,6},{8,9},{9,8},{10,11... | collective-permute-start | bytes 36872 | tf_op jit(solution)/shard_map/ppermute | solution.py:189
  24.1 3.7 %collective-permute-start.4 = (bf16[3,8,256]{2,1,0:T(8,128)(2,1)S(1)}, bf16[3,8,256]{2,1,0:T(8,128)(2,1)S(1)}, u32[]{:S(2)}, u32[]{:S(2)}) collective-permute-start(bf16[3,8,256]{2,1,0:T(8,128)(2,1)S(1)} %get-tuple-element.15), channel_id=1, source_target_pairs={{0,2},{1,3},{2,0},{3,1},{4,6},{5,7},{6,4},{7,5},{8,10},{9,11},{10,... | collective-permute-start | bytes 36872 | tf_op jit(solution)/shard_map/ppermute | solution.py:189
  25.6 3.1 %collective-permute-start.5 = (bf16[3,8,256]{2,1,0:T(8,128)(2,1)S(1)}, bf16[3,8,256]{2,1,0:T(8,128)(2,1)S(1)}, u32[]{:S(2)}, u32[]{:S(2)}) collective-permute-start(bf16[3,8,256]{2,1,0:T(8,128)(2,1)S(1)} %get-tuple-element.14), channel_id=1, source_target_pairs={{0,3},{1,2},{2,1},{3,0},{4,7},{5,6},{6,5},{7,4},{8,11},{9,10},{10,... | collective-permute-start | bytes 36872 | tf_op jit(solution)/shard_map/ppermute | solution.py:189

commit v13 on v12

--- a/solution.py
+++ b/solution.py
@@ -97,11 +97,10 @@
         lane = lax.broadcasted_iota(jnp.int32, (1, 128), 1)
         for n, q in enumerate(rounds):
             spectra(part_refs[n], specp)
-            base = q * slots * 2
             for r in range(slots):
                 slot = (sid ^ (r // share)) * share + r % share
-                a = jnp.minimum(jnp.maximum(pl_ref[base + 2 * slot], 0), events - 1)
-                b = jnp.minimum(jnp.maximum(pl_ref[base + 2 * slot + 1], 0), events - 1)
+                a = jnp.minimum(jnp.maximum(pl_ref[q, slot, 0], 0), events - 1)
+                b = jnp.minimum(jnp.maximum(pl_ref[q, slot, 1], 0), events - 1)
                 left = specl[pl.ds(pl.multiple_of(a * pad, pad), pad), :]
                 right = specp[pl.ds(pl.multiple_of(b * pad, pad), pad), :]
                 lr, li = left[:, :half], left[:, half:]
@@ -200,7 +199,7 @@
     inv = jnp.asarray(inv_np)
     flat = waveforms.reshape(events * chans, length)
     sid = lax.axis_index("station").astype(jnp.int32).reshape(1)
-    pairs = pair_lists.reshape(-1)
+    pairs = pair_lists
     counts = pair_counts.reshape(-1)
     partners = {q: swapped(flat, "region", q) for q in reversed(range(rounds))}
     crosses, spec = rounds_call(pairs, counts, sid, flat, [partners[0]], fwd, inv,

time: 29.7 us -> 29.8 us (level)
    reshape x1 -> x0, local copies, waits for them, and re-layouts: 0.72 us -> none  [shards(): pairs = pair_lists.reshape(-1)]
    unnamed x14, local copies, waits for them, and re-layouts: 3.18 us -> 3.79 us
  transfers between devices with their start and end apart: 6 -> 6, of which waited for: 3 -> 3; matrix products, arithmetic and copies ran while one was open for 3% -> 2% of each run, Pallas kernels for 25% -> 25%
where the time goes in v13:
time: 29.8 us; the launch traced here: 29.5 us
  Pallas kernels  11.3 us (38%)
  starting transfers between devices  9.09 us (31%)
  local copies, waits for them, and re-layouts  4.71 us (16%)
  waiting for transfers between devices  3.68 us (12%)
  other arithmetic  0.62 us (2%)
    pallas_call x3, Pallas kernels, rounds_call(): pl.pallas_call(kernel, out_shape=out_shape, in_specs=[smem, smem, smem] +...  11.3 us
    ppermute x3, starting transfers between devices, swapped(): return lax.ppermute(block, axis, route)  7.23 us
    unnamed x14, local copies, waits for them, and re-layouts  3.79 us
    ppermute x3, waiting for transfers between devices, station_sum(): lax.ppermute(send[j - 1], 'station', perm).astype(jnp.float32)  2.75 us
    ppermute x3, starting transfers between devices, station_sum(): lax.ppermute(send[j - 1], 'station', perm).astype(jnp.float32)  1.86 us
    ppermute x3, waiting for transfers between devices, swapped(): return lax.ppermute(block, axis, route)  0.93 us
    squeeze x1, local copies, waits for them, and re-layouts, station_sum(): send[j - 1]  0.75 us
    add x1, other arithmetic, station_sum(): total + lax.ppermute(send[j - 1], 'station', perm).astype(jnp.float32)  0.62 us
  transfers between devices with their start and end apart: 6, of which 3 were waited for; matrix products, arithmetic and copies ran while one was open for 2% of the time, Pallas kernels for 25%

profile of v13, /device:TPU:0, one launch (start us, length us, event | category | flops | bytes accessed | tf_op | source)
XLA Modules:
  0.0 29.5 jit_solution(690858509117462322)
XLA Ops:
  0.0 1.0 %copy.10 = bf16[16,4,3,512]{3,2,1,0:T(4,128)(2,1)S(1)} copy(bf16[16,4,3,512]{3,1,2,0:T(4,128)(2,1)} %param.5) | data formatting | bytes 393216 | tf_op args[0]
  1.1 0.0 copy-start.5
  1.1 0.2 reshape.11.refs_3_
  1.2 0.0 copy-start
  1.2 3.1 %collective-permute-start = (bf16[192,512]{1,0:T(8,128)(2,1)S(1)}, bf16[192,512]{1,0:T(8,128)(2,1)S(1)}, u32[]{:S(2)}, u32[]{:S(2)}) collective-permute-start(bf16[192,512]{1,0:T(8,128)(2,1)S(1)} %reshape.11.refs_3_), channel_id=1, source_target_pairs={{0,4},{4,0},{8,12},{12,8},{16,20},{20,16},{24,28},{28,24},{1,5},{5... | collective-permute-start | bytes 589832 | tf_op jit(solution)/shard_map/ppermute | solution.py:24
  4.3 1.6 %collective-permute-start.2 = (bf16[192,512]{1,0:T(8,128)(2,1)S(1)}, bf16[192,512]{1,0:T(8,128)(2,1)S(1)}, u32[]{:S(2)}, u32[]{:S(2)}) collective-permute-start(bf16[192,512]{1,0:T(8,128)(2,1)S(1)} %reshape.11.refs_3_), channel_id=1, source_target_pairs={{0,8},{8,0},{4,12},{12,4},{16,24},{24,16},{20,28},{28,20},{1,9},{9... | collective-permute-start | bytes 589832 | tf_op jit(solution)/shard_map/ppermute | solution.py:24
  5.9 2.6 %collective-permute-start.1 = (bf16[192,512]{1,0:T(8,128)(2,1)S(1)}, bf16[192,512]{1,0:T(8,128)(2,1)S(1)}, u32[]{:S(2)}, u32[]{:S(2)}) collective-permute-start(bf16[192,512]{1,0:T(8,128)(2,1)S(1)} %reshape.11.refs_3_), channel_id=1, source_target_pairs={{0,16},{16,0},{4,20},{20,4},{8,24},{24,8},{12,28},{28,12},{1,17},{... | collective-permute-start | bytes 589832 | tf_op jit(solution)/shard_map/ppermute | solution.py:24
  8.5 0.0 copy-done.5
  8.5 0.7 %copy.13.refs_0_ = s32[3,32,2]{2,1,0:T(8,128)} copy(s32[3,32,2]{1,2,0:T(2,128)S(1)} %copy-done.5) | data formatting | bytes 1536 | tf_op args[1]
  9.2 0.0 collective-permute-done.refs_4_
  9.2 0.0 copy-start.3
  9.2 0.0 copy-done
  9.2 0.7 %copy-done.3 = bf16[192,512]{1,0:T(8,128)(2,1)} copy-done((bf16[192,512]{1,0:T(8,128)(2,1)}, bf16[192,512]{1,0:T(8,128)(2,1)S(1)}, u32[]{:S(2)}) %copy-start.3) | copy-done | bytes 196632
  9.9 4.0 %shard_map.55 = (bf16[1,32,1024]{2,1,0:T(8,128)(2,1)}, bf16[256,1024]{1,0:T(8,128)(2,1)}) custom-call(s32[3,32,2]{2,1,0:T(8,128)} %copy.13.refs_0_, s32[3]{0:T(128)} %bitcast.8, s32[1]{0:T(128)} %bitcast.1.refs_2_, bf16[192,512]{1,0:T(8,128)(2,1)} %copy-done, bf16[192,512]{1,0:T(8,128)(2,1)} %copy-done.3, bf16[512,1024]{1,0:T(8,128)(2,1)} %constant.8.clone.refs_5_), custom_call_target="tpu_custom_call" | custom-call | tf_op jit(solution)/shard_map/pallas_call | solution.py:175
  13.9 0.9 %collective-permute-done.2.refs_4_ = bf16[192,512]{1,0:T(8,128)(2,1)S(1)} collective-permute-done((bf16[192,512]{1,0:T(8,128)(2,1)S(1)}, bf16[192,512]{1,0:T(8,128)(2,1)S(1)}, u32[]{:S(2)}, u32[]{:S(2)}) %collective-permute-start.2) | collective-permute-done | bytes 196640 | tf_op jit(solution)/shard_map/ppermute | solution.py:24
  14.8 0.0 copy-start.2
  14.8 0.7 %copy-done.2 = bf16[192,512]{1,0:T(8,128)(2,1)} copy-done((bf16[192,512]{1,0:T(8,128)(2,1)}, bf16[192,512]{1,0:T(8,128)(2,1)S(1)}, u32[]{:S(2)}) %copy-start.2) | copy-done | bytes 196632
  15.4 3.5 %shard_map.56.refs_7_ = bf16[2,32,1024]{2,1,0:T(8,128)(2,1)} custom-call(s32[3,32,2]{2,1,0:T(8,128)} %copy.13.refs_0_, s32[3]{0:T(128)} %bitcast.9, s32[1]{0:T(128)} %bitcast.1.refs_2_, bf16[256,1024]{1,0:T(8,128)(2,1)} %get-tuple-element.9.refs_3_, bf16[192,512]{1,0:T(8,128)(2,1)} %copy-done.2, bf16[512,1024]{1,0:T(8,128)(2,1)} %constant.8.clone.refs_5_, ...), custom_call_target="tpu_custom_call" | custom-call | tf_op jit(solution)/shard_map/pallas_call | solution.py:175
  19.0 0.0 collective-permute-done.1.refs_4_
  19.0 0.0 copy-start.1
  19.0 0.7 %copy-done.1 = bf16[192,512]{1,0:T(8,128)(2,1)} copy-done((bf16[192,512]{1,0:T(8,128)(2,1)}, bf16[192,512]{1,0:T(8,128)(2,1)S(1)}, u32[]{:S(2)}) %copy-start.1) | copy-done | bytes 196632
  19.7 3.8 %shard_map.57 = (f32[3,8,256]{2,1,0:T(8,128)}, bf16[3,3,8,256]{3,2,1,0:T(8,128)(2,1)}) custom-call(s32[3,32,2]{2,1,0:T(8,128)} %copy.13.refs_0_, s32[3]{0:T(128)} %bitcast.10, s32[1]{0:T(128)} %bitcast.1.refs_2_, bf16[256,1024]{1,0:T(8,128)(2,1)} %get-tuple-element.9.refs_3_, bf16[192,512]{1,0:T(8,128)(2,1)} %copy-done.1, ...), custom_call_target="tpu_custom_call" | custom-call | tf_op jit(solution)/shard_map/pallas_call | solution.py:175
  23.5 0.0 copy-start.4
  23.5 0.7 %slice_bitcast_fusion.2 = (bf16[3,8,256]{2,1,0:T(8,128)(2,1)S(1)}, bf16[3,8,256]{2,1,0:T(8,128)(2,1)S(1)}, bf16[3,8,256]{2,1,0:T(8,128)(2,1)S(1)}) fusion(bf16[3,3,8,256]{3,2,1,0:T(8,128)(2,1)} %get-tuple-element.12), kind=kLoop, calls=%fused_computation.3 | loop fusion | bytes 73728 | tf_op jit(solution)/shard_map/squeeze | solution.py:188
  24.2 0.0 collective-permute-start.3
  24.2 1.5 %collective-permute-start.4 = (bf16[3,8,256]{2,1,0:T(8,128)(2,1)S(1)}, bf16[3,8,256]{2,1,0:T(8,128)(2,1)S(1)}, u32[]{:S(2)}, u32[]{:S(2)}) collective-permute-start(bf16[3,8,256]{2,1,0:T(8,128)(2,1)S(1)} %get-tuple-element.15), channel_id=1, source_target_pairs={{0,2},{1,3},{2,0},{3,1},{4,6},{5,7},{6,4},{7,5},{8,10},{9,11},{10,... | collective-permute-start | bytes 36872 | tf_op jit(solution)/shard_map/ppermute | solution.py:188
  25.7 0.4 %collective-permute-start.5 = (bf16[3,8,256]{2,1,0:T(8,128)(2,1)S(1)}, bf16[3,8,256]{2,1,0:T(8,128)(2,1)S(1)}, u32[]{:S(2)}, u32[]{:S(2)}) collective-permute-start(bf16[3,8,256]{2,1,0:T(8,128)(2,1)S(1)} %get-tuple-element.14), channel_id=1, source_target_pairs={{0,3},{1,2},{2,1},{3,0},{4,7},{5,6},{6,5},{7,4},{8,11},{9,10},{10,... | collective-permute-start | bytes 36872 | tf_op jit(solution)/shard_map/ppermute | solution.py:188
  26.1 0.0 collective-permute-done.3
  26.1 1.8 %collective-permute-done.4 = bf16[3,8,256]{2,1,0:T(8,128)(2,1)S(1)} collective-permute-done((bf16[3,8,256]{2,1,0:T(8,128)(2,1)S(1)}, bf16[3,8,256]{2,1,0:T(8,128)(2,1)S(1)}, u32[]{:S(2)}, u32[]{:S(2)}) %collective-permute-start.4) | collective-permute-done | bytes 12320 | tf_op jit(solution)/shard_map/ppermute | solution.py:188
  27.9 0.9 %collective-permute-done.5 = bf16[3,8,256]{2,1,0:T(8,128)(2,1)S(1)} collective-permute-done((bf16[3,8,256]{2,1,0:T(8,128)(2,1)S(1)}, bf16[3,8,256]{2,1,0:T(8,128)(2,1)S(1)}, u32[]{:S(2)}, u32[]{:S(2)}) %collective-permute-start.5) | collective-permute-done | bytes 12320 | tf_op jit(solution)/shard_map/ppermute | solution.py:188
  28.9 0.0 copy-done.4
  28.9 0.6 %convert_add_fusion = f32[3,8,256]{2,1,0:T(8,128)} fusion(bf16[3,8,256]{2,1,0:T(8,128)(2,1)S(1)} %collective-permute-done.5, bf16[3,8,256]{2,1,0:T(8,128)(2,1)S(1)} %collective-permute-done.4, f32[3,8,256]{2,1,0:T(8,128)S(1)} %copy-done.4, bf16[3,8,256]{2,1,0:T(8,128)(2,1)S(1)} %collective-permute-done.3), kind=kLoop, calls=%fused_computation | loop fusion | flops 36864 | bytes 86016 | tf_op jit(solution)/shard_map/add | solution.py:188
Async XLA Ops:
  1.1 7.4 %copy-start.5 = (s32[3,32,2]{1,2,0:T(2,128)S(1)}, s32[3,32,2]{1,2,0:T(2,128)}, u32[]{:S(2)}) copy-start(s32[3,32,2]{1,2,0:T(2,128)} %param.6) | copy-start | bytes 2308
  1.2 8.0 %copy-start = (bf16[192,512]{1,0:T(8,128)(2,1)}, bf16[192,512]{1,0:T(8,128)(2,1)S(1)}, u32[]{:S(2)}) copy-start(bf16[192,512]{1,0:T(8,128)(2,1)S(1)} %reshape.11.refs_3_) | copy-start | bytes 589828
  1.2 8.0 %collective-permute-start = (bf16[192,512]{1,0:T(8,128)(2,1)S(1)}, bf16[192,512]{1,0:T(8,128)(2,1)S(1)}, u32[]{:S(2)}, u32[]{:S(2)}) collective-permute-start(bf16[192,512]{1,0:T(8,128)(2,1)S(1)} %reshape.11.refs_3_), channel_id=1, source_target_pairs={{0,4},{4,0},{8,12},{12,8},{16,20},{20,16},{24,28},{28,24},{1,5},{5... | collective-permute-start | bytes 589832 | tf_op jit(solution)/shard_map/ppermute | solution.py:24
  4.3 10.5 %collective-permute-start.2 = (bf16[192,512]{1,0:T(8,128)(2,1)S(1)}, bf16[192,512]{1,0:T(8,128)(2,1)S(1)}, u32[]{:S(2)}, u32[]{:S(2)}) collective-permute-start(bf16[192,512]{1,0:T(8,128)(2,1)S(1)} %reshape.11.refs_3_), channel_id=1, source_target_pairs={{0,8},{8,0},{4,12},{12,4},{16,24},{24,16},{20,28},{28,20},{1,9},{9... | collective-permute-start | bytes 589832 | tf_op jit(solution)/shard_map/ppermute | solution.py:24
  5.9 13.1 %collective-permute-start.1 = (bf16[192,512]{1,0:T(8,128)(2,1)S(1)}, bf16[192,512]{1,0:T(8,128)(2,1)S(1)}, u32[]{:S(2)}, u32[]{:S(2)}) collective-permute-start(bf16[192,512]{1,0:T(8,128)(2,1)S(1)} %reshape.11.refs_3_), channel_id=1, source_target_pairs={{0,16},{16,0},{4,20},{20,4},{8,24},{24,8},{12,28},{28,12},{1,17},{... | collective-permute-start | bytes 589832 | tf_op jit(solution)/shard_map/ppermute | solution.py:24
  9.2 0.7 %copy-start.3 = (bf16[192,512]{1,0:T(8,128)(2,1)}, bf16[192,512]{1,0:T(8,128)(2,1)S(1)}, u32[]{:S(2)}) copy-start(bf16[192,512]{1,0:T(8,128)(2,1)S(1)} %collective-permute-done.refs_4_) | copy-start | bytes 589828
  14.8 0.7 %copy-start.2 = (bf16[192,512]{1,0:T(8,128)(2,1)}, bf16[192,512]{1,0:T(8,128)(2,1)S(1)}, u32[]{:S(2)}) copy-start(bf16[192,512]{1,0:T(8,128)(2,1)S(1)} %collective-permute-done.2.refs_4_) | copy-start | bytes 589828
  19.0 0.7 %copy-start.1 = (bf16[192,512]{1,0:T(8,128)(2,1)}, bf16[192,512]{1,0:T(8,128)(2,1)S(1)}, u32[]{:S(2)}) copy-start(bf16[192,512]{1,0:T(8,128)(2,1)S(1)} %collective-permute-done.1.refs_4_) | copy-start | bytes 589828
  23.5 5.4 %copy-start.4 = (f32[3,8,256]{2,1,0:T(8,128)S(1)}, f32[3,8,256]{2,1,0:T(8,128)}, u32[]{:S(2)}) copy-start(f32[3,8,256]{2,1,0:T(8,128)} %get-tuple-element.11) | copy-start | bytes 73732
  24.2 1.9 %collective-permute-start.3 = (bf16[3,8,256]{2,1,0:T(8,128)(2,1)S(1)}, bf16[3,8,256]{2,1,0:T(8,128)(2,1)S(1)}, u32[]{:S(2)}, u32[]{:S(2)}) collective-permute-start(bf16[3,8,256]{2,1,0:T(8,128)(2,1)S(1)} %get-tuple-element.13), channel_id=1, source_target_pairs={{0,1},{1,0},{2,3},{3,2},{4,5},{5,4},{6,7},{7,6},{8,9},{9,8},{10,11... | collective-permute-start | bytes 36872 | tf_op jit(solution)/shard_map/ppermute | solution.py:188
  24.2 3.7 %collective-permute-start.4 = (bf16[3,8,256]{2,1,0:T(8,128)(2,1)S(1)}, bf16[3,8,256]{2,1,0:T(8,128)(2,1)S(1)}, u32[]{:S(2)}, u32[]{:S(2)}) collective-permute-start(bf16[3,8,256]{2,1,0:T(8,128)(2,1)S(1)} %get-tuple-element.15), channel_id=1, source_target_pairs={{0,2},{1,3},{2,0},{3,1},{4,6},{5,7},{6,4},{7,5},{8,10},{9,11},{10,... | collective-permute-start | bytes 36872 | tf_op jit(solution)/shard_map/ppermute | solution.py:188
  25.7 3.1 %collective-permute-start.5 = (bf16[3,8,256]{2,1,0:T(8,128)(2,1)S(1)}, bf16[3,8,256]{2,1,0:T(8,128)(2,1)S(1)}, u32[]{:S(2)}, u32[]{:S(2)}) collective-permute-start(bf16[3,8,256]{2,1,0:T(8,128)(2,1)S(1)} %get-tuple-element.14), channel_id=1, source_target_pairs={{0,3},{1,2},{2,1},{3,0},{4,7},{5,6},{6,5},{7,4},{8,11},{9,10},{10,... | collective-permute-start | bytes 36872 | tf_op jit(solution)/shard_map/ppermute | solution.py:188

commit v14 on v13

--- a/solution.py
+++ b/solution.py
@@ -99,8 +99,8 @@
             spectra(part_refs[n], specp)
             for r in range(slots):
                 slot = (sid ^ (r // share)) * share + r % share
-                a = jnp.minimum(jnp.maximum(pl_ref[q, slot, 0], 0), events - 1)
-                b = jnp.minimum(jnp.maximum(pl_ref[q, slot, 1], 0), events - 1)
+                a = jnp.minimum(jnp.maximum(pl_ref[q, 0, slot], 0), events - 1)
+                b = jnp.minimum(jnp.maximum(pl_ref[q, 1, slot], 0), events - 1)
                 left = specl[pl.ds(pl.multiple_of(a * pad, pad), pad), :]
                 right = specp[pl.ds(pl.multiple_of(b * pad, pad), pad), :]
                 lr, li = left[:, :half], left[:, half:]
@@ -199,7 +199,7 @@
     inv = jnp.asarray(inv_np)
     flat = waveforms.reshape(events * chans, length)
     sid = lax.axis_index("station").astype(jnp.int32).reshape(1)
-    pairs = pair_lists
+    pairs = jnp.transpose(pair_lists, (0, 2, 1))
     counts = pair_counts.reshape(-1)
     partners = {q: swapped(flat, "region", q) for q in reversed(range(rounds))}
     crosses, spec = rounds_call(pairs, counts, sid, flat, [partners[0]], fwd, inv,

time: 29.8 us -> 29.6 us (level)
  waiting for transfers between devices: 3.68 us -> 4.57 us
  local copies, waits for them, and re-layouts: 4.71 us -> 4.01 us
  Pallas kernels: 11.3 us -> 11 us
    ppermute x3, waiting for transfers between devices: 0.93 us -> 1.81 us  [swapped(): return lax.ppermute(block, axis, route)]
    unnamed x14 -> x11, local copies, waits for them, and re-layouts: 3.79 us -> 3.09 us
  transfers between devices with their start and end apart: 6 -> 6, of which waited for: 3 -> 4; matrix products, arithmetic and copies ran while one was open for 2% -> 0% of each run, Pallas kernels for 25% -> 25%
where the time goes in v14:
time: 29.6 us; the launch traced here: 29.4 us
  Pallas kernels  11 us (37%)
  starting transfers between devices  9.09 us (31%)
  waiting for transfers between devices  4.57 us (15%)
  local copies, waits for them, and re-layouts  4.01 us (14%)
  other arithmetic  0.62 us (2%)
    pallas_call x3, Pallas kernels, rounds_call(): pl.pallas_call(kernel, out_shape=out_shape, in_specs=[smem, smem, smem] +...  11 us
    ppermute x3, starting transfers between devices, swapped(): return lax.ppermute(block, axis, route)  7.23 us
    unnamed x11, local copies, waits for them, and re-layouts  3.09 us
    ppermute x3, waiting for transfers between devices, station_sum(): lax.ppermute(send[j - 1], 'station', perm).astype(jnp.float32)  2.75 us
    ppermute x3, starting transfers between devices, station_sum(): lax.ppermute(send[j - 1], 'station', perm).astype(jnp.float32)  1.86 us
    ppermute x3, waiting for transfers between devices, swapped(): return lax.ppermute(block, axis, route)  1.81 us
    squeeze x1, local copies, waits for them, and re-layouts, station_sum(): send[j - 1]  0.75 us
    add x1, other arithmetic, station_sum(): total + lax.ppermute(send[j - 1], 'station', perm).astype(jnp.float32)  0.62 us
  transfers between devices with their start and end apart: 6, of which 4 were waited for; matrix products, arithmetic and copies ran while one was open for 0% of the time, Pallas kernels for 25%

profile of v14, /device:TPU:0, one launch (start us, length us, event | category | flops | bytes accessed | tf_op | source)
XLA Modules:
  0.0 29.4 jit_solution(8552550812778340023)
XLA Ops:
  0.0 1.0 %copy.7 = bf16[16,4,3,512]{3,2,1,0:T(4,128)(2,1)S(1)} copy(bf16[16,4,3,512]{3,1,2,0:T(4,128)(2,1)} %param.5) | data formatting | bytes 393216 | tf_op args[0]
  1.1 0.2 reshape.11.refs_3_
  1.2 0.0 copy-start
  1.2 3.1 %collective-permute-start = (bf16[192,512]{1,0:T(8,128)(2,1)S(1)}, bf16[192,512]{1,0:T(8,128)(2,1)S(1)}, u32[]{:S(2)}, u32[]{:S(2)}) collective-permute-start(bf16[192,512]{1,0:T(8,128)(2,1)S(1)} %reshape.11.refs_3_), channel_id=1, source_target_pairs={{0,4},{4,0},{8,12},{12,8},{16,20},{20,16},{24,28},{28,24},{1,5},{5... | collective-permute-start | bytes 589832 | tf_op jit(solution)/shard_map/ppermute | solution.py:24
  4.3 1.6 %collective-permute-start.2 = (bf16[192,512]{1,0:T(8,128)(2,1)S(1)}, bf16[192,512]{1,0:T(8,128)(2,1)S(1)}, u32[]{:S(2)}, u32[]{:S(2)}) collective-permute-start(bf16[192,512]{1,0:T(8,128)(2,1)S(1)} %reshape.11.refs_3_), channel_id=1, source_target_pairs={{0,8},{8,0},{4,12},{12,4},{16,24},{24,16},{20,28},{28,20},{1,9},{9... | collective-permute-start | bytes 589832 | tf_op jit(solution)/shard_map/ppermute | solution.py:24
  5.9 2.6 %collective-permute-start.1 = (bf16[192,512]{1,0:T(8,128)(2,1)S(1)}, bf16[192,512]{1,0:T(8,128)(2,1)S(1)}, u32[]{:S(2)}, u32[]{:S(2)}) collective-permute-start(bf16[192,512]{1,0:T(8,128)(2,1)S(1)} %reshape.11.refs_3_), channel_id=1, source_target_pairs={{0,16},{16,0},{4,20},{20,4},{8,24},{24,8},{12,28},{28,12},{1,17},{... | collective-permute-start | bytes 589832 | tf_op jit(solution)/shard_map/ppermute | solution.py:24
  8.5 0.7 %collective-permute-done.refs_4_ = bf16[192,512]{1,0:T(8,128)(2,1)S(1)} collective-permute-done((bf16[192,512]{1,0:T(8,128)(2,1)S(1)}, bf16[192,512]{1,0:T(8,128)(2,1)S(1)}, u32[]{:S(2)}, u32[]{:S(2)}) %collective-permute-start) | collective-permute-done | bytes 196640 | tf_op jit(solution)/shard_map/ppermute | solution.py:24
  9.2 0.0 copy-start.2
  9.2 0.0 copy-done
  9.2 0.7 %copy-done.2 = bf16[192,512]{1,0:T(8,128)(2,1)} copy-done((bf16[192,512]{1,0:T(8,128)(2,1)}, bf16[192,512]{1,0:T(8,128)(2,1)S(1)}, u32[]{:S(2)}) %copy-start.2) | copy-done | bytes 196632
  9.9 3.8 %shard_map.55 = (bf16[1,32,1024]{2,1,0:T(8,128)(2,1)}, bf16[256,1024]{1,0:T(8,128)(2,1)}) custom-call(s32[3,2,32]{2,1,0:T(2,128)} %bitcast.9, s32[3]{0:T(128)} %bitcast.12, s32[1]{0:T(128)} %bitcast.2.refs_2_, bf16[192,512]{1,0:T(8,128)(2,1)} %copy-done, bf16[192,512]{1,0:T(8,128)(2,1)} %copy-done.2, bf16[512,1024]{1,0:T(8,128)(2,1)} %constant.8.clone.refs_5_), custom_call_target="tpu_custom_call" | custom-call | tf_op jit(solution)/shard_map/pallas_call | solution.py:175
  13.7 1.1 %collective-permute-done.2.refs_4_ = bf16[192,512]{1,0:T(8,128)(2,1)S(1)} collective-permute-done((bf16[192,512]{1,0:T(8,128)(2,1)S(1)}, bf16[192,512]{1,0:T(8,128)(2,1)S(1)}, u32[]{:S(2)}, u32[]{:S(2)}) %collective-permute-start.2) | collective-permute-done | bytes 196640 | tf_op jit(solution)/shard_map/ppermute | solution.py:24
  14.8 0.0 copy-start.3
  14.8 0.7 %copy-done.3 = bf16[192,512]{1,0:T(8,128)(2,1)} copy-done((bf16[192,512]{1,0:T(8,128)(2,1)}, bf16[192,512]{1,0:T(8,128)(2,1)S(1)}, u32[]{:S(2)}) %copy-start.3) | copy-done | bytes 196632
  15.4 3.4 %shard_map.56.refs_7_ = bf16[2,32,1024]{2,1,0:T(8,128)(2,1)} custom-call(s32[3,2,32]{2,1,0:T(2,128)} %bitcast.10, s32[3]{0:T(128)} %bitcast.13, s32[1]{0:T(128)} %bitcast.2.refs_2_, bf16[256,1024]{1,0:T(8,128)(2,1)} %get-tuple-element.9.refs_3_, bf16[192,512]{1,0:T(8,128)(2,1)} %copy-done.3, bf16[512,1024]{1,0:T(8,128)(2,1)} %constant.8.clone.refs_5_, ...), custom_call_target="tpu_custom_call" | custom-call | tf_op jit(solution)/shard_map/pallas_call | solution.py:175
  18.9 0.0 collective-permute-done.1.refs_4_
  18.9 0.0 copy-start.1
  18.9 0.7 %copy-done.1 = bf16[192,512]{1,0:T(8,128)(2,1)} copy-done((bf16[192,512]{1,0:T(8,128)(2,1)}, bf16[192,512]{1,0:T(8,128)(2,1)S(1)}, u32[]{:S(2)}) %copy-start.1) | copy-done | bytes 196632
  19.5 3.8 %shard_map.57 = (f32[3,8,256]{2,1,0:T(8,128)}, bf16[3,3,8,256]{3,2,1,0:T(8,128)(2,1)}) custom-call(s32[3,2,32]{2,1,0:T(2,128)} %bitcast.11, s32[3]{0:T(128)} %bitcast.14, s32[1]{0:T(128)} %bitcast.2.refs_2_, bf16[256,1024]{1,0:T(8,128)(2,1)} %get-tuple-element.9.refs_3_, bf16[192,512]{1,0:T(8,128)(2,1)} %copy-done.1, ...), custom_call_target="tpu_custom_call" | custom-call | tf_op jit(solution)/shard_map/pallas_call | solution.py:175
  23.4 0.0 copy-start.4
  23.4 0.7 %slice_bitcast_fusion.2 = (bf16[3,8,256]{2,1,0:T(8,128)(2,1)S(1)}, bf16[3,8,256]{2,1,0:T(8,128)(2,1)S(1)}, bf16[3,8,256]{2,1,0:T(8,128)(2,1)S(1)}) fusion(bf16[3,3,8,256]{3,2,1,0:T(8,128)(2,1)} %get-tuple-element.12), kind=kLoop, calls=%fused_computation.3 | loop fusion | bytes 73728 | tf_op jit(solution)/shard_map/squeeze | solution.py:188
  24.1 0.0 collective-permute-start.3
  24.1 1.5 %collective-permute-start.4 = (bf16[3,8,256]{2,1,0:T(8,128)(2,1)S(1)}, bf16[3,8,256]{2,1,0:T(8,128)(2,1)S(1)}, u32[]{:S(2)}, u32[]{:S(2)}) collective-permute-start(bf16[3,8,256]{2,1,0:T(8,128)(2,1)S(1)} %get-tuple-element.15), channel_id=1, source_target_pairs={{0,2},{1,3},{2,0},{3,1},{4,6},{5,7},{6,4},{7,5},{8,10},{9,11},{10,... | collective-permute-start | bytes 36872 | tf_op jit(solution)/shard_map/ppermute | solution.py:188
  25.6 0.4 %collective-permute-start.5 = (bf16[3,8,256]{2,1,0:T(8,128)(2,1)S(1)}, bf16[3,8,256]{2,1,0:T(8,128)(2,1)S(1)}, u32[]{:S(2)}, u32[]{:S(2)}) collective-permute-start(bf16[3,8,256]{2,1,0:T(8,128)(2,1)S(1)} %get-tuple-element.14), channel_id=1, source_target_pairs={{0,3},{1,2},{2,1},{3,0},{4,7},{5,6},{6,5},{7,4},{8,11},{9,10},{10,... | collective-permute-start | bytes 36872 | tf_op jit(solution)/shard_map/ppermute | solution.py:188
  26.0 0.0 collective-permute-done.3
  26.0 1.8 %collective-permute-done.4 = bf16[3,8,256]{2,1,0:T(8,128)(2,1)S(1)} collective-permute-done((bf16[3,8,256]{2,1,0:T(8,128)(2,1)S(1)}, bf16[3,8,256]{2,1,0:T(8,128)(2,1)S(1)}, u32[]{:S(2)}, u32[]{:S(2)}) %collective-permute-start.4) | collective-permute-done | bytes 12320 | tf_op jit(solution)/shard_map/ppermute | solution.py:188
  27.8 0.9 %collective-permute-done.5 = bf16[3,8,256]{2,1,0:T(8,128)(2,1)S(1)} collective-permute-done((bf16[3,8,256]{2,1,0:T(8,128)(2,1)S(1)}, bf16[3,8,256]{2,1,0:T(8,128)(2,1)S(1)}, u32[]{:S(2)}, u32[]{:S(2)}) %collective-permute-start.5) | collective-permute-done | bytes 12320 | tf_op jit(solution)/shard_map/ppermute | solution.py:188
  28.7 0.0 copy-done.4
  28.7 0.6 %convert_add_fusion = f32[3,8,256]{2,1,0:T(8,128)} fusion(bf16[3,8,256]{2,1,0:T(8,128)(2,1)S(1)} %collective-permute-done.5, bf16[3,8,256]{2,1,0:T(8,128)(2,1)S(1)} %collective-permute-done.4, f32[3,8,256]{2,1,0:T(8,128)S(1)} %copy-done.4, bf16[3,8,256]{2,1,0:T(8,128)(2,1)S(1)} %collective-permute-done.3), kind=kLoop, calls=%fused_computation | loop fusion | flops 36864 | bytes 86016 | tf_op jit(solution)/shard_map/add | solution.py:188
Async XLA Ops:
  1.2 8.0 %copy-start = (bf16[192,512]{1,0:T(8,128)(2,1)}, bf16[192,512]{1,0:T(8,128)(2,1)S(1)}, u32[]{:S(2)}) copy-start(bf16[192,512]{1,0:T(8,128)(2,1)S(1)} %reshape.11.refs_3_) | copy-start | bytes 589828
  1.2 8.0 %collective-permute-start = (bf16[192,512]{1,0:T(8,128)(2,1)S(1)}, bf16[192,512]{1,0:T(8,128)(2,1)S(1)}, u32[]{:S(2)}, u32[]{:S(2)}) collective-permute-start(bf16[192,512]{1,0:T(8,128)(2,1)S(1)} %reshape.11.refs_3_), channel_id=1, source_target_pairs={{0,4},{4,0},{8,12},{12,8},{16,20},{20,16},{24,28},{28,24},{1,5},{5... | collective-permute-start | bytes 589832 | tf_op jit(solution)/shard_map/ppermute | solution.py:24
  4.3 10.5 %collective-permute-start.2 = (bf16[192,512]{1,0:T(8,128)(2,1)S(1)}, bf16[192,512]{1,0:T(8,128)(2,1)S(1)}, u32[]{:S(2)}, u32[]{:S(2)}) collective-permute-start(bf16[192,512]{1,0:T(8,128)(2,1)S(1)} %reshape.11.refs_3_), channel_id=1, source_target_pairs={{0,8},{8,0},{4,12},{12,4},{16,24},{24,16},{20,28},{28,20},{1,9},{9... | collective-permute-start | bytes 589832 | tf_op jit(solution)/shard_map/ppermute | solution.py:24
  5.9 13.0 %collective-permute-start.1 = (bf16[192,512]{1,0:T(8,128)(2,1)S(1)}, bf16[192,512]{1,0:T(8,128)(2,1)S(1)}, u32[]{:S(2)}, u32[]{:S(2)}) collective-permute-start(bf16[192,512]{1,0:T(8,128)(2,1)S(1)} %reshape.11.refs_3_), channel_id=1, source_target_pairs={{0,16},{16,0},{4,20},{20,4},{8,24},{24,8},{12,28},{28,12},{1,17},{... | collective-permute-start | bytes 589832 | tf_op jit(solution)/shard_map/ppermute | solution.py:24
  9.2 0.7 %copy-start.2 = (bf16[192,512]{1,0:T(8,128)(2,1)}, bf16[192,512]{1,0:T(8,128)(2,1)S(1)}, u32[]{:S(2)}) copy-start(bf16[192,512]{1,0:T(8,128)(2,1)S(1)} %collective-permute-done.refs_4_) | copy-start | bytes 589828
  14.8 0.7 %copy-start.3 = (bf16[192,512]{1,0:T(8,128)(2,1)}, bf16[192,512]{1,0:T(8,128)(2,1)S(1)}, u32[]{:S(2)}) copy-start(bf16[192,512]{1,0:T(8,128)(2,1)S(1)} %collective-permute-done.2.refs_4_) | copy-start | bytes 589828
  18.9 0.7 %copy-start.1 = (bf16[192,512]{1,0:T(8,128)(2,1)}, bf16[192,512]{1,0:T(8,128)(2,1)S(1)}, u32[]{:S(2)}) copy-start(bf16[192,512]{1,0:T(8,128)(2,1)S(1)} %collective-permute-done.1.refs_4_) | copy-start | bytes 589828
  23.4 5.4 %copy-start.4 = (f32[3,8,256]{2,1,0:T(8,128)S(1)}, f32[3,8,256]{2,1,0:T(8,128)}, u32[]{:S(2)}) copy-start(f32[3,8,256]{2,1,0:T(8,128)} %get-tuple-element.11) | copy-start | bytes 73732
  24.1 1.9 %collective-permute-start.3 = (bf16[3,8,256]{2,1,0:T(8,128)(2,1)S(1)}, bf16[3,8,256]{2,1,0:T(8,128)(2,1)S(1)}, u32[]{:S(2)}, u32[]{:S(2)}) collective-permute-start(bf16[3,8,256]{2,1,0:T(8,128)(2,1)S(1)} %get-tuple-element.13), channel_id=1, source_target_pairs={{0,1},{1,0},{2,3},{3,2},{4,5},{5,4},{6,7},{7,6},{8,9},{9,8},{10,11... | collective-permute-start | bytes 36872 | tf_op jit(solution)/shard_map/ppermute | solution.py:188
  24.1 3.7 %collective-permute-start.4 = (bf16[3,8,256]{2,1,0:T(8,128)(2,1)S(1)}, bf16[3,8,256]{2,1,0:T(8,128)(2,1)S(1)}, u32[]{:S(2)}, u32[]{:S(2)}) collective-permute-start(bf16[3,8,256]{2,1,0:T(8,128)(2,1)S(1)} %get-tuple-element.15), channel_id=1, source_target_pairs={{0,2},{1,3},{2,0},{3,1},{4,6},{5,7},{6,4},{7,5},{8,10},{9,11},{10,... | collective-permute-start | bytes 36872 | tf_op jit(solution)/shard_map/ppermute | solution.py:188
  25.6 3.1 %collective-permute-start.5 = (bf16[3,8,256]{2,1,0:T(8,128)(2,1)S(1)}, bf16[3,8,256]{2,1,0:T(8,128)(2,1)S(1)}, u32[]{:S(2)}, u32[]{:S(2)}) collective-permute-start(bf16[3,8,256]{2,1,0:T(8,128)(2,1)S(1)} %get-tuple-element.14), channel_id=1, source_target_pairs={{0,3},{1,2},{2,1},{3,0},{4,7},{5,6},{6,5},{7,4},{8,11},{9,10},{10,... | collective-permute-start | bytes 36872 | tf_op jit(solution)/shard_map/ppermute | solution.py:188

commit v15 on v14

--- a/solution.py
+++ b/solution.py
@@ -204,11 +204,9 @@
     partners = {q: swapped(flat, "region", q) for q in reversed(range(rounds))}
     crosses, spec = rounds_call(pairs, counts, sid, flat, [partners[0]], fwd, inv,
                                 [0], events, chans, slots, groups)
-    for q in range(1, rounds - 1):
-        (crosses,) = rounds_call(pairs, counts, sid, spec, [partners[q]], fwd, inv,
-                                 [q], events, chans, slots, groups, prev=crosses)
-    keep, send = rounds_call(pairs, counts, sid, spec, [partners[rounds - 1]], fwd, inv,
-                             [rounds - 1], events, chans, slots, groups, prev=crosses, final=True)
+    rest = list(range(1, rounds))
+    keep, send = rounds_call(pairs, counts, sid, spec, [partners[q] for q in rest], fwd, inv,
+                             rest, events, chans, slots, groups, prev=crosses, final=True)
     return station_sum(keep, send, groups)
 
 

time: 29.6 us -> 28.8 us (0.973)
  Pallas kernels: 11 us -> 8.53 us
  waiting for transfers between devices: 4.57 us -> 6.92 us
  local copies, waits for them, and re-layouts: 4.01 us -> 3.33 us
    pallas_call x3 -> x2, Pallas kernels: 11 us -> 8.53 us  [rounds_call(): pl.pallas_call(kernel, out_shape=out_shape, in_specs=[smem, smem, smem] +...]
    ppermute x3, waiting for transfers between devices: 1.81 us -> 4.17 us  [swapped(): return lax.ppermute(block, axis, route)]
    unnamed x11, local copies, waits for them, and re-layouts: 3.09 us -> 2.41 us
  transfers between devices with their start and end apart: 6 -> 6, of which waited for: 4 -> 5; matrix products, arithmetic and copies ran while one was open for 0% -> 0% of each run, Pallas kernels for 25% -> 13%
where the time goes in v15:
time: 28.8 us; the launch traced here: 28.5 us
  starting transfers between devices  9.09 us (32%)
  Pallas kernels  8.53 us (30%)
  waiting for transfers between devices  6.92 us (24%)
  local copies, waits for them, and re-layouts  3.33 us (12%)
  other arithmetic  0.62 us (2%)
    pallas_call x2, Pallas kernels, rounds_call(): pl.pallas_call(kernel, out_shape=out_shape, in_specs=[smem, smem, smem] +...  8.53 us
    ppermute x3, starting transfers between devices, swapped(): return lax.ppermute(block, axis, route)  7.23 us
    ppermute x3, waiting for transfers between devices, swapped(): return lax.ppermute(block, axis, route)  4.17 us
    ppermute x3, waiting for transfers between devices, station_sum(): lax.ppermute(send[j - 1], 'station', perm).astype(jnp.float32)  2.75 us
    unnamed x11, local copies, waits for them, and re-layouts  2.41 us
    ppermute x3, starting transfers between devices, station_sum(): lax.ppermute(send[j - 1], 'station', perm).astype(jnp.float32)  1.86 us
    squeeze x1, local copies, waits for them, and re-layouts, station_sum(): send[j - 1]  0.75 us
    add x1, other arithmetic, station_sum(): total + lax.ppermute(send[j - 1], 'station', perm).astype(jnp.float32)  0.62 us
  transfers between devices with their start and end apart: 6, of which 5 were waited for; matrix products, arithmetic and copies ran while one was open for 0% of the time, Pallas kernels for 13%

profile of v15, /device:TPU:0, one launch (start us, length us, event | category | flops | bytes accessed | tf_op | source)
XLA Modules:
  0.0 28.5 jit_solution(5574548246739925320)
XLA Ops:
  0.0 1.0 %copy.7 = bf16[16,4,3,512]{3,2,1,0:T(4,128)(2,1)S(1)} copy(bf16[16,4,3,512]{3,1,2,0:T(4,128)(2,1)} %param.5) | data formatting | bytes 393216 | tf_op args[0]
  1.1 0.2 reshape.11.refs_3_
  1.2 0.0 copy-start
  1.2 3.1 %collective-permute-start = (bf16[192,512]{1,0:T(8,128)(2,1)S(1)}, bf16[192,512]{1,0:T(8,128)(2,1)S(1)}, u32[]{:S(2)}, u32[]{:S(2)}) collective-permute-start(bf16[192,512]{1,0:T(8,128)(2,1)S(1)} %reshape.11.refs_3_), channel_id=1, source_target_pairs={{0,4},{4,0},{8,12},{12,8},{16,20},{20,16},{24,28},{28,24},{1,5},{5... | collective-permute-start | bytes 589832 | tf_op jit(solution)/shard_map/ppermute | solution.py:24
  4.3 1.6 %collective-permute-start.1 = (bf16[192,512]{1,0:T(8,128)(2,1)S(1)}, bf16[192,512]{1,0:T(8,128)(2,1)S(1)}, u32[]{:S(2)}, u32[]{:S(2)}) collective-permute-start(bf16[192,512]{1,0:T(8,128)(2,1)S(1)} %reshape.11.refs_3_), channel_id=1, source_target_pairs={{0,8},{8,0},{4,12},{12,4},{16,24},{24,16},{20,28},{28,20},{1,9},{9... | collective-permute-start | bytes 589832 | tf_op jit(solution)/shard_map/ppermute | solution.py:24
  5.9 2.6 %collective-permute-start.2 = (bf16[192,512]{1,0:T(8,128)(2,1)S(1)}, bf16[192,512]{1,0:T(8,128)(2,1)S(1)}, u32[]{:S(2)}, u32[]{:S(2)}) collective-permute-start(bf16[192,512]{1,0:T(8,128)(2,1)S(1)} %reshape.11.refs_3_), channel_id=1, source_target_pairs={{0,16},{16,0},{4,20},{20,4},{8,24},{24,8},{12,28},{28,12},{1,17},{... | collective-permute-start | bytes 589832 | tf_op jit(solution)/shard_map/ppermute | solution.py:24
  8.5 0.7 %collective-permute-done.refs_4_ = bf16[192,512]{1,0:T(8,128)(2,1)S(1)} collective-permute-done((bf16[192,512]{1,0:T(8,128)(2,1)S(1)}, bf16[192,512]{1,0:T(8,128)(2,1)S(1)}, u32[]{:S(2)}, u32[]{:S(2)}) %collective-permute-start) | collective-permute-done | bytes 196640 | tf_op jit(solution)/shard_map/ppermute | solution.py:24
  9.2 0.0 copy-start.3
  9.2 0.0 copy-done
  9.2 0.7 %copy-done.3 = bf16[192,512]{1,0:T(8,128)(2,1)} copy-done((bf16[192,512]{1,0:T(8,128)(2,1)}, bf16[192,512]{1,0:T(8,128)(2,1)S(1)}, u32[]{:S(2)}) %copy-start.3) | copy-done | bytes 196632
  9.9 3.8 %shard_map.55 = (bf16[1,32,1024]{2,1,0:T(8,128)(2,1)}, bf16[256,1024]{1,0:T(8,128)(2,1)}) custom-call(s32[3,2,32]{2,1,0:T(2,128)} %bitcast.9, s32[3]{0:T(128)} %bitcast.11, s32[1]{0:T(128)} %bitcast.2.refs_2_, bf16[192,512]{1,0:T(8,128)(2,1)} %copy-done, bf16[192,512]{1,0:T(8,128)(2,1)} %copy-done.3, bf16[512,1024]{1,0:T(8,128)(2,1)} %constant.8.clone.refs_5_.refs_6_), custom_call_target="tpu_custom_call" | custom-call | tf_op jit(solution)/shard_map/pallas_call | solution.py:175
  13.7 1.1 %collective-permute-done.1.refs_4_ = bf16[192,512]{1,0:T(8,128)(2,1)S(1)} collective-permute-done((bf16[192,512]{1,0:T(8,128)(2,1)S(1)}, bf16[192,512]{1,0:T(8,128)(2,1)S(1)}, u32[]{:S(2)}, u32[]{:S(2)}) %collective-permute-start.1) | collective-permute-done | bytes 196640 | tf_op jit(solution)/shard_map/ppermute | solution.py:24
  14.8 0.0 copy-start.1
  14.8 2.4 %collective-permute-done.2.refs_5_ = bf16[192,512]{1,0:T(8,128)(2,1)S(1)} collective-permute-done((bf16[192,512]{1,0:T(8,128)(2,1)S(1)}, bf16[192,512]{1,0:T(8,128)(2,1)S(1)}, u32[]{:S(2)}, u32[]{:S(2)}) %collective-permute-start.2) | collective-permute-done | bytes 196640 | tf_op jit(solution)/shard_map/ppermute | solution.py:24
  17.1 0.0 copy-start.2
  17.1 0.0 copy-done.1
  17.1 0.7 %copy-done.2 = bf16[192,512]{1,0:T(8,128)(2,1)} copy-done((bf16[192,512]{1,0:T(8,128)(2,1)}, bf16[192,512]{1,0:T(8,128)(2,1)S(1)}, u32[]{:S(2)}) %copy-start.2) | copy-done | bytes 196632
  17.8 4.7 %shard_map.56 = (f32[3,8,256]{2,1,0:T(8,128)}, bf16[3,3,8,256]{3,2,1,0:T(8,128)(2,1)}) custom-call(s32[3,2,32]{2,1,0:T(2,128)} %bitcast.10, s32[3]{0:T(128)} %bitcast.12, s32[1]{0:T(128)} %bitcast.2.refs_2_, bf16[256,1024]{1,0:T(8,128)(2,1)} %get-tuple-element.9.refs_3_, bf16[192,512]{1,0:T(8,128)(2,1)} %copy-done.1, bf16[192,512]{1,0:T(8,128)(2,1)} %copy-done.2, ...), custom_call_target="tpu_custom_call" | custom-call | tf_op jit(solution)/shard_map/pallas_call | solution.py:175
  22.5 0.0 copy-start.4
  22.5 0.7 %slice_bitcast_fusion.2 = (bf16[3,8,256]{2,1,0:T(8,128)(2,1)S(1)}, bf16[3,8,256]{2,1,0:T(8,128)(2,1)S(1)}, bf16[3,8,256]{2,1,0:T(8,128)(2,1)S(1)}) fusion(bf16[3,3,8,256]{3,2,1,0:T(8,128)(2,1)} %get-tuple-element.12), kind=kLoop, calls=%fused_computation.3 | loop fusion | bytes 73728 | tf_op jit(solution)/shard_map/squeeze | solution.py:188
  23.3 0.0 collective-permute-start.3
  23.3 1.5 %collective-permute-start.4 = (bf16[3,8,256]{2,1,0:T(8,128)(2,1)S(1)}, bf16[3,8,256]{2,1,0:T(8,128)(2,1)S(1)}, u32[]{:S(2)}, u32[]{:S(2)}) collective-permute-start(bf16[3,8,256]{2,1,0:T(8,128)(2,1)S(1)} %get-tuple-element.15), channel_id=1, source_target_pairs={{0,2},{1,3},{2,0},{3,1},{4,6},{5,7},{6,4},{7,5},{8,10},{9,11},{10,... | collective-permute-start | bytes 36872 | tf_op jit(solution)/shard_map/ppermute | solution.py:188
  24.8 0.4 %collective-permute-start.5 = (bf16[3,8,256]{2,1,0:T(8,128)(2,1)S(1)}, bf16[3,8,256]{2,1,0:T(8,128)(2,1)S(1)}, u32[]{:S(2)}, u32[]{:S(2)}) collective-permute-start(bf16[3,8,256]{2,1,0:T(8,128)(2,1)S(1)} %get-tuple-element.14), channel_id=1, source_target_pairs={{0,3},{1,2},{2,1},{3,0},{4,7},{5,6},{6,5},{7,4},{8,11},{9,10},{10,... | collective-permute-start | bytes 36872 | tf_op jit(solution)/shard_map/ppermute | solution.py:188
  25.1 0.0 collective-permute-done.3
  25.2 1.8 %collective-permute-done.4 = bf16[3,8,256]{2,1,0:T(8,128)(2,1)S(1)} collective-permute-done((bf16[3,8,256]{2,1,0:T(8,128)(2,1)S(1)}, bf16[3,8,256]{2,1,0:T(8,128)(2,1)S(1)}, u32[]{:S(2)}, u32[]{:S(2)}) %collective-permute-start.4) | collective-permute-done | bytes 12320 | tf_op jit(solution)/shard_map/ppermute | solution.py:188
  27.0 0.9 %collective-permute-done.5 = bf16[3,8,256]{2,1,0:T(8,128)(2,1)S(1)} collective-permute-done((bf16[3,8,256]{2,1,0:T(8,128)(2,1)S(1)}, bf16[3,8,256]{2,1,0:T(8,128)(2,1)S(1)}, u32[]{:S(2)}, u32[]{:S(2)}) %collective-permute-start.5) | collective-permute-done | bytes 12320 | tf_op jit(solution)/shard_map/ppermute | solution.py:188
  27.9 0.0 copy-done.4
  27.9 0.6 %convert_add_fusion = f32[3,8,256]{2,1,0:T(8,128)} fusion(bf16[3,8,256]{2,1,0:T(8,128)(2,1)S(1)} %collective-permute-done.5, bf16[3,8,256]{2,1,0:T(8,128)(2,1)S(1)} %collective-permute-done.4, f32[3,8,256]{2,1,0:T(8,128)S(1)} %copy-done.4, bf16[3,8,256]{2,1,0:T(8,128)(2,1)S(1)} %collective-permute-done.3), kind=kLoop, calls=%fused_computation | loop fusion | flops 36864 | bytes 86016 | tf_op jit(solution)/shard_map/add | solution.py:188
Async XLA Ops:
  1.2 8.0 %copy-start = (bf16[192,512]{1,0:T(8,128)(2,1)}, bf16[192,512]{1,0:T(8,128)(2,1)S(1)}, u32[]{:S(2)}) copy-start(bf16[192,512]{1,0:T(8,128)(2,1)S(1)} %reshape.11.refs_3_) | copy-start | bytes 589828
  1.2 8.0 %collective-permute-start = (bf16[192,512]{1,0:T(8,128)(2,1)S(1)}, bf16[192,512]{1,0:T(8,128)(2,1)S(1)}, u32[]{:S(2)}, u32[]{:S(2)}) collective-permute-start(bf16[192,512]{1,0:T(8,128)(2,1)S(1)} %reshape.11.refs_3_), channel_id=1, source_target_pairs={{0,4},{4,0},{8,12},{12,8},{16,20},{20,16},{24,28},{28,24},{1,5},{5... | collective-permute-start | bytes 589832 | tf_op jit(solution)/shard_map/ppermute | solution.py:24
  4.3 10.5 %collective-permute-start.1 = (bf16[192,512]{1,0:T(8,128)(2,1)S(1)}, bf16[192,512]{1,0:T(8,128)(2,1)S(1)}, u32[]{:S(2)}, u32[]{:S(2)}) collective-permute-start(bf16[192,512]{1,0:T(8,128)(2,1)S(1)} %reshape.11.refs_3_), channel_id=1, source_target_pairs={{0,8},{8,0},{4,12},{12,4},{16,24},{24,16},{20,28},{28,20},{1,9},{9... | collective-permute-start | bytes 589832 | tf_op jit(solution)/shard_map/ppermute | solution.py:24
  5.9 11.2 %collective-permute-start.2 = (bf16[192,512]{1,0:T(8,128)(2,1)S(1)}, bf16[192,512]{1,0:T(8,128)(2,1)S(1)}, u32[]{:S(2)}, u32[]{:S(2)}) collective-permute-start(bf16[192,512]{1,0:T(8,128)(2,1)S(1)} %reshape.11.refs_3_), channel_id=1, source_target_pairs={{0,16},{16,0},{4,20},{20,4},{8,24},{24,8},{12,28},{28,12},{1,17},{... | collective-permute-start | bytes 589832 | tf_op jit(solution)/shard_map/ppermute | solution.py:24
  9.2 0.7 %copy-start.3 = (bf16[192,512]{1,0:T(8,128)(2,1)}, bf16[192,512]{1,0:T(8,128)(2,1)S(1)}, u32[]{:S(2)}) copy-start(bf16[192,512]{1,0:T(8,128)(2,1)S(1)} %collective-permute-done.refs_4_) | copy-start | bytes 589828
  14.8 2.4 %copy-start.1 = (bf16[192,512]{1,0:T(8,128)(2,1)}, bf16[192,512]{1,0:T(8,128)(2,1)S(1)}, u32[]{:S(2)}) copy-start(bf16[192,512]{1,0:T(8,128)(2,1)S(1)} %collective-permute-done.1.refs_4_) | copy-start | bytes 589828
  17.1 0.7 %copy-start.2 = (bf16[192,512]{1,0:T(8,128)(2,1)}, bf16[192,512]{1,0:T(8,128)(2,1)S(1)}, u32[]{:S(2)}) copy-start(bf16[192,512]{1,0:T(8,128)(2,1)S(1)} %collective-permute-done.2.refs_5_) | copy-start | bytes 589828
  22.5 5.4 %copy-start.4 = (f32[3,8,256]{2,1,0:T(8,128)S(1)}, f32[3,8,256]{2,1,0:T(8,128)}, u32[]{:S(2)}) copy-start(f32[3,8,256]{2,1,0:T(8,128)} %get-tuple-element.11) | copy-start | bytes 73732
  23.3 1.9 %collective-permute-start.3 = (bf16[3,8,256]{2,1,0:T(8,128)(2,1)S(1)}, bf16[3,8,256]{2,1,0:T(8,128)(2,1)S(1)}, u32[]{:S(2)}, u32[]{:S(2)}) collective-permute-start(bf16[3,8,256]{2,1,0:T(8,128)(2,1)S(1)} %get-tuple-element.13), channel_id=1, source_target_pairs={{0,1},{1,0},{2,3},{3,2},{4,5},{5,4},{6,7},{7,6},{8,9},{9,8},{10,11... | collective-permute-start | bytes 36872 | tf_op jit(solution)/shard_map/ppermute | solution.py:188
  23.3 3.7 %collective-permute-start.4 = (bf16[3,8,256]{2,1,0:T(8,128)(2,1)S(1)}, bf16[3,8,256]{2,1,0:T(8,128)(2,1)S(1)}, u32[]{:S(2)}, u32[]{:S(2)}) collective-permute-start(bf16[3,8,256]{2,1,0:T(8,128)(2,1)S(1)} %get-tuple-element.15), channel_id=1, source_target_pairs={{0,2},{1,3},{2,0},{3,1},{4,6},{5,7},{6,4},{7,5},{8,10},{9,11},{10,... | collective-permute-start | bytes 36872 | tf_op jit(solution)/shard_map/ppermute | solution.py:188
  24.8 3.1 %collective-permute-start.5 = (bf16[3,8,256]{2,1,0:T(8,128)(2,1)S(1)}, bf16[3,8,256]{2,1,0:T(8,128)(2,1)S(1)}, u32[]{:S(2)}, u32[]{:S(2)}) collective-permute-start(bf16[3,8,256]{2,1,0:T(8,128)(2,1)S(1)} %get-tuple-element.14), channel_id=1, source_target_pairs={{0,3},{1,2},{2,1},{3,0},{4,7},{5,6},{6,5},{7,4},{8,11},{9,10},{10,... | collective-permute-start | bytes 36872 | tf_op jit(solution)/shard_map/ppermute | solution.py:188

commit v16 on v15

--- a/solution.py
+++ b/solution.py
@@ -67,25 +67,29 @@
         else:
             xout = rest.pop(0)
             spec_out = rest.pop(0) if from_waves else None
-        nscr, xpad, specl, specp, cross = rest[:5]
+        nscr, xpad, specl, specall, cross = rest[:5]
         allx = rest[5] if final else None
-
-        def spectra(w_ref, spec_ref):
+        sources = ([own_ref] if from_waves else []) + list(part_refs)
+        block = events * pad
+
+        xpad[...] = jnp.zeros(xpad.shape, jnp.float32)
+        for m, w_ref in enumerate(sources):
             x = w_ref[...].astype(jnp.float32)
             x = x - jnp.mean(x, axis=-1, keepdims=True)
             x = x * lax.rsqrt(jnp.mean(x * x, axis=-1, keepdims=True) + EPS)
             nscr[...] = x
             for e in range(events):
-                xpad[e * pad:e * pad + chans, :] = nscr[e * chans:(e + 1) * chans, :]
-            xb = xpad[...].astype(jnp.bfloat16)
-            spec = jnp.dot(xb, f_ref[...], preferred_element_type=jnp.float32)
-            spec_ref[...] = spec.astype(jnp.bfloat16).astype(jnp.float32)
-
-        xpad[...] = jnp.zeros(xpad.shape, jnp.float32)
+                row = m * block + e * pad
+                xpad[row:row + chans, :] = nscr[e * chans:(e + 1) * chans, :]
+        xb = xpad[...].astype(jnp.bfloat16)
+        spec = jnp.dot(xb, f_ref[...], preferred_element_type=jnp.float32)
+        specall[...] = spec.astype(jnp.bfloat16).astype(jnp.float32)
+
         if from_waves:
-            spectra(own_ref, specl)
-            spec_out[...] = specl[...].astype(jnp.bfloat16)
+            left_ref = specall
+            spec_out[...] = specall[0:block, :].astype(jnp.bfloat16)
         else:
+            left_ref = specl
             specl[...] = own_ref[...].astype(jnp.float32)
             for n in range(n_prev):
                 if final:
@@ -96,13 +100,13 @@
         sid = sid_ref[0]
         lane = lax.broadcasted_iota(jnp.int32, (1, 128), 1)
         for n, q in enumerate(rounds):
-            spectra(part_refs[n], specp)
+            off = (n + int(from_waves)) * block
             for r in range(slots):
                 slot = (sid ^ (r // share)) * share + r % share
                 a = jnp.minimum(jnp.maximum(pl_ref[q, 0, slot], 0), events - 1)
                 b = jnp.minimum(jnp.maximum(pl_ref[q, 1, slot], 0), events - 1)
-                left = specl[pl.ds(pl.multiple_of(a * pad, pad), pad), :]
-                right = specp[pl.ds(pl.multiple_of(b * pad, pad), pad), :]
+                left = left_ref[pl.ds(pl.multiple_of(a * pad, pad), pad), :]
+                right = specall[pl.ds(pl.multiple_of(off + b * pad, pad), pad), :]
                 lr, li = left[:, :half], left[:, half:]
                 rr, ri = right[:, :half], right[:, half:]
                 pp = lr * rr
@@ -163,11 +167,12 @@
             out_shape += (jax.ShapeDtypeStruct((events * pad, 2 * length), jnp.bfloat16),)
     if prev is not None:
         inputs.append(prev)
+    n_src = len(partners) + int(from_waves)
     scratch = [
         pltpu.VMEM((events * chans, length), jnp.float32),
-        pltpu.VMEM((events * pad, length), jnp.float32),
+        pltpu.VMEM((n_src * events * pad, length), jnp.float32),
         pltpu.VMEM((events * pad, 2 * length), jnp.float32),
-        pltpu.VMEM((events * pad, 2 * length), jnp.float32),
+        pltpu.VMEM((n_src * events * pad, 2 * length), jnp.float32),
         pltpu.VMEM((slots, 2 * length), jnp.float32),
     ]
     if final:

time: 28.8 us -> 29 us (level)
  Pallas kernels: 8.53 us -> 8.82 us
where the time goes in v16:
time: 29 us; the launch traced here: 28.7 us
  starting transfers between devices  9.09 us (31%)
  Pallas kernels  8.82 us (30%)
  waiting for transfers between devices  6.84 us (24%)
  local copies, waits for them, and re-layouts  3.33 us (11%)
  other arithmetic  0.62 us (2%)
    pallas_call x2, Pallas kernels, rounds_call(): pl.pallas_call(kernel, out_shape=out_shape, in_specs=[smem, smem, smem] +...  8.82 us
    ppermute x3, starting transfers between devices, swapped(): return lax.ppermute(block, axis, route)  7.23 us
    ppermute x3, waiting for transfers between devices, swapped(): return lax.ppermute(block, axis, route)  4.09 us
    ppermute x3, waiting for transfers between devices, station_sum(): lax.ppermute(send[j - 1], 'station', perm).astype(jnp.float32)  2.75 us
    unnamed x11, local copies, waits for them, and re-layouts  2.41 us
    ppermute x3, starting transfers between devices, station_sum(): lax.ppermute(send[j - 1], 'station', perm).astype(jnp.float32)  1.86 us
    squeeze x1, local copies, waits for them, and re-layouts, station_sum(): send[j - 1]  0.75 us
    add x1, other arithmetic, station_sum(): total + lax.ppermute(send[j - 1], 'station', perm).astype(jnp.float32)  0.62 us
  transfers between devices with their start and end apart: 6, of which 5 were waited for; matrix products, arithmetic and copies ran while one was open for 0% of the time, Pallas kernels for 13%

profile of v16, /device:TPU:0, one launch (start us, length us, event | category | flops | bytes accessed | tf_op | source)
XLA Modules:
  0.0 28.7 jit_solution(14000526810985044013)
XLA Ops:
  0.0 1.0 %copy.7 = bf16[16,4,3,512]{3,2,1,0:T(4,128)(2,1)S(1)} copy(bf16[16,4,3,512]{3,1,2,0:T(4,128)(2,1)} %param.5) | data formatting | bytes 393216 | tf_op args[0]
  1.1 0.2 reshape.11.refs_3_
  1.2 0.0 copy-start
  1.2 3.1 %collective-permute-start = (bf16[192,512]{1,0:T(8,128)(2,1)S(1)}, bf16[192,512]{1,0:T(8,128)(2,1)S(1)}, u32[]{:S(2)}, u32[]{:S(2)}) collective-permute-start(bf16[192,512]{1,0:T(8,128)(2,1)S(1)} %reshape.11.refs_3_), channel_id=1, source_target_pairs={{0,4},{4,0},{8,12},{12,8},{16,20},{20,16},{24,28},{28,24},{1,5},{5... | collective-permute-start | bytes 589832 | tf_op jit(solution)/shard_map/ppermute | solution.py:24
  4.3 1.6 %collective-permute-start.1 = (bf16[192,512]{1,0:T(8,128)(2,1)S(1)}, bf16[192,512]{1,0:T(8,128)(2,1)S(1)}, u32[]{:S(2)}, u32[]{:S(2)}) collective-permute-start(bf16[192,512]{1,0:T(8,128)(2,1)S(1)} %reshape.11.refs_3_), channel_id=1, source_target_pairs={{0,8},{8,0},{4,12},{12,4},{16,24},{24,16},{20,28},{28,20},{1,9},{9... | collective-permute-start | bytes 589832 | tf_op jit(solution)/shard_map/ppermute | solution.py:24
  5.9 2.6 %collective-permute-start.2 = (bf16[192,512]{1,0:T(8,128)(2,1)S(1)}, bf16[192,512]{1,0:T(8,128)(2,1)S(1)}, u32[]{:S(2)}, u32[]{:S(2)}) collective-permute-start(bf16[192,512]{1,0:T(8,128)(2,1)S(1)} %reshape.11.refs_3_), channel_id=1, source_target_pairs={{0,16},{16,0},{4,20},{20,4},{8,24},{24,8},{12,28},{28,12},{1,17},{... | collective-permute-start | bytes 589832 | tf_op jit(solution)/shard_map/ppermute | solution.py:24
  8.5 0.7 %collective-permute-done.refs_4_ = bf16[192,512]{1,0:T(8,128)(2,1)S(1)} collective-permute-done((bf16[192,512]{1,0:T(8,128)(2,1)S(1)}, bf16[192,512]{1,0:T(8,128)(2,1)S(1)}, u32[]{:S(2)}, u32[]{:S(2)}) %collective-permute-start) | collective-permute-done | bytes 196640 | tf_op jit(solution)/shard_map/ppermute | solution.py:24
  9.2 0.0 copy-start.3
  9.2 0.0 copy-done
  9.2 0.7 %copy-done.3 = bf16[192,512]{1,0:T(8,128)(2,1)} copy-done((bf16[192,512]{1,0:T(8,128)(2,1)}, bf16[192,512]{1,0:T(8,128)(2,1)S(1)}, u32[]{:S(2)}) %copy-start.3) | copy-done | bytes 196632
  9.9 3.9 %shard_map.55 = (bf16[1,32,1024]{2,1,0:T(8,128)(2,1)}, bf16[256,1024]{1,0:T(8,128)(2,1)}) custom-call(s32[3,2,32]{2,1,0:T(2,128)} %bitcast.9, s32[3]{0:T(128)} %bitcast.11, s32[1]{0:T(128)} %bitcast.2.refs_2_, bf16[192,512]{1,0:T(8,128)(2,1)} %copy-done, bf16[192,512]{1,0:T(8,128)(2,1)} %copy-done.3, bf16[512,1024]{1,0:T(8,128)(2,1)} %constant.8.clone.refs_5_.refs_6_), custom_call_target="tpu_custom_call" | custom-call | tf_op jit(solution)/shard_map/pallas_call | solution.py:180
  13.8 1.0 %collective-permute-done.1.refs_4_ = bf16[192,512]{1,0:T(8,128)(2,1)S(1)} collective-permute-done((bf16[192,512]{1,0:T(8,128)(2,1)S(1)}, bf16[192,512]{1,0:T(8,128)(2,1)S(1)}, u32[]{:S(2)}, u32[]{:S(2)}) %collective-permute-start.1) | collective-permute-done | bytes 196640 | tf_op jit(solution)/shard_map/ppermute | solution.py:24
  14.8 0.0 copy-start.1
  14.8 2.4 %collective-permute-done.2.refs_5_ = bf16[192,512]{1,0:T(8,128)(2,1)S(1)} collective-permute-done((bf16[192,512]{1,0:T(8,128)(2,1)S(1)}, bf16[192,512]{1,0:T(8,128)(2,1)S(1)}, u32[]{:S(2)}, u32[]{:S(2)}) %collective-permute-start.2) | collective-permute-done | bytes 196640 | tf_op jit(solution)/shard_map/ppermute | solution.py:24
  17.1 0.0 copy-start.2
  17.1 0.0 copy-done.1
  17.1 0.7 %copy-done.2 = bf16[192,512]{1,0:T(8,128)(2,1)} copy-done((bf16[192,512]{1,0:T(8,128)(2,1)}, bf16[192,512]{1,0:T(8,128)(2,1)S(1)}, u32[]{:S(2)}) %copy-start.2) | copy-done | bytes 196632
  17.8 5.0 %shard_map.56 = (f32[3,8,256]{2,1,0:T(8,128)}, bf16[3,3,8,256]{3,2,1,0:T(8,128)(2,1)}) custom-call(s32[3,2,32]{2,1,0:T(2,128)} %bitcast.10, s32[3]{0:T(128)} %bitcast.12, s32[1]{0:T(128)} %bitcast.2.refs_2_, bf16[256,1024]{1,0:T(8,128)(2,1)} %get-tuple-element.9.refs_3_, bf16[192,512]{1,0:T(8,128)(2,1)} %copy-done.1, bf16[192,512]{1,0:T(8,128)(2,1)} %copy-done.2, ...), custom_call_target="tpu_custom_call" | custom-call | tf_op jit(solution)/shard_map/pallas_call | solution.py:180
  22.8 0.0 copy-start.4
  22.8 0.7 %slice_bitcast_fusion.2 = (bf16[3,8,256]{2,1,0:T(8,128)(2,1)S(1)}, bf16[3,8,256]{2,1,0:T(8,128)(2,1)S(1)}, bf16[3,8,256]{2,1,0:T(8,128)(2,1)S(1)}) fusion(bf16[3,3,8,256]{3,2,1,0:T(8,128)(2,1)} %get-tuple-element.12), kind=kLoop, calls=%fused_computation.3 | loop fusion | bytes 73728 | tf_op jit(solution)/shard_map/squeeze | solution.py:193
  23.5 0.0 collective-permute-start.3
  23.5 1.5 %collective-permute-start.4 = (bf16[3,8,256]{2,1,0:T(8,128)(2,1)S(1)}, bf16[3,8,256]{2,1,0:T(8,128)(2,1)S(1)}, u32[]{:S(2)}, u32[]{:S(2)}) collective-permute-start(bf16[3,8,256]{2,1,0:T(8,128)(2,1)S(1)} %get-tuple-element.15), channel_id=1, source_target_pairs={{0,2},{1,3},{2,0},{3,1},{4,6},{5,7},{6,4},{7,5},{8,10},{9,11},{10,... | collective-permute-start | bytes 36872 | tf_op jit(solution)/shard_map/ppermute | solution.py:193
  25.0 0.4 %collective-permute-start.5 = (bf16[3,8,256]{2,1,0:T(8,128)(2,1)S(1)}, bf16[3,8,256]{2,1,0:T(8,128)(2,1)S(1)}, u32[]{:S(2)}, u32[]{:S(2)}) collective-permute-start(bf16[3,8,256]{2,1,0:T(8,128)(2,1)S(1)} %get-tuple-element.14), channel_id=1, source_target_pairs={{0,3},{1,2},{2,1},{3,0},{4,7},{5,6},{6,5},{7,4},{8,11},{9,10},{10,... | collective-permute-start | bytes 36872 | tf_op jit(solution)/shard_map/ppermute | solution.py:193
  25.4 0.0 collective-permute-done.3
  25.4 1.8 %collective-permute-done.4 = bf16[3,8,256]{2,1,0:T(8,128)(2,1)S(1)} collective-permute-done((bf16[3,8,256]{2,1,0:T(8,128)(2,1)S(1)}, bf16[3,8,256]{2,1,0:T(8,128)(2,1)S(1)}, u32[]{:S(2)}, u32[]{:S(2)}) %collective-permute-start.4) | collective-permute-done | bytes 12320 | tf_op jit(solution)/shard_map/ppermute | solution.py:193
  27.2 0.9 %collective-permute-done.5 = bf16[3,8,256]{2,1,0:T(8,128)(2,1)S(1)} collective-permute-done((bf16[3,8,256]{2,1,0:T(8,128)(2,1)S(1)}, bf16[3,8,256]{2,1,0:T(8,128)(2,1)S(1)}, u32[]{:S(2)}, u32[]{:S(2)}) %collective-permute-start.5) | collective-permute-done | bytes 12320 | tf_op jit(solution)/shard_map/ppermute | solution.py:193
  28.1 0.0 copy-done.4
  28.1 0.6 %convert_add_fusion = f32[3,8,256]{2,1,0:T(8,128)} fusion(bf16[3,8,256]{2,1,0:T(8,128)(2,1)S(1)} %collective-permute-done.5, bf16[3,8,256]{2,1,0:T(8,128)(2,1)S(1)} %collective-permute-done.4, f32[3,8,256]{2,1,0:T(8,128)S(1)} %copy-done.4, bf16[3,8,256]{2,1,0:T(8,128)(2,1)S(1)} %collective-permute-done.3), kind=kLoop, calls=%fused_computation | loop fusion | flops 36864 | bytes 86016 | tf_op jit(solution)/shard_map/add | solution.py:193
Async XLA Ops:
  1.2 8.0 %copy-start = (bf16[192,512]{1,0:T(8,128)(2,1)}, bf16[192,512]{1,0:T(8,128)(2,1)S(1)}, u32[]{:S(2)}) copy-start(bf16[192,512]{1,0:T(8,128)(2,1)S(1)} %reshape.11.refs_3_) | copy-start | bytes 589828
  1.2 8.0 %collective-permute-start = (bf16[192,512]{1,0:T(8,128)(2,1)S(1)}, bf16[192,512]{1,0:T(8,128)(2,1)S(1)}, u32[]{:S(2)}, u32[]{:S(2)}) collective-permute-start(bf16[192,512]{1,0:T(8,128)(2,1)S(1)} %reshape.11.refs_3_), channel_id=1, source_target_pairs={{0,4},{4,0},{8,12},{12,8},{16,20},{20,16},{24,28},{28,24},{1,5},{5... | collective-permute-start | bytes 589832 | tf_op jit(solution)/shard_map/ppermute | solution.py:24
  4.3 10.5 %collective-permute-start.1 = (bf16[192,512]{1,0:T(8,128)(2,1)S(1)}, bf16[192,512]{1,0:T(8,128)(2,1)S(1)}, u32[]{:S(2)}, u32[]{:S(2)}) collective-permute-start(bf16[192,512]{1,0:T(8,128)(2,1)S(1)} %reshape.11.refs_3_), channel_id=1, source_target_pairs={{0,8},{8,0},{4,12},{12,4},{16,24},{24,16},{20,28},{28,20},{1,9},{9... | collective-permute-start | bytes 589832 | tf_op jit(solution)/shard_map/ppermute | solution.py:24
  5.9 11.2 %collective-permute-start.2 = (bf16[192,512]{1,0:T(8,128)(2,1)S(1)}, bf16[192,512]{1,0:T(8,128)(2,1)S(1)}, u32[]{:S(2)}, u32[]{:S(2)}) collective-permute-start(bf16[192,512]{1,0:T(8,128)(2,1)S(1)} %reshape.11.refs_3_), channel_id=1, source_target_pairs={{0,16},{16,0},{4,20},{20,4},{8,24},{24,8},{12,28},{28,12},{1,17},{... | collective-permute-start | bytes 589832 | tf_op jit(solution)/shard_map/ppermute | solution.py:24
  9.2 0.7 %copy-start.3 = (bf16[192,512]{1,0:T(8,128)(2,1)}, bf16[192,512]{1,0:T(8,128)(2,1)S(1)}, u32[]{:S(2)}) copy-start(bf16[192,512]{1,0:T(8,128)(2,1)S(1)} %collective-permute-done.refs_4_) | copy-start | bytes 589828
  14.8 2.4 %copy-start.1 = (bf16[192,512]{1,0:T(8,128)(2,1)}, bf16[192,512]{1,0:T(8,128)(2,1)S(1)}, u32[]{:S(2)}) copy-start(bf16[192,512]{1,0:T(8,128)(2,1)S(1)} %collective-permute-done.1.refs_4_) | copy-start | bytes 589828
  17.1 0.7 %copy-start.2 = (bf16[192,512]{1,0:T(8,128)(2,1)}, bf16[192,512]{1,0:T(8,128)(2,1)S(1)}, u32[]{:S(2)}) copy-start(bf16[192,512]{1,0:T(8,128)(2,1)S(1)} %collective-permute-done.2.refs_5_) | copy-start | bytes 589828
  22.8 5.4 %copy-start.4 = (f32[3,8,256]{2,1,0:T(8,128)S(1)}, f32[3,8,256]{2,1,0:T(8,128)}, u32[]{:S(2)}) copy-start(f32[3,8,256]{2,1,0:T(8,128)} %get-tuple-element.11) | copy-start | bytes 73732
  23.5 1.9 %collective-permute-start.3 = (bf16[3,8,256]{2,1,0:T(8,128)(2,1)S(1)}, bf16[3,8,256]{2,1,0:T(8,128)(2,1)S(1)}, u32[]{:S(2)}, u32[]{:S(2)}) collective-permute-start(bf16[3,8,256]{2,1,0:T(8,128)(2,1)S(1)} %get-tuple-element.13), channel_id=1, source_target_pairs={{0,1},{1,0},{2,3},{3,2},{4,5},{5,4},{6,7},{7,6},{8,9},{9,8},{10,11... | collective-permute-start | bytes 36872 | tf_op jit(solution)/shard_map/ppermute | solution.py:193
  23.5 3.7 %collective-permute-start.4 = (bf16[3,8,256]{2,1,0:T(8,128)(2,1)S(1)}, bf16[3,8,256]{2,1,0:T(8,128)(2,1)S(1)}, u32[]{:S(2)}, u32[]{:S(2)}) collective-permute-start(bf16[3,8,256]{2,1,0:T(8,128)(2,1)S(1)} %get-tuple-element.15), channel_id=1, source_target_pairs={{0,2},{1,3},{2,0},{3,1},{4,6},{5,7},{6,4},{7,5},{8,10},{9,11},{10,... | collective-permute-start | bytes 36872 | tf_op jit(solution)/shard_map/ppermute | solution.py:193
  25.0 3.1 %collective-permute-start.5 = (bf16[3,8,256]{2,1,0:T(8,128)(2,1)S(1)}, bf16[3,8,256]{2,1,0:T(8,128)(2,1)S(1)}, u32[]{:S(2)}, u32[]{:S(2)}) collective-permute-start(bf16[3,8,256]{2,1,0:T(8,128)(2,1)S(1)} %get-tuple-element.14), channel_id=1, source_target_pairs={{0,3},{1,2},{2,1},{3,0},{4,7},{5,6},{6,5},{7,4},{8,11},{9,10},{10,... | collective-permute-start | bytes 36872 | tf_op jit(solution)/shard_map/ppermute | solution.py:193

commit v17 on v15

--- a/solution.py
+++ b/solution.py
@@ -50,9 +50,10 @@
     return fwd, inv.astype(ml_dtypes.bfloat16)
 
 
-def make_kernel(events, chans, pad, length, slots, groups, share, rounds, n_prev, from_waves, final):
+def make_kernel(events, chans, pad, length, slots, groups, share, rounds, prev_rounds, from_waves, final):
     half = length
     n_part = len(rounds)
+    n_prev = len(prev_rounds)
     total_rounds = n_prev + n_part
 
     def kernel(*refs):
@@ -87,9 +88,9 @@
             spec_out[...] = specl[...].astype(jnp.bfloat16)
         else:
             specl[...] = own_ref[...].astype(jnp.float32)
-            for n in range(n_prev):
+            for n, q in enumerate(prev_rounds):
                 if final:
-                    allx[n * slots:(n + 1) * slots, :] = prev_ref[n]
+                    allx[q * slots:(q + 1) * slots, :] = prev_ref[n]
                 else:
                     xout[n] = prev_ref[n]
 
@@ -117,7 +118,7 @@
                 cross[r:r + 1, half + 128:] = im[:, 128:]
             cb = cross[...].astype(jnp.bfloat16)
             if final:
-                allx[(n_prev + n) * slots:(n_prev + n + 1) * slots, :] = cb
+                allx[q * slots:(q + 1) * slots, :] = cb
             else:
                 xout[n_prev + n] = cb
 
@@ -141,7 +142,7 @@
 
 
 def rounds_call(pairs, counts, sid, own, partners, fwd, inv, rounds, events, chans, slots, groups,
-                prev=None, final=False):
+                prev=None, prev_rounds=(), final=False):
     length = fwd.shape[0]
     lags = inv.shape[1]
     pad = 16
@@ -149,7 +150,8 @@
     from_waves = prev is None and own.shape[0] == events * chans
     n_prev = 0 if prev is None else prev.shape[0]
     total = n_prev + len(rounds)
-    kernel = make_kernel(events, chans, pad, length, slots, groups, share, rounds, n_prev, from_waves, final)
+    kernel = make_kernel(events, chans, pad, length, slots, groups, share, rounds, list(prev_rounds),
+                         from_waves, final)
     smem = pl.BlockSpec(memory_space=pltpu.SMEM)
     vmem = pl.BlockSpec(memory_space=pltpu.VMEM)
     inputs = [pairs, counts, sid, own, *partners, fwd]
@@ -202,11 +204,13 @@
     pairs = jnp.transpose(pair_lists, (0, 2, 1))
     counts = pair_counts.reshape(-1)
     partners = {q: swapped(flat, "region", q) for q in reversed(range(rounds))}
-    crosses, spec = rounds_call(pairs, counts, sid, flat, [partners[0]], fwd, inv,
-                                [0], events, chans, slots, groups)
-    rest = list(range(1, rounds))
+    first = [1 % rounds]
+    rest = [q for q in reversed(range(rounds)) if q not in first]
+    crosses, spec = rounds_call(pairs, counts, sid, flat, [partners[q] for q in first], fwd, inv,
+                                first, events, chans, slots, groups)
     keep, send = rounds_call(pairs, counts, sid, spec, [partners[q] for q in rest], fwd, inv,
-                             rest, events, chans, slots, groups, prev=crosses, final=True)
+                             rest, events, chans, slots, groups, prev=crosses, prev_rounds=first,
+                             final=True)
     return station_sum(keep, send, groups)
 
 

time: 28.8 us -> 29.7 us (1.031)
  waiting for transfers between devices: 6.92 us -> 7.81 us
    ppermute x3, waiting for transfers between devices: 4.17 us -> 4.89 us  [swapped(): return lax.ppermute(block, axis, route)]
  transfers between devices with their start and end apart: 6 -> 6, of which waited for: 5 -> 3; matrix products, arithmetic and copies ran while one was open for 0% -> 0% of each run, Pallas kernels for 13% -> 13%
where the time goes in v17:
time: 29.7 us; the launch traced here: 29.5 us
  starting transfers between devices  9.09 us (31%)
  Pallas kernels  8.53 us (29%)
  waiting for transfers between devices  7.81 us (26%)
  local copies, waits for them, and re-layouts  3.38 us (11%)
  other arithmetic  0.62 us (2%)
    pallas_call x2, Pallas kernels, rounds_call(): pl.pallas_call(kernel, out_shape=out_shape, in_specs=[smem, smem, smem] +...  8.53 us
    ppermute x3, starting transfers between devices, swapped(): return lax.ppermute(block, axis, route)  7.23 us
    ppermute x3, waiting for transfers between devices, swapped(): return lax.ppermute(block, axis, route)  4.89 us
    ppermute x3, waiting for transfers between devices, station_sum(): lax.ppermute(send[j - 1], 'station', perm).astype(jnp.float32)  2.91 us
    unnamed x11, local copies, waits for them, and re-layouts  2.46 us
    ppermute x3, starting transfers between devices, station_sum(): lax.ppermute(send[j - 1], 'station', perm).astype(jnp.float32)  1.86 us
    squeeze x1, local copies, waits for them, and re-layouts, station_sum(): send[j - 1]  0.75 us
    add x1, other arithmetic, station_sum(): total + lax.ppermute(send[j - 1], 'station', perm).astype(jnp.float32)  0.62 us
  transfers between devices with their start and end apart: 6, of which 3 were waited for; matrix products, arithmetic and copies ran while one was open for 0% of the time, Pallas kernels for 13%

profile of v17, /device:TPU:0, one launch (start us, length us, event | category | flops | bytes accessed | tf_op | source)
XLA Modules:
  0.0 29.5 jit_solution(4389964758363526711)
XLA Ops:
  0.0 1.0 %copy.7 = bf16[16,4,3,512]{3,2,1,0:T(4,128)(2,1)S(1)} copy(bf16[16,4,3,512]{3,1,2,0:T(4,128)(2,1)} %param.5) | data formatting | bytes 393216 | tf_op args[0]
  1.1 0.2 reshape.11.refs_3_
  1.2 0.0 copy-start
  1.2 3.1 %collective-permute-start = (bf16[192,512]{1,0:T(8,128)(2,1)S(1)}, bf16[192,512]{1,0:T(8,128)(2,1)S(1)}, u32[]{:S(2)}, u32[]{:S(2)}) collective-permute-start(bf16[192,512]{1,0:T(8,128)(2,1)S(1)} %reshape.11.refs_3_), channel_id=1, source_target_pairs={{0,8},{8,0},{4,12},{12,4},{16,24},{24,16},{20,28},{28,20},{1,9},{9... | collective-permute-start | bytes 589832 | tf_op jit(solution)/shard_map/ppermute | solution.py:24
  4.4 2.6 %collective-permute-start.1 = (bf16[192,512]{1,0:T(8,128)(2,1)S(1)}, bf16[192,512]{1,0:T(8,128)(2,1)S(1)}, u32[]{:S(2)}, u32[]{:S(2)}) collective-permute-start(bf16[192,512]{1,0:T(8,128)(2,1)S(1)} %reshape.11.refs_3_), channel_id=1, source_target_pairs={{0,16},{16,0},{4,20},{20,4},{8,24},{24,8},{12,28},{28,12},{1,17},{... | collective-permute-start | bytes 589832 | tf_op jit(solution)/shard_map/ppermute | solution.py:24
  6.9 1.5 %collective-permute-start.2 = (bf16[192,512]{1,0:T(8,128)(2,1)S(1)}, bf16[192,512]{1,0:T(8,128)(2,1)S(1)}, u32[]{:S(2)}, u32[]{:S(2)}) collective-permute-start(bf16[192,512]{1,0:T(8,128)(2,1)S(1)} %reshape.11.refs_3_), channel_id=1, source_target_pairs={{0,4},{4,0},{8,12},{12,8},{16,20},{20,16},{24,28},{28,24},{1,5},{5... | collective-permute-start | bytes 589832 | tf_op jit(solution)/shard_map/ppermute | solution.py:24
  8.5 4.9 %collective-permute-done.refs_4_ = bf16[192,512]{1,0:T(8,128)(2,1)S(1)} collective-permute-done((bf16[192,512]{1,0:T(8,128)(2,1)S(1)}, bf16[192,512]{1,0:T(8,128)(2,1)S(1)}, u32[]{:S(2)}, u32[]{:S(2)}) %collective-permute-start) | collective-permute-done | bytes 196640 | tf_op jit(solution)/shard_map/ppermute | solution.py:24
  13.4 0.0 copy-start.3
  13.4 0.0 copy-done
  13.4 0.7 %copy-done.3 = bf16[192,512]{1,0:T(8,128)(2,1)} copy-done((bf16[192,512]{1,0:T(8,128)(2,1)}, bf16[192,512]{1,0:T(8,128)(2,1)S(1)}, u32[]{:S(2)}) %copy-start.3) | copy-done | bytes 196632
  14.0 3.8 %shard_map.55 = (bf16[1,32,1024]{2,1,0:T(8,128)(2,1)}, bf16[256,1024]{1,0:T(8,128)(2,1)}) custom-call(s32[3,2,32]{2,1,0:T(2,128)} %bitcast.9, s32[3]{0:T(128)} %bitcast.11, s32[1]{0:T(128)} %bitcast.2.refs_2_, bf16[192,512]{1,0:T(8,128)(2,1)} %copy-done, bf16[192,512]{1,0:T(8,128)(2,1)} %copy-done.3, bf16[512,1024]{1,0:T(8,128)(2,1)} %constant.8.clone.refs_5_.refs_6_), custom_call_target="tpu_custom_call" | custom-call | tf_op jit(solution)/shard_map/pallas_call | solution.py:177
  17.8 0.0 collective-permute-done.1.refs_4_
  17.8 0.0 copy-start.1
  17.8 0.0 collective-permute-done.2.refs_5_
  17.9 0.0 copy-start.2
  17.9 0.7 %copy-done.1 = bf16[192,512]{1,0:T(8,128)(2,1)} copy-done((bf16[192,512]{1,0:T(8,128)(2,1)}, bf16[192,512]{1,0:T(8,128)(2,1)S(1)}, u32[]{:S(2)}) %copy-start.1) | copy-done | bytes 196632
  18.5 0.1 copy-done.2
  18.6 4.7 %shard_map.56 = (f32[3,8,256]{2,1,0:T(8,128)}, bf16[3,3,8,256]{3,2,1,0:T(8,128)(2,1)}) custom-call(s32[3,2,32]{2,1,0:T(2,128)} %bitcast.10, s32[3]{0:T(128)} %bitcast.12, s32[1]{0:T(128)} %bitcast.2.refs_2_, bf16[256,1024]{1,0:T(8,128)(2,1)} %get-tuple-element.9.refs_3_, bf16[192,512]{1,0:T(8,128)(2,1)} %copy-done.1, bf16[192,512]{1,0:T(8,128)(2,1)} %copy-done.2, ...), custom_call_target="tpu_custom_call" | custom-call | tf_op jit(solution)/shard_map/pallas_call | solution.py:177
  23.3 0.0 copy-start.4
  23.3 0.7 %slice_bitcast_fusion.2 = (bf16[3,8,256]{2,1,0:T(8,128)(2,1)S(1)}, bf16[3,8,256]{2,1,0:T(8,128)(2,1)S(1)}, bf16[3,8,256]{2,1,0:T(8,128)(2,1)S(1)}) fusion(bf16[3,3,8,256]{3,2,1,0:T(8,128)(2,1)} %get-tuple-element.12), kind=kLoop, calls=%fused_computation.3 | loop fusion | bytes 73728 | tf_op jit(solution)/shard_map/squeeze | solution.py:190
  24.1 0.0 collective-permute-start.3
  24.1 1.7 %collective-permute-start.4 = (bf16[3,8,256]{2,1,0:T(8,128)(2,1)S(1)}, bf16[3,8,256]{2,1,0:T(8,128)(2,1)S(1)}, u32[]{:S(2)}, u32[]{:S(2)}) collective-permute-start(bf16[3,8,256]{2,1,0:T(8,128)(2,1)S(1)} %get-tuple-element.15), channel_id=1, source_target_pairs={{0,2},{1,3},{2,0},{3,1},{4,6},{5,7},{6,4},{7,5},{8,10},{9,11},{10,... | collective-permute-start | bytes 36872 | tf_op jit(solution)/shard_map/ppermute | solution.py:190
  25.7 0.2 collective-permute-start.5
  25.9 0.0 collective-permute-done.3
  25.9 1.8 %collective-permute-done.4 = bf16[3,8,256]{2,1,0:T(8,128)(2,1)S(1)} collective-permute-done((bf16[3,8,256]{2,1,0:T(8,128)(2,1)S(1)}, bf16[3,8,256]{2,1,0:T(8,128)(2,1)S(1)}, u32[]{:S(2)}, u32[]{:S(2)}) %collective-permute-start.4) | collective-permute-done | bytes 12320 | tf_op jit(solution)/shard_map/ppermute | solution.py:190
  27.8 1.1 %collective-permute-done.5 = bf16[3,8,256]{2,1,0:T(8,128)(2,1)S(1)} collective-permute-done((bf16[3,8,256]{2,1,0:T(8,128)(2,1)S(1)}, bf16[3,8,256]{2,1,0:T(8,128)(2,1)S(1)}, u32[]{:S(2)}, u32[]{:S(2)}) %collective-permute-start.5) | collective-permute-done | bytes 12320 | tf_op jit(solution)/shard_map/ppermute | solution.py:190
  28.8 0.0 copy-done.4
  28.8 0.6 %convert_add_fusion = f32[3,8,256]{2,1,0:T(8,128)} fusion(bf16[3,8,256]{2,1,0:T(8,128)(2,1)S(1)} %collective-permute-done.5, bf16[3,8,256]{2,1,0:T(8,128)(2,1)S(1)} %collective-permute-done.4, f32[3,8,256]{2,1,0:T(8,128)S(1)} %copy-done.4, bf16[3,8,256]{2,1,0:T(8,128)(2,1)S(1)} %collective-permute-done.3), kind=kLoop, calls=%fused_computation | loop fusion | flops 36864 | bytes 86016 | tf_op jit(solution)/shard_map/add | solution.py:190
Async XLA Ops:
  1.2 12.1 %copy-start = (bf16[192,512]{1,0:T(8,128)(2,1)}, bf16[192,512]{1,0:T(8,128)(2,1)S(1)}, u32[]{:S(2)}) copy-start(bf16[192,512]{1,0:T(8,128)(2,1)S(1)} %reshape.11.refs_3_) | copy-start | bytes 589828
  1.2 12.1 %collective-permute-start = (bf16[192,512]{1,0:T(8,128)(2,1)S(1)}, bf16[192,512]{1,0:T(8,128)(2,1)S(1)}, u32[]{:S(2)}, u32[]{:S(2)}) collective-permute-start(bf16[192,512]{1,0:T(8,128)(2,1)S(1)} %reshape.11.refs_3_), channel_id=1, source_target_pairs={{0,8},{8,0},{4,12},{12,4},{16,24},{24,16},{20,28},{28,20},{1,9},{9... | collective-permute-start | bytes 589832 | tf_op jit(solution)/shard_map/ppermute | solution.py:24
  4.4 13.5 %collective-permute-start.1 = (bf16[192,512]{1,0:T(8,128)(2,1)S(1)}, bf16[192,512]{1,0:T(8,128)(2,1)S(1)}, u32[]{:S(2)}, u32[]{:S(2)}) collective-permute-start(bf16[192,512]{1,0:T(8,128)(2,1)S(1)} %reshape.11.refs_3_), channel_id=1, source_target_pairs={{0,16},{16,0},{4,20},{20,4},{8,24},{24,8},{12,28},{28,12},{1,17},{... | collective-permute-start | bytes 589832 | tf_op jit(solution)/shard_map/ppermute | solution.py:24
  6.9 10.9 %collective-permute-start.2 = (bf16[192,512]{1,0:T(8,128)(2,1)S(1)}, bf16[192,512]{1,0:T(8,128)(2,1)S(1)}, u32[]{:S(2)}, u32[]{:S(2)}) collective-permute-start(bf16[192,512]{1,0:T(8,128)(2,1)S(1)} %reshape.11.refs_3_), channel_id=1, source_target_pairs={{0,4},{4,0},{8,12},{12,8},{16,20},{20,16},{24,28},{28,24},{1,5},{5... | collective-permute-start | bytes 589832 | tf_op jit(solution)/shard_map/ppermute | solution.py:24
  13.4 0.7 %copy-start.3 = (bf16[192,512]{1,0:T(8,128)(2,1)}, bf16[192,512]{1,0:T(8,128)(2,1)S(1)}, u32[]{:S(2)}) copy-start(bf16[192,512]{1,0:T(8,128)(2,1)S(1)} %collective-permute-done.refs_4_) | copy-start | bytes 589828
  17.8 0.7 %copy-start.1 = (bf16[192,512]{1,0:T(8,128)(2,1)}, bf16[192,512]{1,0:T(8,128)(2,1)S(1)}, u32[]{:S(2)}) copy-start(bf16[192,512]{1,0:T(8,128)(2,1)S(1)} %collective-permute-done.1.refs_4_) | copy-start | bytes 589828
  17.9 0.7 %copy-start.2 = (bf16[192,512]{1,0:T(8,128)(2,1)}, bf16[192,512]{1,0:T(8,128)(2,1)S(1)}, u32[]{:S(2)}) copy-start(bf16[192,512]{1,0:T(8,128)(2,1)S(1)} %collective-permute-done.2.refs_5_) | copy-start | bytes 589828
  23.3 5.5 %copy-start.4 = (f32[3,8,256]{2,1,0:T(8,128)S(1)}, f32[3,8,256]{2,1,0:T(8,128)}, u32[]{:S(2)}) copy-start(f32[3,8,256]{2,1,0:T(8,128)} %get-tuple-element.11) | copy-start | bytes 73732
  24.1 1.9 %collective-permute-start.3 = (bf16[3,8,256]{2,1,0:T(8,128)(2,1)S(1)}, bf16[3,8,256]{2,1,0:T(8,128)(2,1)S(1)}, u32[]{:S(2)}, u32[]{:S(2)}) collective-permute-start(bf16[3,8,256]{2,1,0:T(8,128)(2,1)S(1)} %get-tuple-element.13), channel_id=1, source_target_pairs={{0,1},{1,0},{2,3},{3,2},{4,5},{5,4},{6,7},{7,6},{8,9},{9,8},{10,11... | collective-permute-start | bytes 36872 | tf_op jit(solution)/shard_map/ppermute | solution.py:190
  24.1 3.7 %collective-permute-start.4 = (bf16[3,8,256]{2,1,0:T(8,128)(2,1)S(1)}, bf16[3,8,256]{2,1,0:T(8,128)(2,1)S(1)}, u32[]{:S(2)}, u32[]{:S(2)}) collective-permute-start(bf16[3,8,256]{2,1,0:T(8,128)(2,1)S(1)} %get-tuple-element.15), channel_id=1, source_target_pairs={{0,2},{1,3},{2,0},{3,1},{4,6},{5,7},{6,4},{7,5},{8,10},{9,11},{10,... | collective-permute-start | bytes 36872 | tf_op jit(solution)/shard_map/ppermute | solution.py:190
  25.7 3.1 %collective-permute-start.5 = (bf16[3,8,256]{2,1,0:T(8,128)(2,1)S(1)}, bf16[3,8,256]{2,1,0:T(8,128)(2,1)S(1)}, u32[]{:S(2)}, u32[]{:S(2)}) collective-permute-start(bf16[3,8,256]{2,1,0:T(8,128)(2,1)S(1)} %get-tuple-element.14), channel_id=1, source_target_pairs={{0,3},{1,2},{2,1},{3,0},{4,7},{5,6},{6,5},{7,4},{8,11},{9,10},{10,... | collective-permute-start | bytes 36872 | tf_op jit(solution)/shard_map/ppermute | solution.py:190

commit v18 on v15

--- a/solution.py
+++ b/solution.py
@@ -63,7 +63,8 @@
         g_ref = rest.pop(0) if final else None
         prev_ref = rest.pop(0) if n_prev else None
         if final:
-            keep_ref, send_ref = rest.pop(0), rest.pop(0)
+            keep_ref = rest.pop(0)
+            send_refs = [rest.pop(0) for _ in range(groups - 1)]
         else:
             xout = rest.pop(0)
             spec_out = rest.pop(0) if from_waves else None
@@ -135,7 +136,7 @@
                 keep_ref[q] = corr[q * slots:q * slots + share]
                 for j in range(1, groups):
                     lo = q * slots + j * share
-                    send_ref[j - 1, q] = corr[lo:lo + share].astype(jnp.bfloat16)
+                    send_refs[j - 1][q] = corr[lo:lo + share]
 
     return kernel
 
@@ -155,8 +156,7 @@
     inputs = [pairs, counts, sid, own, *partners, fwd]
     if final:
         inputs.append(inv)
-        out_shape = (jax.ShapeDtypeStruct((total, share, lags), jnp.float32),
-                     jax.ShapeDtypeStruct((groups - 1, total, share, lags), jnp.bfloat16))
+        out_shape = tuple(jax.ShapeDtypeStruct((total, share, lags), jnp.float32) for _ in range(groups))
     else:
         out_shape = (jax.ShapeDtypeStruct((total, slots, 2 * length), jnp.bfloat16),)
         if from_waves:
@@ -205,7 +205,7 @@
     crosses, spec = rounds_call(pairs, counts, sid, flat, [partners[0]], fwd, inv,
                                 [0], events, chans, slots, groups)
     rest = list(range(1, rounds))
-    keep, send = rounds_call(pairs, counts, sid, spec, [partners[q] for q in rest], fwd, inv,
+    keep, *send = rounds_call(pairs, counts, sid, spec, [partners[q] for q in rest], fwd, inv,
                              rest, events, chans, slots, groups, prev=crosses, final=True)
     return station_sum(keep, send, groups)
 

time: 28.8 us -> 29.2 us (1.014)
  local copies, waits for them, and re-layouts: 3.33 us -> 2.56 us
  other arithmetic: 0.62 us -> 1.35 us
  waiting for transfers between devices: 6.92 us -> 7.33 us
    squeeze x1 -> x0, local copies, waits for them, and re-layouts: 0.75 us -> none  [station_sum(): send[j - 1]]
    add x1, other arithmetic: 0.62 us -> 1.35 us  [station_sum(): total + lax.ppermute(send[j - 1], 'station', perm).astype(jnp.float32)]
    ppermute x3, waiting for transfers between devices: 2.75 us -> 3.15 us  [station_sum(): lax.ppermute(send[j - 1], 'station', perm).astype(jnp.float32)]
    unnamed x11 -> x9, local copies, waits for them, and re-layouts: 2.41 us -> 2.39 us
where the time goes in v18:
time: 29.2 us; the launch traced here: 28.9 us
  starting transfers between devices  9.09 us (31%)
  Pallas kernels  8.52 us (29%)
  waiting for transfers between devices  7.33 us (25%)
  local copies, waits for them, and re-layouts  2.56 us (9%)
  other arithmetic  1.35 us (5%)
    pallas_call x2, Pallas kernels, rounds_call(): pl.pallas_call(kernel, out_shape=out_shape, in_specs=[smem, smem, smem] +...  8.52 us
    ppermute x3, starting transfers between devices, swapped(): return lax.ppermute(block, axis, route)  7.23 us
    ppermute x3, waiting for transfers between devices, swapped(): return lax.ppermute(block, axis, route)  4.18 us
    ppermute x3, waiting for transfers between devices, station_sum(): lax.ppermute(send[j - 1], 'station', perm).astype(jnp.float32)  3.15 us
    unnamed x9, local copies, waits for them, and re-layouts  2.39 us
    ppermute x3, starting transfers between devices, station_sum(): lax.ppermute(send[j - 1], 'station', perm).astype(jnp.float32)  1.86 us
    add x1, other arithmetic, station_sum(): total + lax.ppermute(send[j - 1], 'station', perm).astype(jnp.float32)  1.35 us
  transfers between devices with their start and end apart: 6, of which 5 were waited for; matrix products, arithmetic and copies ran while one was open for 0% of the time, Pallas kernels for 13%

profile of v18, /device:TPU:0, one launch (start us, length us, event | category | flops | bytes accessed | tf_op | source)
XLA Modules:
  0.0 28.9 jit_solution(17542561319548260214)
XLA Ops:
  0.0 1.0 %copy.7 = bf16[16,4,3,512]{3,2,1,0:T(4,128)(2,1)S(1)} copy(bf16[16,4,3,512]{3,1,2,0:T(4,128)(2,1)} %param.5) | data formatting | bytes 393216 | tf_op args[0]
  1.1 0.2 reshape.11.refs_3_
  1.2 0.0 copy-start
  1.2 3.1 %collective-permute-start = (bf16[192,512]{1,0:T(8,128)(2,1)S(1)}, bf16[192,512]{1,0:T(8,128)(2,1)S(1)}, u32[]{:S(2)}, u32[]{:S(2)}) collective-permute-start(bf16[192,512]{1,0:T(8,128)(2,1)S(1)} %reshape.11.refs_3_), channel_id=1, source_target_pairs={{0,4},{4,0},{8,12},{12,8},{16,20},{20,16},{24,28},{28,24},{1,5},{5... | collective-permute-start | bytes 589832 | tf_op jit(solution)/shard_map/ppermute | solution.py:24
  4.3 1.6 %collective-permute-start.1 = (bf16[192,512]{1,0:T(8,128)(2,1)S(1)}, bf16[192,512]{1,0:T(8,128)(2,1)S(1)}, u32[]{:S(2)}, u32[]{:S(2)}) collective-permute-start(bf16[192,512]{1,0:T(8,128)(2,1)S(1)} %reshape.11.refs_3_), channel_id=1, source_target_pairs={{0,8},{8,0},{4,12},{12,4},{16,24},{24,16},{20,28},{28,20},{1,9},{9... | collective-permute-start | bytes 589832 | tf_op jit(solution)/shard_map/ppermute | solution.py:24
  5.9 2.6 %collective-permute-start.2 = (bf16[192,512]{1,0:T(8,128)(2,1)S(1)}, bf16[192,512]{1,0:T(8,128)(2,1)S(1)}, u32[]{:S(2)}, u32[]{:S(2)}) collective-permute-start(bf16[192,512]{1,0:T(8,128)(2,1)S(1)} %reshape.11.refs_3_), channel_id=1, source_target_pairs={{0,16},{16,0},{4,20},{20,4},{8,24},{24,8},{12,28},{28,12},{1,17},{... | collective-permute-start | bytes 589832 | tf_op jit(solution)/shard_map/ppermute | solution.py:24
  8.5 0.7 %collective-permute-done.refs_4_ = bf16[192,512]{1,0:T(8,128)(2,1)S(1)} collective-permute-done((bf16[192,512]{1,0:T(8,128)(2,1)S(1)}, bf16[192,512]{1,0:T(8,128)(2,1)S(1)}, u32[]{:S(2)}, u32[]{:S(2)}) %collective-permute-start) | collective-permute-done | bytes 196640 | tf_op jit(solution)/shard_map/ppermute | solution.py:24
  9.2 0.0 copy-start.3
  9.2 0.0 copy-done
  9.2 0.7 %copy-done.3 = bf16[192,512]{1,0:T(8,128)(2,1)} copy-done((bf16[192,512]{1,0:T(8,128)(2,1)}, bf16[192,512]{1,0:T(8,128)(2,1)S(1)}, u32[]{:S(2)}) %copy-start.3) | copy-done | bytes 196632
  9.9 3.8 %shard_map.55 = (bf16[1,32,1024]{2,1,0:T(8,128)(2,1)}, bf16[256,1024]{1,0:T(8,128)(2,1)}) custom-call(s32[3,2,32]{2,1,0:T(2,128)} %bitcast.3, s32[3]{0:T(128)} %bitcast.5, s32[1]{0:T(128)} %bitcast.2.refs_2_, bf16[192,512]{1,0:T(8,128)(2,1)} %copy-done, bf16[192,512]{1,0:T(8,128)(2,1)} %copy-done.3, bf16[512,1024]{1,0:T(8,128)(2,1)} %constant.8.clone.refs_5_.refs_6_), custom_call_target="tpu_custom_call" | custom-call | tf_op jit(solution)/shard_map/pallas_call | solution.py:175
  13.7 1.1 %collective-permute-done.1.refs_4_ = bf16[192,512]{1,0:T(8,128)(2,1)S(1)} collective-permute-done((bf16[192,512]{1,0:T(8,128)(2,1)S(1)}, bf16[192,512]{1,0:T(8,128)(2,1)S(1)}, u32[]{:S(2)}, u32[]{:S(2)}) %collective-permute-start.1) | collective-permute-done | bytes 196640 | tf_op jit(solution)/shard_map/ppermute | solution.py:24
  14.8 0.0 copy-start.1
  14.8 2.4 %collective-permute-done.2.refs_5_ = bf16[192,512]{1,0:T(8,128)(2,1)S(1)} collective-permute-done((bf16[192,512]{1,0:T(8,128)(2,1)S(1)}, bf16[192,512]{1,0:T(8,128)(2,1)S(1)}, u32[]{:S(2)}, u32[]{:S(2)}) %collective-permute-start.2) | collective-permute-done | bytes 196640 | tf_op jit(solution)/shard_map/ppermute | solution.py:24
  17.1 0.0 copy-start.2
  17.1 0.0 copy-done.1
  17.1 0.7 %copy-done.2 = bf16[192,512]{1,0:T(8,128)(2,1)} copy-done((bf16[192,512]{1,0:T(8,128)(2,1)}, bf16[192,512]{1,0:T(8,128)(2,1)S(1)}, u32[]{:S(2)}) %copy-start.2) | copy-done | bytes 196632
  17.8 4.7 %shard_map.56 = (f32[3,8,256]{2,1,0:T(8,128)}, f32[3,8,256]{2,1,0:T(8,128)}, f32[3,8,256]{2,1,0:T(8,128)}, f32[3,8,256]{2,1,0:T(8,128)}) custom-call(s32[3,2,32]{2,1,0:T(2,128)} %bitcast.4, s32[3]{0:T(128)} %bitcast.6, s32[1]{0:T(128)} %bitcast.2.refs_2_, bf16[256,1024]{1,0:T(8,128)(2,1)} %get-tuple-element.11.refs_3_, bf16[192,512]{1,0:T(8,128)(2,1)} %copy-done.1, ...), custom_call_target="tpu_custom_call" | custom-call | tf_op jit(solution)/shard_map/pallas_call | solution.py:175
  22.5 0.0 collective-permute-start.3
  22.5 1.6 %collective-permute-start.4 = (f32[3,8,256]{2,1,0:T(8,128)}, f32[3,8,256]{2,1,0:T(8,128)S(1)}, u32[]{:S(2)}, u32[]{:S(2)}) collective-permute-start(f32[3,8,256]{2,1,0:T(8,128)} %get-tuple-element.15), channel_id=1, source_target_pairs={{0,2},{1,3},{2,0},{3,1},{4,6},{5,7},{6,4},{7,5},{8,10},{9,11},{10,... | collective-permute-start | bytes 73736 | tf_op jit(solution)/shard_map/ppermute | solution.py:188
  24.1 0.3 %collective-permute-start.5 = (f32[3,8,256]{2,1,0:T(8,128)}, f32[3,8,256]{2,1,0:T(8,128)S(1)}, u32[]{:S(2)}, u32[]{:S(2)}) collective-permute-start(f32[3,8,256]{2,1,0:T(8,128)} %get-tuple-element.16), channel_id=1, source_target_pairs={{0,3},{1,2},{2,1},{3,0},{4,7},{5,6},{6,5},{7,4},{8,11},{9,10},{10,... | collective-permute-start | bytes 73736 | tf_op jit(solution)/shard_map/ppermute | solution.py:188
  24.4 0.0 collective-permute-done.3
  24.4 2.2 %collective-permute-done.4 = f32[3,8,256]{2,1,0:T(8,128)S(1)} collective-permute-done((f32[3,8,256]{2,1,0:T(8,128)}, f32[3,8,256]{2,1,0:T(8,128)S(1)}, u32[]{:S(2)}, u32[]{:S(2)}) %collective-permute-start.4) | collective-permute-done | bytes 24608 | tf_op jit(solution)/shard_map/ppermute | solution.py:188
  26.6 0.9 %collective-permute-done.5 = f32[3,8,256]{2,1,0:T(8,128)S(1)} collective-permute-done((f32[3,8,256]{2,1,0:T(8,128)}, f32[3,8,256]{2,1,0:T(8,128)S(1)}, u32[]{:S(2)}, u32[]{:S(2)}) %collective-permute-start.5) | collective-permute-done | bytes 24608 | tf_op jit(solution)/shard_map/ppermute | solution.py:188
  27.5 1.4 %add_add_fusion = f32[3,8,256]{2,1,0:T(8,128)} fusion(f32[3,8,256]{2,1,0:T(8,128)S(1)} %collective-permute-done.5, f32[3,8,256]{2,1,0:T(8,128)S(1)} %collective-permute-done.4, f32[3,8,256]{2,1,0:T(8,128)} %get-tuple-element.13, f32[3,8,256]{2,1,0:T(8,128)S(1)} %collective-permute-done.3), kind=kLoop, calls=%fused_computation | loop fusion | flops 18432 | bytes 122880 | tf_op jit(solution)/shard_map/add | solution.py:188
Async XLA Ops:
  1.2 8.0 %copy-start = (bf16[192,512]{1,0:T(8,128)(2,1)}, bf16[192,512]{1,0:T(8,128)(2,1)S(1)}, u32[]{:S(2)}) copy-start(bf16[192,512]{1,0:T(8,128)(2,1)S(1)} %reshape.11.refs_3_) | copy-start | bytes 589828
  1.2 8.0 %collective-permute-start = (bf16[192,512]{1,0:T(8,128)(2,1)S(1)}, bf16[192,512]{1,0:T(8,128)(2,1)S(1)}, u32[]{:S(2)}, u32[]{:S(2)}) collective-permute-start(bf16[192,512]{1,0:T(8,128)(2,1)S(1)} %reshape.11.refs_3_), channel_id=1, source_target_pairs={{0,4},{4,0},{8,12},{12,8},{16,20},{20,16},{24,28},{28,24},{1,5},{5... | collective-permute-start | bytes 589832 | tf_op jit(solution)/shard_map/ppermute | solution.py:24
  4.3 10.5 %collective-permute-start.1 = (bf16[192,512]{1,0:T(8,128)(2,1)S(1)}, bf16[192,512]{1,0:T(8,128)(2,1)S(1)}, u32[]{:S(2)}, u32[]{:S(2)}) collective-permute-start(bf16[192,512]{1,0:T(8,128)(2,1)S(1)} %reshape.11.refs_3_), channel_id=1, source_target_pairs={{0,8},{8,0},{4,12},{12,4},{16,24},{24,16},{20,28},{28,20},{1,9},{9... | collective-permute-start | bytes 589832 | tf_op jit(solution)/shard_map/ppermute | solution.py:24
  5.9 11.2 %collective-permute-start.2 = (bf16[192,512]{1,0:T(8,128)(2,1)S(1)}, bf16[192,512]{1,0:T(8,128)(2,1)S(1)}, u32[]{:S(2)}, u32[]{:S(2)}) collective-permute-start(bf16[192,512]{1,0:T(8,128)(2,1)S(1)} %reshape.11.refs_3_), channel_id=1, source_target_pairs={{0,16},{16,0},{4,20},{20,4},{8,24},{24,8},{12,28},{28,12},{1,17},{... | collective-permute-start | bytes 589832 | tf_op jit(solution)/shard_map/ppermute | solution.py:24
  9.2 0.7 %copy-start.3 = (bf16[192,512]{1,0:T(8,128)(2,1)}, bf16[192,512]{1,0:T(8,128)(2,1)S(1)}, u32[]{:S(2)}) copy-start(bf16[192,512]{1,0:T(8,128)(2,1)S(1)} %collective-permute-done.refs_4_) | copy-start | bytes 589828
  14.8 2.4 %copy-start.1 = (bf16[192,512]{1,0:T(8,128)(2,1)}, bf16[192,512]{1,0:T(8,128)(2,1)S(1)}, u32[]{:S(2)}) copy-start(bf16[192,512]{1,0:T(8,128)(2,1)S(1)} %collective-permute-done.1.refs_4_) | copy-start | bytes 589828
  17.1 0.7 %copy-start.2 = (bf16[192,512]{1,0:T(8,128)(2,1)}, bf16[192,512]{1,0:T(8,128)(2,1)S(1)}, u32[]{:S(2)}) copy-start(bf16[192,512]{1,0:T(8,128)(2,1)S(1)} %collective-permute-done.2.refs_5_) | copy-start | bytes 589828
  22.5 1.9 %collective-permute-start.3 = (f32[3,8,256]{2,1,0:T(8,128)}, f32[3,8,256]{2,1,0:T(8,128)S(1)}, u32[]{:S(2)}, u32[]{:S(2)}) collective-permute-start(f32[3,8,256]{2,1,0:T(8,128)} %get-tuple-element.14), channel_id=1, source_target_pairs={{0,1},{1,0},{2,3},{3,2},{4,5},{5,4},{6,7},{7,6},{8,9},{9,8},{10,11... | collective-permute-start | bytes 73736 | tf_op jit(solution)/shard_map/ppermute | solution.py:188
  22.5 4.1 %collective-permute-start.4 = (f32[3,8,256]{2,1,0:T(8,128)}, f32[3,8,256]{2,1,0:T(8,128)S(1)}, u32[]{:S(2)}, u32[]{:S(2)}) collective-permute-start(f32[3,8,256]{2,1,0:T(8,128)} %get-tuple-element.15), channel_id=1, source_target_pairs={{0,2},{1,3},{2,0},{3,1},{4,6},{5,7},{6,4},{7,5},{8,10},{9,11},{10,... | collective-permute-start | bytes 73736 | tf_op jit(solution)/shard_map/ppermute | solution.py:188
  24.1 3.5 %collective-permute-start.5 = (f32[3,8,256]{2,1,0:T(8,128)}, f32[3,8,256]{2,1,0:T(8,128)S(1)}, u32[]{:S(2)}, u32[]{:S(2)}) collective-permute-start(f32[3,8,256]{2,1,0:T(8,128)} %get-tuple-element.16), channel_id=1, source_target_pairs={{0,3},{1,2},{2,1},{3,0},{4,7},{5,6},{6,5},{7,4},{8,11},{9,10},{10,... | collective-permute-start | bytes 73736 | tf_op jit(solution)/shard_map/ppermute | solution.py:188

commit v19 on v15

--- a/solution.py
+++ b/solution.py
@@ -197,7 +197,7 @@
     fwd_np, inv_np = half_tables(length, stations * groups * comps, LAGS)
     fwd = jnp.asarray(fwd_np)
     inv = jnp.asarray(inv_np)
-    flat = waveforms.reshape(events * chans, length)
+    flat = jnp.transpose(waveforms, (0, 2, 1, 3)).reshape(events * chans, length)
     sid = lax.axis_index("station").astype(jnp.int32).reshape(1)
     pairs = jnp.transpose(pair_lists, (0, 2, 1))
     counts = pair_counts.reshape(-1)

time: 28.8 us -> 28.5 us (0.990)
    unnamed x11 -> x10, local copies, waits for them, and re-layouts: 2.41 us -> 1.37 us
    reshape x1, local copies, waits for them, and re-layouts: 0.17 us -> 0.98 us  [shards(): jnp.transpose(waveforms, (0, 2, 1, 3)).reshape(events * chans, length)]
where the time goes in v19:
time: 28.5 us; the launch traced here: 28.3 us
  starting transfers between devices  9.09 us (32%)
  Pallas kernels  8.53 us (30%)
  waiting for transfers between devices  6.92 us (24%)
  local copies, waits for them, and re-layouts  3.1 us (11%)
  other arithmetic  0.62 us (2%)
    pallas_call x2, Pallas kernels, rounds_call(): pl.pallas_call(kernel, out_shape=out_shape, in_specs=[smem, smem, smem] +...  8.53 us
    ppermute x3, starting transfers between devices, swapped(): return lax.ppermute(block, axis, route)  7.23 us
    ppermute x3, waiting for transfers between devices, swapped(): return lax.ppermute(block, axis, route)  4.16 us
    ppermute x3, waiting for transfers between devices, station_sum(): lax.ppermute(send[j - 1], 'station', perm).astype(jnp.float32)  2.75 us
    ppermute x3, starting transfers between devices, station_sum(): lax.ppermute(send[j - 1], 'station', perm).astype(jnp.float32)  1.86 us
    unnamed x10, local copies, waits for them, and re-layouts  1.37 us
    reshape x1, local copies, waits for them, and re-layouts, shards(): jnp.transpose(waveforms, (0, 2, 1, 3)).reshape(events * chans, length)  0.98 us
    squeeze x1, local copies, waits for them, and re-layouts, station_sum(): send[j - 1]  0.75 us
  transfers between devices with their start and end apart: 6, of which 5 were waited for; matrix products, arithmetic and copies ran while one was open for 0% of the time, Pallas kernels for 13%

profile of v19, /device:TPU:0, one launch (start us, length us, event | category | flops | bytes accessed | tf_op | source)
XLA Modules:
  0.0 28.3 jit_solution(14380093063038957376)
XLA Ops:
  0.0 1.0 %reshape.11.refs_3_ = bf16[192,512]{1,0:T(8,128)(2,1)S(1)} reshape(bf16[16,3,4,512]{3,2,1,0:T(4,128)(2,1)} %bitcast.10) | data formatting | bytes 393216 | tf_op jit(solution)/shard_map/reshape | solution.py:200
  1.0 0.0 copy-start
  1.0 3.1 %collective-permute-start = (bf16[192,512]{1,0:T(8,128)(2,1)S(1)}, bf16[192,512]{1,0:T(8,128)(2,1)S(1)}, u32[]{:S(2)}, u32[]{:S(2)}) collective-permute-start(bf16[192,512]{1,0:T(8,128)(2,1)S(1)} %reshape.11.refs_3_), channel_id=1, source_target_pairs={{0,4},{4,0},{8,12},{12,8},{16,20},{20,16},{24,28},{28,24},{1,5},{5... | collective-permute-start | bytes 589832 | tf_op jit(solution)/shard_map/ppermute | solution.py:24
  4.1 1.6 %collective-permute-start.1 = (bf16[192,512]{1,0:T(8,128)(2,1)S(1)}, bf16[192,512]{1,0:T(8,128)(2,1)S(1)}, u32[]{:S(2)}, u32[]{:S(2)}) collective-permute-start(bf16[192,512]{1,0:T(8,128)(2,1)S(1)} %reshape.11.refs_3_), channel_id=1, source_target_pairs={{0,8},{8,0},{4,12},{12,4},{16,24},{24,16},{20,28},{28,20},{1,9},{9... | collective-permute-start | bytes 589832 | tf_op jit(solution)/shard_map/ppermute | solution.py:24
  5.6 2.6 %collective-permute-start.2 = (bf16[192,512]{1,0:T(8,128)(2,1)S(1)}, bf16[192,512]{1,0:T(8,128)(2,1)S(1)}, u32[]{:S(2)}, u32[]{:S(2)}) collective-permute-start(bf16[192,512]{1,0:T(8,128)(2,1)S(1)} %reshape.11.refs_3_), channel_id=1, source_target_pairs={{0,16},{16,0},{4,20},{20,4},{8,24},{24,8},{12,28},{28,12},{1,17},{... | collective-permute-start | bytes 589832 | tf_op jit(solution)/shard_map/ppermute | solution.py:24
  8.2 0.7 %collective-permute-done.refs_4_ = bf16[192,512]{1,0:T(8,128)(2,1)S(1)} collective-permute-done((bf16[192,512]{1,0:T(8,128)(2,1)S(1)}, bf16[192,512]{1,0:T(8,128)(2,1)S(1)}, u32[]{:S(2)}, u32[]{:S(2)}) %collective-permute-start) | collective-permute-done | bytes 196640 | tf_op jit(solution)/shard_map/ppermute | solution.py:24
  9.0 0.0 copy-start.3
  9.0 0.0 copy-done
  9.0 0.7 %copy-done.3 = bf16[192,512]{1,0:T(8,128)(2,1)} copy-done((bf16[192,512]{1,0:T(8,128)(2,1)}, bf16[192,512]{1,0:T(8,128)(2,1)S(1)}, u32[]{:S(2)}) %copy-start.3) | copy-done | bytes 196632
  9.6 3.8 %shard_map.55 = (bf16[1,32,1024]{2,1,0:T(8,128)(2,1)}, bf16[256,1024]{1,0:T(8,128)(2,1)}) custom-call(s32[3,2,32]{2,1,0:T(2,128)} %bitcast.11, s32[3]{0:T(128)} %bitcast.13, s32[1]{0:T(128)} %bitcast.2.refs_2_, bf16[192,512]{1,0:T(8,128)(2,1)} %copy-done, bf16[192,512]{1,0:T(8,128)(2,1)} %copy-done.3, bf16[512,1024]{1,0:T(8,128)(2,1)} %constant.8.clone.refs_5_.refs_6_), custom_call_target="tpu_custom_call" | custom-call | tf_op jit(solution)/shard_map/pallas_call | solution.py:175
  13.4 1.1 %collective-permute-done.1.refs_4_ = bf16[192,512]{1,0:T(8,128)(2,1)S(1)} collective-permute-done((bf16[192,512]{1,0:T(8,128)(2,1)S(1)}, bf16[192,512]{1,0:T(8,128)(2,1)S(1)}, u32[]{:S(2)}, u32[]{:S(2)}) %collective-permute-start.1) | collective-permute-done | bytes 196640 | tf_op jit(solution)/shard_map/ppermute | solution.py:24
  14.5 0.0 copy-start.1
  14.5 2.4 %collective-permute-done.2.refs_5_ = bf16[192,512]{1,0:T(8,128)(2,1)S(1)} collective-permute-done((bf16[192,512]{1,0:T(8,128)(2,1)S(1)}, bf16[192,512]{1,0:T(8,128)(2,1)S(1)}, u32[]{:S(2)}, u32[]{:S(2)}) %collective-permute-start.2) | collective-permute-done | bytes 196640 | tf_op jit(solution)/shard_map/ppermute | solution.py:24
  16.9 0.0 copy-start.2
  16.9 0.0 copy-done.1
  16.9 0.7 %copy-done.2 = bf16[192,512]{1,0:T(8,128)(2,1)} copy-done((bf16[192,512]{1,0:T(8,128)(2,1)}, bf16[192,512]{1,0:T(8,128)(2,1)S(1)}, u32[]{:S(2)}) %copy-start.2) | copy-done | bytes 196632
  17.6 4.7 %shard_map.56 = (f32[3,8,256]{2,1,0:T(8,128)}, bf16[3,3,8,256]{3,2,1,0:T(8,128)(2,1)}) custom-call(s32[3,2,32]{2,1,0:T(2,128)} %bitcast.12, s32[3]{0:T(128)} %bitcast.14, s32[1]{0:T(128)} %bitcast.2.refs_2_, bf16[256,1024]{1,0:T(8,128)(2,1)} %get-tuple-element.9.refs_3_, bf16[192,512]{1,0:T(8,128)(2,1)} %copy-done.1, bf16[192,512]{1,0:T(8,128)(2,1)} %copy-done.2, ...), custom_call_target="tpu_custom_call" | custom-call | tf_op jit(solution)/shard_map/pallas_call | solution.py:175
  22.3 0.0 copy-start.4
  22.3 0.7 %slice_bitcast_fusion.2 = (bf16[3,8,256]{2,1,0:T(8,128)(2,1)S(1)}, bf16[3,8,256]{2,1,0:T(8,128)(2,1)S(1)}, bf16[3,8,256]{2,1,0:T(8,128)(2,1)S(1)}) fusion(bf16[3,3,8,256]{3,2,1,0:T(8,128)(2,1)} %get-tuple-element.12), kind=kLoop, calls=%fused_computation.3 | loop fusion | bytes 73728 | tf_op jit(solution)/shard_map/squeeze | solution.py:188
  23.0 0.0 collective-permute-start.3
  23.0 1.5 %collective-permute-start.4 = (bf16[3,8,256]{2,1,0:T(8,128)(2,1)S(1)}, bf16[3,8,256]{2,1,0:T(8,128)(2,1)S(1)}, u32[]{:S(2)}, u32[]{:S(2)}) collective-permute-start(bf16[3,8,256]{2,1,0:T(8,128)(2,1)S(1)} %get-tuple-element.15), channel_id=1, source_target_pairs={{0,2},{1,3},{2,0},{3,1},{4,6},{5,7},{6,4},{7,5},{8,10},{9,11},{10,... | collective-permute-start | bytes 36872 | tf_op jit(solution)/shard_map/ppermute | solution.py:188
  24.5 0.4 %collective-permute-start.5 = (bf16[3,8,256]{2,1,0:T(8,128)(2,1)S(1)}, bf16[3,8,256]{2,1,0:T(8,128)(2,1)S(1)}, u32[]{:S(2)}, u32[]{:S(2)}) collective-permute-start(bf16[3,8,256]{2,1,0:T(8,128)(2,1)S(1)} %get-tuple-element.14), channel_id=1, source_target_pairs={{0,3},{1,2},{2,1},{3,0},{4,7},{5,6},{6,5},{7,4},{8,11},{9,10},{10,... | collective-permute-start | bytes 36872 | tf_op jit(solution)/shard_map/ppermute | solution.py:188
  24.9 0.0 collective-permute-done.3
  24.9 1.8 %collective-permute-done.4 = bf16[3,8,256]{2,1,0:T(8,128)(2,1)S(1)} collective-permute-done((bf16[3,8,256]{2,1,0:T(8,128)(2,1)S(1)}, bf16[3,8,256]{2,1,0:T(8,128)(2,1)S(1)}, u32[]{:S(2)}, u32[]{:S(2)}) %collective-permute-start.4) | collective-permute-done | bytes 12320 | tf_op jit(solution)/shard_map/ppermute | solution.py:188
  26.7 0.9 %collective-permute-done.5 = bf16[3,8,256]{2,1,0:T(8,128)(2,1)S(1)} collective-permute-done((bf16[3,8,256]{2,1,0:T(8,128)(2,1)S(1)}, bf16[3,8,256]{2,1,0:T(8,128)(2,1)S(1)}, u32[]{:S(2)}, u32[]{:S(2)}) %collective-permute-start.5) | collective-permute-done | bytes 12320 | tf_op jit(solution)/shard_map/ppermute | solution.py:188
  27.7 0.0 copy-done.4
  27.7 0.6 %convert_add_fusion = f32[3,8,256]{2,1,0:T(8,128)} fusion(bf16[3,8,256]{2,1,0:T(8,128)(2,1)S(1)} %collective-permute-done.5, bf16[3,8,256]{2,1,0:T(8,128)(2,1)S(1)} %collective-permute-done.4, f32[3,8,256]{2,1,0:T(8,128)S(1)} %copy-done.4, bf16[3,8,256]{2,1,0:T(8,128)(2,1)S(1)} %collective-permute-done.3), kind=kLoop, calls=%fused_computation | loop fusion | flops 36864 | bytes 86016 | tf_op jit(solution)/shard_map/add | solution.py:188
Async XLA Ops:
  1.0 8.0 %copy-start = (bf16[192,512]{1,0:T(8,128)(2,1)}, bf16[192,512]{1,0:T(8,128)(2,1)S(1)}, u32[]{:S(2)}) copy-start(bf16[192,512]{1,0:T(8,128)(2,1)S(1)} %reshape.11.refs_3_) | copy-start | bytes 589828
  1.0 8.0 %collective-permute-start = (bf16[192,512]{1,0:T(8,128)(2,1)S(1)}, bf16[192,512]{1,0:T(8,128)(2,1)S(1)}, u32[]{:S(2)}, u32[]{:S(2)}) collective-permute-start(bf16[192,512]{1,0:T(8,128)(2,1)S(1)} %reshape.11.refs_3_), channel_id=1, source_target_pairs={{0,4},{4,0},{8,12},{12,8},{16,20},{20,16},{24,28},{28,24},{1,5},{5... | collective-permute-start | bytes 589832 | tf_op jit(solution)/shard_map/ppermute | solution.py:24
  4.1 10.5 %collective-permute-start.1 = (bf16[192,512]{1,0:T(8,128)(2,1)S(1)}, bf16[192,512]{1,0:T(8,128)(2,1)S(1)}, u32[]{:S(2)}, u32[]{:S(2)}) collective-permute-start(bf16[192,512]{1,0:T(8,128)(2,1)S(1)} %reshape.11.refs_3_), channel_id=1, source_target_pairs={{0,8},{8,0},{4,12},{12,4},{16,24},{24,16},{20,28},{28,20},{1,9},{9... | collective-permute-start | bytes 589832 | tf_op jit(solution)/shard_map/ppermute | solution.py:24
  5.6 11.2 %collective-permute-start.2 = (bf16[192,512]{1,0:T(8,128)(2,1)S(1)}, bf16[192,512]{1,0:T(8,128)(2,1)S(1)}, u32[]{:S(2)}, u32[]{:S(2)}) collective-permute-start(bf16[192,512]{1,0:T(8,128)(2,1)S(1)} %reshape.11.refs_3_), channel_id=1, source_target_pairs={{0,16},{16,0},{4,20},{20,4},{8,24},{24,8},{12,28},{28,12},{1,17},{... | collective-permute-start | bytes 589832 | tf_op jit(solution)/shard_map/ppermute | solution.py:24
  9.0 0.7 %copy-start.3 = (bf16[192,512]{1,0:T(8,128)(2,1)}, bf16[192,512]{1,0:T(8,128)(2,1)S(1)}, u32[]{:S(2)}) copy-start(bf16[192,512]{1,0:T(8,128)(2,1)S(1)} %collective-permute-done.refs_4_) | copy-start | bytes 589828
  14.5 2.4 %copy-start.1 = (bf16[192,512]{1,0:T(8,128)(2,1)}, bf16[192,512]{1,0:T(8,128)(2,1)S(1)}, u32[]{:S(2)}) copy-start(bf16[192,512]{1,0:T(8,128)(2,1)S(1)} %collective-permute-done.1.refs_4_) | copy-start | bytes 589828
  16.9 0.7 %copy-start.2 = (bf16[192,512]{1,0:T(8,128)(2,1)}, bf16[192,512]{1,0:T(8,128)(2,1)S(1)}, u32[]{:S(2)}) copy-start(bf16[192,512]{1,0:T(8,128)(2,1)S(1)} %collective-permute-done.2.refs_5_) | copy-start | bytes 589828
  22.3 5.4 %copy-start.4 = (f32[3,8,256]{2,1,0:T(8,128)S(1)}, f32[3,8,256]{2,1,0:T(8,128)}, u32[]{:S(2)}) copy-start(f32[3,8,256]{2,1,0:T(8,128)} %get-tuple-element.11) | copy-start | bytes 73732
  23.0 1.9 %collective-permute-start.3 = (bf16[3,8,256]{2,1,0:T(8,128)(2,1)S(1)}, bf16[3,8,256]{2,1,0:T(8,128)(2,1)S(1)}, u32[]{:S(2)}, u32[]{:S(2)}) collective-permute-start(bf16[3,8,256]{2,1,0:T(8,128)(2,1)S(1)} %get-tuple-element.13), channel_id=1, source_target_pairs={{0,1},{1,0},{2,3},{3,2},{4,5},{5,4},{6,7},{7,6},{8,9},{9,8},{10,11... | collective-permute-start | bytes 36872 | tf_op jit(solution)/shard_map/ppermute | solution.py:188
  23.0 3.7 %collective-permute-start.4 = (bf16[3,8,256]{2,1,0:T(8,128)(2,1)S(1)}, bf16[3,8,256]{2,1,0:T(8,128)(2,1)S(1)}, u32[]{:S(2)}, u32[]{:S(2)}) collective-permute-start(bf16[3,8,256]{2,1,0:T(8,128)(2,1)S(1)} %get-tuple-element.15), channel_id=1, source_target_pairs={{0,2},{1,3},{2,0},{3,1},{4,6},{5,7},{6,4},{7,5},{8,10},{9,11},{10,... | collective-permute-start | bytes 36872 | tf_op jit(solution)/shard_map/ppermute | solution.py:188
  24.5 3.1 %collective-permute-start.5 = (bf16[3,8,256]{2,1,0:T(8,128)(2,1)S(1)}, bf16[3,8,256]{2,1,0:T(8,128)(2,1)S(1)}, u32[]{:S(2)}, u32[]{:S(2)}) collective-permute-start(bf16[3,8,256]{2,1,0:T(8,128)(2,1)S(1)} %get-tuple-element.14), channel_id=1, source_target_pairs={{0,3},{1,2},{2,1},{3,0},{4,7},{5,6},{6,5},{7,4},{8,11},{9,10},{10,... | collective-permute-start | bytes 36872 | tf_op jit(solution)/shard_map/ppermute | solution.py:188

commit v20 on v19

--- a/solution.py
+++ b/solution.py
@@ -197,11 +197,13 @@
     fwd_np, inv_np = half_tables(length, stations * groups * comps, LAGS)
     fwd = jnp.asarray(fwd_np)
     inv = jnp.asarray(inv_np)
-    flat = jnp.transpose(waveforms, (0, 2, 1, 3)).reshape(events * chans, length)
+    stored = jnp.transpose(waveforms, (0, 2, 1, 3))
+    flat = stored.reshape(events * chans, length)
     sid = lax.axis_index("station").astype(jnp.int32).reshape(1)
     pairs = jnp.transpose(pair_lists, (0, 2, 1))
     counts = pair_counts.reshape(-1)
-    partners = {q: swapped(flat, "region", q) for q in reversed(range(rounds))}
+    partners = {q: swapped(stored, "region", q).reshape(events * chans, length)
+                for q in reversed(range(rounds))}
     crosses, spec = rounds_call(pairs, counts, sid, flat, [partners[0]], fwd, inv,
                                 [0], events, chans, slots, groups)
     rest = list(range(1, rounds))

time: 28.5 us -> 27.7 us (0.972)
  waiting for transfers between devices: 6.92 us -> 4.7 us
  local copies, waits for them, and re-layouts: 3.1 us -> 4.59 us
    reshape x1 -> x4, local copies, waits for them, and re-layouts: 0.98 us -> 3.84 us  [the longest x3 2.16 us: shards(): swapped(stored, 'region', q).reshape(events * chans, length)]
    ppermute x3, waiting for transfers between devices: 4.16 us -> 1.95 us  [swapped(): return lax.ppermute(block, axis, route)]
    unnamed x10 -> x2, local copies, waits for them, and re-layouts: 1.37 us -> 0.01 us
  transfers between devices with their start and end apart: 6 -> 6, of which waited for: 5 -> 4; matrix products, arithmetic and copies ran while one was open for 0% -> 11% of each run, Pallas kernels for 13% -> 14%
where the time goes in v20:
time: 27.7 us; the launch traced here: 27.5 us
  starting transfers between devices  9.02 us (33%)
  Pallas kernels  8.53 us (31%)
  waiting for transfers between devices  4.7 us (17%)
  local copies, waits for them, and re-layouts  4.59 us (17%)
  other arithmetic  0.62 us (2%)
    pallas_call x2, Pallas kernels, rounds_call(): pl.pallas_call(kernel, out_shape=out_shape, in_specs=[smem, smem, smem] +...  8.53 us
    ppermute x3, starting transfers between devices, swapped(): return lax.ppermute(block, axis, route)  7.16 us
    ppermute x3, waiting for transfers between devices, station_sum(): lax.ppermute(send[j - 1], 'station', perm).astype(jnp.float32)  2.75 us
    reshape x3, local copies, waits for them, and re-layouts, shards(): swapped(stored, 'region', q).reshape(events * chans, length)  2.16 us
    ppermute x3, waiting for transfers between devices, swapped(): return lax.ppermute(block, axis, route)  1.95 us
    ppermute x3, starting transfers between devices, station_sum(): lax.ppermute(send[j - 1], 'station', perm).astype(jnp.float32)  1.86 us
    reshape x1, local copies, waits for them, and re-layouts, shards(): flat = stored.reshape(events * chans, length)  1.68 us
    squeeze x1, local copies, waits for them, and re-layouts, station_sum(): send[j - 1]  0.75 us
  transfers between devices with their start and end apart: 6, of which 4 were waited for; matrix products, arithmetic and copies ran while one was open for 11% of the time, Pallas kernels for 14%

profile of v20, /device:TPU:0, one launch (start us, length us, event | category | flops | bytes accessed | tf_op | source)
XLA Modules:
  0.0 27.5 jit_solution(2789435625618254769)
XLA Ops:
  0.0 3.0 %collective-permute-start = (bf16[16,3,4,512]{3,2,1,0:T(4,128)(2,1)}, bf16[16,3,4,512]{3,2,1,0:T(4,128)(2,1)S(1)}, u32[]{:S(2)}, u32[]{:S(2)}) collective-permute-start(bf16[16,3,4,512]{3,2,1,0:T(4,128)(2,1)} %bitcast.10), channel_id=1, source_target_pairs={{0,4},{4,0},{8,12},{12,8},{16,20},{20,16},{24,28},{28,24},{1,5},{5... | collective-permute-start | bytes 589832 | tf_op jit(solution)/shard_map/ppermute | solution.py:24
  3.0 1.6 %collective-permute-start.1 = (bf16[16,3,4,512]{3,2,1,0:T(4,128)(2,1)}, bf16[16,3,4,512]{3,2,1,0:T(4,128)(2,1)S(1)}, u32[]{:S(2)}, u32[]{:S(2)}) collective-permute-start(bf16[16,3,4,512]{3,2,1,0:T(4,128)(2,1)} %bitcast.11), channel_id=1, source_target_pairs={{0,8},{8,0},{4,12},{12,4},{16,24},{24,16},{20,28},{28,20},{1,9},{9... | collective-permute-start | bytes 589832 | tf_op jit(solution)/shard_map/ppermute | solution.py:24
  4.6 2.6 %collective-permute-start.2 = (bf16[16,3,4,512]{3,2,1,0:T(4,128)(2,1)}, bf16[16,3,4,512]{3,2,1,0:T(4,128)(2,1)S(1)}, u32[]{:S(2)}, u32[]{:S(2)}) collective-permute-start(bf16[16,3,4,512]{3,2,1,0:T(4,128)(2,1)} %bitcast.12), channel_id=1, source_target_pairs={{0,16},{16,0},{4,20},{20,4},{8,24},{24,8},{12,28},{28,12},{1,17},{... | collective-permute-start | bytes 589832 | tf_op jit(solution)/shard_map/ppermute | solution.py:24
  7.2 1.7 %reshape.20.refs_3_ = bf16[192,512]{1,0:T(8,128)(2,1)} reshape(bf16[16,3,4,512]{3,2,1,0:T(4,128)(2,1)} %bitcast.13) | data formatting | bytes 393216 | tf_op jit(solution)/shard_map/reshape | solution.py:201
  8.8 0.0 collective-permute-done
  8.8 0.7 %reshape.21.refs_4_ = bf16[192,512]{1,0:T(8,128)(2,1)} reshape(bf16[16,3,4,512]{3,2,1,0:T(4,128)(2,1)S(1)} %collective-permute-done) | data formatting | bytes 393216 | tf_op jit(solution)/shard_map/reshape | solution.py:205
  9.6 3.8 %shard_map.55 = (bf16[1,32,1024]{2,1,0:T(8,128)(2,1)}, bf16[256,1024]{1,0:T(8,128)(2,1)}) custom-call(s32[3,2,32]{2,1,0:T(2,128)} %bitcast.14, s32[3]{0:T(128)} %bitcast.16, s32[1]{0:T(128)} %bitcast.2.refs_2_, bf16[192,512]{1,0:T(8,128)(2,1)} %reshape.20.refs_3_, bf16[192,512]{1,0:T(8,128)(2,1)} %reshape.21.refs_4_, ...), custom_call_target="tpu_custom_call" | custom-call | tf_op jit(solution)/shard_map/pallas_call | solution.py:175
  13.4 0.3 %collective-permute-done.1 = bf16[16,3,4,512]{3,2,1,0:T(4,128)(2,1)S(1)} collective-permute-done((bf16[16,3,4,512]{3,2,1,0:T(4,128)(2,1)}, bf16[16,3,4,512]{3,2,1,0:T(4,128)(2,1)S(1)}, u32[]{:S(2)}, u32[]{:S(2)}) %collective-permute-start.1) | collective-permute-done | bytes 196640 | tf_op jit(solution)/shard_map/ppermute | solution.py:24
  13.7 0.7 %reshape.22.refs_4_ = bf16[192,512]{1,0:T(8,128)(2,1)} reshape(bf16[16,3,4,512]{3,2,1,0:T(4,128)(2,1)S(1)} %collective-permute-done.1) | data formatting | bytes 393216 | tf_op jit(solution)/shard_map/reshape | solution.py:205
  14.4 1.7 %collective-permute-done.2 = bf16[16,3,4,512]{3,2,1,0:T(4,128)(2,1)S(1)} collective-permute-done((bf16[16,3,4,512]{3,2,1,0:T(4,128)(2,1)}, bf16[16,3,4,512]{3,2,1,0:T(4,128)(2,1)S(1)}, u32[]{:S(2)}, u32[]{:S(2)}) %collective-permute-start.2) | collective-permute-done | bytes 196640 | tf_op jit(solution)/shard_map/ppermute | solution.py:24
  16.0 0.7 %reshape.23.refs_5_ = bf16[192,512]{1,0:T(8,128)(2,1)} reshape(bf16[16,3,4,512]{3,2,1,0:T(4,128)(2,1)S(1)} %collective-permute-done.2) | data formatting | bytes 393216 | tf_op jit(solution)/shard_map/reshape | solution.py:205
  16.8 4.7 %shard_map.56 = (f32[3,8,256]{2,1,0:T(8,128)}, bf16[3,3,8,256]{3,2,1,0:T(8,128)(2,1)}) custom-call(s32[3,2,32]{2,1,0:T(2,128)} %bitcast.15, s32[3]{0:T(128)} %bitcast.17, s32[1]{0:T(128)} %bitcast.2.refs_2_, bf16[256,1024]{1,0:T(8,128)(2,1)} %get-tuple-element.9.refs_3_, bf16[192,512]{1,0:T(8,128)(2,1)} %reshape.22.refs_4_, ...), custom_call_target="tpu_custom_call" | custom-call | tf_op jit(solution)/shard_map/pallas_call | solution.py:175
  21.5 0.0 copy-start
  21.5 0.7 %slice_bitcast_fusion.2 = (bf16[3,8,256]{2,1,0:T(8,128)(2,1)S(1)}, bf16[3,8,256]{2,1,0:T(8,128)(2,1)S(1)}, bf16[3,8,256]{2,1,0:T(8,128)(2,1)S(1)}) fusion(bf16[3,3,8,256]{3,2,1,0:T(8,128)(2,1)} %get-tuple-element.12), kind=kLoop, calls=%fused_computation.3 | loop fusion | bytes 73728 | tf_op jit(solution)/shard_map/squeeze | solution.py:188
  22.2 0.0 collective-permute-start.3
  22.2 1.5 %collective-permute-start.4 = (bf16[3,8,256]{2,1,0:T(8,128)(2,1)S(1)}, bf16[3,8,256]{2,1,0:T(8,128)(2,1)S(1)}, u32[]{:S(2)}, u32[]{:S(2)}) collective-permute-start(bf16[3,8,256]{2,1,0:T(8,128)(2,1)S(1)} %get-tuple-element.15), channel_id=1, source_target_pairs={{0,2},{1,3},{2,0},{3,1},{4,6},{5,7},{6,4},{7,5},{8,10},{9,11},{10,... | collective-permute-start | bytes 36872 | tf_op jit(solution)/shard_map/ppermute | solution.py:188
  23.7 0.4 %collective-permute-start.5 = (bf16[3,8,256]{2,1,0:T(8,128)(2,1)S(1)}, bf16[3,8,256]{2,1,0:T(8,128)(2,1)S(1)}, u32[]{:S(2)}, u32[]{:S(2)}) collective-permute-start(bf16[3,8,256]{2,1,0:T(8,128)(2,1)S(1)} %get-tuple-element.14), channel_id=1, source_target_pairs={{0,3},{1,2},{2,1},{3,0},{4,7},{5,6},{6,5},{7,4},{8,11},{9,10},{10,... | collective-permute-start | bytes 36872 | tf_op jit(solution)/shard_map/ppermute | solution.py:188
  24.1 0.0 collective-permute-done.3
  24.1 1.8 %collective-permute-done.4 = bf16[3,8,256]{2,1,0:T(8,128)(2,1)S(1)} collective-permute-done((bf16[3,8,256]{2,1,0:T(8,128)(2,1)S(1)}, bf16[3,8,256]{2,1,0:T(8,128)(2,1)S(1)}, u32[]{:S(2)}, u32[]{:S(2)}) %collective-permute-start.4) | collective-permute-done | bytes 12320 | tf_op jit(solution)/shard_map/ppermute | solution.py:188
  25.9 0.9 %collective-permute-done.5 = bf16[3,8,256]{2,1,0:T(8,128)(2,1)S(1)} collective-permute-done((bf16[3,8,256]{2,1,0:T(8,128)(2,1)S(1)}, bf16[3,8,256]{2,1,0:T(8,128)(2,1)S(1)}, u32[]{:S(2)}, u32[]{:S(2)}) %collective-permute-start.5) | collective-permute-done | bytes 12320 | tf_op jit(solution)/shard_map/ppermute | solution.py:188
  26.9 0.0 copy-done
  26.9 0.6 %convert_add_fusion = f32[3,8,256]{2,1,0:T(8,128)} fusion(bf16[3,8,256]{2,1,0:T(8,128)(2,1)S(1)} %collective-permute-done.5, bf16[3,8,256]{2,1,0:T(8,128)(2,1)S(1)} %collective-permute-done.4, f32[3,8,256]{2,1,0:T(8,128)S(1)} %copy-done, bf16[3,8,256]{2,1,0:T(8,128)(2,1)S(1)} %collective-permute-done.3), kind=kLoop, calls=%fused_computation | loop fusion | flops 36864 | bytes 86016 | tf_op jit(solution)/shard_map/add | solution.py:188
Async XLA Ops:
  0.0 8.8 %collective-permute-start = (bf16[16,3,4,512]{3,2,1,0:T(4,128)(2,1)}, bf16[16,3,4,512]{3,2,1,0:T(4,128)(2,1)S(1)}, u32[]{:S(2)}, u32[]{:S(2)}) collective-permute-start(bf16[16,3,4,512]{3,2,1,0:T(4,128)(2,1)} %bitcast.10), channel_id=1, source_target_pairs={{0,4},{4,0},{8,12},{12,8},{16,20},{20,16},{24,28},{28,24},{1,5},{5... | collective-permute-start | bytes 589832 | tf_op jit(solution)/shard_map/ppermute | solution.py:24
  3.0 10.7 %collective-permute-start.1 = (bf16[16,3,4,512]{3,2,1,0:T(4,128)(2,1)}, bf16[16,3,4,512]{3,2,1,0:T(4,128)(2,1)S(1)}, u32[]{:S(2)}, u32[]{:S(2)}) collective-permute-start(bf16[16,3,4,512]{3,2,1,0:T(4,128)(2,1)} %bitcast.11), channel_id=1, source_target_pairs={{0,8},{8,0},{4,12},{12,4},{16,24},{24,16},{20,28},{28,20},{1,9},{9... | collective-permute-start | bytes 589832 | tf_op jit(solution)/shard_map/ppermute | solution.py:24
  4.6 11.5 %collective-permute-start.2 = (bf16[16,3,4,512]{3,2,1,0:T(4,128)(2,1)}, bf16[16,3,4,512]{3,2,1,0:T(4,128)(2,1)S(1)}, u32[]{:S(2)}, u32[]{:S(2)}) collective-permute-start(bf16[16,3,4,512]{3,2,1,0:T(4,128)(2,1)} %bitcast.12), channel_id=1, source_target_pairs={{0,16},{16,0},{4,20},{20,4},{8,24},{24,8},{12,28},{28,12},{1,17},{... | collective-permute-start | bytes 589832 | tf_op jit(solution)/shard_map/ppermute | solution.py:24
  21.5 5.4 %copy-start = (f32[3,8,256]{2,1,0:T(8,128)S(1)}, f32[3,8,256]{2,1,0:T(8,128)}, u32[]{:S(2)}) copy-start(f32[3,8,256]{2,1,0:T(8,128)} %get-tuple-element.11) | copy-start | bytes 73732
  22.2 1.9 %collective-permute-start.3 = (bf16[3,8,256]{2,1,0:T(8,128)(2,1)S(1)}, bf16[3,8,256]{2,1,0:T(8,128)(2,1)S(1)}, u32[]{:S(2)}, u32[]{:S(2)}) collective-permute-start(bf16[3,8,256]{2,1,0:T(8,128)(2,1)S(1)} %get-tuple-element.13), channel_id=1, source_target_pairs={{0,1},{1,0},{2,3},{3,2},{4,5},{5,4},{6,7},{7,6},{8,9},{9,8},{10,11... | collective-permute-start | bytes 36872 | tf_op jit(solution)/shard_map/ppermute | solution.py:188
  22.2 3.7 %collective-permute-start.4 = (bf16[3,8,256]{2,1,0:T(8,128)(2,1)S(1)}, bf16[3,8,256]{2,1,0:T(8,128)(2,1)S(1)}, u32[]{:S(2)}, u32[]{:S(2)}) collective-permute-start(bf16[3,8,256]{2,1,0:T(8,128)(2,1)S(1)} %get-tuple-element.15), channel_id=1, source_target_pairs={{0,2},{1,3},{2,0},{3,1},{4,6},{5,7},{6,4},{7,5},{8,10},{9,11},{10,... | collective-permute-start | bytes 36872 | tf_op jit(solution)/shard_map/ppermute | solution.py:188
  23.7 3.1 %collective-permute-start.5 = (bf16[3,8,256]{2,1,0:T(8,128)(2,1)S(1)}, bf16[3,8,256]{2,1,0:T(8,128)(2,1)S(1)}, u32[]{:S(2)}, u32[]{:S(2)}) collective-permute-start(bf16[3,8,256]{2,1,0:T(8,128)(2,1)S(1)} %get-tuple-element.14), channel_id=1, source_target_pairs={{0,3},{1,2},{2,1},{3,0},{4,7},{5,6},{6,5},{7,4},{8,11},{9,10},{10,... | collective-permute-start | bytes 36872 | tf_op jit(solution)/shard_map/ppermute | solution.py:188

commit v21 on v20

--- a/solution.py
+++ b/solution.py
@@ -183,7 +183,8 @@
 
 def station_sum(keep, send, groups):
     total = keep
-    for j in range(1, groups):
+    order = [j for j in range(1, groups) if j & (groups // 2)] + [j for j in range(1, groups) if not j & (groups // 2)]
+    for j in order:
         perm = [(s, s ^ j) for s in range(groups)]
         total = total + lax.ppermute(send[j - 1], "station", perm).astype(jnp.float32)
     return total

time: 27.7 us -> 27.7 us (level)
  starting transfers between devices: 9.02 us -> 9.3 us
  waiting for transfers between devices: 4.7 us -> 4.42 us
    ppermute x3, waiting for transfers between devices: 2.75 us -> 2.47 us  [station_sum(): lax.ppermute(send[j - 1], 'station', perm).astype(jnp.float32)]
    ppermute x3, starting transfers between devices: 1.86 us -> 2.14 us  [station_sum(): lax.ppermute(send[j - 1], 'station', perm).astype(jnp.float32)]
where the time goes in v21:
time: 27.7 us; the launch traced here: 27.5 us
  starting transfers between devices  9.3 us (34%)
  Pallas kernels  8.53 us (31%)
  local copies, waits for them, and re-layouts  4.59 us (17%)
  waiting for transfers between devices  4.42 us (16%)
  other arithmetic  0.62 us (2%)
    pallas_call x2, Pallas kernels, rounds_call(): pl.pallas_call(kernel, out_shape=out_shape, in_specs=[smem, smem, smem] +...  8.53 us
    ppermute x3, starting transfers between devices, swapped(): return lax.ppermute(block, axis, route)  7.16 us
    ppermute x3, waiting for transfers between devices, station_sum(): lax.ppermute(send[j - 1], 'station', perm).astype(jnp.float32)  2.47 us
    reshape x3, local copies, waits for them, and re-layouts, shards(): swapped(stored, 'region', q).reshape(events * chans, length)  2.16 us
    ppermute x3, starting transfers between devices, station_sum(): lax.ppermute(send[j - 1], 'station', perm).astype(jnp.float32)  2.14 us
    ppermute x3, waiting for transfers between devices, swapped(): return lax.ppermute(block, axis, route)  1.95 us
    reshape x1, local copies, waits for them, and re-layouts, shards(): flat = stored.reshape(events * chans, length)  1.68 us
    squeeze x1, local copies, waits for them, and re-layouts, station_sum(): send[j - 1]  0.75 us
  transfers between devices with their start and end apart: 6, of which 4 were waited for; matrix products, arithmetic and copies ran while one was open for 11% of the time, Pallas kernels for 14%

profile of v21, /device:TPU:0, one launch (start us, length us, event | category | flops | bytes accessed | tf_op | source)
XLA Modules:
  0.0 27.5 jit_solution(13146792513044179061)
XLA Ops:
  0.0 3.0 %collective-permute-start = (bf16[16,3,4,512]{3,2,1,0:T(4,128)(2,1)}, bf16[16,3,4,512]{3,2,1,0:T(4,128)(2,1)S(1)}, u32[]{:S(2)}, u32[]{:S(2)}) collective-permute-start(bf16[16,3,4,512]{3,2,1,0:T(4,128)(2,1)} %bitcast.10), channel_id=1, source_target_pairs={{0,4},{4,0},{8,12},{12,8},{16,20},{20,16},{24,28},{28,24},{1,5},{5... | collective-permute-start | bytes 589832 | tf_op jit(solution)/shard_map/ppermute | solution.py:24
  3.0 1.6 %collective-permute-start.1 = (bf16[16,3,4,512]{3,2,1,0:T(4,128)(2,1)}, bf16[16,3,4,512]{3,2,1,0:T(4,128)(2,1)S(1)}, u32[]{:S(2)}, u32[]{:S(2)}) collective-permute-start(bf16[16,3,4,512]{3,2,1,0:T(4,128)(2,1)} %bitcast.11), channel_id=1, source_target_pairs={{0,8},{8,0},{4,12},{12,4},{16,24},{24,16},{20,28},{28,20},{1,9},{9... | collective-permute-start | bytes 589832 | tf_op jit(solution)/shard_map/ppermute | solution.py:24
  4.6 2.6 %collective-permute-start.2 = (bf16[16,3,4,512]{3,2,1,0:T(4,128)(2,1)}, bf16[16,3,4,512]{3,2,1,0:T(4,128)(2,1)S(1)}, u32[]{:S(2)}, u32[]{:S(2)}) collective-permute-start(bf16[16,3,4,512]{3,2,1,0:T(4,128)(2,1)} %bitcast.12), channel_id=1, source_target_pairs={{0,16},{16,0},{4,20},{20,4},{8,24},{24,8},{12,28},{28,12},{1,17},{... | collective-permute-start | bytes 589832 | tf_op jit(solution)/shard_map/ppermute | solution.py:24
  7.2 1.7 %reshape.20.refs_3_ = bf16[192,512]{1,0:T(8,128)(2,1)} reshape(bf16[16,3,4,512]{3,2,1,0:T(4,128)(2,1)} %bitcast.13) | data formatting | bytes 393216 | tf_op jit(solution)/shard_map/reshape | solution.py:202
  8.8 0.0 collective-permute-done
  8.8 0.7 %reshape.21.refs_4_ = bf16[192,512]{1,0:T(8,128)(2,1)} reshape(bf16[16,3,4,512]{3,2,1,0:T(4,128)(2,1)S(1)} %collective-permute-done) | data formatting | bytes 393216 | tf_op jit(solution)/shard_map/reshape | solution.py:206
  9.6 3.8 %shard_map.55 = (bf16[1,32,1024]{2,1,0:T(8,128)(2,1)}, bf16[256,1024]{1,0:T(8,128)(2,1)}) custom-call(s32[3,2,32]{2,1,0:T(2,128)} %bitcast.14, s32[3]{0:T(128)} %bitcast.16, s32[1]{0:T(128)} %bitcast.2.refs_2_, bf16[192,512]{1,0:T(8,128)(2,1)} %reshape.20.refs_3_, bf16[192,512]{1,0:T(8,128)(2,1)} %reshape.21.refs_4_, ...), custom_call_target="tpu_custom_call" | custom-call | tf_op jit(solution)/shard_map/pallas_call | solution.py:175
  13.4 0.3 collective-permute-done.1
  13.7 0.7 %reshape.22.refs_4_ = bf16[192,512]{1,0:T(8,128)(2,1)} reshape(bf16[16,3,4,512]{3,2,1,0:T(4,128)(2,1)S(1)} %collective-permute-done.1) | data formatting | bytes 393216 | tf_op jit(solution)/shard_map/reshape | solution.py:206
  14.4 1.7 %collective-permute-done.2 = bf16[16,3,4,512]{3,2,1,0:T(4,128)(2,1)S(1)} collective-permute-done((bf16[16,3,4,512]{3,2,1,0:T(4,128)(2,1)}, bf16[16,3,4,512]{3,2,1,0:T(4,128)(2,1)S(1)}, u32[]{:S(2)}, u32[]{:S(2)}) %collective-permute-start.2) | collective-permute-done | bytes 196640 | tf_op jit(solution)/shard_map/ppermute | solution.py:24
  16.0 0.7 %reshape.23.refs_5_ = bf16[192,512]{1,0:T(8,128)(2,1)} reshape(bf16[16,3,4,512]{3,2,1,0:T(4,128)(2,1)S(1)} %collective-permute-done.2) | data formatting | bytes 393216 | tf_op jit(solution)/shard_map/reshape | solution.py:206
  16.8 4.7 %shard_map.56 = (f32[3,8,256]{2,1,0:T(8,128)}, bf16[3,3,8,256]{3,2,1,0:T(8,128)(2,1)}) custom-call(s32[3,2,32]{2,1,0:T(2,128)} %bitcast.15, s32[3]{0:T(128)} %bitcast.17, s32[1]{0:T(128)} %bitcast.2.refs_2_, bf16[256,1024]{1,0:T(8,128)(2,1)} %get-tuple-element.9.refs_3_, bf16[192,512]{1,0:T(8,128)(2,1)} %reshape.22.refs_4_, ...), custom_call_target="tpu_custom_call" | custom-call | tf_op jit(solution)/shard_map/pallas_call | solution.py:175
  21.5 0.0 copy-start
  21.5 0.7 %slice_bitcast_fusion.2 = (bf16[3,8,256]{2,1,0:T(8,128)(2,1)S(1)}, bf16[3,8,256]{2,1,0:T(8,128)(2,1)S(1)}, bf16[3,8,256]{2,1,0:T(8,128)(2,1)S(1)}) fusion(bf16[3,3,8,256]{3,2,1,0:T(8,128)(2,1)} %get-tuple-element.12), kind=kLoop, calls=%fused_computation.3 | loop fusion | bytes 73728 | tf_op jit(solution)/shard_map/squeeze | solution.py:189
  22.2 1.5 %collective-permute-start.3 = (bf16[3,8,256]{2,1,0:T(8,128)(2,1)S(1)}, bf16[3,8,256]{2,1,0:T(8,128)(2,1)S(1)}, u32[]{:S(2)}, u32[]{:S(2)}) collective-permute-start(bf16[3,8,256]{2,1,0:T(8,128)(2,1)S(1)} %get-tuple-element.13), channel_id=1, source_target_pairs={{0,2},{1,3},{2,0},{3,1},{4,6},{5,7},{6,4},{7,5},{8,10},{9,11},{10,... | collective-permute-start | bytes 36872 | tf_op jit(solution)/shard_map/ppermute | solution.py:189
  23.7 0.0 collective-permute-start.4
  23.7 0.7 %collective-permute-start.5 = (bf16[3,8,256]{2,1,0:T(8,128)(2,1)S(1)}, bf16[3,8,256]{2,1,0:T(8,128)(2,1)S(1)}, u32[]{:S(2)}, u32[]{:S(2)}) collective-permute-start(bf16[3,8,256]{2,1,0:T(8,128)(2,1)S(1)} %get-tuple-element.14), channel_id=1, source_target_pairs={{0,1},{1,0},{2,3},{3,2},{4,5},{5,4},{6,7},{7,6},{8,9},{9,8},{10,11... | collective-permute-start | bytes 36872 | tf_op jit(solution)/shard_map/ppermute | solution.py:189
  24.4 1.6 %collective-permute-done.3 = bf16[3,8,256]{2,1,0:T(8,128)(2,1)S(1)} collective-permute-done((bf16[3,8,256]{2,1,0:T(8,128)(2,1)S(1)}, bf16[3,8,256]{2,1,0:T(8,128)(2,1)S(1)}, u32[]{:S(2)}, u32[]{:S(2)}) %collective-permute-start.3) | collective-permute-done | bytes 12320 | tf_op jit(solution)/shard_map/ppermute | solution.py:189
  25.9 0.9 %collective-permute-done.4 = bf16[3,8,256]{2,1,0:T(8,128)(2,1)S(1)} collective-permute-done((bf16[3,8,256]{2,1,0:T(8,128)(2,1)S(1)}, bf16[3,8,256]{2,1,0:T(8,128)(2,1)S(1)}, u32[]{:S(2)}, u32[]{:S(2)}) %collective-permute-start.4) | collective-permute-done | bytes 12320 | tf_op jit(solution)/shard_map/ppermute | solution.py:189
  26.9 0.0 collective-permute-done.5
  26.9 0.0 copy-done
  26.9 0.6 %convert_add_fusion = f32[3,8,256]{2,1,0:T(8,128)} fusion(bf16[3,8,256]{2,1,0:T(8,128)(2,1)S(1)} %collective-permute-done.5, bf16[3,8,256]{2,1,0:T(8,128)(2,1)S(1)} %collective-permute-done.4, f32[3,8,256]{2,1,0:T(8,128)S(1)} %copy-done, bf16[3,8,256]{2,1,0:T(8,128)(2,1)S(1)} %collective-permute-done.3), kind=kLoop, calls=%fused_computation | loop fusion | flops 36864 | bytes 86016 | tf_op jit(solution)/shard_map/add | solution.py:189
Async XLA Ops:
  0.0 8.8 %collective-permute-start = (bf16[16,3,4,512]{3,2,1,0:T(4,128)(2,1)}, bf16[16,3,4,512]{3,2,1,0:T(4,128)(2,1)S(1)}, u32[]{:S(2)}, u32[]{:S(2)}) collective-permute-start(bf16[16,3,4,512]{3,2,1,0:T(4,128)(2,1)} %bitcast.10), channel_id=1, source_target_pairs={{0,4},{4,0},{8,12},{12,8},{16,20},{20,16},{24,28},{28,24},{1,5},{5... | collective-permute-start | bytes 589832 | tf_op jit(solution)/shard_map/ppermute | solution.py:24
  3.0 10.7 %collective-permute-start.1 = (bf16[16,3,4,512]{3,2,1,0:T(4,128)(2,1)}, bf16[16,3,4,512]{3,2,1,0:T(4,128)(2,1)S(1)}, u32[]{:S(2)}, u32[]{:S(2)}) collective-permute-start(bf16[16,3,4,512]{3,2,1,0:T(4,128)(2,1)} %bitcast.11), channel_id=1, source_target_pairs={{0,8},{8,0},{4,12},{12,4},{16,24},{24,16},{20,28},{28,20},{1,9},{9... | collective-permute-start | bytes 589832 | tf_op jit(solution)/shard_map/ppermute | solution.py:24
  4.6 11.5 %collective-permute-start.2 = (bf16[16,3,4,512]{3,2,1,0:T(4,128)(2,1)}, bf16[16,3,4,512]{3,2,1,0:T(4,128)(2,1)S(1)}, u32[]{:S(2)}, u32[]{:S(2)}) collective-permute-start(bf16[16,3,4,512]{3,2,1,0:T(4,128)(2,1)} %bitcast.12), channel_id=1, source_target_pairs={{0,16},{16,0},{4,20},{20,4},{8,24},{24,8},{12,28},{28,12},{1,17},{... | collective-permute-start | bytes 589832 | tf_op jit(solution)/shard_map/ppermute | solution.py:24
  21.5 5.4 %copy-start = (f32[3,8,256]{2,1,0:T(8,128)S(1)}, f32[3,8,256]{2,1,0:T(8,128)}, u32[]{:S(2)}) copy-start(f32[3,8,256]{2,1,0:T(8,128)} %get-tuple-element.11) | copy-start | bytes 73732
  22.2 3.7 %collective-permute-start.3 = (bf16[3,8,256]{2,1,0:T(8,128)(2,1)S(1)}, bf16[3,8,256]{2,1,0:T(8,128)(2,1)S(1)}, u32[]{:S(2)}, u32[]{:S(2)}) collective-permute-start(bf16[3,8,256]{2,1,0:T(8,128)(2,1)S(1)} %get-tuple-element.13), channel_id=1, source_target_pairs={{0,2},{1,3},{2,0},{3,1},{4,6},{5,7},{6,4},{7,5},{8,10},{9,11},{10,... | collective-permute-start | bytes 36872 | tf_op jit(solution)/shard_map/ppermute | solution.py:189
  23.7 3.1 %collective-permute-start.4 = (bf16[3,8,256]{2,1,0:T(8,128)(2,1)S(1)}, bf16[3,8,256]{2,1,0:T(8,128)(2,1)S(1)}, u32[]{:S(2)}, u32[]{:S(2)}) collective-permute-start(bf16[3,8,256]{2,1,0:T(8,128)(2,1)S(1)} %get-tuple-element.15), channel_id=1, source_target_pairs={{0,3},{1,2},{2,1},{3,0},{4,7},{5,6},{6,5},{7,4},{8,11},{9,10},{10,... | collective-permute-start | bytes 36872 | tf_op jit(solution)/shard_map/ppermute | solution.py:189
  23.7 3.1 %collective-permute-start.5 = (bf16[3,8,256]{2,1,0:T(8,128)(2,1)S(1)}, bf16[3,8,256]{2,1,0:T(8,128)(2,1)S(1)}, u32[]{:S(2)}, u32[]{:S(2)}) collective-permute-start(bf16[3,8,256]{2,1,0:T(8,128)(2,1)S(1)} %get-tuple-element.14), channel_id=1, source_target_pairs={{0,1},{1,0},{2,3},{3,2},{4,5},{5,4},{6,7},{7,6},{8,9},{9,8},{10,11... | collective-permute-start | bytes 36872 | tf_op jit(solution)/shard_map/ppermute | solution.py:189
